TPU v7x, 32 devices: a whole 2x2x4 slice. The times are simulated.
32 devices in a mesh: ctx: 8 (over z, x), dp: 4 (over y, core).
Axes of the slice: x: 2, y: 2, z: 4, core: 2. Of those that a mesh axis runs over, the one named last changes fastest.
Arguments:
- queries: bfloat16 [4, 2048, 512], P('dp', 'ctx'), may hold values from -3 to 3
- keys: bfloat16 [4, 2048, 512], P('dp', 'ctx'), may hold values from -6 to 6
- values: bfloat16 [4, 2048, 512], P('dp', 'ctx'), may hold values from -6 to 6
- gates: bfloat16 [4, 2048, 512], P('dp', 'ctx'), may hold values from -6 to 6
- out_grad: bfloat16 [4, 2048, 512], P('dp', 'ctx'), may hold values from -6 to 6
- time_bucket: int32 [4, 2048], P('dp'), may hold values from 0 to 127
- lengths: int32 [4, 6], P('dp'), may hold values from 1 to 1024, 2048 in all within a row
- block_map: int32 [4, 16, 16], P('dp'), may hold values 0 or 1
- bucket_bias_matrix: bfloat16 [4, 128, 128], replicated, may hold values from 1 to 3
- w_out: bfloat16 [512, 512], replicated, may hold values from -0.25 to 0.25
Outputs:
- query_grad: bfloat16 [4, 2048, 512], P('dp', 'ctx')
- key_grad: bfloat16 [4, 2048, 512], P('dp', 'ctx')
- value_grad: bfloat16 [4, 2048, 512], P('dp', 'ctx')
- gate_grad: bfloat16 [4, 2048, 512], P('dp', 'ctx')
- w_out_grad: float32 [512, 512], P('dp')
- table_grad: float32 [4, 128, 128], replicated
Inputs may be any that keep to these rules, and one draw needn't show every extreme that they name: Each row of lengths sums to 2048, and its largest entry is 1024. `block_map`: 1 marks a visible pair of blocks.
All inputs are finite; a program needn't handle non-finite values.
Results may differ from a plain program's by a relative error of at most 0.0059.
Values may be sent and summed in bfloat16 or wider, within the bound.
No kernel may reach another device: no remote copies, remote signals or barrier semaphores. Data moves between devices by JAX's collectives and lax.ppermute only.
A program may use at most 64 MiB of HBM per device.

v0:
```python
import jax
import jax.numpy as jnp
from jax import lax
from jax.sharding import PartitionSpec as P

BLK = 128


NORM_EPSILON = 1e-05


def passed_along(value, axis, by):
    length = lax.axis_size(axis)
    pairs = [(i, i + by) for i in range(length) if 0 <= i + by < length]
    return lax.ppermute(value, axis, pairs)


def silu_slope(scores):
    sigmoid = jax.nn.sigmoid(scores)
    return sigmoid * (1.0 + scores * (1.0 - sigmoid))


def expand_blocks(block_rows, block_size):
    return jnp.repeat(jnp.repeat(block_rows, block_size, axis=0), block_size, axis=1)


def shards(
    queries,
    keys,
    values,
    gates,
    out_grad,
    time_bucket,
    lengths,
    block_map,
    bucket_bias_matrix,
    w_out,
):
    query_rows = queries[0]
    key_rows = keys[0]
    value_rows = values[0]
    gate_rows = gates[0]
    grad_rows = out_grad[0]
    local_rows, width = query_rows.shape
    head_count = bucket_bias_matrix.shape[0]
    bucket_count = bucket_bias_matrix.shape[1]
    head_dim = width // head_count
    scale = head_dim ** (-0.5)
    blocks_here = local_rows // BLK
    cycle_index = lax.axis_index("ctx")
    row_start = cycle_index * local_rows
    offsets = jnp.cumsum(lengths[0], dtype=jnp.int32) - lengths[0]

    def segment_of(positions):
        return jnp.sum(
            (positions[:, None] >= offsets[None, 1:]).astype(jnp.int32), axis=1, dtype=jnp.int32
        )

    bucket_ids = jnp.arange(bucket_count, dtype=jnp.int32)
    query_pos = row_start + jnp.arange(local_rows, dtype=jnp.int32)
    query_seg = segment_of(query_pos)
    query_bucket = lax.dynamic_slice_in_dim(time_bucket[0], row_start, local_rows, 0)
    query_bucket_indicator = (query_bucket[:, None] == bucket_ids[None, :]).astype(jnp.bfloat16)
    bias_matrix_rows = jnp.einsum(
        "lf,sfq->slq",
        query_bucket_indicator,
        bucket_bias_matrix,
        preferred_element_type=jnp.float32,
    ).astype(jnp.bfloat16)
    map_rows = lax.dynamic_slice_in_dim(block_map[0], cycle_index * blocks_here, blocks_here, 0)
    query_heads = query_rows.reshape(local_rows, head_count, head_dim)
    stacked = jnp.stack([key_rows, value_rows])
    window = [stacked, passed_along(stacked, "ctx", 1), passed_along(stacked, "ctx", 2)]
    tiles = []
    attended = jnp.zeros((local_rows, head_count, head_dim), jnp.float32)
    for distance in range(3):
        key_first = row_start - distance * local_rows
        key_pos = key_first + jnp.arange(local_rows, dtype=jnp.int32)
        safe_first = jnp.maximum(key_first, 0)
        key_bucket = lax.dynamic_slice_in_dim(time_bucket[0], safe_first, local_rows, 0)
        key_bucket_indicator = (key_bucket[:, None] == bucket_ids[None, :]).astype(jnp.bfloat16)
        map_cols = lax.dynamic_slice_in_dim(map_rows, safe_first // BLK, blocks_here, 1)
        same_block = query_pos[:, None] // BLK == key_pos[None, :] // BLK
        key_visible = (
            (query_seg[:, None] == segment_of(key_pos)[None, :])
            & (key_pos[None, :] <= query_pos[:, None])
            & (key_pos[None, :] >= 0)
            & ((expand_blocks(map_cols, BLK) == 1) | same_block)
        )
        key_bias_terms = jnp.einsum(
            "vqx,px->vqp",
            bias_matrix_rows,
            key_bucket_indicator,
            preferred_element_type=jnp.float32,
        )
        visible, bias_terms, key_bucket_indicator = (
            key_visible,
            key_bias_terms,
            key_bucket_indicator,
        )
        forward_pair = window[distance]
        forward_key_heads = forward_pair[0].reshape(local_rows, head_count, head_dim)
        forward_value_heads = forward_pair[1].reshape(local_rows, head_count, head_dim)
        forward_scores = (
            jnp.einsum(
                "ihd,jhd->hij", query_heads, forward_key_heads, preferred_element_type=jnp.float32
            )
            * scale
            + bias_terms
        )
        forward_weights = jnp.where(visible[None], jax.nn.silu(forward_scores), 0.0).astype(
            jnp.bfloat16
        )
        attended_part = jnp.einsum(
            "hij,jhd->ihd", forward_weights, forward_value_heads, preferred_element_type=jnp.float32
        )
        attended = attended + attended_part
        tiles.append((visible, forward_scores, forward_weights, key_bucket_indicator))
    attended = attended.reshape(local_rows, width)
    centered = attended - jnp.mean(attended, axis=1, keepdims=True)
    inverse = lax.rsqrt(jnp.mean(centered * centered, axis=1, keepdims=True) + NORM_EPSILON)
    normed = centered * inverse
    dz_rows = lax.dot_general(
        grad_rows, w_out, (((1,), (1,)), ((), ())), preferred_element_type=jnp.float32
    )
    gate_float = gate_rows.astype(jnp.float32)
    gate_grad = (dz_rows * normed).astype(jnp.bfloat16)
    mixed = (normed * gate_float).astype(jnp.bfloat16)
    lifted = dz_rows * gate_float
    attended_grad = (
        (
            lifted
            - jnp.mean(lifted, axis=1, keepdims=True)
            - normed * jnp.mean(lifted * normed, axis=1, keepdims=True)
        )
        * inverse
    ).astype(jnp.bfloat16)
    grad_heads = attended_grad.reshape(local_rows, head_count, head_dim)
    indicator_float = query_bucket_indicator.astype(jnp.float32)
    query_sum = jnp.zeros((local_rows, width), jnp.float32)
    table_local = jnp.zeros((head_count, bucket_count, bucket_count), jnp.float32)
    key_terms = []
    for distance in range(3):
        visible, scores, weights, key_bucket_indicator = tiles[distance]
        pair = window[distance]
        key_heads = pair[0].reshape(local_rows, head_count, head_dim)
        value_heads = pair[1].reshape(local_rows, head_count, head_dim)
        weight_grad = jnp.einsum(
            "ihd,jhd->hij", grad_heads, value_heads, preferred_element_type=jnp.float32
        )
        value_part = jnp.einsum(
            "hij,ihd->jhd", weights, grad_heads, preferred_element_type=jnp.float32
        ).reshape(local_rows, width)
        score_gradient = jnp.where(visible[None], weight_grad * silu_slope(scores), 0.0).astype(
            jnp.bfloat16
        )
        query_part = jnp.einsum(
            "hij,jhd->ihd", score_gradient, key_heads, preferred_element_type=jnp.float32
        ).reshape(local_rows, width)
        key_part = (
            jnp.einsum(
                "hij,ihd->jhd", score_gradient, query_heads, preferred_element_type=jnp.float32
            ).reshape(local_rows, width)
            * scale
        )
        bucket_share_piece = jnp.einsum(
            "rmw,wx->rmx", score_gradient, key_bucket_indicator, preferred_element_type=jnp.float32
        )
        table_part = jnp.einsum(
            "qp,cqk->cpk", indicator_float, bucket_share_piece, precision=lax.Precision.HIGHEST
        )
        query_sum = query_sum + query_part
        table_local = table_local + table_part
        key_terms.append(jnp.stack([key_part, value_part]))
    gathered = (
        key_terms[0] + passed_along(key_terms[1], "ctx", -1) + passed_along(key_terms[2], "ctx", -2)
    )
    query_grad = (query_sum * scale).astype(jnp.bfloat16)
    key_grad = gathered[0].astype(jnp.bfloat16)
    value_grad = gathered[1].astype(jnp.bfloat16)
    weight_rows = lax.psum_scatter(
        lax.dot_general(
            mixed, grad_rows, (((0,), (0,)), ((), ())), preferred_element_type=jnp.float32
        ),
        "dp",
        scatter_dimension=0,
        tiled=True,
    )
    projection_grad = lax.psum(weight_rows, "ctx")
    table_grad = lax.psum(table_local, ("ctx", "dp"))
    return (
        query_grad[None],
        key_grad[None],
        value_grad[None],
        gate_grad[None],
        projection_grad,
        table_grad,
    )


def solution(mesh):
    return jax.shard_map(
        shards,
        mesh=mesh,
        in_specs=(
            P("dp", "ctx", None),
            P("dp", "ctx", None),
            P("dp", "ctx", None),
            P("dp", "ctx", None),
            P("dp", "ctx", None),
            P("dp", None),
            P("dp", None),
            P("dp", None, None),
            P(),
            P(),
        ),
        out_specs=(
            P("dp", "ctx", None),
            P("dp", "ctx", None),
            P("dp", "ctx", None),
            P("dp", "ctx", None),
            P("dp", None),
            P(),
        ),
        check_vma=False,
    )
```

profile of v0, /device:TPU:0, one launch (start us, length us, event | category | flops | bytes accessed | tf_op | source)
XLA Modules:
  0.0 265.2 jit_solution(2168080147234761298)
XLA Ops:
  8.1 1.2 copy.148
  10.2 5.8 %collective-permute-start.1 = (bf16[2,256,512]{1,2,0:T(8,128)(2,1)}, bf16[2,256,512]{1,2,0:T(8,128)(2,1)}, u32[]{:S(2)}, u32[]{:S(2)}) collective-permute-start(bf16[2,256,512]{1,2,0:T(8,128)(2,1)} %pad_maximum_fusion.2), channel_id=1, source_target_pairs={{0,8},{4,12},{8,16},{12,20},{16,24},{20,28},{1,9},{5,13},{9,17},{1... | collective-permute-start | bytes 1572872 | tf_op jit(solution)/shard_map/ppermute | solution.py:15
  16.0 4.2 %collective-permute-start = (bf16[2,256,512]{1,2,0:T(8,128)(2,1)}, bf16[2,256,512]{1,2,0:T(8,128)(2,1)}, u32[]{:S(2)}, u32[]{:S(2)}) collective-permute-start(bf16[2,256,512]{1,2,0:T(8,128)(2,1)} %pad_maximum_fusion.2), channel_id=1, source_target_pairs={{0,4},{4,8},{8,12},{12,16},{16,20},{20,24},{24,28},{1,5},{5,9},{9,... | collective-permute-start | bytes 1572872 | tf_op jit(solution)/shard_map/ppermute | solution.py:15
  20.4 0.9 compare_bitcast_fusion.1
  24.6 1.5 select_convert_fusion.2
  28.3 1.1 fusion.66
  29.4 1.5 select_convert_fusion
  31.7 1.1 fusion.65
  32.8 1.5 select_convert_fusion.1
  36.9 0.9 fusion.20
  38.9 1.0 fusion.70
  39.9 1.9 fusion.9
  43.8 2.1 copy.129
  48.1 1.2 fusion.16
  49.3 2.3 fusion.21
  51.6 1.0 fusion.68
  52.7 1.2 copy.121
  54.0 2.1 fusion.69
  56.1 2.0 copy.125
  58.1 1.0 convolution_multiply_fusion.7
  59.1 2.0 copy.124
  61.2 1.0 convolution_multiply_fusion.6
  62.2 2.0 copy.128
  64.2 2.3 pad_maximum_fusion.1
  66.6 1.3 collective-permute-start.3
  67.9 1.1 pad_maximum_fusion
  68.9 1.4 collective-permute-start.2
  73.2 111.2 %all-reduce.5.cloned.1.call-done = f32[4,128,128]{1,2,0:T(8,128)} async-done(((f32[4,128,128]{1,2,0:T(8,128)}), f32[4,128,128]{1,2,0:T(8,128)}) %all-reduce.5.cloned.1.call-update) | async-done | bytes 262160 | tf_op jit(solution)/shard_map/psum | solution.py:190
  184.5 1.8 copy.135
  186.3 1.8 fusion.19
  189.0 67.1 %all-reduce.3.cloned.1.call-done = f32[128,512]{1,0:T(8,128)} async-done(((f32[128,512]{1,0:T(8,128)}), f32[128,512]{1,0:T(8,128)}) %all-reduce.3.cloned.1.call-update) | async-done | bytes 262160 | tf_op jit(solution)/shard_map/psum | solution.py:189
  256.1 1.7 copy.163
  (130 shorter events, 18.8 us)
Async XLA Ops:
  8.0 28.2 %copy-start = (bf16[512,512]{1,0:T(8,128)(2,1)S(1)}, bf16[512,512]{1,0:T(8,128)(2,1)}, u32[]{:S(2)}) copy-start(bf16[512,512]{1,0:T(8,128)(2,1)} %param.19) | copy-start | bytes 1572868
  8.0 1.2 copy-start.9
  8.0 176.5 %all-reduce.5.cloned.1.call-start = ((), (), s32[]{:S(2)}) async-start(), calls=%async_computation.3 | async-start | bytes 524288 | tf_op jit(solution)/shard_map/psum | solution.py:190
  10.2 18.1 %collective-permute-start.1 = (bf16[2,256,512]{1,2,0:T(8,128)(2,1)}, bf16[2,256,512]{1,2,0:T(8,128)(2,1)}, u32[]{:S(2)}, u32[]{:S(2)}) collective-permute-start(bf16[2,256,512]{1,2,0:T(8,128)(2,1)} %pad_maximum_fusion.2), channel_id=1, source_target_pairs={{0,8},{4,12},{8,16},{12,20},{16,24},{20,28},{1,9},{5,13},{9,17},{1... | collective-permute-start | bytes 1572872 | tf_op jit(solution)/shard_map/ppermute | solution.py:15
  16.0 15.7 %collective-permute-start = (bf16[2,256,512]{1,2,0:T(8,128)(2,1)}, bf16[2,256,512]{1,2,0:T(8,128)(2,1)}, u32[]{:S(2)}, u32[]{:S(2)}) collective-permute-start(bf16[2,256,512]{1,2,0:T(8,128)(2,1)} %pad_maximum_fusion.2), channel_id=1, source_target_pairs={{0,4},{4,8},{8,12},{12,16},{16,20},{20,24},{24,28},{1,5},{5,9},{9,... | collective-permute-start | bytes 1572872 | tf_op jit(solution)/shard_map/ppermute | solution.py:15
  20.2 1.6 copy-start.28
  20.3 5.8 %copy-start.7 = (bf16[256,4,128]{2,1,0:T(4,128)(2,1)}, bf16[256,4,128]{2,1,0:T(4,128)(2,1)S(1)}, u32[]{:S(2)}) copy-start(bf16[256,4,128]{2,1,0:T(4,128)(2,1)S(1)} %reshape_squeeze_stack_squeeze.9) | copy-start | bytes 786436
  20.3 2.7 %copy-start.19 = (bf16[1,256,512]{2,1,0:T(8,128)(2,1)S(1)}, bf16[1,256,512]{2,1,0:T(8,128)(2,1)}, u32[]{:S(2)}) copy-start(bf16[1,256,512]{2,1,0:T(8,128)(2,1)} %param.10) | copy-start | bytes 786436
  23.9 4.1 %copy-start.23 = (s32[1,256]{1,0:T(1,128)}, s32[1,256]{1,0:T(1,128)S(1)}, u32[]{:S(2)}) copy-start(s32[1,256]{1,0:T(1,128)S(1)} %get-tuple-element.40) | copy-start | bytes 3076
  26.5 1.0 copy-start.1
  27.4 2.0 copy-start.21
  29.4 1.5 copy-start.10
  29.4 1.5 copy-start.12
  32.8 1.5 copy-start.17
  32.8 1.5 copy-start.14
  35.4 1.0 copy-start.16
  37.8 1.0 copy-start.3
  38.9 1.0 copy-start.13
  38.9 1.0 copy-start.22
  39.9 1.9 copy-start.15
  39.9 1.9 copy-start.30
  41.8 1.0 copy-start.8
  41.9 1.3 copy-start.29
  43.8 2.1 copy-start.26
  49.3 137.0 %reduce-scatter.2.cloned.1.call-start = ((), (), s32[]{:S(2)}) async-start(), calls=%async_computation.1 | async-start | bytes 1310720 | tf_op jit(solution)/shard_map/reduce_scatter | solution.py:181
  53.9 202.1 %all-reduce.3.cloned.1.call-start = ((), (), s32[]{:S(2)}) async-start(), calls=%async_computation.2 | async-start | bytes 524288 | tf_op jit(solution)/shard_map/psum | solution.py:189
  64.2 3.6 %copy-start.5 = (f32[1,256,512]{2,1,0:T(8,128)S(1)}, f32[1,256,512]{2,1,0:T(8,128)}, u32[]{:S(2)}) copy-start(f32[1,256,512]{2,1,0:T(8,128)} %copy.125) | copy-start | bytes 1572868
  64.2 3.6 %copy-start.6 = (f32[1,256,512]{2,1,0:T(8,128)S(1)}, f32[1,256,512]{2,1,0:T(8,128)}, u32[]{:S(2)}) copy-start(f32[1,256,512]{2,1,0:T(8,128)} %copy.124) | copy-start | bytes 1572868
  66.6 119.8 %collective-permute-start.3 = (f32[2,256,512]{2,1,0:T(8,128)}, f32[2,256,512]{2,1,0:T(8,128)}, u32[]{:S(2)}, u32[]{:S(2)}) collective-permute-start(f32[2,256,512]{2,1,0:T(8,128)} %pad_maximum_fusion.1), channel_id=1, source_target_pairs={{8,0},{12,4},{16,8},{20,12},{24,16},{28,20},{9,1},{13,5},{17,9},{2... | collective-permute-start | bytes 3145736 | tf_op jit(solution)/shard_map/ppermute | solution.py:15
  68.9 1.7 copy-start.11
  68.9 117.4 %collective-permute-start.2 = (f32[2,256,512]{2,1,0:T(8,128)}, f32[2,256,512]{2,1,0:T(8,128)}, u32[]{:S(2)}, u32[]{:S(2)}) collective-permute-start(f32[2,256,512]{2,1,0:T(8,128)} %pad_maximum_fusion), channel_id=1, source_target_pairs={{4,0},{8,4},{12,8},{16,12},{20,16},{24,20},{28,24},{5,1},{9,5},{13... | collective-permute-start | bytes 3145736 | tf_op jit(solution)/shard_map/ppermute | solution.py:15
  70.7 1.0 copy-start.18
  (6 other events, 4.7 us)
Sparse Core Ops, SparseCore 0:
  49.4 135.0 all-reduce.4
Sparse Core Ops, SparseCore 1:
  54.0 33.1 reduce-scatter.1
  186.4 69.6 all-reduce.2
where the time goes:
time: 266 us; the launch traced here: 265 us
  waiting for transfers between devices  178 us (67%)
  local copies, waits for them, and re-layouts  25 us (9%)
  matrix products  23.2 us (9%)
  between operations  16.1 us (6%)
  starting transfers between devices  12.8 us (5%)
  other arithmetic  9.79 us (4%)
    psum x1, waiting for transfers between devices, shards(): table_grad = lax.psum(table_local, ('ctx', 'dp'))  111 us
    psum x1, waiting for transfers between devices, shards(): projection_grad = lax.psum(weight_rows, 'ctx')  67.1 us
    ppermute x4, starting transfers between devices, passed_along(): return lax.ppermute(value, axis, pairs)  12.6 us
    unnamed x70, local copies, waits for them, and re-layouts  9.61 us
    another operation x3, local copies, waits for them, and re-layouts, shards(): key_terms.append(jnp.stack([key_part, value_part]))  5.33 us
  transfers between devices with their start and end apart: 7, of which 2 were waited for; matrix products, arithmetic and copies ran while one was open for 13% of the time, Pallas kernels for 0%

commit v1 on v0

--- a/solution.py
+++ b/solution.py
@@ -13,6 +13,51 @@
     length = lax.axis_size(axis)
     pairs = [(i, i + by) for i in range(length) if 0 <= i + by < length]
     return lax.ppermute(value, axis, pairs)
+
+
+def exchanged(value, axis, mask):
+    length = lax.axis_size(axis)
+    pairs = [(i, i ^ mask) for i in range(length)]
+    return lax.ppermute(value, axis, pairs)
+
+
+def axis_bits(axis):
+    length = lax.axis_size(axis)
+    bits = []
+    mask = 1
+    while mask < length:
+        bits.append(mask)
+        mask *= 2
+    return bits
+
+
+def scatter_blocks(blocks, axis):
+    index = lax.axis_index(axis)
+    for mask in axis_bits(axis):
+        bit = (index // mask) % 2
+        pairs = blocks.reshape(blocks.shape[0] // 2, 2, blocks.shape[1])
+        keep = lax.dynamic_index_in_dim(pairs, bit, axis=1, keepdims=False)
+        send = lax.dynamic_index_in_dim(pairs, 1 - bit, axis=1, keepdims=False)
+        blocks = keep + exchanged(send, axis, mask)
+    return blocks[0]
+
+
+def gather_blocks(chunk, axis):
+    index = lax.axis_index(axis)
+    held = chunk[None]
+    for mask in reversed(axis_bits(axis)):
+        bit = (index // mask) % 2
+        other = exchanged(held, axis, mask)
+        low = jnp.where(bit == 0, held, other)
+        high = jnp.where(bit == 0, other, held)
+        held = jnp.stack([low, high], axis=1).reshape(held.shape[0] * 2, held.shape[1])
+    return held
+
+
+def summed_over(flat, axis):
+    size = lax.axis_size(axis)
+    part = scatter_blocks(flat.reshape(size, flat.shape[0] // size), axis)
+    return gather_blocks(part, axis).reshape(flat.shape)
 
 
 def silu_slope(scores):
@@ -178,16 +223,15 @@
     query_grad = (query_sum * scale).astype(jnp.bfloat16)
     key_grad = gathered[0].astype(jnp.bfloat16)
     value_grad = gathered[1].astype(jnp.bfloat16)
-    weight_rows = lax.psum_scatter(
-        lax.dot_general(
-            mixed, grad_rows, (((0,), (0,)), ((), ())), preferred_element_type=jnp.float32
-        ),
-        "dp",
-        scatter_dimension=0,
-        tiled=True,
-    )
-    projection_grad = lax.psum(weight_rows, "ctx")
-    table_grad = lax.psum(table_local, ("ctx", "dp"))
+    dp_size = lax.axis_size("dp")
+    weight_term = lax.dot_general(
+        mixed, grad_rows, (((0,), (0,)), ((), ())), preferred_element_type=jnp.float32
+    )
+    weight_rows = scatter_blocks(weight_term.reshape(dp_size, -1), "dp")
+    projection_grad = summed_over(weight_rows, "ctx").reshape(width // dp_size, width)
+    table_rows = scatter_blocks(table_local.reshape(dp_size, -1), "dp")
+    table_rows = summed_over(table_rows, "ctx")
+    table_grad = gather_blocks(table_rows, "dp").reshape(table_local.shape)
     return (
         query_grad[None],
         key_grad[None],

time: 266 us -> 176 us (0.66)
  waiting for transfers between devices: 178 us -> 58.9 us
  starting transfers between devices: 12.8 us -> 44.6 us
  between operations: 16.1 us -> 1.7 us
  local copies, waits for them, and re-layouts: 25 us -> 32.8 us
  other arithmetic: 9.79 us -> 14 us
    psum x2 -> x0, waiting for transfers between devices: 178 us -> none  [the longest x1 111 us: shards(): table_grad = lax.psum(table_local, ('ctx', 'dp'))]
    ppermute x0 -> x18, waiting for transfers between devices: none -> 58.9 us  [exchanged(): return lax.ppermute(value, axis, pairs)]
    ppermute x0 -> x18, starting transfers between devices: none -> 32.1 us  [exchanged(): return lax.ppermute(value, axis, pairs)]
    another operation x0 -> x17, local copies, waits for them, and re-layouts: none -> 5.69 us  [the longest x4 3.07 us: scatter_blocks(): pairs = blocks.reshape(blocks.shape[0] // 2, 2, blocks.shape[1])]
    dynamic_slice x0 -> x6, local copies, waits for them, and re-layouts: none -> 4.21 us  [scatter_blocks(): keep = lax.dynamic_index_in_dim(pairs, bit, axis=1, keepdims=False)]
    add x0 -> x10, other arithmetic: none -> 3.95 us  [scatter_blocks(): blocks = keep + exchanged(send, axis, mask)]
    another operation x3, local copies, waits for them, and re-layouts: 5.33 us -> 2.19 us  [shards(): key_terms.append(jnp.stack([key_part, value_part]))]
    unnamed x70 -> x100, local copies, waits for them, and re-layouts: 9.61 us -> 9.95 us
  transfers between devices with their start and end apart: 7 -> 22, of which waited for: 2 -> 12; matrix products, arithmetic and copies ran while one was open for 13% -> 24% of each run, Pallas kernels for 0% -> 0%
where the time goes in v1:
time: 176 us; the launch traced here: 175 us
  waiting for transfers between devices  58.9 us (33%)
  starting transfers between devices  44.6 us (25%)
  local copies, waits for them, and re-layouts  32.8 us (19%)
  matrix products  23.3 us (13%)
  other arithmetic  14 us (8%)
    ppermute x18, waiting for transfers between devices, exchanged(): return lax.ppermute(value, axis, pairs)  58.9 us
    ppermute x18, starting transfers between devices, exchanged(): return lax.ppermute(value, axis, pairs)  32.1 us
    ppermute x4, starting transfers between devices, passed_along(): return lax.ppermute(value, axis, pairs)  12.5 us
    unnamed x100, local copies, waits for them, and re-layouts  9.95 us
    dynamic_slice x6, local copies, waits for them, and re-layouts, scatter_blocks(): keep = lax.dynamic_index_in_dim(pairs, bit, axis=1, keepdims=False)  4.21 us
    add x10, other arithmetic, scatter_blocks(): blocks = keep + exchanged(send, axis, mask)  3.95 us
  transfers between devices with their start and end apart: 22, of which 12 were waited for; matrix products, arithmetic and copies ran while one was open for 24% of the time, Pallas kernels for 0%

profile of v1, /device:TPU:0, one launch (start us, length us, event | category | flops | bytes accessed | tf_op | source)
XLA Modules:
  0.0 175.3 jit_solution(7198211605460076543)
XLA Ops:
  2.8 5.8 %collective-permute-start.1 = (bf16[2,256,512]{1,2,0:T(8,128)(2,1)}, bf16[2,256,512]{1,2,0:T(8,128)(2,1)}, u32[]{:S(2)}, u32[]{:S(2)}) collective-permute-start(bf16[2,256,512]{1,2,0:T(8,128)(2,1)} %pad_maximum_fusion.2), channel_id=1, source_target_pairs={{0,8},{4,12},{8,16},{12,20},{16,24},{20,28},{1,9},{5,13},{9,17},{1... | collective-permute-start | bytes 1572872 | tf_op jit(solution)/shard_map/ppermute | solution.py:15
  8.6 4.2 %collective-permute-start = (bf16[2,256,512]{1,2,0:T(8,128)(2,1)}, bf16[2,256,512]{1,2,0:T(8,128)(2,1)}, u32[]{:S(2)}, u32[]{:S(2)}) collective-permute-start(bf16[2,256,512]{1,2,0:T(8,128)(2,1)} %pad_maximum_fusion.2), channel_id=1, source_target_pairs={{0,4},{4,8},{8,12},{12,16},{16,20},{20,24},{24,28},{1,5},{5,9},{9,... | collective-permute-start | bytes 1572872 | tf_op jit(solution)/shard_map/ppermute | solution.py:15
  17.2 1.5 select_convert_fusion.2
  22.9 1.5 select_convert_fusion
  25.8 1.5 select_convert_fusion.1
  28.5 1.4 fusion.30
  44.8 2.7 %reshape_reshape.9 = f32[2,2,65536]{2,1,0:T(2,128)} reshape(f32[512,512]{1,0:T(8,128)} %fusion.21) | data formatting | bytes 2097152 | tf_op jit(solution)/shard_map/reshape;reshape | solution.py:38
  47.5 3.5 %constant_dynamic-slice_fusion.15 = (f32[2,1,65536]{2,1,0:T(1,128)S(1)}, f32[2,1,65536]{2,1,0:T(1,128)}) fusion(f32[2,2,65536]{2,1,0:T(2,128)} %reshape_reshape.9, s32[]{:T(128)S(6)} %select_n.340, s32[]{:T(128)S(6)} %select_n.341), kind=kLoop, calls=%fused_computation.158 | loop fusion | bytes 2097160 | tf_op jit(solution)/shard_map/jit(dynamic_index_in_dim)/dynamic_slice | solution.py:39
  54.3 1.6 collective-permute-start.13
  57.0 1.7 collective-permute-done.13
  59.1 7.3 %collective-permute-start.14 = (f32[4,2048]{1,0:T(4,128)S(1)}, f32[4,2048]{1,0:T(4,128)S(1)}, u32[]{:S(2)}, u32[]{:S(2)}) collective-permute-start(f32[4,2048]{1,0:T(4,128)S(1)} %bitcast.298), channel_id=1, source_target_pairs={{0,4},{4,0},{8,12},{12,8},{16,20},{20,16},{24,28},{28,24},{1,5},{5... | collective-permute-start | bytes 98312 | tf_op jit(solution)/shard_map/ppermute | solution.py:21
  68.4 4.0 %collective-permute-start.15 = (f32[2,2048]{1,0:T(2,128)S(1)}, f32[2,2048]{1,0:T(2,128)S(1)}, u32[]{:S(2)}, u32[]{:S(2)}) collective-permute-start(f32[2,2048]{1,0:T(2,128)S(1)} %bitcast.303), channel_id=1, source_target_pairs={{0,8},{4,12},{8,0},{12,4},{16,24},{20,28},{24,16},{28,20},{1,9},{5... | collective-permute-start | bytes 49160 | tf_op jit(solution)/shard_map/ppermute | solution.py:21
  74.2 3.1 %collective-permute-start.16 = (f32[1,2048]{1,0:T(1,128)S(1)}, f32[1,2048]{1,0:T(1,128)S(1)}, u32[]{:S(2)}, u32[]{:S(2)}) collective-permute-start(f32[1,2048]{1,0:T(1,128)S(1)} %constant_dynamic-slice_fusion), channel_id=1, source_target_pairs={{0,16},{4,20},{8,24},{12,28},{16,0},{20,4},{24,8},{28,12},{1,17},{... | collective-permute-start | bytes 24584 | tf_op jit(solution)/shard_map/ppermute | solution.py:21
  82.6 2.1 %copy.182 = f32[1,256,512]{2,1,0:T(8,128)} copy(f32[1,256,512]{1,2,0:T(8,128)} %bitcast.284) | data formatting | bytes 1048576 | tf_op jit(solution)/shard_map/mul | solution.py:206
  85.8 2.3 %copy.247 = f32[2,1,65536]{2,0,1:T(2,128)} copy(f32[2,1,65536]{2,1,0:T(1,128)} %get-tuple-element.38) | data formatting | bytes 1048576
  90.6 2.1 %collective-permute-done.17 = f32[1,2048]{1,0:T(1,128)S(1)} collective-permute-done((f32[1,2048]{1,0:T(1,128)S(1)}, f32[1,2048]{1,0:T(1,128)S(1)}, u32[]{:S(2)}, u32[]{:S(2)}) %collective-permute-start.17) | collective-permute-done | bytes 8224 | tf_op jit(solution)/shard_map/ppermute | solution.py:21
  92.8 1.6 collective-permute-start.18
  96.8 21.0 %collective-permute-done.18 = f32[2,2048]{1,0:T(2,128)S(1)} collective-permute-done((f32[2,2048]{1,0:T(2,128)S(1)}, f32[2,2048]{1,0:T(2,128)S(1)}, u32[]{:S(2)}, u32[]{:S(2)}) %collective-permute-start.18) | collective-permute-done | bytes 16416 | tf_op jit(solution)/shard_map/ppermute | solution.py:21
  118.0 1.6 bitcast_add_fusion
  119.8 1.6 collective-permute-start.5
  121.4 18.1 %collective-permute-done.19 = f32[4,2048]{1,0:T(4,128)S(1)} collective-permute-done((f32[4,2048]{1,0:T(4,128)S(1)}, f32[4,2048]{1,0:T(4,128)S(1)}, u32[]{:S(2)}, u32[]{:S(2)}) %collective-permute-start.19) | collective-permute-done | bytes 32800 | tf_op jit(solution)/shard_map/ppermute | solution.py:21
  139.8 1.6 collective-permute-start.20
  142.7 2.5 %collective-permute-start.6 = (f32[4,8192]{1,0:T(4,128)S(1)}, f32[4,8192]{1,0:T(4,128)S(1)}, u32[]{:S(2)}, u32[]{:S(2)}) collective-permute-start(f32[4,8192]{1,0:T(4,128)S(1)} %bitcast.296), channel_id=1, source_target_pairs={{0,4},{4,0},{8,12},{12,8},{16,20},{20,16},{24,28},{28,24},{1,5},{5... | collective-permute-start | bytes 393224 | tf_op jit(solution)/shard_map/ppermute | solution.py:21
  145.3 3.3 %collective-permute-done.6 = f32[4,8192]{1,0:T(4,128)S(1)} collective-permute-done((f32[4,8192]{1,0:T(4,128)S(1)}, f32[4,8192]{1,0:T(4,128)S(1)}, u32[]{:S(2)}, u32[]{:S(2)}) %collective-permute-start.6) | collective-permute-done | bytes 131104 | tf_op jit(solution)/shard_map/ppermute | solution.py:21
  150.0 3.4 %collective-permute-done.7 = f32[2,8192]{1,0:T(2,128)S(1)} collective-permute-done((f32[2,8192]{1,0:T(2,128)S(1)}, f32[2,8192]{1,0:T(2,128)S(1)}, u32[]{:S(2)}, u32[]{:S(2)}) %collective-permute-start.7) | collective-permute-done | bytes 65568 | tf_op jit(solution)/shard_map/ppermute | solution.py:21
  153.5 3.0 %collective-permute-start.8 = (f32[1,8192]{1,0:T(1,128)S(1)}, f32[1,8192]{1,0:T(1,128)S(1)}, u32[]{:S(2)}, u32[]{:S(2)}) collective-permute-start(f32[1,8192]{1,0:T(1,128)S(1)} %constant_dynamic-slice_fusion.8), channel_id=1, source_target_pairs={{0,16},{4,20},{8,24},{12,28},{16,0},{20,4},{24,8},{28,12},{1,17},{... | collective-permute-start | bytes 98312 | tf_op jit(solution)/shard_map/ppermute | solution.py:21
  156.9 1.8 %collective-permute-done.8 = f32[1,8192]{1,0:T(1,128)S(1)} collective-permute-done((f32[1,8192]{1,0:T(1,128)S(1)}, f32[1,8192]{1,0:T(1,128)S(1)}, u32[]{:S(2)}, u32[]{:S(2)}) %collective-permute-start.8) | collective-permute-done | bytes 32800 | tf_op jit(solution)/shard_map/ppermute | solution.py:21
  158.8 2.6 %collective-permute-start.9 = (f32[1,8192]{1,0:T(1,128)S(1)}, f32[1,8192]{1,0:T(1,128)S(1)}, u32[]{:S(2)}, u32[]{:S(2)}) collective-permute-start(f32[1,8192]{1,0:T(1,128)S(1)} %dynamic-slice_add_fusion), channel_id=1, source_target_pairs={{0,16},{4,20},{8,24},{12,28},{16,0},{20,4},{24,8},{28,12},{1,17},{... | collective-permute-start | bytes 98312 | tf_op jit(solution)/shard_map/ppermute | solution.py:21
  164.3 1.8 %fusion.19 = bf16[2,256,512]{2,1,0:T(8,128)(2,1)S(1)} fusion(f32[2,256,512]{2,1,0:T(8,128)} %collective-permute-done.3, f32[2,256,512]{2,1,0:T(8,128)} %collective-permute-done.2, f32[1,256,512]{2,1,0:T(8,128)S(1)} %copy.179, f32[1,256,512]{2,1,0:T(8,128)S(1)} %copy.178), kind=kLoop, calls=%fused_computation.39 | loop fusion | flops 1048576 | bytes 3670016 | tf_op jit(solution)/shard_map/convert.3
  166.1 2.2 %collective-permute-done.10 = f32[2,8192]{1,0:T(2,128)S(1)} collective-permute-done((f32[2,8192]{1,0:T(2,128)S(1)}, f32[2,8192]{1,0:T(2,128)S(1)}, u32[]{:S(2)}, u32[]{:S(2)}) %collective-permute-start.10) | collective-permute-done | bytes 65568 | tf_op jit(solution)/shard_map/ppermute | solution.py:21
  168.8 1.8 %collective-permute-start.11 = (f32[4,8192]{1,0:T(4,128)S(1)}, f32[4,8192]{1,0:T(4,128)S(1)}, u32[]{:S(2)}, u32[]{:S(2)}) collective-permute-start(f32[4,8192]{1,0:T(4,128)S(1)} %reshape.738), channel_id=1, source_target_pairs={{0,4},{4,0},{8,12},{12,8},{16,20},{20,16},{24,28},{28,24},{1,5},{5... | collective-permute-start | bytes 393224 | tf_op jit(solution)/shard_map/ppermute | solution.py:21
  171.4 2.4 %collective-permute-done.11 = f32[4,8192]{1,0:T(4,128)S(1)} collective-permute-done((f32[4,8192]{1,0:T(4,128)S(1)}, f32[4,8192]{1,0:T(4,128)S(1)}, u32[]{:S(2)}, u32[]{:S(2)}) %collective-permute-start.11) | collective-permute-done | bytes 131104 | tf_op jit(solution)/shard_map/ppermute | solution.py:21
  (245 shorter events, 56.7 us)
Async XLA Ops:
  0.6 27.8 %copy-start = (bf16[512,512]{1,0:T(8,128)(2,1)S(1)}, bf16[512,512]{1,0:T(8,128)(2,1)}, u32[]{:S(2)}) copy-start(bf16[512,512]{1,0:T(8,128)(2,1)} %param.19) | copy-start | bytes 1572868
  2.8 19.0 %collective-permute-start.1 = (bf16[2,256,512]{1,2,0:T(8,128)(2,1)}, bf16[2,256,512]{1,2,0:T(8,128)(2,1)}, u32[]{:S(2)}, u32[]{:S(2)}) collective-permute-start(bf16[2,256,512]{1,2,0:T(8,128)(2,1)} %pad_maximum_fusion.2), channel_id=1, source_target_pairs={{0,8},{4,12},{8,16},{12,20},{16,24},{20,28},{1,9},{5,13},{9,17},{1... | collective-permute-start | bytes 1572872 | tf_op jit(solution)/shard_map/ppermute | solution.py:15
  8.6 16.1 %collective-permute-start = (bf16[2,256,512]{1,2,0:T(8,128)(2,1)}, bf16[2,256,512]{1,2,0:T(8,128)(2,1)}, u32[]{:S(2)}, u32[]{:S(2)}) collective-permute-start(bf16[2,256,512]{1,2,0:T(8,128)(2,1)} %pad_maximum_fusion.2), channel_id=1, source_target_pairs={{0,4},{4,8},{8,12},{12,16},{16,20},{20,24},{24,28},{1,5},{5,9},{9,... | collective-permute-start | bytes 1572872 | tf_op jit(solution)/shard_map/ppermute | solution.py:15
  12.9 5.8 %copy-start.18 = (bf16[256,4,128]{2,1,0:T(4,128)(2,1)}, bf16[256,4,128]{2,1,0:T(4,128)(2,1)S(1)}, u32[]{:S(2)}) copy-start(bf16[256,4,128]{2,1,0:T(4,128)(2,1)S(1)} %reshape_squeeze_stack_squeeze.9) | copy-start | bytes 786436
  16.4 4.6 %copy-start.35 = (s32[1,256]{1,0:T(1,128)}, s32[1,256]{1,0:T(1,128)S(1)}, u32[]{:S(2)}) copy-start(s32[1,256]{1,0:T(1,128)S(1)} %get-tuple-element.77) | copy-start | bytes 3076
  43.3 9.9 %collective-permute-start.12 = (f32[2,16384]{1,0:T(2,128)}, f32[2,16384]{1,0:T(2,128)}, u32[]{:S(2)}, u32[]{:S(2)}) collective-permute-start(f32[2,16384]{1,0:T(2,128)} %bitcast.258), channel_id=1, source_target_pairs={{0,1},{1,0},{2,3},{3,2},{4,5},{5,4},{6,7},{7,6},{8,9},{9,8},{10,11... | collective-permute-start | bytes 393224 | tf_op jit(solution)/shard_map/ppermute | solution.py:21
  47.5 3.5 %copy-start.12 = (f32[256,4,128]{0,2,1:T(8,128)S(1)}, f32[256,4,128]{0,2,1:T(8,128)}, u32[]{:S(2)}) copy-start(f32[256,4,128]{0,2,1:T(8,128)} %convolution_bitcast_fusion.2) | copy-start | bytes 1572868
  47.5 3.5 %copy-start.13 = (f32[256,4,128]{0,2,1:T(8,128)S(1)}, f32[256,4,128]{0,2,1:T(8,128)}, u32[]{:S(2)}) copy-start(f32[256,4,128]{0,2,1:T(8,128)} %convolution_bitcast_fusion) | copy-start | bytes 1572868
  47.5 3.5 %copy-start.30 = (bf16[1,256,512]{1,2,0:T(8,128)(2,1)S(1)}, bf16[1,256,512]{1,2,0:T(8,128)(2,1)}, u32[]{:S(2)}) copy-start(bf16[1,256,512]{1,2,0:T(8,128)(2,1)} %copy-done.29) | copy-start | bytes 786436
  53.2 2.8 %copy-start.3 = (bf16[4,256,256]{2,1,0:T(8,128)(2,1)S(1)}, bf16[4,256,256]{2,1,0:T(8,128)(2,1)}, u32[]{:S(2)}) copy-start(bf16[4,256,256]{2,1,0:T(8,128)(2,1)} %copy-done.2) | copy-start | bytes 1572868
  54.3 4.4 %collective-permute-start.13 = (f32[1,16384]{1,0:T(1,128)S(1)}, f32[1,16384]{1,0:T(1,128)S(1)}, u32[]{:S(2)}, u32[]{:S(2)}) collective-permute-start(f32[1,16384]{1,0:T(1,128)S(1)} %constant_dynamic-slice_fusion.5), channel_id=1, source_target_pairs={{0,2},{1,3},{2,0},{3,1},{4,6},{5,7},{6,4},{7,5},{8,10},{9,11},{10,... | collective-permute-start | bytes 196616 | tf_op jit(solution)/shard_map/ppermute | solution.py:21
  59.1 9.2 %collective-permute-start.14 = (f32[4,2048]{1,0:T(4,128)S(1)}, f32[4,2048]{1,0:T(4,128)S(1)}, u32[]{:S(2)}, u32[]{:S(2)}) collective-permute-start(f32[4,2048]{1,0:T(4,128)S(1)} %bitcast.298), channel_id=1, source_target_pairs={{0,4},{4,0},{8,12},{12,8},{16,20},{20,16},{24,28},{28,24},{1,5},{5... | collective-permute-start | bytes 98312 | tf_op jit(solution)/shard_map/ppermute | solution.py:21
  68.4 5.7 %collective-permute-start.15 = (f32[2,2048]{1,0:T(2,128)S(1)}, f32[2,2048]{1,0:T(2,128)S(1)}, u32[]{:S(2)}, u32[]{:S(2)}) collective-permute-start(f32[2,2048]{1,0:T(2,128)S(1)} %bitcast.303), channel_id=1, source_target_pairs={{0,8},{4,12},{8,0},{12,4},{16,24},{20,28},{24,16},{28,20},{1,9},{5... | collective-permute-start | bytes 49160 | tf_op jit(solution)/shard_map/ppermute | solution.py:21
  74.2 4.1 %copy-start.4 = (f32[4,128,256]{2,1,0:T(8,128)S(1)}, f32[4,128,256]{2,1,0:T(8,128)}, u32[]{:S(2)}) copy-start(f32[4,128,256]{2,1,0:T(8,128)} %fusion.76) | copy-start | bytes 1572868
  74.2 13.9 %collective-permute-start.16 = (f32[1,2048]{1,0:T(1,128)S(1)}, f32[1,2048]{1,0:T(1,128)S(1)}, u32[]{:S(2)}, u32[]{:S(2)}) collective-permute-start(f32[1,2048]{1,0:T(1,128)S(1)} %constant_dynamic-slice_fusion), channel_id=1, source_target_pairs={{0,16},{4,20},{8,24},{12,28},{16,0},{20,4},{24,8},{28,12},{1,17},{... | collective-permute-start | bytes 24584 | tf_op jit(solution)/shard_map/ppermute | solution.py:21
  88.1 30.0 %collective-permute-start.4 = (f32[2,65536]{1,0:T(2,128)}, f32[2,65536]{1,0:T(2,128)}, u32[]{:S(2)}, u32[]{:S(2)}) collective-permute-start(f32[2,65536]{1,0:T(2,128)} %bitcast.257), channel_id=1, source_target_pairs={{0,1},{1,0},{2,3},{3,2},{4,5},{5,4},{6,7},{7,6},{8,9},{9,8},{10,11... | collective-permute-start | bytes 1572872 | tf_op jit(solution)/shard_map/ppermute | solution.py:21
  88.1 6.3 %copy-start.14 = (f32[1,256,512]{2,1,0:T(8,128)S(1)}, f32[1,256,512]{2,1,0:T(8,128)}, u32[]{:S(2)}) copy-start(f32[1,256,512]{2,1,0:T(8,128)} %copy.183) | copy-start | bytes 1572868
  88.1 6.3 %copy-start.15 = (f32[1,256,512]{2,1,0:T(8,128)S(1)}, f32[1,256,512]{2,1,0:T(8,128)}, u32[]{:S(2)}) copy-start(f32[1,256,512]{2,1,0:T(8,128)} %copy.182) | copy-start | bytes 1572868
  88.1 4.6 %collective-permute-start.17 = (f32[1,2048]{1,0:T(1,128)S(1)}, f32[1,2048]{1,0:T(1,128)S(1)}, u32[]{:S(2)}, u32[]{:S(2)}) collective-permute-start(f32[1,2048]{1,0:T(1,128)S(1)} %dynamic-slice_add_fusion.1), channel_id=1, source_target_pairs={{0,16},{4,20},{8,24},{12,28},{16,0},{20,4},{24,8},{28,12},{1,17},{... | collective-permute-start | bytes 24584 | tf_op jit(solution)/shard_map/ppermute | solution.py:21
  89.3 75.0 %collective-permute-start.3 = (f32[2,256,512]{2,1,0:T(8,128)}, f32[2,256,512]{2,1,0:T(8,128)}, u32[]{:S(2)}, u32[]{:S(2)}) collective-permute-start(f32[2,256,512]{2,1,0:T(8,128)} %pad_maximum_fusion.1), channel_id=1, source_target_pairs={{8,0},{12,4},{16,8},{20,12},{24,16},{28,20},{9,1},{13,5},{17,9},{2... | collective-permute-start | bytes 3145736 | tf_op jit(solution)/shard_map/ppermute | solution.py:15
  92.8 25.0 %collective-permute-start.18 = (f32[2,2048]{1,0:T(2,128)S(1)}, f32[2,2048]{1,0:T(2,128)S(1)}, u32[]{:S(2)}, u32[]{:S(2)}) collective-permute-start(f32[2,2048]{1,0:T(2,128)S(1)} %maximum_bitcast_fusion.2), channel_id=1, source_target_pairs={{0,8},{4,12},{8,0},{12,4},{16,24},{20,28},{24,16},{28,20},{1,9},{5... | collective-permute-start | bytes 49160 | tf_op jit(solution)/shard_map/ppermute | solution.py:21
  95.5 68.8 %collective-permute-start.2 = (f32[2,256,512]{2,1,0:T(8,128)}, f32[2,256,512]{2,1,0:T(8,128)}, u32[]{:S(2)}, u32[]{:S(2)}) collective-permute-start(f32[2,256,512]{2,1,0:T(8,128)} %pad_maximum_fusion), channel_id=1, source_target_pairs={{4,0},{8,4},{12,8},{16,12},{20,16},{24,20},{28,24},{5,1},{9,5},{13... | collective-permute-start | bytes 3145736 | tf_op jit(solution)/shard_map/ppermute | solution.py:15
  117.9 21.6 %collective-permute-start.19 = (f32[4,2048]{1,0:T(4,128)S(1)}, f32[4,2048]{1,0:T(4,128)S(1)}, u32[]{:S(2)}, u32[]{:S(2)}) collective-permute-start(f32[4,2048]{1,0:T(4,128)S(1)} %reshape.741), channel_id=1, source_target_pairs={{0,4},{4,0},{8,12},{12,8},{16,20},{20,16},{24,28},{28,24},{1,5},{5... | collective-permute-start | bytes 98312 | tf_op jit(solution)/shard_map/ppermute | solution.py:21
  119.8 21.5 %collective-permute-start.5 = (f32[1,65536]{1,0:T(1,128)S(1)}, f32[1,65536]{1,0:T(1,128)S(1)}, u32[]{:S(2)}, u32[]{:S(2)}) collective-permute-start(f32[1,65536]{1,0:T(1,128)S(1)} %constant_dynamic-slice_fusion.13), channel_id=1, source_target_pairs={{0,2},{1,3},{2,0},{3,1},{4,6},{5,7},{6,4},{7,5},{8,10},{9,11},{10,... | collective-permute-start | bytes 786440 | tf_op jit(solution)/shard_map/ppermute | solution.py:21
  139.8 5.4 %collective-permute-start.20 = (f32[1,16384]{1,0:T(1,128)S(1)}, f32[1,16384]{1,0:T(1,128)S(1)}, u32[]{:S(2)}, u32[]{:S(2)}) collective-permute-start(f32[1,16384]{1,0:T(1,128)S(1)} %broadcast_in_dim_reshape_reshape.3), channel_id=1, source_target_pairs={{0,2},{1,3},{2,0},{3,1},{4,6},{5,7},{6,4},{7,5},{8,10},{9,11},{10,... | collective-permute-start | bytes 196616 | tf_op jit(solution)/shard_map/ppermute | solution.py:21
  142.7 5.9 %collective-permute-start.6 = (f32[4,8192]{1,0:T(4,128)S(1)}, f32[4,8192]{1,0:T(4,128)S(1)}, u32[]{:S(2)}, u32[]{:S(2)}) collective-permute-start(f32[4,8192]{1,0:T(4,128)S(1)} %bitcast.296), channel_id=1, source_target_pairs={{0,4},{4,0},{8,12},{12,8},{16,20},{20,16},{24,28},{28,24},{1,5},{5... | collective-permute-start | bytes 393224 | tf_op jit(solution)/shard_map/ppermute | solution.py:21
  149.0 4.3 %collective-permute-start.7 = (f32[2,8192]{1,0:T(2,128)S(1)}, f32[2,8192]{1,0:T(2,128)S(1)}, u32[]{:S(2)}, u32[]{:S(2)}) collective-permute-start(f32[2,8192]{1,0:T(2,128)S(1)} %bitcast.297), channel_id=1, source_target_pairs={{0,8},{4,12},{8,0},{12,4},{16,24},{20,28},{24,16},{28,20},{1,9},{5... | collective-permute-start | bytes 196616 | tf_op jit(solution)/shard_map/ppermute | solution.py:21
  149.9 6.6 %collective-permute-start.21 = (f32[2,16384]{1,0:T(2,128)S(1)}, f32[2,16384]{1,0:T(2,128)S(1)}, u32[]{:S(2)}, u32[]{:S(2)}) collective-permute-start(f32[2,16384]{1,0:T(2,128)S(1)} %maximum_bitcast_fusion), channel_id=1, source_target_pairs={{0,1},{1,0},{2,3},{3,2},{4,5},{5,4},{6,7},{7,6},{8,9},{9,8},{10,11... | collective-permute-start | bytes 393224 | tf_op jit(solution)/shard_map/ppermute | solution.py:21
  153.5 5.3 %collective-permute-start.8 = (f32[1,8192]{1,0:T(1,128)S(1)}, f32[1,8192]{1,0:T(1,128)S(1)}, u32[]{:S(2)}, u32[]{:S(2)}) collective-permute-start(f32[1,8192]{1,0:T(1,128)S(1)} %constant_dynamic-slice_fusion.8), channel_id=1, source_target_pairs={{0,16},{4,20},{8,24},{12,28},{16,0},{20,4},{24,8},{28,12},{1,17},{... | collective-permute-start | bytes 98312 | tf_op jit(solution)/shard_map/ppermute | solution.py:21
  158.8 5.1 %collective-permute-start.9 = (f32[1,8192]{1,0:T(1,128)S(1)}, f32[1,8192]{1,0:T(1,128)S(1)}, u32[]{:S(2)}, u32[]{:S(2)}) collective-permute-start(f32[1,8192]{1,0:T(1,128)S(1)} %dynamic-slice_add_fusion), channel_id=1, source_target_pairs={{0,16},{4,20},{8,24},{12,28},{16,0},{20,4},{24,8},{28,12},{1,17},{... | collective-permute-start | bytes 98312 | tf_op jit(solution)/shard_map/ppermute | solution.py:21
  164.0 4.3 %collective-permute-start.10 = (f32[2,8192]{1,0:T(2,128)S(1)}, f32[2,8192]{1,0:T(2,128)S(1)}, u32[]{:S(2)}, u32[]{:S(2)}) collective-permute-start(f32[2,8192]{1,0:T(2,128)S(1)} %maximum_bitcast_fusion.1), channel_id=1, source_target_pairs={{0,8},{4,12},{8,0},{12,4},{16,24},{20,28},{24,16},{28,20},{1,9},{5... | collective-permute-start | bytes 196616 | tf_op jit(solution)/shard_map/ppermute | solution.py:21
  168.8 5.0 %collective-permute-start.11 = (f32[4,8192]{1,0:T(4,128)S(1)}, f32[4,8192]{1,0:T(4,128)S(1)}, u32[]{:S(2)}, u32[]{:S(2)}) collective-permute-start(f32[4,8192]{1,0:T(4,128)S(1)} %reshape.738), channel_id=1, source_target_pairs={{0,4},{4,0},{8,12},{12,8},{16,20},{20,16},{24,28},{28,24},{1,5},{5... | collective-permute-start | bytes 393224 | tf_op jit(solution)/shard_map/ppermute | solution.py:21
  (34 other events, 45.5 us)

commit v2 on v1

--- a/solution.py
+++ b/solution.py
@@ -58,6 +58,16 @@
     size = lax.axis_size(axis)
     part = scatter_blocks(flat.reshape(size, flat.shape[0] // size), axis)
     return gather_blocks(part, axis).reshape(flat.shape)
+
+
+def summed_by_exchange(flat, axes):
+    size = 1
+    for axis in axes:
+        size *= lax.axis_size(axis)
+    pieces = lax.all_to_all(flat.reshape(size, -1), axes, 0, 0, tiled=True)
+    total = jnp.sum(pieces, axis=0, keepdims=True)
+    spread = jnp.broadcast_to(total, pieces.shape)
+    return lax.all_to_all(spread, axes, 0, 0, tiled=True).reshape(flat.shape)
 
 
 def silu_slope(scores):
@@ -184,8 +194,8 @@
     indicator_float = query_bucket_indicator.astype(jnp.float32)
     query_sum = jnp.zeros((local_rows, width), jnp.float32)
     table_local = jnp.zeros((head_count, bucket_count, bucket_count), jnp.float32)
-    key_terms = []
-    for distance in range(3):
+    key_terms = [None, None, None]
+    for distance in (2, 1, 0):
         visible, scores, weights, key_bucket_indicator = tiles[distance]
         pair = window[distance]
         key_heads = pair[0].reshape(local_rows, head_count, head_dim)
@@ -216,7 +226,7 @@
         )
         query_sum = query_sum + query_part
         table_local = table_local + table_part
-        key_terms.append(jnp.stack([key_part, value_part]))
+        key_terms[distance] = jnp.stack([key_part, value_part])
     gathered = (
         key_terms[0] + passed_along(key_terms[1], "ctx", -1) + passed_along(key_terms[2], "ctx", -2)
     )
@@ -229,9 +239,9 @@
     )
     weight_rows = scatter_blocks(weight_term.reshape(dp_size, -1), "dp")
     projection_grad = summed_over(weight_rows, "ctx").reshape(width // dp_size, width)
-    table_rows = scatter_blocks(table_local.reshape(dp_size, -1), "dp")
-    table_rows = summed_over(table_rows, "ctx")
-    table_grad = gather_blocks(table_rows, "dp").reshape(table_local.shape)
+    table_grad = summed_by_exchange(table_local.reshape(-1), ("ctx", "dp")).reshape(
+        table_local.shape
+    )
     return (
         query_grad[None],
         key_grad[None],

time: 176 us -> 164 us (0.932)
  waiting for transfers between devices: 58.9 us -> 53.8 us
  local copies, waits for them, and re-layouts: 32.8 us -> 29.2 us
    ppermute x18 -> x8, waiting for transfers between devices: 58.9 us -> 13.4 us  [exchanged(): return lax.ppermute(value, axis, pairs)]
    all_to_all x0 -> x2, waiting for transfers between devices: none -> 22.9 us  [the longest x1 22.9 us: summed_by_exchange(): return lax.all_to_all(spread, axes, 0, 0, tiled=True).reshape(flat.shape)]
    ppermute x18 -> x8, starting transfers between devices: 32.1 us -> 10.4 us  [exchanged(): return lax.ppermute(value, axis, pairs)]
    all_to_all x0 -> x2, starting transfers between devices: none -> 20.6 us  [the longest x1 15.1 us: summed_by_exchange(): pieces = lax.all_to_all(flat.reshape(size, -1), axes, 0, 0, tiled=True)]
    ppermute x4, waiting for transfers between devices: 0.01 us -> 17.6 us  [passed_along(): return lax.ppermute(value, axis, pairs)]
    add x10 -> x5, other arithmetic: 3.95 us -> 1.59 us  [scatter_blocks(): blocks = keep + exchanged(send, axis, mask)]
    another operation x6 -> x3, local copies, waits for them, and re-layouts: 4.38 us -> 2.2 us  [shards(): key_terms[distance] = jnp.stack([key_part, value_part])]
    dynamic_slice x6 -> x3, local copies, waits for them, and re-layouts: 4.21 us -> 2.98 us  [scatter_blocks(): keep = lax.dynamic_index_in_dim(pairs, bit, axis=1, keepdims=False)]
  transfers between devices with their start and end apart: 22 -> 14, of which waited for: 12 -> 7; matrix products, arithmetic and copies ran while one was open for 24% -> 23% of each run, Pallas kernels for 0% -> 0%
where the time goes in v2:
time: 164 us; the launch traced here: 163 us
  waiting for transfers between devices  53.8 us (33%)
  starting transfers between devices  42.9 us (26%)
  local copies, waits for them, and re-layouts  29.2 us (18%)
  matrix products  23.4 us (14%)
  other arithmetic  12.6 us (8%)
    all_to_all x1, waiting for transfers between devices, summed_by_exchange(): return lax.all_to_all(spread, axes, 0, 0, tiled=True).reshape(flat.shape)  22.9 us
    ppermute x4, waiting for transfers between devices, passed_along(): return lax.ppermute(value, axis, pairs)  17.6 us
    all_to_all x1, starting transfers between devices, summed_by_exchange(): pieces = lax.all_to_all(flat.reshape(size, -1), axes, 0, 0, tiled=True)  15.1 us
    ppermute x8, waiting for transfers between devices, exchanged(): return lax.ppermute(value, axis, pairs)  13.4 us
    ppermute x4, starting transfers between devices, passed_along(): return lax.ppermute(value, axis, pairs)  11.9 us
    ppermute x8, starting transfers between devices, exchanged(): return lax.ppermute(value, axis, pairs)  10.4 us
    unnamed x91, local copies, waits for them, and re-layouts  9 us
    all_to_all x1, starting transfers between devices, summed_by_exchange(): return lax.all_to_all(spread, axes, 0, 0, tiled=True).reshape(flat.shape)  5.44 us
  transfers between devices with their start and end apart: 14, of which 7 were waited for; matrix products, arithmetic and copies ran while one was open for 23% of the time, Pallas kernels for 0%

profile of v2, /device:TPU:0, one launch (start us, length us, event | category | flops | bytes accessed | tf_op | source)
XLA Modules:
  0.0 163.4 jit_solution(14266037418123501420)
XLA Ops:
  0.7 1.2 copy.142
  2.8 5.7 %collective-permute-start.1 = (bf16[2,256,512]{1,2,0:T(8,128)(2,1)}, bf16[2,256,512]{1,2,0:T(8,128)(2,1)}, u32[]{:S(2)}, u32[]{:S(2)}) collective-permute-start(bf16[2,256,512]{1,2,0:T(8,128)(2,1)} %pad_maximum_fusion.2), channel_id=1, source_target_pairs={{0,4},{4,8},{8,12},{12,16},{16,20},{20,24},{24,28},{1,5},{5,9},{9,... | collective-permute-start | bytes 1572872 | tf_op jit(solution)/shard_map/ppermute | solution.py:15
  8.5 3.5 %collective-permute-start = (bf16[2,256,512]{1,2,0:T(8,128)(2,1)}, bf16[2,256,512]{1,2,0:T(8,128)(2,1)}, u32[]{:S(2)}, u32[]{:S(2)}) collective-permute-start(bf16[2,256,512]{1,2,0:T(8,128)(2,1)} %pad_maximum_fusion.2), channel_id=1, source_target_pairs={{0,8},{4,12},{8,16},{12,20},{16,24},{20,28},{1,9},{5,13},{9,17},{1... | collective-permute-start | bytes 1572872 | tf_op jit(solution)/shard_map/ppermute | solution.py:15
  16.4 1.5 select_convert_fusion.2
  17.9 1.1 convolution_bitcast_fusion.3
  21.0 1.4 collective-permute-done
  23.5 1.5 select_convert_fusion
  26.9 1.5 select_convert_fusion.1
  29.6 1.4 fusion.30
  32.0 1.1 copy.208
  42.6 1.2 fusion.16
  43.7 1.8 %copy.186 = f32[4,128,128]{2,1,0:T(8,128)} copy(f32[4,128,128]{1,2,0:T(8,128)} %fusion.16) | data formatting | bytes 524288 | tf_op jit(solution)/shard_map/add | solution.py:228
  45.5 15.1 %all-to-all-start = ((f32[32,1,2048]{2,1,0:T(1,128)}), f32[32,1,2048]{2,1,0:T(1,128)}, u32[]{:S(2)}, u32[]{:S(2)}) async-start(f32[32,1,2048]{2,1,0:T(1,128)} %bitcast.243), calls=%async_computation | async-start | bytes 524288 | tf_op jit(solution)/shard_map/all_to_all | solution.py:67
  60.7 2.3 %fusion.21 = f32[512,512]{1,0:T(8,128)} fusion(bf16[256,512]{0,1:T(8,128)(2,1)} %bitcast.251, bf16[1,256,512]{2,1,0:T(8,128)(2,1)} %param.14), kind=kOutput, calls=%fused_computation.59 | convolution fusion | flops 134217728 | bytes 1572864 | tf_op jit(solution)/shard_map/dot_general | solution.py:237
  63.0 2.7 %reshape_reshape.7 = f32[2,2,65536]{2,1,0:T(2,128)} reshape(f32[512,512]{1,0:T(8,128)} %fusion.21) | data formatting | bytes 2097152 | tf_op jit(solution)/shard_map/reshape;reshape | solution.py:38
  65.7 2.6 %constant_dynamic-slice_fusion.7 = (f32[2,1,65536]{2,1,0:T(1,128)S(1)}, f32[2,1,65536]{2,1,0:T(1,128)S(1)}) fusion(f32[2,2,65536]{2,1,0:T(2,128)} %reshape_reshape.7, s32[]{:T(128)S(6)} %select_n.235, s32[]{:T(128)S(6)} %select_n.236), kind=kLoop, calls=%fused_computation.122 | loop fusion | bytes 2097160 | tf_op jit(solution)/shard_map/jit(dynamic_index_in_dim)/dynamic_slice | solution.py:39
  71.7 1.6 collective-permute-start.5
  74.5 5.4 %collective-permute-done.5 = f32[1,65536]{1,0:T(1,128)S(1)} collective-permute-done((f32[1,65536]{1,0:T(1,128)S(1)}, f32[1,65536]{1,0:T(1,128)S(1)}, u32[]{:S(2)}, u32[]{:S(2)}) %collective-permute-start.5) | collective-permute-done | bytes 262176 | tf_op jit(solution)/shard_map/ppermute | solution.py:21
  81.3 1.7 %collective-permute-start.6 = (f32[4,8192]{1,0:T(4,128)S(1)}, f32[4,8192]{1,0:T(4,128)S(1)}, u32[]{:S(2)}, u32[]{:S(2)}) collective-permute-start(f32[4,8192]{1,0:T(4,128)S(1)} %bitcast.256), channel_id=1, source_target_pairs={{0,4},{4,0},{8,12},{12,8},{16,20},{20,16},{24,28},{28,24},{1,5},{5... | collective-permute-start | bytes 393224 | tf_op jit(solution)/shard_map/ppermute | solution.py:21
  83.2 3.1 %collective-permute-done.6 = f32[4,8192]{1,0:T(4,128)S(1)} collective-permute-done((f32[4,8192]{1,0:T(4,128)S(1)}, f32[4,8192]{1,0:T(4,128)S(1)}, u32[]{:S(2)}, u32[]{:S(2)}) %collective-permute-start.6) | collective-permute-done | bytes 131104 | tf_op jit(solution)/shard_map/ppermute | solution.py:21
  86.7 1.7 %collective-permute-start.7 = (f32[2,8192]{1,0:T(2,128)S(1)}, f32[2,8192]{1,0:T(2,128)S(1)}, u32[]{:S(2)}, u32[]{:S(2)}) collective-permute-start(f32[2,8192]{1,0:T(2,128)S(1)} %bitcast.257), channel_id=1, source_target_pairs={{0,8},{4,12},{8,0},{12,4},{16,24},{20,28},{24,16},{28,20},{1,9},{5... | collective-permute-start | bytes 196616 | tf_op jit(solution)/shard_map/ppermute | solution.py:21
  91.7 2.5 %collective-permute-start.8 = (f32[1,8192]{1,0:T(1,128)S(1)}, f32[1,8192]{1,0:T(1,128)S(1)}, u32[]{:S(2)}, u32[]{:S(2)}) collective-permute-start(f32[1,8192]{1,0:T(1,128)S(1)} %constant_dynamic-slice_fusion), channel_id=1, source_target_pairs={{0,16},{4,20},{8,24},{12,28},{16,0},{20,4},{24,8},{28,12},{1,17},{... | collective-permute-start | bytes 98312 | tf_op jit(solution)/shard_map/ppermute | solution.py:21
  94.2 2.1 %pad_maximum_fusion = f32[2,256,512]{2,1,0:T(8,128)} fusion(f32[1,256,512]{2,1,0:T(8,128)S(1)} %copy-done.14, f32[1,256,512]{2,1,0:T(8,128)} %copy.174), kind=kLoop, calls=%fused_computation.39 | loop fusion | flops 262144 | bytes 2097152 | tf_op jit(solution)/shard_map/stack | solution.py:229
  100.3 1.4 collective-permute-start.2
  101.8 1.1 reduce_sum.83
  103.7 5.4 %all-to-all-start.1 = ((f32[32,1,2048]{2,1,0:T(1,128)}), f32[32,1,2048]{2,1,0:T(1,128)S(1)}, u32[]{:S(2)}, u32[]{:S(2)}) async-start(f32[32,1,2048]{2,1,0:T(1,128)} %broadcast_in_dim.63), calls=%async_computation.1 | async-start | bytes 524288 | tf_op jit(solution)/shard_map/all_to_all | solution.py:70
  109.2 2.7 %collective-permute-start.9 = (f32[1,8192]{1,0:T(1,128)S(1)}, f32[1,8192]{1,0:T(1,128)S(1)}, u32[]{:S(2)}, u32[]{:S(2)}) collective-permute-start(f32[1,8192]{1,0:T(1,128)S(1)} %dynamic-slice_add_fusion), channel_id=1, source_target_pairs={{0,16},{4,20},{8,24},{12,28},{16,0},{20,4},{24,8},{28,12},{1,17},{... | collective-permute-start | bytes 98312 | tf_op jit(solution)/shard_map/ppermute | solution.py:21
  113.0 1.3 collective-permute-start.3
  114.3 22.9 %all-to-all-done.1 = f32[32,1,2048]{2,1,0:T(1,128)S(1)} async-done(((f32[32,1,2048]{2,1,0:T(1,128)}), f32[32,1,2048]{2,1,0:T(1,128)S(1)}, u32[]{:S(2)}, u32[]{:S(2)}) %all-to-all-start.1) | async-done | bytes 262176 | tf_op jit(solution)/shard_map/all_to_all | solution.py:70
  138.1 16.2 %collective-permute-done.3 = f32[2,256,512]{2,1,0:T(8,128)S(1)} collective-permute-done((f32[2,256,512]{2,1,0:T(8,128)}, f32[2,256,512]{2,1,0:T(8,128)S(1)}, u32[]{:S(2)}, u32[]{:S(2)}) %collective-permute-start.3) | collective-permute-done | bytes 1048608 | tf_op jit(solution)/shard_map/ppermute | solution.py:15
  154.2 1.5 fusion.19
  157.1 4.1 %collective-permute-done.11 = f32[4,8192]{1,0:T(4,128)S(1)} collective-permute-done((f32[4,8192]{1,0:T(4,128)S(1)}, f32[4,8192]{1,0:T(4,128)S(1)}, u32[]{:S(2)}, u32[]{:S(2)}) %collective-permute-start.11) | collective-permute-done | bytes 131104 | tf_op jit(solution)/shard_map/ppermute | solution.py:21
  (189 shorter events, 41.5 us)
Async XLA Ops:
  0.6 28.9 %copy-start = (bf16[512,512]{1,0:T(8,128)(2,1)S(1)}, bf16[512,512]{1,0:T(8,128)(2,1)}, u32[]{:S(2)}) copy-start(bf16[512,512]{1,0:T(8,128)(2,1)} %param.19) | copy-start | bytes 1572868
  2.8 23.0 %collective-permute-start.1 = (bf16[2,256,512]{1,2,0:T(8,128)(2,1)}, bf16[2,256,512]{1,2,0:T(8,128)(2,1)}, u32[]{:S(2)}, u32[]{:S(2)}) collective-permute-start(bf16[2,256,512]{1,2,0:T(8,128)(2,1)} %pad_maximum_fusion.2), channel_id=1, source_target_pairs={{0,4},{4,8},{8,12},{12,16},{16,20},{20,24},{24,28},{1,5},{5,9},{9,... | collective-permute-start | bytes 1572872 | tf_op jit(solution)/shard_map/ppermute | solution.py:15
  8.5 13.9 %collective-permute-start = (bf16[2,256,512]{1,2,0:T(8,128)(2,1)}, bf16[2,256,512]{1,2,0:T(8,128)(2,1)}, u32[]{:S(2)}, u32[]{:S(2)}) collective-permute-start(bf16[2,256,512]{1,2,0:T(8,128)(2,1)} %pad_maximum_fusion.2), channel_id=1, source_target_pairs={{0,8},{4,12},{8,16},{12,20},{16,24},{20,28},{1,9},{5,13},{9,17},{1... | collective-permute-start | bytes 1572872 | tf_op jit(solution)/shard_map/ppermute | solution.py:15
  12.1 1.6 %copy-start.36 = (s32[1,6]{1,0:T(1,128)S(1)}, s32[1,6]{1,0:T(1,128)}, u32[]{:S(2)}) copy-start(s32[1,6]{1,0:T(1,128)} %param.16) | copy-start | bytes 76
  12.1 5.8 %copy-start.15 = (bf16[256,4,128]{2,1,0:T(4,128)(2,1)}, bf16[256,4,128]{2,1,0:T(4,128)(2,1)S(1)}, u32[]{:S(2)}) copy-start(bf16[256,4,128]{2,1,0:T(4,128)(2,1)S(1)} %reshape_squeeze_stack_squeeze.9) | copy-start | bytes 786436
  12.1 2.7 %copy-start.27 = (bf16[1,256,512]{2,1,0:T(8,128)(2,1)S(1)}, bf16[1,256,512]{2,1,0:T(8,128)(2,1)}, u32[]{:S(2)}) copy-start(bf16[1,256,512]{2,1,0:T(8,128)(2,1)} %param.10) | copy-start | bytes 786436
  15.7 4.9 %copy-start.31 = (s32[1,256]{1,0:T(1,128)}, s32[1,256]{1,0:T(1,128)S(1)}, u32[]{:S(2)}) copy-start(s32[1,256]{1,0:T(1,128)S(1)} %get-tuple-element.58) | copy-start | bytes 3076
  19.2 7.7 %copy-start.29 = (pred[256,256]{1,0:T(8,128)(4,1)}, pred[256,256]{1,0:T(8,128)(4,1)S(1)}, u32[]{:S(2)}) copy-start(pred[256,256]{1,0:T(8,128)(4,1)S(1)} %copy.153) | copy-start | bytes 196612
  23.4 1.6 copy-start.25
  23.5 1.5 copy-start.18
  26.9 1.5 copy-start.20
  26.9 1.5 copy-start.22
  26.9 1.5 copy-start.8
  33.2 2.1 %copy-start.39 = (f32[4,256,256]{2,1,0:T(8,128)S(1)}, f32[4,256,256]{2,1,0:T(8,128)}, u32[]{:S(2)}) copy-start(f32[4,256,256]{2,1,0:T(8,128)} %get-tuple-element.70) | copy-start | bytes 3145732
  38.8 1.3 copy-start.38
  45.5 56.2 %all-to-all-start = ((f32[32,1,2048]{2,1,0:T(1,128)}), f32[32,1,2048]{2,1,0:T(1,128)}, u32[]{:S(2)}, u32[]{:S(2)}) async-start(f32[32,1,2048]{2,1,0:T(1,128)} %bitcast.243), calls=%async_computation | async-start | bytes 524288 | tf_op jit(solution)/shard_map/all_to_all | solution.py:67
  68.8 2.1 %collective-permute-start.4 = (f32[2,65536]{1,0:T(2,128)S(1)}, f32[2,65536]{1,0:T(2,128)S(1)}, u32[]{:S(2)}, u32[]{:S(2)}) collective-permute-start(f32[2,65536]{1,0:T(2,128)S(1)} %bitcast.255), channel_id=1, source_target_pairs={{0,1},{1,0},{2,3},{3,2},{4,5},{5,4},{6,7},{7,6},{8,9},{9,8},{10,11... | collective-permute-start | bytes 1572872 | tf_op jit(solution)/shard_map/ppermute | solution.py:21
  71.7 8.3 %collective-permute-start.5 = (f32[1,65536]{1,0:T(1,128)S(1)}, f32[1,65536]{1,0:T(1,128)S(1)}, u32[]{:S(2)}, u32[]{:S(2)}) collective-permute-start(f32[1,65536]{1,0:T(1,128)S(1)} %constant_dynamic-slice_fusion.5), channel_id=1, source_target_pairs={{0,2},{1,3},{2,0},{3,1},{4,6},{5,7},{6,4},{7,5},{8,10},{9,11},{10,... | collective-permute-start | bytes 786440 | tf_op jit(solution)/shard_map/ppermute | solution.py:21
  81.3 5.0 %collective-permute-start.6 = (f32[4,8192]{1,0:T(4,128)S(1)}, f32[4,8192]{1,0:T(4,128)S(1)}, u32[]{:S(2)}, u32[]{:S(2)}) collective-permute-start(f32[4,8192]{1,0:T(4,128)S(1)} %bitcast.256), channel_id=1, source_target_pairs={{0,4},{4,0},{8,12},{12,8},{16,20},{20,16},{24,28},{28,24},{1,5},{5... | collective-permute-start | bytes 393224 | tf_op jit(solution)/shard_map/ppermute | solution.py:21
  86.7 2.8 %copy-start.3 = (f32[4,128,256]{2,1,0:T(8,128)S(1)}, f32[4,128,256]{2,1,0:T(8,128)}, u32[]{:S(2)}) copy-start(f32[4,128,256]{2,1,0:T(8,128)} %fusion.72) | copy-start | bytes 1572868
  86.7 4.8 %collective-permute-start.7 = (f32[2,8192]{1,0:T(2,128)S(1)}, f32[2,8192]{1,0:T(2,128)S(1)}, u32[]{:S(2)}, u32[]{:S(2)}) collective-permute-start(f32[2,8192]{1,0:T(2,128)S(1)} %bitcast.257), channel_id=1, source_target_pairs={{0,8},{4,12},{8,0},{12,4},{16,24},{20,28},{24,16},{28,20},{1,9},{5... | collective-permute-start | bytes 196616 | tf_op jit(solution)/shard_map/ppermute | solution.py:21
  90.5 3.6 %copy-start.14 = (f32[1,256,512]{2,1,0:T(8,128)S(1)}, f32[1,256,512]{2,1,0:T(8,128)}, u32[]{:S(2)}) copy-start(f32[1,256,512]{2,1,0:T(8,128)} %copy.175) | copy-start | bytes 1572868
  91.6 4.6 %copy-start.2 = (f32[4,128,256]{2,1,0:T(8,128)S(1)}, f32[4,128,256]{2,1,0:T(8,128)}, u32[]{:S(2)}) copy-start(f32[4,128,256]{2,1,0:T(8,128)} %fusion.73) | copy-start | bytes 1572868
  91.7 17.5 %collective-permute-start.8 = (f32[1,8192]{1,0:T(1,128)S(1)}, f32[1,8192]{1,0:T(1,128)S(1)}, u32[]{:S(2)}, u32[]{:S(2)}) collective-permute-start(f32[1,8192]{1,0:T(1,128)S(1)} %constant_dynamic-slice_fusion), channel_id=1, source_target_pairs={{0,16},{4,20},{8,24},{12,28},{16,0},{20,4},{24,8},{28,12},{1,17},{... | collective-permute-start | bytes 98312 | tf_op jit(solution)/shard_map/ppermute | solution.py:21
  100.3 11.7 %copy-start.10 = (f32[1,256,512]{2,1,0:T(8,128)S(1)}, f32[1,256,512]{2,1,0:T(8,128)}, u32[]{:S(2)}) copy-start(f32[1,256,512]{2,1,0:T(8,128)} %copy.179) | copy-start | bytes 1572868
  100.3 11.7 %copy-start.13 = (f32[1,256,512]{2,1,0:T(8,128)S(1)}, f32[1,256,512]{2,1,0:T(8,128)}, u32[]{:S(2)}) copy-start(f32[1,256,512]{2,1,0:T(8,128)} %copy.178) | copy-start | bytes 1572868
  100.3 37.7 %collective-permute-start.2 = (f32[2,256,512]{2,1,0:T(8,128)}, f32[2,256,512]{2,1,0:T(8,128)}, u32[]{:S(2)}, u32[]{:S(2)}) collective-permute-start(f32[2,256,512]{2,1,0:T(8,128)} %pad_maximum_fusion), channel_id=1, source_target_pairs={{4,0},{8,4},{12,8},{16,12},{20,16},{24,20},{28,24},{5,1},{9,5},{13... | collective-permute-start | bytes 3145736 | tf_op jit(solution)/shard_map/ppermute | solution.py:15
  103.7 33.4 %all-to-all-start.1 = ((f32[32,1,2048]{2,1,0:T(1,128)}), f32[32,1,2048]{2,1,0:T(1,128)S(1)}, u32[]{:S(2)}, u32[]{:S(2)}) async-start(f32[32,1,2048]{2,1,0:T(1,128)} %broadcast_in_dim.63), calls=%async_computation.1 | async-start | bytes 524288 | tf_op jit(solution)/shard_map/all_to_all | solution.py:70
  109.2 28.6 %collective-permute-start.9 = (f32[1,8192]{1,0:T(1,128)S(1)}, f32[1,8192]{1,0:T(1,128)S(1)}, u32[]{:S(2)}, u32[]{:S(2)}) collective-permute-start(f32[1,8192]{1,0:T(1,128)S(1)} %dynamic-slice_add_fusion), channel_id=1, source_target_pairs={{0,16},{4,20},{8,24},{12,28},{16,0},{20,4},{24,8},{28,12},{1,17},{... | collective-permute-start | bytes 98312 | tf_op jit(solution)/shard_map/ppermute | solution.py:21
  113.0 41.2 %collective-permute-start.3 = (f32[2,256,512]{2,1,0:T(8,128)}, f32[2,256,512]{2,1,0:T(8,128)S(1)}, u32[]{:S(2)}, u32[]{:S(2)}) collective-permute-start(f32[2,256,512]{2,1,0:T(8,128)} %pad_maximum_fusion.1), channel_id=1, source_target_pairs={{8,0},{12,4},{16,8},{20,12},{24,16},{28,20},{9,1},{13,5},{17,9},{2... | collective-permute-start | bytes 3145736 | tf_op jit(solution)/shard_map/ppermute | solution.py:15
  138.0 17.8 %collective-permute-start.10 = (f32[2,8192]{1,0:T(2,128)S(1)}, f32[2,8192]{1,0:T(2,128)S(1)}, u32[]{:S(2)}, u32[]{:S(2)}) collective-permute-start(f32[2,8192]{1,0:T(2,128)S(1)} %maximum_bitcast_fusion), channel_id=1, source_target_pairs={{0,8},{4,12},{8,0},{12,4},{16,24},{20,28},{24,16},{28,20},{1,9},{5... | collective-permute-start | bytes 196616 | tf_op jit(solution)/shard_map/ppermute | solution.py:21
  156.2 5.0 %collective-permute-start.11 = (f32[4,8192]{1,0:T(4,128)S(1)}, f32[4,8192]{1,0:T(4,128)S(1)}, u32[]{:S(2)}, u32[]{:S(2)}) collective-permute-start(f32[4,8192]{1,0:T(4,128)S(1)} %reshape.726), channel_id=1, source_target_pairs={{0,4},{4,0},{8,12},{12,8},{16,20},{20,16},{24,28},{28,24},{1,5},{5... | collective-permute-start | bytes 393224 | tf_op jit(solution)/shard_map/ppermute | solution.py:21
  (22 other events, 21.5 us)

commit v3 on v2

--- a/solution.py
+++ b/solution.py
@@ -58,6 +58,21 @@
     size = lax.axis_size(axis)
     part = scatter_blocks(flat.reshape(size, flat.shape[0] // size), axis)
     return gather_blocks(part, axis).reshape(flat.shape)
+
+
+def plan_step(blocks, kind, axis, mask):
+    bit = (lax.axis_index(axis) // mask) % 2
+    if kind == "split":
+        if blocks.shape[0] == 1:
+            blocks = blocks.reshape(2, -1)
+        pairs = blocks.reshape(blocks.shape[0] // 2, 2, blocks.shape[1])
+        keep = lax.dynamic_index_in_dim(pairs, bit, axis=1, keepdims=False)
+        send = lax.dynamic_index_in_dim(pairs, 1 - bit, axis=1, keepdims=False)
+        return keep + exchanged(send, axis, mask)
+    other = exchanged(blocks, axis, mask)
+    low = jnp.where(bit == 0, blocks, other)
+    high = jnp.where(bit == 0, other, blocks)
+    return jnp.concatenate([low, high], axis=1)
 
 
 def summed_by_exchange(flat, axes):
@@ -192,12 +207,32 @@
     ).astype(jnp.bfloat16)
     grad_heads = attended_grad.reshape(local_rows, head_count, head_dim)
     indicator_float = query_bucket_indicator.astype(jnp.float32)
+    dp_size = lax.axis_size("dp")
+    weight_term = lax.dot_general(
+        mixed, grad_rows, (((0,), (0,)), ((), ())), preferred_element_type=jnp.float32
+    )
+    weight_plan = [("split", "dp", mask) for mask in axis_bits("dp")]
+    weight_plan += [("split", "ctx", mask) for mask in axis_bits("ctx")]
+    weight_plan += [("join", "ctx", mask) for mask in reversed(axis_bits("ctx"))]
+    weight_state = [weight_term.reshape(dp_size, -1), 0]
+
+    def slot(anchor):
+        blocks, done = weight_state
+        if done < len(weight_plan):
+            blocks, anchor = lax.optimization_barrier((blocks, anchor))
+            weight_state[0] = plan_step(blocks, *weight_plan[done])
+            weight_state[1] = done + 1
+        return anchor
+
     query_sum = jnp.zeros((local_rows, width), jnp.float32)
-    table_local = jnp.zeros((head_count, bucket_count, bucket_count), jnp.float32)
+    share_sum = None
     key_terms = [None, None, None]
+    sent = [None, None, None]
     for distance in (2, 1, 0):
         visible, scores, weights, key_bucket_indicator = tiles[distance]
-        pair = window[distance]
+        pair = slot(window[distance])
+        if distance == 0:
+            sent[2], pair = lax.optimization_barrier((sent[2], pair))
         key_heads = pair[0].reshape(local_rows, head_count, head_dim)
         value_heads = pair[1].reshape(local_rows, head_count, head_dim)
         weight_grad = jnp.einsum(
@@ -209,6 +244,7 @@
         score_gradient = jnp.where(visible[None], weight_grad * silu_slope(scores), 0.0).astype(
             jnp.bfloat16
         )
+        score_gradient = slot(score_gradient)
         query_part = jnp.einsum(
             "hij,jhd->ihd", score_gradient, key_heads, preferred_element_type=jnp.float32
         ).reshape(local_rows, width)
@@ -221,24 +257,22 @@
         bucket_share_piece = jnp.einsum(
             "rmw,wx->rmx", score_gradient, key_bucket_indicator, preferred_element_type=jnp.float32
         )
-        table_part = jnp.einsum(
-            "qp,cqk->cpk", indicator_float, bucket_share_piece, precision=lax.Precision.HIGHEST
-        )
+        share_sum = bucket_share_piece if share_sum is None else share_sum + bucket_share_piece
         query_sum = query_sum + query_part
-        table_local = table_local + table_part
         key_terms[distance] = jnp.stack([key_part, value_part])
-    gathered = (
-        key_terms[0] + passed_along(key_terms[1], "ctx", -1) + passed_along(key_terms[2], "ctx", -2)
-    )
+        if distance > 0:
+            sent[distance] = passed_along(key_terms[distance], "ctx", -distance)
+    table_local = jnp.einsum(
+        "qp,cqk->cpk", indicator_float, share_sum, precision=lax.Precision.HIGHEST
+    )
+    table_local = slot(table_local)
+    while weight_state[1] < len(weight_plan):
+        table_local = slot(table_local)
+    gathered = key_terms[0] + sent[1] + sent[2]
     query_grad = (query_sum * scale).astype(jnp.bfloat16)
     key_grad = gathered[0].astype(jnp.bfloat16)
     value_grad = gathered[1].astype(jnp.bfloat16)
-    dp_size = lax.axis_size("dp")
-    weight_term = lax.dot_general(
-        mixed, grad_rows, (((0,), (0,)), ((), ())), preferred_element_type=jnp.float32
-    )
-    weight_rows = scatter_blocks(weight_term.reshape(dp_size, -1), "dp")
-    projection_grad = summed_over(weight_rows, "ctx").reshape(width // dp_size, width)
+    projection_grad = weight_state[0].reshape(width // dp_size, width)
     table_grad = summed_by_exchange(table_local.reshape(-1), ("ctx", "dp")).reshape(
         table_local.shape
     )

time: 164 us -> 153 us (0.933)
  waiting for transfers between devices: 53.8 us -> 46.1 us
  matrix products: 23.4 us -> 18.8 us
  starting transfers between devices: 42.9 us -> 38.7 us
  other arithmetic: 12.6 us -> 16.4 us
    ppermute x4, waiting for transfers between devices: 17.6 us -> 0.01 us  [passed_along(): return lax.ppermute(value, axis, pairs)]
    ppermute x8, waiting for transfers between devices: 13.4 us -> 29.2 us  [exchanged(): return lax.ppermute(value, axis, pairs)]
    all_to_all x1, waiting for transfers between devices: 22.9 us -> 7.91 us  [summed_by_exchange(): return lax.all_to_all(spread, axes, 0, 0, tiled=True).reshape(flat.shape)]
    all_to_all x1, starting transfers between devices: 15.1 us -> 4.8 us  [summed_by_exchange(): pieces = lax.all_to_all(flat.reshape(size, -1), axes, 0, 0, tiled=True)]
    all_to_all x1, waiting for transfers between devices: 0.01 us -> 8.92 us  [summed_by_exchange(): pieces = lax.all_to_all(flat.reshape(size, -1), axes, 0, 0, tiled=True)]
    ppermute x8, starting transfers between devices: 10.4 us -> 19.3 us  [exchanged(): return lax.ppermute(value, axis, pairs)]
    another operation x7 -> x4, local copies, waits for them, and re-layouts: 4.16 us -> 0.33 us  [the longest x3 0.27 us: plan_step(): pairs = blocks.reshape(blocks.shape[0] // 2, 2, blocks.shape[1])]
    optimization_barrier x0 -> x3, other arithmetic: none -> 2.94 us  [slot(): blocks, anchor = lax.optimization_barrier((blocks, anchor))]
  transfers between devices with their start and end apart: 14 -> 14, of which waited for: 7 -> 7; matrix products, arithmetic and copies ran while one was open for 23% -> 28% of each run, Pallas kernels for 0% -> 0%
where the time goes in v3:
time: 153 us; the launch traced here: 152 us
  waiting for transfers between devices  46.1 us (30%)
  starting transfers between devices  38.7 us (25%)
  local copies, waits for them, and re-layouts  30.6 us (20%)
  matrix products  18.8 us (12%)
  other arithmetic  16.4 us (11%)
  between operations  1.53 us (1%)
    ppermute x8, waiting for transfers between devices, exchanged(): return lax.ppermute(value, axis, pairs)  29.2 us
    ppermute x8, starting transfers between devices, exchanged(): return lax.ppermute(value, axis, pairs)  19.3 us
    ppermute x4, starting transfers between devices, passed_along(): return lax.ppermute(value, axis, pairs)  12 us
    unnamed x80, local copies, waits for them, and re-layouts  11.5 us
    all_to_all x1, waiting for transfers between devices, summed_by_exchange(): pieces = lax.all_to_all(flat.reshape(size, -1), axes, 0, 0, tiled=True)  8.92 us
    all_to_all x1, waiting for transfers between devices, summed_by_exchange(): return lax.all_to_all(spread, axes, 0, 0, tiled=True).reshape(flat.shape)  7.91 us
    all_to_all x1, starting transfers between devices, summed_by_exchange(): pieces = lax.all_to_all(flat.reshape(size, -1), axes, 0, 0, tiled=True)  4.8 us
    another operation x2, other arithmetic, shards(): key_terms[distance] = jnp.stack([key_part, value_part])  4.22 us
  transfers between devices with their start and end apart: 14, of which 7 were waited for; matrix products, arithmetic and copies ran while one was open for 28% of the time, Pallas kernels for 0%

profile of v3, /device:TPU:0, one launch (start us, length us, event | category | flops | bytes accessed | tf_op | source)
XLA Modules:
  0.0 152.2 jit_solution(10337306045160019367)
XLA Ops:
  0.7 1.2 copy.179
  2.0 4.9 %collective-permute-start = (bf16[2,256,512]{1,2,0:T(8,128)(2,1)S(1)}, bf16[2,256,512]{1,2,0:T(8,128)(2,1)S(1)}, u32[]{:S(2)}, u32[]{:S(2)}) collective-permute-start(bf16[2,256,512]{1,2,0:T(8,128)(2,1)S(1)} %pad_maximum_fusion.2), channel_id=1, source_target_pairs={{0,4},{4,8},{8,12},{12,16},{16,20},{20,24},{24,28},{1,5},{5,9},{9,... | collective-permute-start | bytes 1572872 | tf_op jit(solution)/shard_map/ppermute | solution.py:15
  6.9 4.3 %collective-permute-start.1 = (bf16[2,256,512]{1,2,0:T(8,128)(2,1)S(1)}, bf16[2,256,512]{1,2,0:T(8,128)(2,1)}, u32[]{:S(2)}, u32[]{:S(2)}) collective-permute-start(bf16[2,256,512]{1,2,0:T(8,128)(2,1)S(1)} %pad_maximum_fusion.2), channel_id=1, source_target_pairs={{0,8},{4,12},{8,16},{12,20},{16,24},{20,28},{1,9},{5,13},{9,17},{1... | collective-permute-start | bytes 1572872 | tf_op jit(solution)/shard_map/ppermute | solution.py:15
  16.1 1.5 select_convert_fusion.2
  18.4 1.1 convolution_bitcast_fusion.2
  22.5 1.5 select_convert_fusion
  25.6 1.5 select_convert_fusion.1
  38.0 1.2 copy.207
  41.6 1.8 %fusion.61 = (bf16[1,256,512]{1,2,0:T(8,128)(2,1)}, bf16[1,256,512]{1,2,0:T(8,128)(2,1)S(1)}) fusion(bf16[2,256,512]{1,2,0:T(8,128)(2,1)} %collective-permute-done.1), kind=kLoop, calls=%fused_computation.156 | loop fusion | bytes 1048576 | tf_op jit(solution)/shard_map/slice | solution.py:236
  43.4 1.7 %fusion.7 = bf16[4,256,256]{2,1,0:T(8,128)(2,1)S(1)} fusion(bf16[256,4,128]{0,2,1:T(8,128)(2,1)S(1)} %bitcast.246, f32[4,256,256]{2,1,0:T(8,128)} %get-tuple-element.104, pred[256,256]{1,0:T(8,128)(4,1)S(1)} %copy.143, bf16[256,512]{1,0:T(8,128)(2,1)S(1)} %copy-done.17), kind=kOutput, calls=%fused_computation.14 | convolution fusion | flops 69730304 | bytes 2162688 | tf_op jit(solution)/shard_map/ihd,jhd->hij/dot_general | solution.py:238
  46.6 1.5 %collective-permute-start.3 = (f32[1,65536]{1,0:T(1,128)}, f32[1,65536]{1,0:T(1,128)}, u32[]{:S(2)}, u32[]{:S(2)}) collective-permute-start(f32[1,65536]{1,0:T(1,128)} %constant_dynamic-slice_fusion), channel_id=1, source_target_pairs={{0,2},{1,3},{2,0},{3,1},{4,6},{5,7},{6,4},{7,5},{8,10},{9,11},{10,... | collective-permute-start | bytes 786440 | tf_op jit(solution)/shard_map/ppermute | solution.py:21
  49.4 2.1 %pad_maximum_fusion = f32[2,256,512]{2,1,0:T(8,128)} fusion(f32[1,256,512]{2,1,0:T(8,128)S(1)} %copy-done.15, f32[1,256,512]{2,1,0:T(8,128)} %copy.155), kind=kLoop, calls=%fused_computation.34 | loop fusion | flops 262144 | bytes 2097152 | tf_op jit(solution)/shard_map/stack | solution.py:262
  51.5 1.6 %collective-permute-start.5 = (f32[2,256,512]{2,1,0:T(8,128)}, f32[2,256,512]{2,1,0:T(8,128)}, u32[]{:S(2)}, u32[]{:S(2)}) collective-permute-start(f32[2,256,512]{2,1,0:T(8,128)} %pad_maximum_fusion), channel_id=1, source_target_pairs={{8,0},{12,4},{16,8},{20,12},{24,16},{28,20},{9,1},{13,5},{17,9},{2... | collective-permute-start | bytes 3145736 | tf_op jit(solution)/shard_map/ppermute | solution.py:15
  53.1 2.5 %collective-permute-done.3 = f32[1,65536]{1,0:T(1,128)} collective-permute-done((f32[1,65536]{1,0:T(1,128)}, f32[1,65536]{1,0:T(1,128)}, u32[]{:S(2)}, u32[]{:S(2)}) %collective-permute-start.3) | collective-permute-done | bytes 262176 | tf_op jit(solution)/shard_map/ppermute | solution.py:21
  55.6 1.3 dynamic-slice_add_fusion
  58.3 1.2 reduce.16
  59.8 9.5 %collective-permute-start.4 = (f32[1,32768]{1,0:T(1,128)S(1)}, f32[1,32768]{1,0:T(1,128)S(1)}, u32[]{:S(2)}, u32[]{:S(2)}) collective-permute-start(f32[1,32768]{1,0:T(1,128)S(1)} %dynamic-slice_bitcast_fusion), channel_id=1, source_target_pairs={{0,4},{4,0},{8,12},{12,8},{16,20},{20,16},{24,28},{28,24},{1,5},{5... | collective-permute-start | bytes 393224 | tf_op jit(solution)/shard_map/ppermute | solution.py:21
  69.3 1.7 %fusion.8 = bf16[4,256,256]{2,1,0:T(8,128)(2,1)S(1)} fusion(bf16[256,4,128]{0,2,1:T(8,128)(2,1)S(1)} %bitcast.244, f32[4,256,256]{2,1,0:T(8,128)} %get-tuple-element.108, pred[256,256]{1,0:T(8,128)(4,1)S(1)} %copy.138, bf16[256,512]{1,0:T(8,128)(2,1)S(1)} %copy-done.18), kind=kOutput, calls=%fused_computation.15 | convolution fusion | flops 69730304 | bytes 2162688 | tf_op jit(solution)/shard_map/ihd,jhd->hij/dot_general | solution.py:238
  71.1 1.6 %collective-permute-done.4 = f32[1,32768]{1,0:T(1,128)S(1)} collective-permute-done((f32[1,32768]{1,0:T(1,128)S(1)}, f32[1,32768]{1,0:T(1,128)S(1)}, u32[]{:S(2)}, u32[]{:S(2)}) %collective-permute-start.4) | collective-permute-done | bytes 131104 | tf_op jit(solution)/shard_map/ppermute | solution.py:21
  74.5 2.6 %collective-permute-start.6 = (f32[1,16384]{1,0:T(1,128)}, f32[1,16384]{1,0:T(1,128)}, u32[]{:S(2)}, u32[]{:S(2)}) collective-permute-start(f32[1,16384]{1,0:T(1,128)} %dynamic-slice_bitcast_fusion.1), channel_id=1, source_target_pairs={{0,8},{4,12},{8,0},{12,4},{16,24},{20,28},{24,16},{28,20},{1,9},{5... | collective-permute-start | bytes 196616 | tf_op jit(solution)/shard_map/ppermute | solution.py:21
  78.4 2.1 %pad_maximum_fusion.1 = f32[2,256,512]{2,1,0:T(8,128)} fusion(f32[1,256,512]{2,1,0:T(8,128)S(1)} %copy-done.14, f32[1,256,512]{2,1,0:T(8,128)} %copy.165), kind=kLoop, calls=%fused_computation.38 | loop fusion | flops 262144 | bytes 2097152 | tf_op jit(solution)/shard_map/stack | solution.py:262
  80.5 1.3 collective-permute-start.8
  85.3 3.3 %collective-permute-start.7 = (f32[1,8192]{1,0:T(1,128)S(1)}, f32[1,8192]{1,0:T(1,128)S(1)}, u32[]{:S(2)}, u32[]{:S(2)}) collective-permute-start(f32[1,8192]{1,0:T(1,128)S(1)} %dynamic-slice_bitcast_fusion.2), channel_id=1, source_target_pairs={{0,16},{4,20},{8,24},{12,28},{16,0},{20,4},{24,8},{28,12},{1,17},{... | collective-permute-start | bytes 98312 | tf_op jit(solution)/shard_map/ppermute | solution.py:21
  89.0 19.4 %collective-permute-done.7 = f32[1,8192]{1,0:T(1,128)S(1)} collective-permute-done((f32[1,8192]{1,0:T(1,128)S(1)}, f32[1,8192]{1,0:T(1,128)S(1)}, u32[]{:S(2)}, u32[]{:S(2)}) %collective-permute-start.7) | collective-permute-done | bytes 32800 | tf_op jit(solution)/shard_map/ppermute | solution.py:21
  111.1 3.8 %collective-permute-done.9 = f32[1,8192]{1,0:T(1,128)S(1)} collective-permute-done((f32[1,8192]{1,0:T(1,128)S(1)}, f32[1,8192]{1,0:T(1,128)S(1)}, u32[]{:S(2)}, u32[]{:S(2)}) %collective-permute-start.9) | collective-permute-done | bytes 32800 | tf_op jit(solution)/shard_map/ppermute | solution.py:21
  115.0 2.2 %collective-permute-start.10 = (f32[1,16384]{1,0:T(1,128)S(1)}, f32[1,16384]{1,0:T(1,128)S(1)}, u32[]{:S(2)}, u32[]{:S(2)}) collective-permute-start(f32[1,16384]{1,0:T(1,128)S(1)} %pad_maximum_fusion.4), channel_id=1, source_target_pairs={{0,8},{4,12},{8,0},{12,4},{16,24},{20,28},{24,16},{28,20},{1,9},{5... | collective-permute-start | bytes 196616 | tf_op jit(solution)/shard_map/ppermute | solution.py:21
  117.6 1.9 %collective-permute-done.10 = f32[1,16384]{1,0:T(1,128)S(1)} collective-permute-done((f32[1,16384]{1,0:T(1,128)S(1)}, f32[1,16384]{1,0:T(1,128)S(1)}, u32[]{:S(2)}, u32[]{:S(2)}) %collective-permute-start.10) | collective-permute-done | bytes 65568 | tf_op jit(solution)/shard_map/ppermute | solution.py:21
  121.9 4.8 %all-to-all-start = ((f32[32,1,2048]{2,1,0:T(1,128)}), f32[32,1,2048]{2,1,0:T(1,128)S(1)}, u32[]{:S(2)}, u32[]{:S(2)}) async-start(f32[32,1,2048]{2,1,0:T(1,128)} %bitcast.61), calls=%async_computation | async-start | bytes 524288 | tf_op jit(solution)/shard_map/all_to_all | solution.py:82
  128.4 8.9 %all-to-all-done = f32[32,1,2048]{2,1,0:T(1,128)S(1)} async-done(((f32[32,1,2048]{2,1,0:T(1,128)}), f32[32,1,2048]{2,1,0:T(1,128)S(1)}, u32[]{:S(2)}, u32[]{:S(2)}) %all-to-all-start) | async-done | bytes 262176 | tf_op jit(solution)/shard_map/all_to_all | solution.py:82
  138.3 2.6 %all-to-all-start.1 = ((f32[32,1,2048]{2,1,0:T(1,128)}), f32[32,1,2048]{2,1,0:T(1,128)S(1)}, u32[]{:S(2)}, u32[]{:S(2)}) async-start(f32[32,1,2048]{2,1,0:T(1,128)} %broadcast_in_dim.63), calls=%async_computation.1 | async-start | bytes 524288 | tf_op jit(solution)/shard_map/all_to_all | solution.py:85
  140.9 1.8 %fusion.16 = bf16[2,256,512]{2,1,0:T(8,128)(2,1)S(1)} fusion(f32[2,256,512]{2,1,0:T(8,128)} %collective-permute-done.5, f32[2,256,512]{2,1,0:T(8,128)} %collective-permute-done.8, f32[1,256,512]{2,1,0:T(8,128)S(1)} %copy.162, f32[1,256,512]{2,1,0:T(8,128)S(1)} %copy.161), kind=kLoop, calls=%fused_computation.37 | loop fusion | flops 1048576 | bytes 3670016 | tf_op jit(solution)/shard_map/convert.3
  143.5 7.9 %all-to-all-done.1 = f32[32,1,2048]{2,1,0:T(1,128)S(1)} async-done(((f32[32,1,2048]{2,1,0:T(1,128)}), f32[32,1,2048]{2,1,0:T(1,128)S(1)}, u32[]{:S(2)}, u32[]{:S(2)}) %all-to-all-start.1) | async-done | bytes 262176 | tf_op jit(solution)/shard_map/all_to_all | solution.py:85
  (181 shorter events, 44.2 us)
Async XLA Ops:
  0.6 27.2 %copy-start = (bf16[512,512]{1,0:T(8,128)(2,1)S(1)}, bf16[512,512]{1,0:T(8,128)(2,1)}, u32[]{:S(2)}) copy-start(bf16[512,512]{1,0:T(8,128)(2,1)} %param.19) | copy-start | bytes 1572868
  0.6 1.2 copy-start.20
  2.0 11.9 %copy-start.2 = (bf16[2,256,512]{1,2,0:T(8,128)(2,1)}, bf16[2,256,512]{1,2,0:T(8,128)(2,1)S(1)}, u32[]{:S(2)}) copy-start(bf16[2,256,512]{1,2,0:T(8,128)(2,1)S(1)} %pad_maximum_fusion.2) | copy-start | bytes 1572868
  2.0 22.8 %collective-permute-start = (bf16[2,256,512]{1,2,0:T(8,128)(2,1)S(1)}, bf16[2,256,512]{1,2,0:T(8,128)(2,1)S(1)}, u32[]{:S(2)}, u32[]{:S(2)}) collective-permute-start(bf16[2,256,512]{1,2,0:T(8,128)(2,1)S(1)} %pad_maximum_fusion.2), channel_id=1, source_target_pairs={{0,4},{4,8},{8,12},{12,16},{16,20},{20,24},{24,28},{1,5},{5,9},{9,... | collective-permute-start | bytes 1572872 | tf_op jit(solution)/shard_map/ppermute | solution.py:15
  6.9 14.5 %collective-permute-start.1 = (bf16[2,256,512]{1,2,0:T(8,128)(2,1)S(1)}, bf16[2,256,512]{1,2,0:T(8,128)(2,1)}, u32[]{:S(2)}, u32[]{:S(2)}) collective-permute-start(bf16[2,256,512]{1,2,0:T(8,128)(2,1)S(1)} %pad_maximum_fusion.2), channel_id=1, source_target_pairs={{0,8},{4,12},{8,16},{12,20},{16,24},{20,28},{1,9},{5,13},{9,17},{1... | collective-permute-start | bytes 1572872 | tf_op jit(solution)/shard_map/ppermute | solution.py:15
  11.3 2.5 %copy-start.25 = (bf16[1,256,512]{2,1,0:T(8,128)(2,1)S(1)}, bf16[1,256,512]{2,1,0:T(8,128)(2,1)}, u32[]{:S(2)}) copy-start(bf16[1,256,512]{2,1,0:T(8,128)(2,1)} %param.10) | copy-start | bytes 786436
  14.0 1.5 copy-start.26
  14.9 1.2 copy-start.27
  15.5 5.6 %copy-start.29 = (s32[1,256]{1,0:T(1,128)}, s32[1,256]{1,0:T(1,128)S(1)}, u32[]{:S(2)}) copy-start(s32[1,256]{1,0:T(1,128)S(1)} %get-tuple-element.99) | copy-start | bytes 3076
  25.6 1.5 copy-start.13
  30.1 1.1 copy-start.9
  32.2 1.1 copy-start.7
  38.0 1.2 copy-start.10
  39.2 5.9 %collective-permute-start.2 = (f32[2,65536]{1,0:T(2,128)}, f32[2,65536]{1,0:T(2,128)S(1)}, u32[]{:S(2)}, u32[]{:S(2)}) collective-permute-start(f32[2,65536]{1,0:T(2,128)} %bitcast.216), channel_id=1, source_target_pairs={{0,1},{1,0},{2,3},{3,2},{4,5},{5,4},{6,7},{7,6},{8,9},{9,8},{10,11... | collective-permute-start | bytes 1572872 | tf_op jit(solution)/shard_map/ppermute | solution.py:21
  41.5 1.8 %copy-start.17 = (bf16[256,512]{1,0:T(8,128)(2,1)S(1)}, bf16[256,512]{1,0:T(8,128)(2,1)}, u32[]{:S(2)}) copy-start(bf16[256,512]{1,0:T(8,128)(2,1)} %copy-done.16) | copy-start | bytes 786436
  46.6 9.0 %collective-permute-start.3 = (f32[1,65536]{1,0:T(1,128)}, f32[1,65536]{1,0:T(1,128)}, u32[]{:S(2)}, u32[]{:S(2)}) collective-permute-start(f32[1,65536]{1,0:T(1,128)} %constant_dynamic-slice_fusion), channel_id=1, source_target_pairs={{0,2},{1,3},{2,0},{3,1},{4,6},{5,7},{6,4},{7,5},{8,10},{9,11},{10,... | collective-permute-start | bytes 786440 | tf_op jit(solution)/shard_map/ppermute | solution.py:21
  51.5 5.5 %copy-start.5 = (bf16[2,256,512]{1,2,0:T(8,128)(2,1)S(1)}, bf16[2,256,512]{1,2,0:T(8,128)(2,1)}, u32[]{:S(2)}) copy-start(bf16[2,256,512]{1,2,0:T(8,128)(2,1)} %copy-done.4) | copy-start | bytes 1572868
  51.5 56.9 %collective-permute-start.5 = (f32[2,256,512]{2,1,0:T(8,128)}, f32[2,256,512]{2,1,0:T(8,128)}, u32[]{:S(2)}, u32[]{:S(2)}) collective-permute-start(f32[2,256,512]{2,1,0:T(8,128)} %pad_maximum_fusion), channel_id=1, source_target_pairs={{8,0},{12,4},{16,8},{20,12},{24,16},{28,20},{9,1},{13,5},{17,9},{2... | collective-permute-start | bytes 3145736 | tf_op jit(solution)/shard_map/ppermute | solution.py:15
  59.7 9.7 %copy-start.18 = (bf16[256,512]{1,0:T(8,128)(2,1)S(1)}, bf16[256,512]{1,0:T(8,128)(2,1)}, u32[]{:S(2)}) copy-start(bf16[256,512]{1,0:T(8,128)(2,1)} %copy-done.16) | copy-start | bytes 786436
  59.8 12.8 %collective-permute-start.4 = (f32[1,32768]{1,0:T(1,128)S(1)}, f32[1,32768]{1,0:T(1,128)S(1)}, u32[]{:S(2)}, u32[]{:S(2)}) collective-permute-start(f32[1,32768]{1,0:T(1,128)S(1)} %dynamic-slice_bitcast_fusion), channel_id=1, source_target_pairs={{0,4},{4,0},{8,12},{12,8},{16,20},{20,16},{24,28},{28,24},{1,5},{5... | collective-permute-start | bytes 393224 | tf_op jit(solution)/shard_map/ppermute | solution.py:21
  74.5 8.9 %collective-permute-start.6 = (f32[1,16384]{1,0:T(1,128)}, f32[1,16384]{1,0:T(1,128)}, u32[]{:S(2)}, u32[]{:S(2)}) collective-permute-start(f32[1,16384]{1,0:T(1,128)} %dynamic-slice_bitcast_fusion.1), channel_id=1, source_target_pairs={{0,8},{4,12},{8,0},{12,4},{16,24},{20,28},{24,16},{28,20},{1,9},{5... | collective-permute-start | bytes 196616 | tf_op jit(solution)/shard_map/ppermute | solution.py:21
  78.4 3.4 %copy-start.22 = (bf16[1,256,512]{1,2,0:T(8,128)(2,1)S(1)}, bf16[1,256,512]{1,2,0:T(8,128)(2,1)}, u32[]{:S(2)}) copy-start(bf16[1,256,512]{1,2,0:T(8,128)(2,1)} %get-tuple-element.82) | copy-start | bytes 786436
  80.5 60.4 %collective-permute-start.8 = (f32[2,256,512]{2,1,0:T(8,128)}, f32[2,256,512]{2,1,0:T(8,128)}, u32[]{:S(2)}, u32[]{:S(2)}) collective-permute-start(f32[2,256,512]{2,1,0:T(8,128)} %pad_maximum_fusion.1), channel_id=1, source_target_pairs={{4,0},{8,4},{12,8},{16,12},{20,16},{24,20},{28,24},{5,1},{9,5},{13... | collective-permute-start | bytes 3145736 | tf_op jit(solution)/shard_map/ppermute | solution.py:15
  85.2 3.4 %copy-start.30 = (s32[1,256]{1,0:T(1,128)S(1)}, s32[1,256]{1,0:T(1,128)}, u32[]{:S(2)}) copy-start(s32[1,256]{1,0:T(1,128)} %copy-done.29) | copy-start | bytes 3076
  85.3 23.2 %copy-start.3 = (bf16[2,256,512]{1,2,0:T(8,128)(2,1)S(1)}, bf16[2,256,512]{1,2,0:T(8,128)(2,1)}, u32[]{:S(2)}) copy-start(bf16[2,256,512]{1,2,0:T(8,128)(2,1)} %copy-done.2) | copy-start | bytes 1572868
  85.3 23.2 %copy-start.35 = (f32[4,256,256]{2,1,0:T(8,128)S(1)}, f32[4,256,256]{2,1,0:T(8,128)}, u32[]{:S(2)}) copy-start(f32[4,256,256]{2,1,0:T(8,128)} %get-tuple-element.106) | copy-start | bytes 3145732
  85.3 23.1 %collective-permute-start.7 = (f32[1,8192]{1,0:T(1,128)S(1)}, f32[1,8192]{1,0:T(1,128)S(1)}, u32[]{:S(2)}, u32[]{:S(2)}) collective-permute-start(f32[1,8192]{1,0:T(1,128)S(1)} %dynamic-slice_bitcast_fusion.2), channel_id=1, source_target_pairs={{0,16},{4,20},{8,24},{12,28},{16,0},{20,4},{24,8},{28,12},{1,17},{... | collective-permute-start | bytes 98312 | tf_op jit(solution)/shard_map/ppermute | solution.py:21
  109.9 5.0 %collective-permute-start.9 = (f32[1,8192]{1,0:T(1,128)S(1)}, f32[1,8192]{1,0:T(1,128)S(1)}, u32[]{:S(2)}, u32[]{:S(2)}) collective-permute-start(f32[1,8192]{1,0:T(1,128)S(1)} %bitcast_add_fusion.3), channel_id=1, source_target_pairs={{0,16},{4,20},{8,24},{12,28},{16,0},{20,4},{24,8},{28,12},{1,17},{... | collective-permute-start | bytes 98312 | tf_op jit(solution)/shard_map/ppermute | solution.py:21
  115.0 4.5 %collective-permute-start.10 = (f32[1,16384]{1,0:T(1,128)S(1)}, f32[1,16384]{1,0:T(1,128)S(1)}, u32[]{:S(2)}, u32[]{:S(2)}) collective-permute-start(f32[1,16384]{1,0:T(1,128)S(1)} %pad_maximum_fusion.4), channel_id=1, source_target_pairs={{0,8},{4,12},{8,0},{12,4},{16,24},{20,28},{24,16},{28,20},{1,9},{5... | collective-permute-start | bytes 196616 | tf_op jit(solution)/shard_map/ppermute | solution.py:21
  119.7 7.0 %collective-permute-start.11 = (f32[1,32768]{1,0:T(1,128)S(1)}, f32[1,32768]{1,0:T(1,128)S(1)}, u32[]{:S(2)}, u32[]{:S(2)}) collective-permute-start(f32[1,32768]{1,0:T(1,128)S(1)} %pad_maximum_fusion.3), channel_id=1, source_target_pairs={{0,4},{4,0},{8,12},{12,8},{16,20},{20,16},{24,28},{28,24},{1,5},{5... | collective-permute-start | bytes 393224 | tf_op jit(solution)/shard_map/ppermute | solution.py:21
  121.9 15.4 %all-to-all-start = ((f32[32,1,2048]{2,1,0:T(1,128)}), f32[32,1,2048]{2,1,0:T(1,128)S(1)}, u32[]{:S(2)}, u32[]{:S(2)}) async-start(f32[32,1,2048]{2,1,0:T(1,128)} %bitcast.61), calls=%async_computation | async-start | bytes 524288 | tf_op jit(solution)/shard_map/all_to_all | solution.py:82
  138.3 13.2 %all-to-all-start.1 = ((f32[32,1,2048]{2,1,0:T(1,128)}), f32[32,1,2048]{2,1,0:T(1,128)S(1)}, u32[]{:S(2)}, u32[]{:S(2)}) async-start(f32[32,1,2048]{2,1,0:T(1,128)} %broadcast_in_dim.63), calls=%async_computation.1 | async-start | bytes 524288 | tf_op jit(solution)/shard_map/all_to_all | solution.py:85
  (18 other events, 15.7 us)

commit v4 on v3

--- a/solution.py
+++ b/solution.py
@@ -212,15 +212,18 @@
         mixed, grad_rows, (((0,), (0,)), ((), ())), preferred_element_type=jnp.float32
     )
     weight_plan = [("split", "dp", mask) for mask in axis_bits("dp")]
-    weight_plan += [("split", "ctx", mask) for mask in axis_bits("ctx")]
-    weight_plan += [("join", "ctx", mask) for mask in reversed(axis_bits("ctx"))]
+    weight_plan.append(("exchange", "ctx", 0))
     weight_state = [weight_term.reshape(dp_size, -1), 0]
 
     def slot(anchor):
         blocks, done = weight_state
         if done < len(weight_plan):
             blocks, anchor = lax.optimization_barrier((blocks, anchor))
-            weight_state[0] = plan_step(blocks, *weight_plan[done])
+            kind, axis, mask = weight_plan[done]
+            if kind == "exchange":
+                weight_state[0] = summed_by_exchange(blocks.reshape(-1), (axis,))
+            else:
+                weight_state[0] = plan_step(blocks, kind, axis, mask)
             weight_state[1] = done + 1
         return anchor
 
@@ -265,9 +268,6 @@
     table_local = jnp.einsum(
         "qp,cqk->cpk", indicator_float, share_sum, precision=lax.Precision.HIGHEST
     )
-    table_local = slot(table_local)
-    while weight_state[1] < len(weight_plan):
-        table_local = slot(table_local)
     gathered = key_terms[0] + sent[1] + sent[2]
     query_grad = (query_sum * scale).astype(jnp.bfloat16)
     key_grad = gathered[0].astype(jnp.bfloat16)

time: 153 us -> 153 us (level)
  other arithmetic: 16.4 us -> 14.5 us
    ppermute x8 -> x2, waiting for transfers between devices: 29.2 us -> 2.5 us  [exchanged(): return lax.ppermute(value, axis, pairs)]
    all_to_all x1 -> x2, waiting for transfers between devices: 8.92 us -> 32.6 us  [summed_by_exchange(): pieces = lax.all_to_all(flat.reshape(size, -1), axes, 0, 0, tiled=True)]
    ppermute x8 -> x2, starting transfers between devices: 19.3 us -> 1.55 us  [exchanged(): return lax.ppermute(value, axis, pairs)]
    all_to_all x1 -> x2, starting transfers between devices: 4.8 us -> 18.5 us  [summed_by_exchange(): pieces = lax.all_to_all(flat.reshape(size, -1), axes, 0, 0, tiled=True)]
    all_to_all x1 -> x2, starting transfers between devices: 2.59 us -> 6.63 us  [summed_by_exchange(): return lax.all_to_all(spread, axes, 0, 0, tiled=True).reshape(flat.shape)]
    all_to_all x1 -> x2, waiting for transfers between devices: 7.91 us -> 11.6 us  [summed_by_exchange(): return lax.all_to_all(spread, axes, 0, 0, tiled=True).reshape(flat.shape)]
    optimization_barrier x3 -> x0, other arithmetic: 2.94 us -> none  [slot(): blocks, anchor = lax.optimization_barrier((blocks, anchor))]
    all_to_all x0 -> x1, other arithmetic: none -> 1.57 us  [summed_by_exchange(): return lax.all_to_all(spread, axes, 0, 0, tiled=True).reshape(flat.shape)]
  transfers between devices with their start and end apart: 14 -> 10, of which waited for: 7 -> 5; matrix products, arithmetic and copies ran while one was open for 28% -> 28% of each run, Pallas kernels for 0% -> 0%
where the time goes in v4:
time: 153 us; the launch traced here: 152 us
  waiting for transfers between devices  46.6 us (30%)
  starting transfers between devices  38.7 us (25%)
  local copies, waits for them, and re-layouts  30.9 us (20%)
  matrix products  19.7 us (13%)
  other arithmetic  14.5 us (9%)
    all_to_all x2, waiting for transfers between devices, summed_by_exchange(): pieces = lax.all_to_all(flat.reshape(size, -1), axes, 0, 0, tiled=True)  32.6 us
    all_to_all x2, starting transfers between devices, summed_by_exchange(): pieces = lax.all_to_all(flat.reshape(size, -1), axes, 0, 0, tiled=True)  18.5 us
    ppermute x4, starting transfers between devices, passed_along(): return lax.ppermute(value, axis, pairs)  12.1 us
    unnamed x80, local copies, waits for them, and re-layouts  11.9 us
    all_to_all x2, waiting for transfers between devices, summed_by_exchange(): return lax.all_to_all(spread, axes, 0, 0, tiled=True).reshape(flat.shape)  11.6 us
    all_to_all x2, starting transfers between devices, summed_by_exchange(): return lax.all_to_all(spread, axes, 0, 0, tiled=True).reshape(flat.shape)  6.63 us
    another operation x2, other arithmetic, shards(): key_terms[distance] = jnp.stack([key_part, value_part])  4.19 us
    dot_general x3, matrix products, shards(): jnp.einsum('ihd,jhd->hij', grad_heads, value_heads, preferred_element_typ...  4.01 us
  transfers between devices with their start and end apart: 10, of which 5 were waited for; matrix products, arithmetic and copies ran while one was open for 28% of the time, Pallas kernels for 0%

profile of v4, /device:TPU:0, one launch (start us, length us, event | category | flops | bytes accessed | tf_op | source)
XLA Modules:
  0.0 151.8 jit_solution(15484474628892925388)
XLA Ops:
  0.7 1.2 copy.179
  2.0 4.9 %collective-permute-start = (bf16[2,256,512]{1,2,0:T(8,128)(2,1)S(1)}, bf16[2,256,512]{1,2,0:T(8,128)(2,1)S(1)}, u32[]{:S(2)}, u32[]{:S(2)}) collective-permute-start(bf16[2,256,512]{1,2,0:T(8,128)(2,1)S(1)} %pad_maximum_fusion.2), channel_id=1, source_target_pairs={{0,4},{4,8},{8,12},{12,16},{16,20},{20,24},{24,28},{1,5},{5,9},{9,... | collective-permute-start | bytes 1572872 | tf_op jit(solution)/shard_map/ppermute | solution.py:15
  6.9 4.3 %collective-permute-start.1 = (bf16[2,256,512]{1,2,0:T(8,128)(2,1)S(1)}, bf16[2,256,512]{1,2,0:T(8,128)(2,1)}, u32[]{:S(2)}, u32[]{:S(2)}) collective-permute-start(bf16[2,256,512]{1,2,0:T(8,128)(2,1)S(1)} %pad_maximum_fusion.2), channel_id=1, source_target_pairs={{0,8},{4,12},{8,16},{12,20},{16,24},{20,28},{1,9},{5,13},{9,17},{1... | collective-permute-start | bytes 1572872 | tf_op jit(solution)/shard_map/ppermute | solution.py:15
  16.1 1.5 select_convert_fusion.2
  18.4 1.1 convolution_bitcast_fusion.2
  21.4 1.1 fusion.64
  22.5 1.5 %select_convert_fusion = (bf16[4,256,256]{2,1,0:T(8,128)(2,1)S(1)}, f32[4,256,256]{2,1,0:T(8,128)}) fusion(pred[256,256]{1,0:T(8,128)(4,1)S(1)} %copy.143, f32[4,256,256]{2,1,0:T(8,128)S(1)} %fusion.46, bf16[256,4,128]{0,2,1:T(8,128)(2,1)S(1)} %bitcast.209, bf16[256,4,128]{0,2,1:T(8,128)(2,1)S(1)} %bitcast.236), kind=kOutput, calls=%fused_computation.39 | convolution fusion | flops 69206016 | bytes 3211264 | tf_op jit(solution)/shard_map/ihd,jhd->hij/dot_general | solution.py:175
  25.6 1.5 select_convert_fusion.1
  32.2 1.0 fusion.69
  38.0 1.2 copy.207
  41.5 1.8 %fusion.61 = (bf16[1,256,512]{1,2,0:T(8,128)(2,1)}, bf16[1,256,512]{1,2,0:T(8,128)(2,1)S(1)}) fusion(bf16[2,256,512]{1,2,0:T(8,128)(2,1)} %collective-permute-done.1), kind=kLoop, calls=%fused_computation.141 | loop fusion | bytes 1048576 | tf_op jit(solution)/shard_map/slice | solution.py:239
  43.3 1.7 %fusion.7 = bf16[4,256,256]{2,1,0:T(8,128)(2,1)S(1)} fusion(bf16[256,4,128]{0,2,1:T(8,128)(2,1)S(1)} %bitcast.234, f32[4,256,256]{2,1,0:T(8,128)} %get-tuple-element.78, pred[256,256]{1,0:T(8,128)(4,1)S(1)} %copy-done.28, bf16[256,512]{1,0:T(8,128)(2,1)S(1)} %copy-done.17), kind=kOutput, calls=%fused_computation.14 | convolution fusion | flops 69730304 | bytes 2162688 | tf_op jit(solution)/shard_map/ihd,jhd->hij/dot_general | solution.py:241
  46.5 1.5 %collective-permute-start.3 = (f32[1,65536]{1,0:T(1,128)}, f32[1,65536]{1,0:T(1,128)}, u32[]{:S(2)}, u32[]{:S(2)}) collective-permute-start(f32[1,65536]{1,0:T(1,128)} %constant_dynamic-slice_fusion), channel_id=1, source_target_pairs={{0,2},{1,3},{2,0},{3,1},{4,6},{5,7},{6,4},{7,5},{8,10},{9,11},{10,... | collective-permute-start | bytes 786440 | tf_op jit(solution)/shard_map/ppermute | solution.py:21
  49.4 2.1 %pad_maximum_fusion = f32[2,256,512]{2,1,0:T(8,128)} fusion(f32[1,256,512]{2,1,0:T(8,128)S(1)} %copy-done.15, f32[1,256,512]{2,1,0:T(8,128)} %copy.155), kind=kLoop, calls=%fused_computation.34 | loop fusion | flops 262144 | bytes 2097152 | tf_op jit(solution)/shard_map/stack | solution.py:265
  51.5 1.6 %collective-permute-start.4 = (f32[2,256,512]{2,1,0:T(8,128)}, f32[2,256,512]{2,1,0:T(8,128)}, u32[]{:S(2)}, u32[]{:S(2)}) collective-permute-start(f32[2,256,512]{2,1,0:T(8,128)} %pad_maximum_fusion), channel_id=1, source_target_pairs={{8,0},{12,4},{16,8},{20,12},{24,16},{28,20},{9,1},{13,5},{17,9},{2... | collective-permute-start | bytes 3145736 | tf_op jit(solution)/shard_map/ppermute | solution.py:15
  53.1 2.5 %collective-permute-done.3 = f32[1,65536]{1,0:T(1,128)} collective-permute-done((f32[1,65536]{1,0:T(1,128)}, f32[1,65536]{1,0:T(1,128)}, u32[]{:S(2)}, u32[]{:S(2)}) %collective-permute-start.3) | collective-permute-done | bytes 262176 | tf_op jit(solution)/shard_map/ppermute | solution.py:21
  55.6 2.0 %dynamic-slice_add_fusion = f32[1,65536]{1,0:T(1,128)} fusion(f32[1,65536]{1,0:T(1,128)} %collective-permute-done.3, f32[2,65536]{1,0:T(2,128)S(1)} %bitcast_add_fusion, s32[]{:T(128)S(6)} %select_n.144), kind=kLoop, calls=%fused_computation.64 | loop fusion | flops 65536 | bytes 786436 | tf_op jit(solution)/shard_map/add | solution.py:71
  60.4 2.1 %pad_maximum_fusion.1 = f32[2,256,512]{2,1,0:T(8,128)} fusion(f32[1,256,512]{2,1,0:T(8,128)S(1)} %copy-done.14, f32[1,256,512]{2,1,0:T(8,128)} %copy.165), kind=kLoop, calls=%fused_computation.38 | loop fusion | flops 262144 | bytes 2097152 | tf_op jit(solution)/shard_map/stack | solution.py:265
  62.5 1.3 collective-permute-start.5
  63.8 15.9 %all-to-all-start = ((f32[8,1,8192]{2,1,0:T(1,128)}), f32[8,1,8192]{2,1,0:T(1,128)}, u32[]{:S(2)}, u32[]{:S(2)}) async-start(f32[8,1,8192]{2,1,0:T(1,128)} %bitcast.54), calls=%async_computation | async-start | bytes 524288 | tf_op jit(solution)/shard_map/all_to_all | solution.py:82
  82.6 26.9 %all-to-all-done = f32[8,1,8192]{2,1,0:T(1,128)} async-done(((f32[8,1,8192]{2,1,0:T(1,128)}), f32[8,1,8192]{2,1,0:T(1,128)}, u32[]{:S(2)}, u32[]{:S(2)}) %all-to-all-start) | async-done | bytes 262176 | tf_op jit(solution)/shard_map/all_to_all | solution.py:82
  109.5 1.1 reduce_sum.92
  111.5 4.0 %all-to-all-start.1 = ((f32[8,1,8192]{2,1,0:T(1,128)}), f32[8,1,8192]{2,1,0:T(1,128)}, u32[]{:S(2)}, u32[]{:S(2)}) async-start(f32[8,1,8192]{2,1,0:T(1,128)} %broadcast_in_dim.65), calls=%async_computation.1 | async-start | bytes 524288 | tf_op jit(solution)/shard_map/all_to_all | solution.py:85
  116.5 1.7 %fusion.9 = bf16[4,256,256]{2,1,0:T(8,128)(2,1)S(1)} fusion(bf16[256,4,128]{0,2,1:T(8,128)(2,1)S(1)} %bitcast.233, f32[4,256,256]{2,1,0:T(8,128)} %get-tuple-element.80, pred[256,256]{1,0:T(8,128)(4,1)S(1)} %copy.130, bf16[256,512]{1,0:T(8,128)(2,1)S(1)} %copy-done.19), kind=kOutput, calls=%fused_computation.16 | convolution fusion | flops 69730304 | bytes 2162688 | tf_op jit(solution)/shard_map/ihd,jhd->hij/dot_general | solution.py:241
  120.1 3.7 %all-to-all-done.1 = f32[8,1,8192]{2,1,0:T(1,128)} async-done(((f32[8,1,8192]{2,1,0:T(1,128)}), f32[8,1,8192]{2,1,0:T(1,128)}, u32[]{:S(2)}, u32[]{:S(2)}) %all-to-all-start.1) | async-done | bytes 262176 | tf_op jit(solution)/shard_map/all_to_all | solution.py:85
  123.7 2.6 %all-to-all-start.2 = ((f32[32,1,2048]{2,1,0:T(1,128)}), f32[32,1,2048]{2,1,0:T(1,128)S(1)}, u32[]{:S(2)}, u32[]{:S(2)}) async-start(f32[32,1,2048]{2,1,0:T(1,128)} %bitcast.56), calls=%async_computation.2 | async-start | bytes 524288 | tf_op jit(solution)/shard_map/all_to_all | solution.py:82
  126.8 1.3 fusion.13
  128.9 1.6 %reduce.4 = f32[8,8192]{1,0:T(8,128)S(1)} reduce(f32[8,1,8192]{2,1,0:T(1,128)} %all-to-all-done.1, f32[]{:T(128)} %constant.229), dimensions={1}, to_apply=%all_to_all.22.reduce_sub_computation | reduce | bytes 524292 | tf_op jit(solution)/shard_map/all_to_all | solution.py:85
  131.2 5.7 %all-to-all-done.2 = f32[32,1,2048]{2,1,0:T(1,128)S(1)} async-done(((f32[32,1,2048]{2,1,0:T(1,128)}), f32[32,1,2048]{2,1,0:T(1,128)S(1)}, u32[]{:S(2)}, u32[]{:S(2)}) %all-to-all-start.2) | async-done | bytes 262176 | tf_op jit(solution)/shard_map/all_to_all | solution.py:82
  137.9 2.6 %all-to-all-start.3 = ((f32[32,1,2048]{2,1,0:T(1,128)}), f32[32,1,2048]{2,1,0:T(1,128)S(1)}, u32[]{:S(2)}, u32[]{:S(2)}) async-start(f32[32,1,2048]{2,1,0:T(1,128)} %broadcast_in_dim.66), calls=%async_computation.3 | async-start | bytes 524288 | tf_op jit(solution)/shard_map/all_to_all | solution.py:85
  140.5 1.8 %fusion.16 = bf16[2,256,512]{2,1,0:T(8,128)(2,1)S(1)} fusion(f32[2,256,512]{2,1,0:T(8,128)} %collective-permute-done.4, f32[2,256,512]{2,1,0:T(8,128)} %collective-permute-done.5, f32[1,256,512]{2,1,0:T(8,128)S(1)} %copy.162, f32[1,256,512]{2,1,0:T(8,128)S(1)} %copy.161), kind=kLoop, calls=%fused_computation.37 | loop fusion | flops 1048576 | bytes 3670016 | tf_op jit(solution)/shard_map/convert.3
  143.2 7.9 %all-to-all-done.3 = f32[32,1,2048]{2,1,0:T(1,128)S(1)} async-done(((f32[32,1,2048]{2,1,0:T(1,128)}), f32[32,1,2048]{2,1,0:T(1,128)S(1)}, u32[]{:S(2)}, u32[]{:S(2)}) %all-to-all-start.3) | async-done | bytes 262176 | tf_op jit(solution)/shard_map/all_to_all | solution.py:85
  (157 shorter events, 37.8 us)
Async XLA Ops:
  0.6 27.1 %copy-start = (bf16[512,512]{1,0:T(8,128)(2,1)S(1)}, bf16[512,512]{1,0:T(8,128)(2,1)}, u32[]{:S(2)}) copy-start(bf16[512,512]{1,0:T(8,128)(2,1)} %param.19) | copy-start | bytes 1572868
  0.6 1.2 copy-start.20
  2.0 11.9 %copy-start.2 = (bf16[2,256,512]{1,2,0:T(8,128)(2,1)}, bf16[2,256,512]{1,2,0:T(8,128)(2,1)S(1)}, u32[]{:S(2)}) copy-start(bf16[2,256,512]{1,2,0:T(8,128)(2,1)S(1)} %pad_maximum_fusion.2) | copy-start | bytes 1572868
  2.0 22.8 %collective-permute-start = (bf16[2,256,512]{1,2,0:T(8,128)(2,1)S(1)}, bf16[2,256,512]{1,2,0:T(8,128)(2,1)S(1)}, u32[]{:S(2)}, u32[]{:S(2)}) collective-permute-start(bf16[2,256,512]{1,2,0:T(8,128)(2,1)S(1)} %pad_maximum_fusion.2), channel_id=1, source_target_pairs={{0,4},{4,8},{8,12},{12,16},{16,20},{20,24},{24,28},{1,5},{5,9},{9,... | collective-permute-start | bytes 1572872 | tf_op jit(solution)/shard_map/ppermute | solution.py:15
  6.9 14.4 %collective-permute-start.1 = (bf16[2,256,512]{1,2,0:T(8,128)(2,1)S(1)}, bf16[2,256,512]{1,2,0:T(8,128)(2,1)}, u32[]{:S(2)}, u32[]{:S(2)}) collective-permute-start(bf16[2,256,512]{1,2,0:T(8,128)(2,1)S(1)} %pad_maximum_fusion.2), channel_id=1, source_target_pairs={{0,8},{4,12},{8,16},{12,20},{16,24},{20,28},{1,9},{5,13},{9,17},{1... | collective-permute-start | bytes 1572872 | tf_op jit(solution)/shard_map/ppermute | solution.py:15
  11.3 2.5 %copy-start.25 = (bf16[1,256,512]{2,1,0:T(8,128)(2,1)S(1)}, bf16[1,256,512]{2,1,0:T(8,128)(2,1)}, u32[]{:S(2)}) copy-start(bf16[1,256,512]{2,1,0:T(8,128)(2,1)} %param.10) | copy-start | bytes 786436
  14.0 1.5 copy-start.26
  15.5 5.5 %copy-start.29 = (s32[1,256]{1,0:T(1,128)}, s32[1,256]{1,0:T(1,128)S(1)}, u32[]{:S(2)}) copy-start(s32[1,256]{1,0:T(1,128)S(1)} %get-tuple-element.73) | copy-start | bytes 3076
  20.5 2.0 %copy-start.27 = (pred[256,256]{1,0:T(8,128)(4,1)}, pred[256,256]{1,0:T(8,128)(4,1)S(1)}, u32[]{:S(2)}) copy-start(pred[256,256]{1,0:T(8,128)(4,1)S(1)} %copy.143) | copy-start | bytes 196612
  25.6 1.5 copy-start.13
  30.0 1.1 copy-start.9
  32.2 1.1 copy-start.7
  37.9 1.2 copy-start.10
  39.2 5.9 %collective-permute-start.2 = (f32[2,65536]{1,0:T(2,128)}, f32[2,65536]{1,0:T(2,128)S(1)}, u32[]{:S(2)}, u32[]{:S(2)}) collective-permute-start(f32[2,65536]{1,0:T(2,128)} %bitcast.205), channel_id=1, source_target_pairs={{0,1},{1,0},{2,3},{3,2},{4,5},{5,4},{6,7},{7,6},{8,9},{9,8},{10,11... | collective-permute-start | bytes 1572872 | tf_op jit(solution)/shard_map/ppermute | solution.py:21
  39.2 1.0 copy-start.11
  40.2 1.0 copy-start.12
  41.5 1.8 %copy-start.17 = (bf16[256,512]{1,0:T(8,128)(2,1)S(1)}, bf16[256,512]{1,0:T(8,128)(2,1)}, u32[]{:S(2)}) copy-start(bf16[256,512]{1,0:T(8,128)(2,1)} %copy-done.16) | copy-start | bytes 786436
  41.5 1.8 %copy-start.28 = (pred[256,256]{1,0:T(8,128)(4,1)S(1)}, pred[256,256]{1,0:T(8,128)(4,1)}, u32[]{:S(2)}) copy-start(pred[256,256]{1,0:T(8,128)(4,1)} %copy-done.27) | copy-start | bytes 196612
  46.5 9.0 %collective-permute-start.3 = (f32[1,65536]{1,0:T(1,128)}, f32[1,65536]{1,0:T(1,128)}, u32[]{:S(2)}, u32[]{:S(2)}) collective-permute-start(f32[1,65536]{1,0:T(1,128)} %constant_dynamic-slice_fusion), channel_id=1, source_target_pairs={{0,2},{1,3},{2,0},{3,1},{4,6},{5,7},{6,4},{7,5},{8,10},{9,11},{10,... | collective-permute-start | bytes 786440 | tf_op jit(solution)/shard_map/ppermute | solution.py:21
  48.3 1.0 copy-start.15
  51.5 6.1 %copy-start.5 = (bf16[2,256,512]{1,2,0:T(8,128)(2,1)S(1)}, bf16[2,256,512]{1,2,0:T(8,128)(2,1)}, u32[]{:S(2)}) copy-start(bf16[2,256,512]{1,2,0:T(8,128)(2,1)} %copy-done.4) | copy-start | bytes 1572868
  51.5 6.9 %copy-start.35 = (f32[4,256,256]{2,1,0:T(8,128)S(1)}, f32[4,256,256]{2,1,0:T(8,128)}, u32[]{:S(2)}) copy-start(f32[4,256,256]{2,1,0:T(8,128)} %get-tuple-element.82) | copy-start | bytes 3145732
  51.5 64.0 %collective-permute-start.4 = (f32[2,256,512]{2,1,0:T(8,128)}, f32[2,256,512]{2,1,0:T(8,128)}, u32[]{:S(2)}, u32[]{:S(2)}) collective-permute-start(f32[2,256,512]{2,1,0:T(8,128)} %pad_maximum_fusion), channel_id=1, source_target_pairs={{8,0},{12,4},{16,8},{20,12},{24,16},{28,20},{9,1},{13,5},{17,9},{2... | collective-permute-start | bytes 3145736 | tf_op jit(solution)/shard_map/ppermute | solution.py:15
  57.6 1.0 copy-start.18
  59.4 1.0 copy-start.14
  62.5 78.0 %collective-permute-start.5 = (f32[2,256,512]{2,1,0:T(8,128)}, f32[2,256,512]{2,1,0:T(8,128)}, u32[]{:S(2)}, u32[]{:S(2)}) collective-permute-start(f32[2,256,512]{2,1,0:T(8,128)} %pad_maximum_fusion.1), channel_id=1, source_target_pairs={{4,0},{8,4},{12,8},{16,12},{20,16},{24,20},{28,24},{5,1},{9,5},{13... | collective-permute-start | bytes 3145736 | tf_op jit(solution)/shard_map/ppermute | solution.py:15
  63.8 45.7 %all-to-all-start = ((f32[8,1,8192]{2,1,0:T(1,128)}), f32[8,1,8192]{2,1,0:T(1,128)}, u32[]{:S(2)}, u32[]{:S(2)}) async-start(f32[8,1,8192]{2,1,0:T(1,128)} %bitcast.54), calls=%async_computation | async-start | bytes 524288 | tf_op jit(solution)/shard_map/all_to_all | solution.py:82
  82.6 32.9 %copy-start.3 = (bf16[2,256,512]{1,2,0:T(8,128)(2,1)S(1)}, bf16[2,256,512]{1,2,0:T(8,128)(2,1)}, u32[]{:S(2)}) copy-start(bf16[2,256,512]{1,2,0:T(8,128)(2,1)} %copy-done.2) | copy-start | bytes 1572868
  111.5 12.3 %all-to-all-start.1 = ((f32[8,1,8192]{2,1,0:T(1,128)}), f32[8,1,8192]{2,1,0:T(1,128)}, u32[]{:S(2)}, u32[]{:S(2)}) async-start(f32[8,1,8192]{2,1,0:T(1,128)} %broadcast_in_dim.65), calls=%async_computation.1 | async-start | bytes 524288 | tf_op jit(solution)/shard_map/all_to_all | solution.py:85
  116.5 1.8 %copy-start.32 = (s32[1,256]{1,0:T(1,128)S(1)}, s32[1,256]{1,0:T(1,128)}, u32[]{:S(2)}) copy-start(s32[1,256]{1,0:T(1,128)} %copy-done.31) | copy-start | bytes 3076
  123.7 13.2 %all-to-all-start.2 = ((f32[32,1,2048]{2,1,0:T(1,128)}), f32[32,1,2048]{2,1,0:T(1,128)S(1)}, u32[]{:S(2)}, u32[]{:S(2)}) async-start(f32[32,1,2048]{2,1,0:T(1,128)} %bitcast.56), calls=%async_computation.2 | async-start | bytes 524288 | tf_op jit(solution)/shard_map/all_to_all | solution.py:82
  137.9 13.2 %all-to-all-start.3 = ((f32[32,1,2048]{2,1,0:T(1,128)}), f32[32,1,2048]{2,1,0:T(1,128)S(1)}, u32[]{:S(2)}, u32[]{:S(2)}) async-start(f32[32,1,2048]{2,1,0:T(1,128)} %broadcast_in_dim.66), calls=%async_computation.3 | async-start | bytes 524288 | tf_op jit(solution)/shard_map/all_to_all | solution.py:85
  (14 other events, 11.5 us)

commit v5 on v4

--- a/solution.py
+++ b/solution.py
@@ -264,11 +264,13 @@
         query_sum = query_sum + query_part
         key_terms[distance] = jnp.stack([key_part, value_part])
         if distance > 0:
-            sent[distance] = passed_along(key_terms[distance], "ctx", -distance)
+            sent[distance] = passed_along(
+                key_terms[distance].astype(jnp.bfloat16), "ctx", -distance
+            )
     table_local = jnp.einsum(
         "qp,cqk->cpk", indicator_float, share_sum, precision=lax.Precision.HIGHEST
     )
-    gathered = key_terms[0] + sent[1] + sent[2]
+    gathered = key_terms[0] + sent[1].astype(jnp.float32) + sent[2].astype(jnp.float32)
     query_grad = (query_sum * scale).astype(jnp.bfloat16)
     key_grad = gathered[0].astype(jnp.bfloat16)
     value_grad = gathered[1].astype(jnp.bfloat16)

time: 153 us -> 123 us (0.80)
  waiting for transfers between devices: 46.6 us -> 27.2 us
  other arithmetic: 14.5 us -> 9.68 us
  local copies, waits for them, and re-layouts: 30.9 us -> 26.5 us
  matrix products: 19.7 us -> 17.3 us
    all_to_all x2, waiting for transfers between devices: 32.6 us -> 9.8 us  [summed_by_exchange(): pieces = lax.all_to_all(flat.reshape(size, -1), axes, 0, 0, tiled=True)]
    another operation x2, other arithmetic: 4.19 us -> 1.7 us  [shards(): key_terms[distance] = jnp.stack([key_part, value_part])]
    unnamed x80, local copies, waits for them, and re-layouts: 11.9 us -> 9.88 us
    all_to_all x2, waiting for transfers between devices: 11.6 us -> 13.5 us  [summed_by_exchange(): return lax.all_to_all(spread, axes, 0, 0, tiled=True).reshape(flat.shape)]
  transfers between devices with their start and end apart: 10 -> 10, of which waited for: 5 -> 6; matrix products, arithmetic and copies ran while one was open for 28% -> 26% of each run, Pallas kernels for 0% -> 0%
where the time goes in v5:
time: 123 us; the launch traced here: 122 us
  starting transfers between devices  39.8 us (32%)
  waiting for transfers between devices  27.2 us (22%)
  local copies, waits for them, and re-layouts  26.5 us (22%)
  matrix products  17.3 us (14%)
  other arithmetic  9.68 us (8%)
  between operations  1.45 us (1%)
    all_to_all x2, starting transfers between devices, summed_by_exchange(): pieces = lax.all_to_all(flat.reshape(size, -1), axes, 0, 0, tiled=True)  19.7 us
    all_to_all x2, waiting for transfers between devices, summed_by_exchange(): return lax.all_to_all(spread, axes, 0, 0, tiled=True).reshape(flat.shape)  13.5 us
    ppermute x4, starting transfers between devices, passed_along(): return lax.ppermute(value, axis, pairs)  12 us
    unnamed x80, local copies, waits for them, and re-layouts  9.88 us
    all_to_all x2, waiting for transfers between devices, summed_by_exchange(): pieces = lax.all_to_all(flat.reshape(size, -1), axes, 0, 0, tiled=True)  9.8 us
    all_to_all x2, starting transfers between devices, summed_by_exchange(): return lax.all_to_all(spread, axes, 0, 0, tiled=True).reshape(flat.shape)  6.4 us
    ppermute x2, waiting for transfers between devices, exchanged(): return lax.ppermute(value, axis, pairs)  3.84 us
    dot_general x3, matrix products, shards(): jnp.einsum('ihd,jhd->hij', query_heads, forward_key_heads, preferred_elem...  3.37 us
  transfers between devices with their start and end apart: 10, of which 6 were waited for; matrix products, arithmetic and copies ran while one was open for 26% of the time, Pallas kernels for 0%

profile of v5, /device:TPU:0, one launch (start us, length us, event | category | flops | bytes accessed | tf_op | source)
XLA Modules:
  0.0 121.9 jit_solution(727709828095997914)
XLA Ops:
  0.7 1.2 copy.179
  2.0 5.8 %collective-permute-start.1 = (bf16[2,256,512]{1,2,0:T(8,128)(2,1)S(1)}, bf16[2,256,512]{1,2,0:T(8,128)(2,1)}, u32[]{:S(2)}, u32[]{:S(2)}) collective-permute-start(bf16[2,256,512]{1,2,0:T(8,128)(2,1)S(1)} %pad_maximum_fusion), channel_id=1, source_target_pairs={{0,8},{4,12},{8,16},{12,20},{16,24},{20,28},{1,9},{5,13},{9,17},{1... | collective-permute-start | bytes 1572872 | tf_op jit(solution)/shard_map/ppermute | solution.py:15
  7.8 3.4 %collective-permute-start = (bf16[2,256,512]{1,2,0:T(8,128)(2,1)S(1)}, bf16[2,256,512]{1,2,0:T(8,128)(2,1)S(1)}, u32[]{:S(2)}, u32[]{:S(2)}) collective-permute-start(bf16[2,256,512]{1,2,0:T(8,128)(2,1)S(1)} %pad_maximum_fusion), channel_id=1, source_target_pairs={{0,4},{4,8},{8,12},{12,16},{16,20},{20,24},{24,28},{1,5},{5,9},{9,... | collective-permute-start | bytes 1572872 | tf_op jit(solution)/shard_map/ppermute | solution.py:15
  11.5 0.9 compare_bitcast_fusion.1
  15.7 1.5 %select_convert_fusion.2 = (bf16[4,256,256]{2,1,0:T(8,128)(2,1)S(1)}, f32[4,256,256]{2,1,0:T(8,128)}) fusion(pred[256,256]{1,0:T(8,128)(4,1)S(1)} %copy.130, f32[4,256,256]{2,1,0:T(8,128)S(1)} %convolution_multiply_fusion.5, bf16[4,256,128]{2,1,0:T(8,128)(2,1)S(1)} %fusion.16, s32[256]{0:T(256)S(1)} %bitcast.247), kind=kOutput, calls=%fused_computation.45 | convolution fusion | flops 68976640 | bytes 2950144 | tf_op jit(solution)/shard_map/vqx,px->vqp/dot_general | solution.py:160
  18.0 1.1 convolution_bitcast_fusion.2
  21.0 1.1 fusion.66
  22.1 1.5 %select_convert_fusion = (bf16[4,256,256]{2,1,0:T(8,128)(2,1)S(1)}, f32[4,256,256]{2,1,0:T(8,128)}) fusion(pred[256,256]{1,0:T(8,128)(4,1)S(1)} %copy.143, f32[4,256,256]{2,1,0:T(8,128)S(1)} %fusion.48, bf16[256,4,128]{0,2,1:T(8,128)(2,1)S(1)} %bitcast.209, bf16[256,4,128]{0,2,1:T(8,128)(2,1)S(1)} %bitcast.238), kind=kOutput, calls=%fused_computation.41 | convolution fusion | flops 69206016 | bytes 3211264 | tf_op jit(solution)/shard_map/ihd,jhd->hij/dot_general | solution.py:175
  25.2 1.5 %select_convert_fusion.1 = (bf16[4,256,256]{2,1,0:T(8,128)(2,1)S(1)}, f32[4,256,256]{2,1,0:T(8,128)}) fusion(pred[256,256]{1,0:T(8,128)(4,1)S(1)} %copy.138, f32[4,256,256]{2,1,0:T(8,128)S(1)} %fusion.44, bf16[256,4,128]{0,2,1:T(8,128)(2,1)S(1)} %bitcast.210, bf16[256,4,128]{0,2,1:T(8,128)(2,1)S(1)} %bitcast.239), kind=kOutput, calls=%fused_computation.43 | convolution fusion | flops 69206016 | bytes 3211264 | tf_op jit(solution)/shard_map/ihd,jhd->hij/dot_general | solution.py:175
  28.6 0.9 fusion.19
  30.3 0.9 convolution_convert_fusion
  31.3 0.9 convolution_convert_fusion.1
  32.7 1.0 copy.162
  37.4 0.9 constant_dynamic-slice_fusion.2
  38.9 1.1 fusion.63
  41.5 1.6 %collective-permute-start.3 = (f32[1,65536]{1,0:T(1,128)S(1)}, f32[1,65536]{1,0:T(1,128)}, u32[]{:S(2)}, u32[]{:S(2)}) collective-permute-start(f32[1,65536]{1,0:T(1,128)S(1)} %constant_dynamic-slice_fusion), channel_id=1, source_target_pairs={{0,2},{1,3},{2,0},{3,1},{4,6},{5,7},{6,4},{7,5},{8,10},{9,11},{10,... | collective-permute-start | bytes 786440 | tf_op jit(solution)/shard_map/ppermute | solution.py:21
  44.3 0.9 pad_maximum_fusion.1
  45.2 1.4 %collective-permute-start.4 = (bf16[2,256,512]{2,1,0:T(8,128)(2,1)}, bf16[2,256,512]{2,1,0:T(8,128)(2,1)}, u32[]{:S(2)}, u32[]{:S(2)}) collective-permute-start(bf16[2,256,512]{2,1,0:T(8,128)(2,1)} %pad_maximum_fusion.1), channel_id=1, source_target_pairs={{8,0},{12,4},{16,8},{20,12},{24,16},{28,20},{9,1},{13,5},{17,9},{2... | collective-permute-start | bytes 1572872 | tf_op jit(solution)/shard_map/ppermute | solution.py:15
  46.6 3.6 %collective-permute-done.3 = f32[1,65536]{1,0:T(1,128)} collective-permute-done((f32[1,65536]{1,0:T(1,128)S(1)}, f32[1,65536]{1,0:T(1,128)}, u32[]{:S(2)}, u32[]{:S(2)}) %collective-permute-start.3) | collective-permute-done | bytes 262176 | tf_op jit(solution)/shard_map/ppermute | solution.py:21
  50.2 2.0 %dynamic-slice_add_fusion = f32[1,65536]{1,0:T(1,128)} fusion(f32[1,65536]{1,0:T(1,128)} %collective-permute-done.3, f32[2,65536]{1,0:T(2,128)S(1)} %bitcast_add_fusion, s32[]{:T(128)S(6)} %select_n.144), kind=kLoop, calls=%fused_computation.68 | loop fusion | flops 65536 | bytes 786436 | tf_op jit(solution)/shard_map/add | solution.py:71
  52.2 11.7 %all-to-all-start = ((f32[8,1,8192]{2,1,0:T(1,128)}), f32[8,1,8192]{2,1,0:T(1,128)S(1)}, u32[]{:S(2)}, u32[]{:S(2)}) async-start(f32[8,1,8192]{2,1,0:T(1,128)} %bitcast.54), calls=%async_computation | async-start | bytes 524288 | tf_op jit(solution)/shard_map/all_to_all | solution.py:82
  63.9 1.7 %fusion.8 = bf16[4,256,256]{2,1,0:T(8,128)(2,1)S(1)} fusion(bf16[256,4,128]{0,2,1:T(8,128)(2,1)S(1)} %bitcast.235, f32[4,256,256]{2,1,0:T(8,128)} %get-tuple-element.82, pred[256,256]{1,0:T(8,128)(4,1)S(1)} %copy.138, bf16[256,512]{1,0:T(8,128)(2,1)S(1)} %copy-done.13), kind=kOutput, calls=%fused_computation.15 | convolution fusion | flops 69730304 | bytes 2162688 | tf_op jit(solution)/shard_map/ihd,jhd->hij/dot_general | solution.py:241
  65.7 0.9 fusion.15
  66.6 1.1 copy.165
  68.6 1.4 %collective-permute-start.5 = (bf16[2,256,512]{2,1,0:T(8,128)(2,1)}, bf16[2,256,512]{2,1,0:T(8,128)(2,1)}, u32[]{:S(2)}, u32[]{:S(2)}) collective-permute-start(bf16[2,256,512]{2,1,0:T(8,128)(2,1)} %pad_maximum_fusion.2), channel_id=1, source_target_pairs={{4,0},{8,4},{12,8},{16,12},{20,16},{24,20},{28,24},{5,1},{9,5},{13... | collective-permute-start | bytes 1572872 | tf_op jit(solution)/shard_map/ppermute | solution.py:15
  74.8 8.0 %all-to-all-start.2 = ((f32[32,1,2048]{2,1,0:T(1,128)}), f32[32,1,2048]{2,1,0:T(1,128)S(1)}, u32[]{:S(2)}, u32[]{:S(2)}) async-start(f32[32,1,2048]{2,1,0:T(1,128)} %bitcast.224), calls=%async_computation.2 | async-start | bytes 524288 | tf_op jit(solution)/shard_map/all_to_all | solution.py:82
  83.6 9.7 %all-to-all-done.2 = f32[32,1,2048]{2,1,0:T(1,128)S(1)} async-done(((f32[32,1,2048]{2,1,0:T(1,128)}), f32[32,1,2048]{2,1,0:T(1,128)S(1)}, u32[]{:S(2)}, u32[]{:S(2)}) %all-to-all-start.2) | async-done | bytes 262176 | tf_op jit(solution)/shard_map/all_to_all | solution.py:82
  94.2 3.4 %all-to-all-start.1 = ((f32[8,1,8192]{2,1,0:T(1,128)}), f32[8,1,8192]{2,1,0:T(1,128)S(1)}, u32[]{:S(2)}, u32[]{:S(2)}) async-start(f32[8,1,8192]{2,1,0:T(1,128)} %broadcast_in_dim.65), calls=%async_computation.1 | async-start | bytes 524288 | tf_op jit(solution)/shard_map/all_to_all | solution.py:85
  100.2 6.6 %all-to-all-done.1 = f32[8,1,8192]{2,1,0:T(1,128)S(1)} async-done(((f32[8,1,8192]{2,1,0:T(1,128)}), f32[8,1,8192]{2,1,0:T(1,128)S(1)}, u32[]{:S(2)}, u32[]{:S(2)}) %all-to-all-start.1) | async-done | bytes 262176 | tf_op jit(solution)/shard_map/all_to_all | solution.py:85
  107.6 3.0 %all-to-all-start.3 = ((f32[32,1,2048]{2,1,0:T(1,128)}), f32[32,1,2048]{2,1,0:T(1,128)S(1)}, u32[]{:S(2)}, u32[]{:S(2)}) async-start(f32[32,1,2048]{2,1,0:T(1,128)} %broadcast_in_dim.66), calls=%async_computation.3 | async-start | bytes 524288 | tf_op jit(solution)/shard_map/all_to_all | solution.py:85
  110.6 1.4 %fusion.18 = bf16[2,256,512]{2,1,0:T(8,128)(2,1)S(1)} fusion(f32[1,256,512]{2,1,0:T(8,128)S(1)} %copy-done.2, f32[1,256,512]{2,1,0:T(8,128)S(1)} %copy.161, bf16[2,256,512]{2,1,0:T(8,128)(2,1)} %collective-permute-done.4, bf16[2,256,512]{2,1,0:T(8,128)(2,1)} %collective-permute-done.5), kind=kLoop, calls=%fused_computation.40 | loop fusion | flops 1572864 | bytes 2621440 | tf_op jit(solution)/shard_map/convert.3
  114.3 6.9 %all-to-all-done.3 = f32[32,1,2048]{2,1,0:T(1,128)S(1)} async-done(((f32[32,1,2048]{2,1,0:T(1,128)}), f32[32,1,2048]{2,1,0:T(1,128)S(1)}, u32[]{:S(2)}, u32[]{:S(2)}) %all-to-all-start.3) | async-done | bytes 262176 | tf_op jit(solution)/shard_map/all_to_all | solution.py:85
  (157 shorter events, 31.3 us)
Async XLA Ops:
  0.6 26.8 %copy-start = (bf16[512,512]{1,0:T(8,128)(2,1)S(1)}, bf16[512,512]{1,0:T(8,128)(2,1)}, u32[]{:S(2)}) copy-start(bf16[512,512]{1,0:T(8,128)(2,1)} %param.19) | copy-start | bytes 1572868
  0.6 1.2 copy-start.14
  2.0 12.1 %copy-start.3 = (bf16[2,256,512]{1,2,0:T(8,128)(2,1)}, bf16[2,256,512]{1,2,0:T(8,128)(2,1)S(1)}, u32[]{:S(2)}) copy-start(bf16[2,256,512]{1,2,0:T(8,128)(2,1)S(1)} %pad_maximum_fusion) | copy-start | bytes 1572868
  2.0 18.9 %collective-permute-start.1 = (bf16[2,256,512]{1,2,0:T(8,128)(2,1)S(1)}, bf16[2,256,512]{1,2,0:T(8,128)(2,1)}, u32[]{:S(2)}, u32[]{:S(2)}) collective-permute-start(bf16[2,256,512]{1,2,0:T(8,128)(2,1)S(1)} %pad_maximum_fusion), channel_id=1, source_target_pairs={{0,8},{4,12},{8,16},{12,20},{16,24},{20,28},{1,9},{5,13},{9,17},{1... | collective-permute-start | bytes 1572872 | tf_op jit(solution)/shard_map/ppermute | solution.py:15
  7.8 16.6 %collective-permute-start = (bf16[2,256,512]{1,2,0:T(8,128)(2,1)S(1)}, bf16[2,256,512]{1,2,0:T(8,128)(2,1)S(1)}, u32[]{:S(2)}, u32[]{:S(2)}) collective-permute-start(bf16[2,256,512]{1,2,0:T(8,128)(2,1)S(1)} %pad_maximum_fusion), channel_id=1, source_target_pairs={{0,4},{4,8},{8,12},{12,16},{16,20},{20,24},{24,28},{1,5},{5,9},{9,... | collective-permute-start | bytes 1572872 | tf_op jit(solution)/shard_map/ppermute | solution.py:15
  11.4 1.6 %copy-start.33 = (s32[1,6]{1,0:T(1,128)S(1)}, s32[1,6]{1,0:T(1,128)}, u32[]{:S(2)}) copy-start(s32[1,6]{1,0:T(1,128)} %param.16) | copy-start | bytes 76
  11.4 2.7 %copy-start.24 = (bf16[1,256,512]{2,1,0:T(8,128)(2,1)S(1)}, bf16[1,256,512]{2,1,0:T(8,128)(2,1)}, u32[]{:S(2)}) copy-start(bf16[1,256,512]{2,1,0:T(8,128)(2,1)} %param.10) | copy-start | bytes 786436
  14.9 5.3 %copy-start.28 = (s32[1,256]{1,0:T(1,128)}, s32[1,256]{1,0:T(1,128)S(1)}, u32[]{:S(2)}) copy-start(s32[1,256]{1,0:T(1,128)S(1)} %get-tuple-element.73) | copy-start | bytes 3076
  20.1 2.0 %copy-start.26 = (pred[256,256]{1,0:T(8,128)(4,1)}, pred[256,256]{1,0:T(8,128)(4,1)S(1)}, u32[]{:S(2)}) copy-start(pred[256,256]{1,0:T(8,128)(4,1)S(1)} %copy.143) | copy-start | bytes 196612
  25.2 1.5 %copy-start.11 = (f32[256,4,128]{0,2,1:T(8,128)S(1)}, f32[256,4,128]{0,2,1:T(8,128)}, u32[]{:S(2)}) copy-start(f32[256,4,128]{0,2,1:T(8,128)} %convolution_bitcast_fusion.2) | copy-start | bytes 1572868
  27.2 1.0 copy-start.22
  30.3 1.0 copy-start.10
  31.3 1.0 copy-start.8
  32.7 1.0 copy-start.20
  38.3 1.6 %copy-start.35 = (f32[4,256,256]{2,1,0:T(8,128)S(1)}, f32[4,256,256]{2,1,0:T(8,128)}, u32[]{:S(2)}) copy-start(f32[4,256,256]{2,1,0:T(8,128)} %get-tuple-element.78) | copy-start | bytes 3145732
  38.7 1.2 copy-start.13
  38.8 1.2 copy-start.27
  38.8 2.0 %collective-permute-start.2 = (f32[2,65536]{1,0:T(2,128)S(1)}, f32[2,65536]{1,0:T(2,128)S(1)}, u32[]{:S(2)}, u32[]{:S(2)}) collective-permute-start(f32[2,65536]{1,0:T(2,128)S(1)} %bitcast.234), channel_id=1, source_target_pairs={{0,1},{1,0},{2,3},{3,2},{4,5},{5,4},{6,7},{7,6},{8,9},{9,8},{10,11... | collective-permute-start | bytes 1572872 | tf_op jit(solution)/shard_map/ppermute | solution.py:21
  41.5 8.6 %collective-permute-start.3 = (f32[1,65536]{1,0:T(1,128)S(1)}, f32[1,65536]{1,0:T(1,128)}, u32[]{:S(2)}, u32[]{:S(2)}) collective-permute-start(f32[1,65536]{1,0:T(1,128)S(1)} %constant_dynamic-slice_fusion), channel_id=1, source_target_pairs={{0,2},{1,3},{2,0},{3,1},{4,6},{5,7},{6,4},{7,5},{8,10},{9,11},{10,... | collective-permute-start | bytes 786440 | tf_op jit(solution)/shard_map/ppermute | solution.py:21
  43.4 1.0 copy-start.18
  45.2 7.0 %copy-start.6 = (bf16[2,256,512]{1,2,0:T(8,128)(2,1)S(1)}, bf16[2,256,512]{1,2,0:T(8,128)(2,1)}, u32[]{:S(2)}) copy-start(bf16[2,256,512]{1,2,0:T(8,128)(2,1)} %copy-done.5) | copy-start | bytes 1572868
  45.2 25.7 %collective-permute-start.4 = (bf16[2,256,512]{2,1,0:T(8,128)(2,1)}, bf16[2,256,512]{2,1,0:T(8,128)(2,1)}, u32[]{:S(2)}, u32[]{:S(2)}) collective-permute-start(bf16[2,256,512]{2,1,0:T(8,128)(2,1)} %pad_maximum_fusion.1), channel_id=1, source_target_pairs={{8,0},{12,4},{16,8},{20,12},{24,16},{28,20},{9,1},{13,5},{17,9},{2... | collective-permute-start | bytes 1572872 | tf_op jit(solution)/shard_map/ppermute | solution.py:15
  52.2 22.6 %all-to-all-start = ((f32[8,1,8192]{2,1,0:T(1,128)}), f32[8,1,8192]{2,1,0:T(1,128)S(1)}, u32[]{:S(2)}, u32[]{:S(2)}) async-start(f32[8,1,8192]{2,1,0:T(1,128)} %bitcast.54), calls=%async_computation | async-start | bytes 524288 | tf_op jit(solution)/shard_map/all_to_all | solution.py:82
  66.6 1.1 copy-start.17
  68.6 1.8 %copy-start.29 = (s32[1,256]{1,0:T(1,128)S(1)}, s32[1,256]{1,0:T(1,128)}, u32[]{:S(2)}) copy-start(s32[1,256]{1,0:T(1,128)} %copy-done.28) | copy-start | bytes 3076
  68.6 42.0 %collective-permute-start.5 = (bf16[2,256,512]{2,1,0:T(8,128)(2,1)}, bf16[2,256,512]{2,1,0:T(8,128)(2,1)}, u32[]{:S(2)}, u32[]{:S(2)}) collective-permute-start(bf16[2,256,512]{2,1,0:T(8,128)(2,1)} %pad_maximum_fusion.2), channel_id=1, source_target_pairs={{4,0},{8,4},{12,8},{16,12},{20,16},{24,20},{28,24},{5,1},{9,5},{13... | collective-permute-start | bytes 1572872 | tf_op jit(solution)/shard_map/ppermute | solution.py:15
  70.4 1.0 copy-start.4
  70.4 1.8 %copy-start.34 = (f32[4,256,256]{2,1,0:T(8,128)S(1)}, f32[4,256,256]{2,1,0:T(8,128)}, u32[]{:S(2)}) copy-start(f32[4,256,256]{2,1,0:T(8,128)} %get-tuple-element.80) | copy-start | bytes 3145732
  74.8 18.6 %all-to-all-start.2 = ((f32[32,1,2048]{2,1,0:T(1,128)}), f32[32,1,2048]{2,1,0:T(1,128)S(1)}, u32[]{:S(2)}, u32[]{:S(2)}) async-start(f32[32,1,2048]{2,1,0:T(1,128)} %bitcast.224), calls=%async_computation.2 | async-start | bytes 524288 | tf_op jit(solution)/shard_map/all_to_all | solution.py:82
  94.2 12.6 %all-to-all-start.1 = ((f32[8,1,8192]{2,1,0:T(1,128)}), f32[8,1,8192]{2,1,0:T(1,128)S(1)}, u32[]{:S(2)}, u32[]{:S(2)}) async-start(f32[8,1,8192]{2,1,0:T(1,128)} %broadcast_in_dim.65), calls=%async_computation.1 | async-start | bytes 524288 | tf_op jit(solution)/shard_map/all_to_all | solution.py:85
  100.0 10.6 %copy-start.2 = (f32[1,256,512]{2,1,0:T(8,128)S(1)}, f32[1,256,512]{2,1,0:T(8,128)}, u32[]{:S(2)}) copy-start(f32[1,256,512]{2,1,0:T(8,128)} %copy.162) | copy-start | bytes 1572868
  107.6 13.6 %all-to-all-start.3 = ((f32[32,1,2048]{2,1,0:T(1,128)}), f32[32,1,2048]{2,1,0:T(1,128)S(1)}, u32[]{:S(2)}, u32[]{:S(2)}) async-start(f32[32,1,2048]{2,1,0:T(1,128)} %broadcast_in_dim.66), calls=%async_computation.3 | async-start | bytes 524288 | tf_op jit(solution)/shard_map/all_to_all | solution.py:85
  (14 other events, 11.7 us)

commit v6 on v5

--- a/solution.py
+++ b/solution.py
@@ -231,23 +231,36 @@
     share_sum = None
     key_terms = [None, None, None]
     sent = [None, None, None]
+    held = [None, None, None]
     for distance in (2, 1, 0):
         visible, scores, weights, key_bucket_indicator = tiles[distance]
         pair = slot(window[distance])
-        if distance == 0:
-            sent[2], pair = lax.optimization_barrier((sent[2], pair))
-        key_heads = pair[0].reshape(local_rows, head_count, head_dim)
         value_heads = pair[1].reshape(local_rows, head_count, head_dim)
         weight_grad = jnp.einsum(
             "ihd,jhd->hij", grad_heads, value_heads, preferred_element_type=jnp.float32
         )
+        score_gradient = jnp.where(visible[None], weight_grad * silu_slope(scores), 0.0).astype(
+            jnp.bfloat16
+        )
+        score_gradient = slot(score_gradient)
+        bucket_share_piece = jnp.einsum(
+            "rmw,wx->rmx", score_gradient, key_bucket_indicator, preferred_element_type=jnp.float32
+        )
+        share_sum = bucket_share_piece if share_sum is None else share_sum + bucket_share_piece
+        held[distance] = (score_gradient, pair)
+    table_local = jnp.einsum(
+        "qp,cqk->cpk", indicator_float, share_sum, precision=lax.Precision.HIGHEST
+    )
+    table_grad = summed_by_exchange(table_local.reshape(-1), ("ctx", "dp")).reshape(
+        table_local.shape
+    )
+    for distance in (2, 1, 0):
+        weights = tiles[distance][2]
+        score_gradient, pair = held[distance]
+        key_heads = pair[0].reshape(local_rows, head_count, head_dim)
         value_part = jnp.einsum(
             "hij,ihd->jhd", weights, grad_heads, preferred_element_type=jnp.float32
         ).reshape(local_rows, width)
-        score_gradient = jnp.where(visible[None], weight_grad * silu_slope(scores), 0.0).astype(
-            jnp.bfloat16
-        )
-        score_gradient = slot(score_gradient)
         query_part = jnp.einsum(
             "hij,jhd->ihd", score_gradient, key_heads, preferred_element_type=jnp.float32
         ).reshape(local_rows, width)
@@ -257,27 +270,17 @@
             ).reshape(local_rows, width)
             * scale
         )
-        bucket_share_piece = jnp.einsum(
-            "rmw,wx->rmx", score_gradient, key_bucket_indicator, preferred_element_type=jnp.float32
-        )
-        share_sum = bucket_share_piece if share_sum is None else share_sum + bucket_share_piece
         query_sum = query_sum + query_part
         key_terms[distance] = jnp.stack([key_part, value_part])
         if distance > 0:
             sent[distance] = passed_along(
                 key_terms[distance].astype(jnp.bfloat16), "ctx", -distance
             )
-    table_local = jnp.einsum(
-        "qp,cqk->cpk", indicator_float, share_sum, precision=lax.Precision.HIGHEST
-    )
     gathered = key_terms[0] + sent[1].astype(jnp.float32) + sent[2].astype(jnp.float32)
     query_grad = (query_sum * scale).astype(jnp.bfloat16)
     key_grad = gathered[0].astype(jnp.bfloat16)
     value_grad = gathered[1].astype(jnp.bfloat16)
     projection_grad = weight_state[0].reshape(width // dp_size, width)
-    table_grad = summed_by_exchange(table_local.reshape(-1), ("ctx", "dp")).reshape(
-        table_local.shape
-    )
     return (
         query_grad[None],
         key_grad[None],

time: 123 us -> 128 us (1.041)
  starting transfers between devices: 39.8 us -> 36.3 us
  waiting for transfers between devices: 27.2 us -> 29.9 us
  other arithmetic: 9.68 us -> 12.3 us
  matrix products: 17.3 us -> 19.2 us
    all_to_all x2, starting transfers between devices: 19.7 us -> 16.8 us  [summed_by_exchange(): pieces = lax.all_to_all(flat.reshape(size, -1), axes, 0, 0, tiled=True)]
    all_to_all x2, waiting for transfers between devices: 13.5 us -> 15.5 us  [summed_by_exchange(): return lax.all_to_all(spread, axes, 0, 0, tiled=True).reshape(flat.shape)]
    mul x3, local copies, waits for them, and re-layouts: 1.47 us -> 3.27 us  [shards(): jnp.einsum('hij,ihd->jhd', score_gradient, query_heads, preferred_element...]
    all_to_all x2, waiting for transfers between devices: 9.8 us -> 11.4 us  [summed_by_exchange(): pieces = lax.all_to_all(flat.reshape(size, -1), axes, 0, 0, tiled=True)]
    unnamed x80 -> x82, local copies, waits for them, and re-layouts: 9.88 us -> 9.57 us
  transfers between devices with their start and end apart: 10 -> 10, of which waited for: 6 -> 6; matrix products, arithmetic and copies ran while one was open for 26% -> 25% of each run, Pallas kernels for 0% -> 0%
where the time goes in v6:
time: 128 us; the launch traced here: 127 us
  starting transfers between devices  36.3 us (28%)
  waiting for transfers between devices  29.9 us (23%)
  local copies, waits for them, and re-layouts  27.6 us (22%)
  matrix products  19.2 us (15%)
  other arithmetic  12.3 us (10%)
  between operations  1.45 us (1%)
    all_to_all x2, starting transfers between devices, summed_by_exchange(): pieces = lax.all_to_all(flat.reshape(size, -1), axes, 0, 0, tiled=True)  16.8 us
    all_to_all x2, waiting for transfers between devices, summed_by_exchange(): return lax.all_to_all(spread, axes, 0, 0, tiled=True).reshape(flat.shape)  15.5 us
    all_to_all x2, waiting for transfers between devices, summed_by_exchange(): pieces = lax.all_to_all(flat.reshape(size, -1), axes, 0, 0, tiled=True)  11.4 us
    ppermute x4, starting transfers between devices, passed_along(): return lax.ppermute(value, axis, pairs)  11.3 us
    unnamed x82, local copies, waits for them, and re-layouts  9.57 us
    all_to_all x2, starting transfers between devices, summed_by_exchange(): return lax.all_to_all(spread, axes, 0, 0, tiled=True).reshape(flat.shape)  6.73 us
    dot_general x3, matrix products, shards(): jnp.einsum('ihd,jhd->hij', query_heads, forward_key_heads, preferred_elem...  3.38 us
    mul x3, local copies, waits for them, and re-layouts, shards(): jnp.einsum('hij,ihd->jhd', score_gradient, query_heads, preferred_element...  3.27 us
  transfers between devices with their start and end apart: 10, of which 6 were waited for; matrix products, arithmetic and copies ran while one was open for 25% of the time, Pallas kernels for 0%

profile of v6, /device:TPU:0, one launch (start us, length us, event | category | flops | bytes accessed | tf_op | source)
XLA Modules:
  0.0 126.7 jit_solution(2718298358477026147)
XLA Ops:
  0.7 1.2 copy.185
  2.8 5.0 %collective-permute-start.1 = (bf16[2,256,512]{1,2,0:T(8,128)(2,1)}, bf16[2,256,512]{1,2,0:T(8,128)(2,1)S(1)}, u32[]{:S(2)}, u32[]{:S(2)}) collective-permute-start(bf16[2,256,512]{1,2,0:T(8,128)(2,1)} %pad_maximum_fusion), channel_id=1, source_target_pairs={{0,8},{4,12},{8,16},{12,20},{16,24},{20,28},{1,9},{5,13},{9,17},{1... | collective-permute-start | bytes 1572872 | tf_op jit(solution)/shard_map/ppermute | solution.py:15
  7.8 3.4 %collective-permute-start = (bf16[2,256,512]{1,2,0:T(8,128)(2,1)}, bf16[2,256,512]{1,2,0:T(8,128)(2,1)S(1)}, u32[]{:S(2)}, u32[]{:S(2)}) collective-permute-start(bf16[2,256,512]{1,2,0:T(8,128)(2,1)} %pad_maximum_fusion), channel_id=1, source_target_pairs={{0,4},{4,8},{8,12},{12,16},{16,20},{20,24},{24,28},{1,5},{5,9},{9,... | collective-permute-start | bytes 1572872 | tf_op jit(solution)/shard_map/ppermute | solution.py:15
  15.7 1.5 %select_convert_fusion.2 = (bf16[4,256,256]{2,1,0:T(8,128)(2,1)S(1)}, f32[4,256,256]{2,1,0:T(8,128)}) fusion(pred[256,256]{1,0:T(8,128)(4,1)S(1)} %copy.133, f32[4,256,256]{2,1,0:T(8,128)S(1)} %convolution_multiply_fusion.5, bf16[4,256,128]{2,1,0:T(8,128)(2,1)S(1)} %fusion.18, s32[256]{0:T(256)S(1)} %bitcast.239), kind=kOutput, calls=%fused_computation.47 | convolution fusion | flops 68976640 | bytes 2950144 | tf_op jit(solution)/shard_map/vqx,px->vqp/dot_general | solution.py:160
  18.0 1.1 convolution_bitcast_fusion.3
  21.8 1.5 %select_convert_fusion = (bf16[4,256,256]{2,1,0:T(8,128)(2,1)S(1)}, f32[4,256,256]{2,1,0:T(8,128)}) fusion(pred[256,256]{1,0:T(8,128)(4,1)S(1)} %copy.146, f32[4,256,256]{2,1,0:T(8,128)S(1)} %fusion.45, bf16[256,4,128]{0,2,1:T(8,128)(2,1)S(1)} %bitcast.200, bf16[256,4,128]{0,2,1:T(8,128)(2,1)S(1)} %bitcast.230), kind=kOutput, calls=%fused_computation.43 | convolution fusion | flops 69206016 | bytes 3211264 | tf_op jit(solution)/shard_map/ihd,jhd->hij/dot_general | solution.py:175
  24.4 1.5 %select_convert_fusion.1 = (bf16[4,256,256]{2,1,0:T(8,128)(2,1)S(1)}, f32[4,256,256]{2,1,0:T(8,128)}) fusion(pred[256,256]{1,0:T(8,128)(4,1)S(1)} %copy.141, f32[4,256,256]{2,1,0:T(8,128)S(1)} %fusion.41, bf16[256,4,128]{0,2,1:T(8,128)(2,1)S(1)} %bitcast.201, bf16[256,4,128]{0,2,1:T(8,128)(2,1)S(1)} %bitcast.231), kind=kOutput, calls=%fused_computation.45 | convolution fusion | flops 69206016 | bytes 3211264 | tf_op jit(solution)/shard_map/ihd,jhd->hij/dot_general | solution.py:175
  27.1 1.4 %fusion.31 = (f32[256]{0:T(256)S(1)}, f32[256]{0:T(256)S(1)}, f32[256,512]{1,0:T(8,128)S(1)}) fusion(bf16[1,256,512]{2,1,0:T(8,128)(2,1)S(1)} %copy-done.5, f32[256]{0:T(256)S(1)} %add_rsqrt_fusion, f32[256,512]{1,0:T(8,128)S(1)} %copy.151, f32[256]{0:T(256)S(1)} %broadcast_multiply_fusion.2, bf16[512,512]{1,0:T(8,128)(2,1)S(1)} %copy-done, ...), kind=kOutput, calls=%fused_computation.75 | convolution fusion | flops 135134720 | bytes 2101248 | tf_op jit(solution)/shard_map/dot_general | solution.py:193
  28.5 1.0 fusion.21
  29.5 1.1 copy.186
  31.8 0.9 convolution_convert_fusion.1
  36.8 1.0 copy.162
  38.0 1.0 copy.161
  45.7 1.5 %collective-permute-start.3 = (f32[1,65536]{1,0:T(1,128)}, f32[1,65536]{1,0:T(1,128)}, u32[]{:S(2)}, u32[]{:S(2)}) collective-permute-start(f32[1,65536]{1,0:T(1,128)} %constant_dynamic-slice_fusion), channel_id=1, source_target_pairs={{0,2},{1,3},{2,0},{3,1},{4,6},{5,7},{6,4},{7,5},{8,10},{9,11},{10,... | collective-permute-start | bytes 786440 | tf_op jit(solution)/shard_map/ppermute | solution.py:21
  48.2 1.1 copy.169
  50.1 1.6 %collective-permute-start.5 = (bf16[2,256,512]{2,1,0:T(8,128)(2,1)}, bf16[2,256,512]{2,1,0:T(8,128)(2,1)}, u32[]{:S(2)}, u32[]{:S(2)}) collective-permute-start(bf16[2,256,512]{2,1,0:T(8,128)(2,1)} %pad_maximum_fusion.2), channel_id=1, source_target_pairs={{8,0},{12,4},{16,8},{20,12},{24,16},{28,20},{9,1},{13,5},{17,9},{2... | collective-permute-start | bytes 1572872 | tf_op jit(solution)/shard_map/ppermute | solution.py:15
  51.7 2.6 %collective-permute-done.3 = f32[1,65536]{1,0:T(1,128)} collective-permute-done((f32[1,65536]{1,0:T(1,128)}, f32[1,65536]{1,0:T(1,128)}, u32[]{:S(2)}, u32[]{:S(2)}) %collective-permute-start.3) | collective-permute-done | bytes 262176 | tf_op jit(solution)/shard_map/ppermute | solution.py:21
  54.4 2.0 %dynamic-slice_add_fusion = f32[1,65536]{1,0:T(1,128)} fusion(f32[1,65536]{1,0:T(1,128)} %collective-permute-done.3, f32[2,65536]{1,0:T(2,128)S(1)} %bitcast_add_fusion, s32[]{:T(128)S(6)} %select_n.144), kind=kLoop, calls=%fused_computation.66 | loop fusion | flops 65536 | bytes 786436 | tf_op jit(solution)/shard_map/add | solution.py:71
  57.1 13.4 %all-to-all-start = ((f32[8,1,8192]{2,1,0:T(1,128)}), f32[8,1,8192]{2,1,0:T(1,128)S(1)}, u32[]{:S(2)}, u32[]{:S(2)}) async-start(f32[8,1,8192]{2,1,0:T(1,128)} %bitcast.52), calls=%async_computation | async-start | bytes 524288 | tf_op jit(solution)/shard_map/all_to_all | solution.py:82
  70.6 1.8 %fusion.8 = bf16[4,256,256]{2,1,0:T(8,128)(2,1)S(1)} fusion(bf16[256,4,128]{0,2,1:T(8,128)(2,1)S(1)} %bitcast.210, bf16[256,4,128]{0,2,1:T(8,128)(2,1)S(1)} %bitcast.228, f32[4,256,256]{2,1,0:T(8,128)} %get-tuple-element.76, pred[256,256]{1,0:T(8,128)(4,1)S(1)} %copy.141), kind=kOutput, calls=%fused_computation.15 | convolution fusion | flops 69730304 | bytes 2162688 | tf_op jit(solution)/shard_map/ihd,jhd->hij/dot_general | solution.py:239
  75.6 5.7 %all-to-all-done = f32[8,1,8192]{2,1,0:T(1,128)S(1)} async-done(((f32[8,1,8192]{2,1,0:T(1,128)}), f32[8,1,8192]{2,1,0:T(1,128)S(1)}, u32[]{:S(2)}, u32[]{:S(2)}) %all-to-all-start) | async-done | bytes 262176 | tf_op jit(solution)/shard_map/all_to_all | solution.py:82
  81.3 3.3 %all-to-all-start.2 = ((f32[32,1,2048]{2,1,0:T(1,128)}), f32[32,1,2048]{2,1,0:T(1,128)}, u32[]{:S(2)}, u32[]{:S(2)}) async-start(f32[32,1,2048]{2,1,0:T(1,128)} %bitcast.54), calls=%async_computation.2 | async-start | bytes 524288 | tf_op jit(solution)/shard_map/all_to_all | solution.py:82
  84.6 0.9 fusion.16
  85.5 1.1 copy.165
  87.5 1.3 %collective-permute-start.4 = (bf16[2,256,512]{2,1,0:T(8,128)(2,1)}, bf16[2,256,512]{2,1,0:T(8,128)(2,1)}, u32[]{:S(2)}, u32[]{:S(2)}) collective-permute-start(bf16[2,256,512]{2,1,0:T(8,128)(2,1)} %pad_maximum_fusion.1), channel_id=1, source_target_pairs={{4,0},{8,4},{12,8},{16,12},{20,16},{24,20},{28,24},{5,1},{9,5},{13... | collective-permute-start | bytes 1572872 | tf_op jit(solution)/shard_map/ppermute | solution.py:15
  89.3 5.8 %all-to-all-done.2 = f32[32,1,2048]{2,1,0:T(1,128)} async-done(((f32[32,1,2048]{2,1,0:T(1,128)}), f32[32,1,2048]{2,1,0:T(1,128)}, u32[]{:S(2)}, u32[]{:S(2)}) %all-to-all-start.2) | async-done | bytes 262176 | tf_op jit(solution)/shard_map/all_to_all | solution.py:82
  96.0 3.4 %all-to-all-start.1 = ((f32[8,1,8192]{2,1,0:T(1,128)}), f32[8,1,8192]{2,1,0:T(1,128)S(1)}, u32[]{:S(2)}, u32[]{:S(2)}) async-start(f32[8,1,8192]{2,1,0:T(1,128)} %broadcast_in_dim.65), calls=%async_computation.1 | async-start | bytes 524288 | tf_op jit(solution)/shard_map/all_to_all | solution.py:85
  101.5 1.2 reduce_sum.93
  102.7 8.6 %all-to-all-done.1 = f32[8,1,8192]{2,1,0:T(1,128)S(1)} async-done(((f32[8,1,8192]{2,1,0:T(1,128)}), f32[8,1,8192]{2,1,0:T(1,128)S(1)}, u32[]{:S(2)}, u32[]{:S(2)}) %all-to-all-start.1) | async-done | bytes 262176 | tf_op jit(solution)/shard_map/all_to_all | solution.py:85
  112.1 3.3 %all-to-all-start.3 = ((f32[32,1,2048]{2,1,0:T(1,128)}), f32[32,1,2048]{2,1,0:T(1,128)S(1)}, u32[]{:S(2)}, u32[]{:S(2)}) async-start(f32[32,1,2048]{2,1,0:T(1,128)} %broadcast_in_dim.66), calls=%async_computation.3 | async-start | bytes 524288 | tf_op jit(solution)/shard_map/all_to_all | solution.py:85
  115.5 1.4 %fusion.20 = bf16[2,256,512]{2,1,0:T(8,128)(2,1)S(1)} fusion(f32[1,256,512]{2,1,0:T(8,128)S(1)} %copy-done.6, f32[1,256,512]{2,1,0:T(8,128)S(1)} %copy-done.7, bf16[2,256,512]{2,1,0:T(8,128)(2,1)} %collective-permute-done.5, bf16[2,256,512]{2,1,0:T(8,128)(2,1)} %collective-permute-done.4), kind=kLoop, calls=%fused_computation.42 | loop fusion | flops 1572864 | bytes 2621440 | tf_op jit(solution)/shard_map/convert.3
  119.1 6.9 %all-to-all-done.3 = f32[32,1,2048]{2,1,0:T(1,128)S(1)} async-done(((f32[32,1,2048]{2,1,0:T(1,128)}), f32[32,1,2048]{2,1,0:T(1,128)S(1)}, u32[]{:S(2)}, u32[]{:S(2)}) %all-to-all-start.3) | async-done | bytes 262176 | tf_op jit(solution)/shard_map/all_to_all | solution.py:85
  (158 shorter events, 36.6 us)
Async XLA Ops:
  0.6 26.4 %copy-start = (bf16[512,512]{1,0:T(8,128)(2,1)S(1)}, bf16[512,512]{1,0:T(8,128)(2,1)}, u32[]{:S(2)}) copy-start(bf16[512,512]{1,0:T(8,128)(2,1)} %param.19) | copy-start | bytes 1572868
  0.6 1.2 copy-start.17
  1.8 13.5 %copy-start.3 = (bf16[1,256,512]{1,2,0:T(8,128)(2,1)}, bf16[1,256,512]{1,2,0:T(8,128)(2,1)S(1)}, u32[]{:S(2)}) copy-start(bf16[1,256,512]{1,2,0:T(8,128)(2,1)S(1)} %copy.185) | copy-start | bytes 786436
  2.8 18.2 %collective-permute-start.1 = (bf16[2,256,512]{1,2,0:T(8,128)(2,1)}, bf16[2,256,512]{1,2,0:T(8,128)(2,1)S(1)}, u32[]{:S(2)}, u32[]{:S(2)}) collective-permute-start(bf16[2,256,512]{1,2,0:T(8,128)(2,1)} %pad_maximum_fusion), channel_id=1, source_target_pairs={{0,8},{4,12},{8,16},{12,20},{16,24},{20,28},{1,9},{5,13},{9,17},{1... | collective-permute-start | bytes 1572872 | tf_op jit(solution)/shard_map/ppermute | solution.py:15
  7.8 15.8 %collective-permute-start = (bf16[2,256,512]{1,2,0:T(8,128)(2,1)}, bf16[2,256,512]{1,2,0:T(8,128)(2,1)S(1)}, u32[]{:S(2)}, u32[]{:S(2)}) collective-permute-start(bf16[2,256,512]{1,2,0:T(8,128)(2,1)} %pad_maximum_fusion), channel_id=1, source_target_pairs={{0,4},{4,8},{8,12},{12,16},{16,20},{20,24},{24,28},{1,5},{5,9},{9,... | collective-permute-start | bytes 1572872 | tf_op jit(solution)/shard_map/ppermute | solution.py:15
  11.4 1.6 %copy-start.34 = (s32[1,6]{1,0:T(1,128)S(1)}, s32[1,6]{1,0:T(1,128)}, u32[]{:S(2)}) copy-start(s32[1,6]{1,0:T(1,128)} %param.16) | copy-start | bytes 76
  11.5 2.7 %copy-start.25 = (bf16[1,256,512]{2,1,0:T(8,128)(2,1)S(1)}, bf16[1,256,512]{2,1,0:T(8,128)(2,1)}, u32[]{:S(2)}) copy-start(bf16[1,256,512]{2,1,0:T(8,128)(2,1)} %param.10) | copy-start | bytes 786436
  14.9 5.3 %copy-start.29 = (s32[1,256]{1,0:T(1,128)}, s32[1,256]{1,0:T(1,128)S(1)}, u32[]{:S(2)}) copy-start(s32[1,256]{1,0:T(1,128)S(1)} %get-tuple-element.67) | copy-start | bytes 3076
  20.1 1.7 %copy-start.27 = (pred[256,256]{1,0:T(8,128)(4,1)}, pred[256,256]{1,0:T(8,128)(4,1)S(1)}, u32[]{:S(2)}) copy-start(pred[256,256]{1,0:T(8,128)(4,1)S(1)} %copy.146) | copy-start | bytes 196612
  24.4 1.5 %copy-start.14 = (f32[256,4,128]{0,2,1:T(8,128)S(1)}, f32[256,4,128]{0,2,1:T(8,128)}, u32[]{:S(2)}) copy-start(f32[256,4,128]{0,2,1:T(8,128)} %convolution_bitcast_fusion.3) | copy-start | bytes 1572868
  30.6 3.2 %copy-start.1 = (bf16[256,512]{0,1:T(8,128)(2,1)}, bf16[256,512]{0,1:T(8,128)(2,1)S(1)}, u32[]{:S(2)}) copy-start(bf16[256,512]{0,1:T(8,128)(2,1)S(1)} %copy.186) | copy-start | bytes 786436
  30.6 1.1 copy-start.16
  31.8 1.0 copy-start.13
  32.8 1.2 copy-start.35
  41.8 1.0 copy-start.11
  41.8 1.4 %copy-start.36 = (f32[4,256,256]{2,1,0:T(8,128)S(1)}, f32[4,256,256]{2,1,0:T(8,128)}, u32[]{:S(2)}) copy-start(f32[4,256,256]{2,1,0:T(8,128)} %get-tuple-element.72) | copy-start | bytes 3145732
  42.2 1.1 copy-start.2
  42.2 1.1 copy-start.28
  42.2 2.0 %collective-permute-start.2 = (f32[2,65536]{1,0:T(2,128)S(1)}, f32[2,65536]{1,0:T(2,128)S(1)}, u32[]{:S(2)}, u32[]{:S(2)}) collective-permute-start(f32[2,65536]{1,0:T(2,128)S(1)} %bitcast.227), channel_id=1, source_target_pairs={{0,1},{1,0},{2,3},{3,2},{4,5},{5,4},{6,7},{7,6},{8,9},{9,8},{10,11... | collective-permute-start | bytes 1572872 | tf_op jit(solution)/shard_map/ppermute | solution.py:21
  45.7 8.7 %collective-permute-start.3 = (f32[1,65536]{1,0:T(1,128)}, f32[1,65536]{1,0:T(1,128)}, u32[]{:S(2)}, u32[]{:S(2)}) collective-permute-start(f32[1,65536]{1,0:T(1,128)} %constant_dynamic-slice_fusion), channel_id=1, source_target_pairs={{0,2},{1,3},{2,0},{3,1},{4,6},{5,7},{6,4},{7,5},{8,10},{9,11},{10,... | collective-permute-start | bytes 786440 | tf_op jit(solution)/shard_map/ppermute | solution.py:21
  48.2 1.1 copy-start.21
  50.1 6.2 %copy-start.9 = (bf16[2,256,512]{1,2,0:T(8,128)(2,1)S(1)}, bf16[2,256,512]{1,2,0:T(8,128)(2,1)}, u32[]{:S(2)}) copy-start(bf16[2,256,512]{1,2,0:T(8,128)(2,1)} %copy-done.8) | copy-start | bytes 1572868
  50.1 65.3 %collective-permute-start.5 = (bf16[2,256,512]{2,1,0:T(8,128)(2,1)}, bf16[2,256,512]{2,1,0:T(8,128)(2,1)}, u32[]{:S(2)}, u32[]{:S(2)}) collective-permute-start(bf16[2,256,512]{2,1,0:T(8,128)(2,1)} %pad_maximum_fusion.2), channel_id=1, source_target_pairs={{8,0},{12,4},{16,8},{20,12},{24,16},{28,20},{9,1},{13,5},{17,9},{2... | collective-permute-start | bytes 1572872 | tf_op jit(solution)/shard_map/ppermute | solution.py:15
  57.1 24.1 %all-to-all-start = ((f32[8,1,8192]{2,1,0:T(1,128)}), f32[8,1,8192]{2,1,0:T(1,128)S(1)}, u32[]{:S(2)}, u32[]{:S(2)}) async-start(f32[8,1,8192]{2,1,0:T(1,128)} %bitcast.52), calls=%async_computation | async-start | bytes 524288 | tf_op jit(solution)/shard_map/all_to_all | solution.py:82
  81.3 13.9 %all-to-all-start.2 = ((f32[32,1,2048]{2,1,0:T(1,128)}), f32[32,1,2048]{2,1,0:T(1,128)}, u32[]{:S(2)}, u32[]{:S(2)}) async-start(f32[32,1,2048]{2,1,0:T(1,128)} %bitcast.54), calls=%async_computation.2 | async-start | bytes 524288 | tf_op jit(solution)/shard_map/all_to_all | solution.py:82
  85.5 1.1 copy-start.20
  86.7 2.2 %copy-start.18 = (bf16[1,256,512]{1,2,0:T(8,128)(2,1)S(1)}, bf16[1,256,512]{1,2,0:T(8,128)(2,1)}, u32[]{:S(2)}) copy-start(bf16[1,256,512]{1,2,0:T(8,128)(2,1)} %get-tuple-element.56) | copy-start | bytes 786436
  87.5 27.9 %collective-permute-start.4 = (bf16[2,256,512]{2,1,0:T(8,128)(2,1)}, bf16[2,256,512]{2,1,0:T(8,128)(2,1)}, u32[]{:S(2)}, u32[]{:S(2)}) collective-permute-start(bf16[2,256,512]{2,1,0:T(8,128)(2,1)} %pad_maximum_fusion.1), channel_id=1, source_target_pairs={{4,0},{8,4},{12,8},{16,12},{20,16},{24,20},{28,24},{5,1},{9,5},{13... | collective-permute-start | bytes 1572872 | tf_op jit(solution)/shard_map/ppermute | solution.py:15
  96.0 15.3 %all-to-all-start.1 = ((f32[8,1,8192]{2,1,0:T(1,128)}), f32[8,1,8192]{2,1,0:T(1,128)S(1)}, u32[]{:S(2)}, u32[]{:S(2)}) async-start(f32[8,1,8192]{2,1,0:T(1,128)} %broadcast_in_dim.65), calls=%async_computation.1 | async-start | bytes 524288 | tf_op jit(solution)/shard_map/all_to_all | solution.py:85
  101.5 14.0 %copy-start.6 = (f32[1,256,512]{2,1,0:T(8,128)S(1)}, f32[1,256,512]{2,1,0:T(8,128)}, u32[]{:S(2)}) copy-start(f32[1,256,512]{2,1,0:T(8,128)} %copy.162) | copy-start | bytes 1572868
  101.5 14.0 %copy-start.7 = (f32[1,256,512]{2,1,0:T(8,128)S(1)}, f32[1,256,512]{2,1,0:T(8,128)}, u32[]{:S(2)}) copy-start(f32[1,256,512]{2,1,0:T(8,128)} %copy.161) | copy-start | bytes 1572868
  112.1 13.9 %all-to-all-start.3 = ((f32[32,1,2048]{2,1,0:T(1,128)}), f32[32,1,2048]{2,1,0:T(1,128)S(1)}, u32[]{:S(2)}, u32[]{:S(2)}) async-start(f32[32,1,2048]{2,1,0:T(1,128)} %broadcast_in_dim.66), calls=%async_computation.3 | async-start | bytes 524288 | tf_op jit(solution)/shard_map/all_to_all | solution.py:85
  (15 other events, 12.8 us)

commit v7 on v5

--- a/solution.py
+++ b/solution.py
@@ -212,13 +212,15 @@
         mixed, grad_rows, (((0,), (0,)), ((), ())), preferred_element_type=jnp.float32
     )
     weight_plan = [("split", "dp", mask) for mask in axis_bits("dp")]
-    weight_plan.append(("exchange", "ctx", 0))
+    weight_plan += [("split", "ctx", mask) for mask in axis_bits("ctx")]
+    weight_plan += [("join", "ctx", mask) for mask in reversed(axis_bits("ctx"))]
     weight_state = [weight_term.reshape(dp_size, -1), 0]
 
-    def slot(anchor):
+    def slot(anchor, tied=True):
         blocks, done = weight_state
         if done < len(weight_plan):
-            blocks, anchor = lax.optimization_barrier((blocks, anchor))
+            if tied:
+                blocks, anchor = lax.optimization_barrier((blocks, anchor))
             kind, axis, mask = weight_plan[done]
             if kind == "exchange":
                 weight_state[0] = summed_by_exchange(blocks.reshape(-1), (axis,))
@@ -270,6 +272,8 @@
     table_local = jnp.einsum(
         "qp,cqk->cpk", indicator_float, share_sum, precision=lax.Precision.HIGHEST
     )
+    while weight_state[1] < len(weight_plan):
+        slot(None, tied=False)
     gathered = key_terms[0] + sent[1].astype(jnp.float32) + sent[2].astype(jnp.float32)
     query_grad = (query_sum * scale).astype(jnp.bfloat16)
     key_grad = gathered[0].astype(jnp.bfloat16)

time: 123 us -> 126 us (1.024)
  other arithmetic: 9.68 us -> 13.5 us
  waiting for transfers between devices: 27.2 us -> 28.7 us
  local copies, waits for them, and re-layouts: 26.5 us -> 25.2 us
    ppermute x2 -> x8, starting transfers between devices: 1.65 us -> 20.2 us  [exchanged(): return lax.ppermute(value, axis, pairs)]
    all_to_all x2 -> x1, starting transfers between devices: 19.7 us -> 3.34 us  [summed_by_exchange(): pieces = lax.all_to_all(flat.reshape(size, -1), axes, 0, 0, tiled=True)]
    ppermute x2 -> x8, waiting for transfers between devices: 3.84 us -> 19.5 us  [exchanged(): return lax.ppermute(value, axis, pairs)]
    all_to_all x2 -> x1, waiting for transfers between devices: 9.8 us -> 0.97 us  [summed_by_exchange(): pieces = lax.all_to_all(flat.reshape(size, -1), axes, 0, 0, tiled=True)]
    all_to_all x2 -> x1, waiting for transfers between devices: 13.5 us -> 8.31 us  [summed_by_exchange(): return lax.all_to_all(spread, axes, 0, 0, tiled=True).reshape(flat.shape)]
    optimization_barrier x0 -> x3, other arithmetic: none -> 3.01 us  [slot(): blocks, anchor = lax.optimization_barrier((blocks, anchor))]
    all_to_all x2 -> x1, starting transfers between devices: 6.4 us -> 4.17 us  [summed_by_exchange(): return lax.all_to_all(spread, axes, 0, 0, tiled=True).reshape(flat.shape)]
    add x2 -> x5, other arithmetic: 2.56 us -> 3.01 us  [plan_step(): return keep + exchanged(send, axis, mask)]
  transfers between devices with their start and end apart: 10 -> 14, of which waited for: 6 -> 8; matrix products, arithmetic and copies ran while one was open for 26% -> 27% of each run, Pallas kernels for 0% -> 0%
where the time goes in v7:
time: 126 us; the launch traced here: 125 us
  starting transfers between devices  39.8 us (32%)
  waiting for transfers between devices  28.7 us (23%)
  local copies, waits for them, and re-layouts  25.2 us (20%)
  matrix products  16.6 us (13%)
  other arithmetic  13.5 us (11%)
  between operations  1.65 us (1%)
    ppermute x8, starting transfers between devices, exchanged(): return lax.ppermute(value, axis, pairs)  20.2 us
    ppermute x8, waiting for transfers between devices, exchanged(): return lax.ppermute(value, axis, pairs)  19.5 us
    ppermute x4, starting transfers between devices, passed_along(): return lax.ppermute(value, axis, pairs)  12.1 us
    unnamed x74, local copies, waits for them, and re-layouts  9.44 us
    all_to_all x1, waiting for transfers between devices, summed_by_exchange(): return lax.all_to_all(spread, axes, 0, 0, tiled=True).reshape(flat.shape)  8.31 us
    all_to_all x1, starting transfers between devices, summed_by_exchange(): return lax.all_to_all(spread, axes, 0, 0, tiled=True).reshape(flat.shape)  4.17 us
    dot_general x3, matrix products, shards(): jnp.einsum('ihd,jhd->hij', query_heads, forward_key_heads, preferred_elem...  3.36 us
    all_to_all x1, starting transfers between devices, summed_by_exchange(): pieces = lax.all_to_all(flat.reshape(size, -1), axes, 0, 0, tiled=True)  3.34 us
  transfers between devices with their start and end apart: 14, of which 8 were waited for; matrix products, arithmetic and copies ran while one was open for 27% of the time, Pallas kernels for 0%

profile of v7, /device:TPU:0, one launch (start us, length us, event | category | flops | bytes accessed | tf_op | source)
XLA Modules:
  0.0 125.5 jit_solution(13350402715997163829)
XLA Ops:
  0.7 1.2 copy.179
  2.0 5.8 %collective-permute-start.1 = (bf16[2,256,512]{1,2,0:T(8,128)(2,1)S(1)}, bf16[2,256,512]{1,2,0:T(8,128)(2,1)}, u32[]{:S(2)}, u32[]{:S(2)}) collective-permute-start(bf16[2,256,512]{1,2,0:T(8,128)(2,1)S(1)} %pad_maximum_fusion), channel_id=1, source_target_pairs={{0,8},{4,12},{8,16},{12,20},{16,24},{20,28},{1,9},{5,13},{9,17},{1... | collective-permute-start | bytes 1572872 | tf_op jit(solution)/shard_map/ppermute | solution.py:15
  7.8 3.4 %collective-permute-start = (bf16[2,256,512]{1,2,0:T(8,128)(2,1)S(1)}, bf16[2,256,512]{1,2,0:T(8,128)(2,1)S(1)}, u32[]{:S(2)}, u32[]{:S(2)}) collective-permute-start(bf16[2,256,512]{1,2,0:T(8,128)(2,1)S(1)} %pad_maximum_fusion), channel_id=1, source_target_pairs={{0,4},{4,8},{8,12},{12,16},{16,20},{20,24},{24,28},{1,5},{5,9},{9,... | collective-permute-start | bytes 1572872 | tf_op jit(solution)/shard_map/ppermute | solution.py:15
  15.8 1.5 %select_convert_fusion.2 = (bf16[4,256,256]{2,1,0:T(8,128)(2,1)S(1)}, f32[4,256,256]{2,1,0:T(8,128)}) fusion(pred[256,256]{1,0:T(8,128)(4,1)S(1)} %copy.130, f32[4,256,256]{2,1,0:T(8,128)S(1)} %convolution_multiply_fusion.5, bf16[4,256,128]{2,1,0:T(8,128)(2,1)S(1)} %fusion.16, s32[256]{0:T(256)S(1)} %bitcast.257), kind=kOutput, calls=%fused_computation.45 | convolution fusion | flops 68976640 | bytes 2950144 | tf_op jit(solution)/shard_map/vqx,px->vqp/dot_general | solution.py:160
  18.1 1.1 convolution_bitcast_fusion.2
  21.1 1.1 fusion.66
  22.2 1.5 %select_convert_fusion = (bf16[4,256,256]{2,1,0:T(8,128)(2,1)S(1)}, f32[4,256,256]{2,1,0:T(8,128)}) fusion(pred[256,256]{1,0:T(8,128)(4,1)S(1)} %copy.143, f32[4,256,256]{2,1,0:T(8,128)S(1)} %fusion.48, bf16[256,4,128]{0,2,1:T(8,128)(2,1)S(1)} %bitcast.220, bf16[256,4,128]{0,2,1:T(8,128)(2,1)S(1)} %bitcast.248), kind=kOutput, calls=%fused_computation.41 | convolution fusion | flops 69206016 | bytes 3211264 | tf_op jit(solution)/shard_map/ihd,jhd->hij/dot_general | solution.py:175
  25.3 1.5 %select_convert_fusion.1 = (bf16[4,256,256]{2,1,0:T(8,128)(2,1)S(1)}, f32[4,256,256]{2,1,0:T(8,128)}) fusion(pred[256,256]{1,0:T(8,128)(4,1)S(1)} %copy.138, f32[4,256,256]{2,1,0:T(8,128)S(1)} %fusion.44, bf16[256,4,128]{0,2,1:T(8,128)(2,1)S(1)} %bitcast.221, bf16[256,4,128]{0,2,1:T(8,128)(2,1)S(1)} %bitcast.249), kind=kOutput, calls=%fused_computation.43 | convolution fusion | flops 69206016 | bytes 3211264 | tf_op jit(solution)/shard_map/ihd,jhd->hij/dot_general | solution.py:175
  31.4 0.9 convolution_convert_fusion.1
  32.7 1.0 copy.162
  38.9 1.1 fusion.63
  41.6 1.6 %collective-permute-start.3 = (f32[1,65536]{1,0:T(1,128)S(1)}, f32[1,65536]{1,0:T(1,128)}, u32[]{:S(2)}, u32[]{:S(2)}) collective-permute-start(f32[1,65536]{1,0:T(1,128)S(1)} %constant_dynamic-slice_fusion), channel_id=1, source_target_pairs={{0,2},{1,3},{2,0},{3,1},{4,6},{5,7},{6,4},{7,5},{8,10},{9,11},{10,... | collective-permute-start | bytes 786440 | tf_op jit(solution)/shard_map/ppermute | solution.py:21
  45.2 1.6 %collective-permute-start.5 = (bf16[2,256,512]{2,1,0:T(8,128)(2,1)}, bf16[2,256,512]{2,1,0:T(8,128)(2,1)}, u32[]{:S(2)}, u32[]{:S(2)}) collective-permute-start(bf16[2,256,512]{2,1,0:T(8,128)(2,1)} %pad_maximum_fusion.1), channel_id=1, source_target_pairs={{8,0},{12,4},{16,8},{20,12},{24,16},{28,20},{9,1},{13,5},{17,9},{2... | collective-permute-start | bytes 1572872 | tf_op jit(solution)/shard_map/ppermute | solution.py:15
  46.8 3.4 %collective-permute-done.3 = f32[1,65536]{1,0:T(1,128)} collective-permute-done((f32[1,65536]{1,0:T(1,128)S(1)}, f32[1,65536]{1,0:T(1,128)}, u32[]{:S(2)}, u32[]{:S(2)}) %collective-permute-start.3) | collective-permute-done | bytes 262176 | tf_op jit(solution)/shard_map/ppermute | solution.py:21
  50.2 1.3 %dynamic-slice_add_fusion = f32[1,65536]{1,0:T(1,128)S(1)} fusion(f32[1,65536]{1,0:T(1,128)} %collective-permute-done.3, f32[2,65536]{1,0:T(2,128)S(1)} %bitcast_add_fusion, s32[]{:T(128)S(6)} %select_n.229), kind=kLoop, calls=%fused_computation.69 | loop fusion | flops 65536 | bytes 786436 | tf_op jit(solution)/shard_map/add | solution.py:71
  52.1 1.3 %reduce.16 = f32[65536]{0:T(1024)S(1)} reduce(f32[1,65536]{1,0:T(1,128)S(1)} %dynamic-slice_add_fusion, f32[]{:T(128)} %broadcast.614), dimensions={0}, to_apply=%get-tuple-element.25.reduce_sub_computation.3 | reduce | bytes 524292 | tf_op jit(solution)/shard_map/optimization_barrier | solution.py:223
  53.6 6.5 %collective-permute-start.4 = (f32[1,32768]{1,0:T(1,128)S(1)}, f32[1,32768]{1,0:T(1,128)S(1)}, u32[]{:S(2)}, u32[]{:S(2)}) collective-permute-start(f32[1,32768]{1,0:T(1,128)S(1)} %dynamic-slice_bitcast_fusion), channel_id=1, source_target_pairs={{0,4},{4,0},{8,12},{12,8},{16,20},{20,16},{24,28},{28,24},{1,5},{5... | collective-permute-start | bytes 393224 | tf_op jit(solution)/shard_map/ppermute | solution.py:21
  60.1 1.7 %fusion.8 = bf16[4,256,256]{2,1,0:T(8,128)(2,1)S(1)} fusion(bf16[256,4,128]{0,2,1:T(8,128)(2,1)S(1)} %bitcast.245, f32[4,256,256]{2,1,0:T(8,128)} %get-tuple-element.100, pred[256,256]{1,0:T(8,128)(4,1)S(1)} %copy.138, bf16[256,512]{1,0:T(8,128)(2,1)S(1)} %copy-done.13), kind=kOutput, calls=%fused_computation.15 | convolution fusion | flops 69730304 | bytes 2162688 | tf_op jit(solution)/shard_map/ihd,jhd->hij/dot_general | solution.py:243
  61.9 1.3 %collective-permute-done.4 = f32[1,32768]{1,0:T(1,128)S(1)} collective-permute-done((f32[1,32768]{1,0:T(1,128)S(1)}, f32[1,32768]{1,0:T(1,128)S(1)}, u32[]{:S(2)}, u32[]{:S(2)}) %collective-permute-start.4) | collective-permute-done | bytes 131104 | tf_op jit(solution)/shard_map/ppermute | solution.py:21
  63.3 1.0 reduce.17
  65.1 3.9 %collective-permute-start.6 = (f32[1,16384]{1,0:T(1,128)}, f32[1,16384]{1,0:T(1,128)}, u32[]{:S(2)}, u32[]{:S(2)}) collective-permute-start(f32[1,16384]{1,0:T(1,128)} %dynamic-slice_bitcast_fusion.1), channel_id=1, source_target_pairs={{0,8},{4,12},{8,0},{12,4},{16,24},{20,28},{24,16},{28,20},{1,9},{5... | collective-permute-start | bytes 196616 | tf_op jit(solution)/shard_map/ppermute | solution.py:21
  73.3 3.1 %collective-permute-start.7 = (f32[1,8192]{1,0:T(1,128)S(1)}, f32[1,8192]{1,0:T(1,128)S(1)}, u32[]{:S(2)}, u32[]{:S(2)}) collective-permute-start(f32[1,8192]{1,0:T(1,128)S(1)} %dynamic-slice_bitcast_fusion.2), channel_id=1, source_target_pairs={{0,16},{4,20},{8,24},{12,28},{16,0},{20,4},{24,8},{28,12},{1,17},{... | collective-permute-start | bytes 98312 | tf_op jit(solution)/shard_map/ppermute | solution.py:21
  77.3 1.3 %collective-permute-start.8 = (bf16[2,256,512]{2,1,0:T(8,128)(2,1)}, bf16[2,256,512]{2,1,0:T(8,128)(2,1)}, u32[]{:S(2)}, u32[]{:S(2)}) collective-permute-start(bf16[2,256,512]{2,1,0:T(8,128)(2,1)} %pad_maximum_fusion.2), channel_id=1, source_target_pairs={{4,0},{8,4},{12,8},{16,12},{20,16},{24,20},{28,24},{5,1},{9,5},{13... | collective-permute-start | bytes 1572872 | tf_op jit(solution)/shard_map/ppermute | solution.py:15
  80.0 3.2 %collective-permute-start.9 = (f32[1,8192]{1,0:T(1,128)S(1)}, f32[1,8192]{1,0:T(1,128)S(1)}, u32[]{:S(2)}, u32[]{:S(2)}) collective-permute-start(f32[1,8192]{1,0:T(1,128)S(1)} %bitcast_add_fusion.3), channel_id=1, source_target_pairs={{0,16},{4,20},{8,24},{12,28},{16,0},{20,4},{24,8},{28,12},{1,17},{... | collective-permute-start | bytes 98312 | tf_op jit(solution)/shard_map/ppermute | solution.py:21
  83.9 8.7 %collective-permute-done.9 = f32[1,8192]{1,0:T(1,128)S(1)} collective-permute-done((f32[1,8192]{1,0:T(1,128)S(1)}, f32[1,8192]{1,0:T(1,128)S(1)}, u32[]{:S(2)}, u32[]{:S(2)}) %collective-permute-start.9) | collective-permute-done | bytes 32800 | tf_op jit(solution)/shard_map/ppermute | solution.py:21
  95.1 3.3 %all-to-all-start = ((f32[32,1,2048]{2,1,0:T(1,128)}), f32[32,1,2048]{2,1,0:T(1,128)S(1)}, u32[]{:S(2)}, u32[]{:S(2)}) async-start(f32[32,1,2048]{2,1,0:T(1,128)} %bitcast.61), calls=%async_computation | async-start | bytes 524288 | tf_op jit(solution)/shard_map/all_to_all | solution.py:82
  98.7 1.8 %collective-permute-start.11 = (f32[1,32768]{1,0:T(1,128)S(1)}, f32[1,32768]{1,0:T(1,128)S(1)}, u32[]{:S(2)}, u32[]{:S(2)}) collective-permute-start(f32[1,32768]{1,0:T(1,128)S(1)} %pad_maximum_fusion.3), channel_id=1, source_target_pairs={{0,4},{4,0},{8,12},{12,8},{16,20},{20,16},{24,28},{28,24},{1,5},{5... | collective-permute-start | bytes 393224 | tf_op jit(solution)/shard_map/ppermute | solution.py:21
  101.0 5.4 %collective-permute-done.11 = f32[1,32768]{1,0:T(1,128)S(1)} collective-permute-done((f32[1,32768]{1,0:T(1,128)S(1)}, f32[1,32768]{1,0:T(1,128)S(1)}, u32[]{:S(2)}, u32[]{:S(2)}) %collective-permute-start.11) | collective-permute-done | bytes 131104 | tf_op jit(solution)/shard_map/ppermute | solution.py:21
  108.1 1.0 all-to-all-done
  110.0 4.2 %all-to-all-start.1 = ((f32[32,1,2048]{2,1,0:T(1,128)}), f32[32,1,2048]{2,1,0:T(1,128)S(1)}, u32[]{:S(2)}, u32[]{:S(2)}) async-start(f32[32,1,2048]{2,1,0:T(1,128)} %broadcast_in_dim.63), calls=%async_computation.1 | async-start | bytes 524288 | tf_op jit(solution)/shard_map/all_to_all | solution.py:85
  114.2 1.4 %fusion.18 = bf16[2,256,512]{2,1,0:T(8,128)(2,1)S(1)} fusion(f32[1,256,512]{2,1,0:T(8,128)S(1)} %copy-done.2, f32[1,256,512]{2,1,0:T(8,128)S(1)} %copy.161, bf16[2,256,512]{2,1,0:T(8,128)(2,1)} %collective-permute-done.5, bf16[2,256,512]{2,1,0:T(8,128)(2,1)} %collective-permute-done.8), kind=kLoop, calls=%fused_computation.40 | loop fusion | flops 1572864 | bytes 2621440 | tf_op jit(solution)/shard_map/convert.3
  116.5 8.3 %all-to-all-done.1 = f32[32,1,2048]{2,1,0:T(1,128)S(1)} async-done(((f32[32,1,2048]{2,1,0:T(1,128)}), f32[32,1,2048]{2,1,0:T(1,128)S(1)}, u32[]{:S(2)}, u32[]{:S(2)}) %all-to-all-start.1) | async-done | bytes 262176 | tf_op jit(solution)/shard_map/all_to_all | solution.py:85
  (175 shorter events, 38.6 us)
Async XLA Ops:
  0.6 26.8 %copy-start = (bf16[512,512]{1,0:T(8,128)(2,1)S(1)}, bf16[512,512]{1,0:T(8,128)(2,1)}, u32[]{:S(2)}) copy-start(bf16[512,512]{1,0:T(8,128)(2,1)} %param.19) | copy-start | bytes 1572868
  0.6 1.2 copy-start.14
  2.0 12.1 %copy-start.3 = (bf16[2,256,512]{1,2,0:T(8,128)(2,1)}, bf16[2,256,512]{1,2,0:T(8,128)(2,1)S(1)}, u32[]{:S(2)}) copy-start(bf16[2,256,512]{1,2,0:T(8,128)(2,1)S(1)} %pad_maximum_fusion) | copy-start | bytes 1572868
  2.0 19.0 %collective-permute-start.1 = (bf16[2,256,512]{1,2,0:T(8,128)(2,1)S(1)}, bf16[2,256,512]{1,2,0:T(8,128)(2,1)}, u32[]{:S(2)}, u32[]{:S(2)}) collective-permute-start(bf16[2,256,512]{1,2,0:T(8,128)(2,1)S(1)} %pad_maximum_fusion), channel_id=1, source_target_pairs={{0,8},{4,12},{8,16},{12,20},{16,24},{20,28},{1,9},{5,13},{9,17},{1... | collective-permute-start | bytes 1572872 | tf_op jit(solution)/shard_map/ppermute | solution.py:15
  7.8 16.7 %collective-permute-start = (bf16[2,256,512]{1,2,0:T(8,128)(2,1)S(1)}, bf16[2,256,512]{1,2,0:T(8,128)(2,1)S(1)}, u32[]{:S(2)}, u32[]{:S(2)}) collective-permute-start(bf16[2,256,512]{1,2,0:T(8,128)(2,1)S(1)} %pad_maximum_fusion), channel_id=1, source_target_pairs={{0,4},{4,8},{8,12},{12,16},{16,20},{20,24},{24,28},{1,5},{5,9},{9,... | collective-permute-start | bytes 1572872 | tf_op jit(solution)/shard_map/ppermute | solution.py:15
  11.4 1.6 %copy-start.30 = (s32[1,6]{1,0:T(1,128)S(1)}, s32[1,6]{1,0:T(1,128)}, u32[]{:S(2)}) copy-start(s32[1,6]{1,0:T(1,128)} %param.16) | copy-start | bytes 76
  11.5 2.7 %copy-start.21 = (bf16[1,256,512]{2,1,0:T(8,128)(2,1)S(1)}, bf16[1,256,512]{2,1,0:T(8,128)(2,1)}, u32[]{:S(2)}) copy-start(bf16[1,256,512]{2,1,0:T(8,128)(2,1)} %param.10) | copy-start | bytes 786436
  14.2 1.6 %copy-start.23 = (pred[256,256]{1,0:T(8,128)(4,1)}, pred[256,256]{1,0:T(8,128)(4,1)S(1)}, u32[]{:S(2)}) copy-start(pred[256,256]{1,0:T(8,128)(4,1)S(1)} %copy.130) | copy-start | bytes 196612
  15.0 5.3 %copy-start.25 = (s32[1,256]{1,0:T(1,128)}, s32[1,256]{1,0:T(1,128)S(1)}, u32[]{:S(2)}) copy-start(s32[1,256]{1,0:T(1,128)S(1)} %get-tuple-element.91) | copy-start | bytes 3076
  25.3 1.5 %copy-start.11 = (f32[256,4,128]{0,2,1:T(8,128)S(1)}, f32[256,4,128]{0,2,1:T(8,128)}, u32[]{:S(2)}) copy-start(f32[256,4,128]{0,2,1:T(8,128)} %convolution_bitcast_fusion.2) | copy-start | bytes 1572868
  30.3 1.0 copy-start.10
  31.4 1.0 copy-start.8
  38.4 1.6 %copy-start.32 = (f32[4,256,256]{2,1,0:T(8,128)S(1)}, f32[4,256,256]{2,1,0:T(8,128)}, u32[]{:S(2)}) copy-start(f32[4,256,256]{2,1,0:T(8,128)} %get-tuple-element.96) | copy-start | bytes 3145732
  38.8 1.2 copy-start.13
  38.8 2.0 %collective-permute-start.2 = (f32[2,65536]{1,0:T(2,128)S(1)}, f32[2,65536]{1,0:T(2,128)S(1)}, u32[]{:S(2)}, u32[]{:S(2)}) collective-permute-start(f32[2,65536]{1,0:T(2,128)S(1)} %bitcast.244), channel_id=1, source_target_pairs={{0,1},{1,0},{2,3},{3,2},{4,5},{5,4},{6,7},{7,6},{8,9},{9,8},{10,11... | collective-permute-start | bytes 1572872 | tf_op jit(solution)/shard_map/ppermute | solution.py:21
  41.6 8.6 %collective-permute-start.3 = (f32[1,65536]{1,0:T(1,128)S(1)}, f32[1,65536]{1,0:T(1,128)}, u32[]{:S(2)}, u32[]{:S(2)}) collective-permute-start(f32[1,65536]{1,0:T(1,128)S(1)} %constant_dynamic-slice_fusion), channel_id=1, source_target_pairs={{0,2},{1,3},{2,0},{3,1},{4,6},{5,7},{6,4},{7,5},{8,10},{9,11},{10,... | collective-permute-start | bytes 786440 | tf_op jit(solution)/shard_map/ppermute | solution.py:21
  45.2 6.3 %copy-start.6 = (bf16[2,256,512]{1,2,0:T(8,128)(2,1)S(1)}, bf16[2,256,512]{1,2,0:T(8,128)(2,1)}, u32[]{:S(2)}) copy-start(bf16[2,256,512]{1,2,0:T(8,128)(2,1)} %copy-done.5) | copy-start | bytes 1572868
  45.2 33.4 %collective-permute-start.5 = (bf16[2,256,512]{2,1,0:T(8,128)(2,1)}, bf16[2,256,512]{2,1,0:T(8,128)(2,1)}, u32[]{:S(2)}, u32[]{:S(2)}) collective-permute-start(bf16[2,256,512]{2,1,0:T(8,128)(2,1)} %pad_maximum_fusion.1), channel_id=1, source_target_pairs={{8,0},{12,4},{16,8},{20,12},{24,16},{28,20},{9,1},{13,5},{17,9},{2... | collective-permute-start | bytes 1572872 | tf_op jit(solution)/shard_map/ppermute | solution.py:15
  53.6 9.5 %collective-permute-start.4 = (f32[1,32768]{1,0:T(1,128)S(1)}, f32[1,32768]{1,0:T(1,128)S(1)}, u32[]{:S(2)}, u32[]{:S(2)}) collective-permute-start(f32[1,32768]{1,0:T(1,128)S(1)} %dynamic-slice_bitcast_fusion), channel_id=1, source_target_pairs={{0,4},{4,0},{8,12},{12,8},{16,20},{20,16},{24,28},{28,24},{1,5},{5... | collective-permute-start | bytes 393224 | tf_op jit(solution)/shard_map/ppermute | solution.py:21
  65.1 6.4 %collective-permute-start.6 = (f32[1,16384]{1,0:T(1,128)}, f32[1,16384]{1,0:T(1,128)}, u32[]{:S(2)}, u32[]{:S(2)}) collective-permute-start(f32[1,16384]{1,0:T(1,128)} %dynamic-slice_bitcast_fusion.1), channel_id=1, source_target_pairs={{0,8},{4,12},{8,0},{12,4},{16,24},{20,28},{24,16},{28,20},{1,9},{5... | collective-permute-start | bytes 196616 | tf_op jit(solution)/shard_map/ppermute | solution.py:21
  71.0 5.4 %copy-start.15 = (bf16[1,256,512]{2,1,0:T(8,128)(2,1)S(1)}, bf16[1,256,512]{2,1,0:T(8,128)(2,1)}, u32[]{:S(2)}) copy-start(bf16[1,256,512]{2,1,0:T(8,128)(2,1)} %copy.166) | copy-start | bytes 786436
  73.3 5.3 %copy-start.4 = (bf16[2,256,512]{1,2,0:T(8,128)(2,1)S(1)}, bf16[2,256,512]{1,2,0:T(8,128)(2,1)}, u32[]{:S(2)}) copy-start(bf16[2,256,512]{1,2,0:T(8,128)(2,1)} %copy-done.3) | copy-start | bytes 1572868
  73.3 5.4 %copy-start.31 = (f32[4,256,256]{2,1,0:T(8,128)S(1)}, f32[4,256,256]{2,1,0:T(8,128)}, u32[]{:S(2)}) copy-start(f32[4,256,256]{2,1,0:T(8,128)} %get-tuple-element.98) | copy-start | bytes 3145732
  73.3 5.2 %collective-permute-start.7 = (f32[1,8192]{1,0:T(1,128)S(1)}, f32[1,8192]{1,0:T(1,128)S(1)}, u32[]{:S(2)}, u32[]{:S(2)}) collective-permute-start(f32[1,8192]{1,0:T(1,128)S(1)} %dynamic-slice_bitcast_fusion.2), channel_id=1, source_target_pairs={{0,16},{4,20},{8,24},{12,28},{16,0},{20,4},{24,8},{28,12},{1,17},{... | collective-permute-start | bytes 98312 | tf_op jit(solution)/shard_map/ppermute | solution.py:21
  77.3 36.9 %collective-permute-start.8 = (bf16[2,256,512]{2,1,0:T(8,128)(2,1)}, bf16[2,256,512]{2,1,0:T(8,128)(2,1)}, u32[]{:S(2)}, u32[]{:S(2)}) collective-permute-start(bf16[2,256,512]{2,1,0:T(8,128)(2,1)} %pad_maximum_fusion.2), channel_id=1, source_target_pairs={{4,0},{8,4},{12,8},{16,12},{20,16},{24,20},{28,24},{5,1},{9,5},{13... | collective-permute-start | bytes 1572872 | tf_op jit(solution)/shard_map/ppermute | solution.py:15
  79.5 3.8 %copy-start.28 = (s32[1,256]{1,0:T(1,128)S(1)}, s32[1,256]{1,0:T(1,128)}, u32[]{:S(2)}) copy-start(s32[1,256]{1,0:T(1,128)} %copy-done.27) | copy-start | bytes 3076
  80.0 12.6 %collective-permute-start.9 = (f32[1,8192]{1,0:T(1,128)S(1)}, f32[1,8192]{1,0:T(1,128)S(1)}, u32[]{:S(2)}, u32[]{:S(2)}) collective-permute-start(f32[1,8192]{1,0:T(1,128)S(1)} %bitcast_add_fusion.3), channel_id=1, source_target_pairs={{0,16},{4,20},{8,24},{12,28},{16,0},{20,4},{24,8},{28,12},{1,17},{... | collective-permute-start | bytes 98312 | tf_op jit(solution)/shard_map/ppermute | solution.py:21
  92.7 5.8 %collective-permute-start.10 = (f32[1,16384]{1,0:T(1,128)S(1)}, f32[1,16384]{1,0:T(1,128)S(1)}, u32[]{:S(2)}, u32[]{:S(2)}) collective-permute-start(f32[1,16384]{1,0:T(1,128)S(1)} %pad_maximum_fusion.4), channel_id=1, source_target_pairs={{0,8},{4,12},{8,0},{12,4},{16,24},{20,28},{24,16},{28,20},{1,9},{5... | collective-permute-start | bytes 196616 | tf_op jit(solution)/shard_map/ppermute | solution.py:21
  95.1 13.9 %all-to-all-start = ((f32[32,1,2048]{2,1,0:T(1,128)}), f32[32,1,2048]{2,1,0:T(1,128)S(1)}, u32[]{:S(2)}, u32[]{:S(2)}) async-start(f32[32,1,2048]{2,1,0:T(1,128)} %bitcast.61), calls=%async_computation | async-start | bytes 524288 | tf_op jit(solution)/shard_map/all_to_all | solution.py:82
  98.7 7.7 %collective-permute-start.11 = (f32[1,32768]{1,0:T(1,128)S(1)}, f32[1,32768]{1,0:T(1,128)S(1)}, u32[]{:S(2)}, u32[]{:S(2)}) collective-permute-start(f32[1,32768]{1,0:T(1,128)S(1)} %pad_maximum_fusion.3), channel_id=1, source_target_pairs={{0,4},{4,0},{8,12},{12,8},{16,20},{20,16},{24,28},{28,24},{1,5},{5... | collective-permute-start | bytes 393224 | tf_op jit(solution)/shard_map/ppermute | solution.py:21
  108.1 6.2 %copy-start.2 = (f32[1,256,512]{2,1,0:T(8,128)S(1)}, f32[1,256,512]{2,1,0:T(8,128)}, u32[]{:S(2)}) copy-start(f32[1,256,512]{2,1,0:T(8,128)} %copy.162) | copy-start | bytes 1572868
  110.0 14.8 %all-to-all-start.1 = ((f32[32,1,2048]{2,1,0:T(1,128)}), f32[32,1,2048]{2,1,0:T(1,128)S(1)}, u32[]{:S(2)}, u32[]{:S(2)}) async-start(f32[32,1,2048]{2,1,0:T(1,128)} %broadcast_in_dim.63), calls=%async_computation.1 | async-start | bytes 524288 | tf_op jit(solution)/shard_map/all_to_all | solution.py:85
  (15 other events, 12.9 us)

commit v8 on v5

--- a/solution.py
+++ b/solution.py
@@ -212,7 +212,6 @@
         mixed, grad_rows, (((0,), (0,)), ((), ())), preferred_element_type=jnp.float32
     )
     weight_plan = [("split", "dp", mask) for mask in axis_bits("dp")]
-    weight_plan.append(("exchange", "ctx", 0))
     weight_state = [weight_term.reshape(dp_size, -1), 0]
 
     def slot(anchor):
@@ -270,14 +269,15 @@
     table_local = jnp.einsum(
         "qp,cqk->cpk", indicator_float, share_sum, precision=lax.Precision.HIGHEST
     )
+    table_part = scatter_blocks(table_local.reshape(dp_size, -1), "dp")
+    weight_rows = weight_state[0].reshape(-1)
+    combined = summed_by_exchange(jnp.concatenate([weight_rows, table_part]), ("ctx",))
+    projection_grad = combined[: weight_rows.shape[0]].reshape(width // dp_size, width)
+    table_grad = gather_blocks(combined[weight_rows.shape[0] :], "dp").reshape(table_local.shape)
     gathered = key_terms[0] + sent[1].astype(jnp.float32) + sent[2].astype(jnp.float32)
     query_grad = (query_sum * scale).astype(jnp.bfloat16)
     key_grad = gathered[0].astype(jnp.bfloat16)
     value_grad = gathered[1].astype(jnp.bfloat16)
-    projection_grad = weight_state[0].reshape(width // dp_size, width)
-    table_grad = summed_by_exchange(table_local.reshape(-1), ("ctx", "dp")).reshape(
-        table_local.shape
-    )
     return (
         query_grad[None],
         key_grad[None],

time: 123 us -> 128 us (1.041)
  starting transfers between devices: 39.8 us -> 26.6 us
  waiting for transfers between devices: 27.2 us -> 38.9 us
  other arithmetic: 9.68 us -> 12.5 us
  local copies, waits for them, and re-layouts: 26.5 us -> 28.6 us
  matrix products: 17.3 us -> 19.1 us
    ppermute x4, waiting for transfers between devices: 0.01 us -> 20 us  [passed_along(): return lax.ppermute(value, axis, pairs)]
    all_to_all x2 -> x1, starting transfers between devices: 19.7 us -> 4.16 us  [summed_by_exchange(): pieces = lax.all_to_all(flat.reshape(size, -1), axes, 0, 0, tiled=True)]
    all_to_all x2 -> x1, waiting for transfers between devices: 9.8 us -> 1.38 us  [summed_by_exchange(): pieces = lax.all_to_all(flat.reshape(size, -1), axes, 0, 0, tiled=True)]
    ppermute x2 -> x6, waiting for transfers between devices: 3.84 us -> 7.46 us  [exchanged(): return lax.ppermute(value, axis, pairs)]
    all_to_all x2 -> x1, waiting for transfers between devices: 13.5 us -> 10 us  [summed_by_exchange(): return lax.all_to_all(spread, axes, 0, 0, tiled=True).reshape(flat.shape)]
    ppermute x2 -> x6, starting transfers between devices: 1.65 us -> 3.89 us  [exchanged(): return lax.ppermute(value, axis, pairs)]
    dot_general x3, matrix products: 2.11 us -> 3.98 us  [shards(): jnp.einsum('hij,ihd->jhd', weights, grad_heads, preferred_element_type=jn...]
    dot_general x3, matrix products: 0.92 us -> 2.69 us  [shards(): jnp.einsum('hij,jhd->ihd', score_gradient, key_heads, preferred_element_t...]
  transfers between devices with their start and end apart: 10 -> 12, of which waited for: 6 -> 7; matrix products, arithmetic and copies ran while one was open for 26% -> 24% of each run, Pallas kernels for 0% -> 0%
where the time goes in v8:
time: 128 us; the launch traced here: 127 us
  waiting for transfers between devices  38.9 us (30%)
  local copies, waits for them, and re-layouts  28.6 us (22%)
  starting transfers between devices  26.6 us (21%)
  matrix products  19.1 us (15%)
  other arithmetic  12.5 us (10%)
  between operations  1.44 us (1%)
    ppermute x4, waiting for transfers between devices, passed_along(): return lax.ppermute(value, axis, pairs)  20 us
    ppermute x4, starting transfers between devices, passed_along(): return lax.ppermute(value, axis, pairs)  11.9 us
    unnamed x90, local copies, waits for them, and re-layouts  10.8 us
    all_to_all x1, waiting for transfers between devices, summed_by_exchange(): return lax.all_to_all(spread, axes, 0, 0, tiled=True).reshape(flat.shape)  10 us
    ppermute x6, waiting for transfers between devices, exchanged(): return lax.ppermute(value, axis, pairs)  7.46 us
    all_to_all x1, starting transfers between devices, summed_by_exchange(): return lax.all_to_all(spread, axes, 0, 0, tiled=True).reshape(flat.shape)  6.6 us
    all_to_all x1, starting transfers between devices, summed_by_exchange(): pieces = lax.all_to_all(flat.reshape(size, -1), axes, 0, 0, tiled=True)  4.16 us
    dot_general x3, matrix products, shards(): jnp.einsum('hij,ihd->jhd', weights, grad_heads, preferred_element_type=jn...  3.98 us
  transfers between devices with their start and end apart: 12, of which 7 were waited for; matrix products, arithmetic and copies ran while one was open for 24% of the time, Pallas kernels for 0%

profile of v8, /device:TPU:0, one launch (start us, length us, event | category | flops | bytes accessed | tf_op | source)
XLA Modules:
  0.0 127.1 jit_solution(13944568929087255186)
XLA Ops:
  0.7 1.2 copy.225
  2.0 5.0 %collective-permute-start.1 = (bf16[2,256,512]{1,2,0:T(8,128)(2,1)S(1)}, bf16[2,256,512]{1,2,0:T(8,128)(2,1)S(1)}, u32[]{:S(2)}, u32[]{:S(2)}) collective-permute-start(bf16[2,256,512]{1,2,0:T(8,128)(2,1)S(1)} %pad_maximum_fusion), channel_id=1, source_target_pairs={{0,8},{4,12},{8,16},{12,20},{16,24},{20,28},{1,9},{5,13},{9,17},{1... | collective-permute-start | bytes 1572872 | tf_op jit(solution)/shard_map/ppermute | solution.py:15
  7.0 4.2 %collective-permute-start = (bf16[2,256,512]{1,2,0:T(8,128)(2,1)S(1)}, bf16[2,256,512]{1,2,0:T(8,128)(2,1)}, u32[]{:S(2)}, u32[]{:S(2)}) collective-permute-start(bf16[2,256,512]{1,2,0:T(8,128)(2,1)S(1)} %pad_maximum_fusion), channel_id=1, source_target_pairs={{0,4},{4,8},{8,12},{12,16},{16,20},{20,24},{24,28},{1,5},{5,9},{9,... | collective-permute-start | bytes 1572872 | tf_op jit(solution)/shard_map/ppermute | solution.py:15
  15.6 1.5 %select_convert_fusion.2 = (bf16[4,256,256]{2,1,0:T(8,128)(2,1)S(1)}, f32[4,256,256]{2,1,0:T(8,128)}) fusion(pred[256,256]{1,0:T(8,128)(4,1)S(1)} %copy.175, f32[4,256,256]{2,1,0:T(8,128)S(1)} %convolution_multiply_fusion.5, bf16[4,256,128]{2,1,0:T(8,128)(2,1)S(1)} %fusion.16, s32[256]{0:T(256)S(1)} %bitcast.268), kind=kOutput, calls=%fused_computation.45 | convolution fusion | flops 68976640 | bytes 2950144 | tf_op jit(solution)/shard_map/vqx,px->vqp/dot_general | solution.py:160
  17.1 1.1 convolution_bitcast_fusion.2
  21.0 1.5 %select_convert_fusion = (bf16[4,256,256]{2,1,0:T(8,128)(2,1)S(1)}, f32[4,256,256]{2,1,0:T(8,128)}) fusion(pred[256,256]{1,0:T(8,128)(4,1)S(1)} %copy.188, f32[4,256,256]{2,1,0:T(8,128)S(1)} %fusion.48, bf16[256,4,128]{0,2,1:T(8,128)(2,1)S(1)} %bitcast.226, bf16[256,4,128]{0,2,1:T(8,128)(2,1)S(1)} %bitcast.259), kind=kOutput, calls=%fused_computation.41 | convolution fusion | flops 69206016 | bytes 3211264 | tf_op jit(solution)/shard_map/ihd,jhd->hij/dot_general | solution.py:175
  23.3 1.1 fusion.67
  24.5 1.5 %select_convert_fusion.1 = (bf16[4,256,256]{2,1,0:T(8,128)(2,1)S(1)}, f32[4,256,256]{2,1,0:T(8,128)}) fusion(pred[256,256]{1,0:T(8,128)(4,1)S(1)} %copy-done.30, f32[4,256,256]{2,1,0:T(8,128)S(1)} %fusion.44, bf16[256,4,128]{0,2,1:T(8,128)(2,1)S(1)} %bitcast.227, bf16[256,4,128]{0,2,1:T(8,128)(2,1)S(1)} %bitcast.239), kind=kOutput, calls=%fused_computation.43 | convolution fusion | flops 69206016 | bytes 3211264 | tf_op jit(solution)/shard_map/ihd,jhd->hij/dot_general | solution.py:175
  28.3 0.9 fusion.19
  29.4 1.1 copy-done.12
  30.5 0.9 convolution_convert_fusion.1
  31.4 1.1 fusion.70
  37.3 0.9 constant_dynamic-slice_fusion.5
  40.6 1.4 %bitcast_add_fusion = f32[2,65536]{1,0:T(2,128)} fusion(f32[2,65536]{1,0:T(2,128)S(1)} %collective-permute-done.2, f32[2,1,65536]{2,1,0:T(1,128)S(1)} %get-tuple-element.55), kind=kLoop, calls=%fused_computation.51 | loop fusion | flops 131072 | bytes 1572864 | tf_op jit(solution)/shard_map/add | solution.py:71
  44.0 1.5 %collective-permute-start.3 = (bf16[2,256,512]{2,1,0:T(8,128)(2,1)}, bf16[2,256,512]{2,1,0:T(8,128)(2,1)}, u32[]{:S(2)}, u32[]{:S(2)}) collective-permute-start(bf16[2,256,512]{2,1,0:T(8,128)(2,1)} %pad_maximum_fusion.1), channel_id=1, source_target_pairs={{8,0},{12,4},{16,8},{20,12},{24,16},{28,20},{9,1},{13,5},{17,9},{2... | collective-permute-start | bytes 1572872 | tf_op jit(solution)/shard_map/ppermute | solution.py:15
  48.0 20.0 %collective-permute-done.3 = bf16[2,256,512]{2,1,0:T(8,128)(2,1)} collective-permute-done((bf16[2,256,512]{2,1,0:T(8,128)(2,1)}, bf16[2,256,512]{2,1,0:T(8,128)(2,1)}, u32[]{:S(2)}, u32[]{:S(2)}) %collective-permute-start.3) | collective-permute-done | bytes 524320 | tf_op jit(solution)/shard_map/ppermute | solution.py:15
  72.0 1.6 %collective-permute-start.5 = (f32[1,65536]{1,0:T(1,128)S(1)}, f32[1,65536]{1,0:T(1,128)S(1)}, u32[]{:S(2)}, u32[]{:S(2)}) collective-permute-start(f32[1,65536]{1,0:T(1,128)S(1)} %constant_dynamic-slice_fusion.3), channel_id=1, source_target_pairs={{0,2},{1,3},{2,0},{3,1},{4,6},{5,7},{6,4},{7,5},{8,10},{9,11},{10,... | collective-permute-start | bytes 786440 | tf_op jit(solution)/shard_map/ppermute | solution.py:21
  74.4 6.5 %collective-permute-done.5 = f32[1,65536]{1,0:T(1,128)S(1)} collective-permute-done((f32[1,65536]{1,0:T(1,128)S(1)}, f32[1,65536]{1,0:T(1,128)S(1)}, u32[]{:S(2)}, u32[]{:S(2)}) %collective-permute-start.5) | collective-permute-done | bytes 262176 | tf_op jit(solution)/shard_map/ppermute | solution.py:21
  82.5 4.2 %all-to-all-start = ((f32[8,1,10240]{2,1,0:T(1,128)}), f32[8,1,10240]{2,1,0:T(1,128)S(1)}, u32[]{:S(2)}, u32[]{:S(2)}) async-start(f32[8,1,10240]{2,1,0:T(1,128)} %bitcast.238), calls=%async_computation | async-start | bytes 655360 | tf_op jit(solution)/shard_map/all_to_all | solution.py:82
  86.6 2.0 %convolution_convert_fusion = bf16[4,128,256]{2,1,0:T(8,128)(2,1)} fusion(bf16[256,4,128]{0,2,1:T(8,128)(2,1)S(1)} %bitcast.233, bf16[4,256,256]{2,1,0:T(8,128)(2,1)} %copy-done.13), kind=kOutput, calls=%fused_computation.33 | convolution fusion | flops 67239936 | bytes 1048576 | tf_op jit(solution)/shard_map/hij,ihd->jhd/dot_general | solution.py:243
  88.6 1.8 %copy.211 = bf16[1,256,512]{2,1,0:T(8,128)(2,1)} copy(bf16[1,256,512]{1,2,0:T(8,128)(2,1)} %bitcast.249) | data formatting | bytes 524288 | tf_op jit(solution)/shard_map/stack;reshape | solution.py:264
  90.5 1.9 %pad_maximum_fusion.2 = bf16[2,256,512]{2,1,0:T(8,128)(2,1)} fusion(bf16[1,256,512]{2,1,0:T(8,128)(2,1)} %copy.211, bf16[1,256,512]{2,1,0:T(8,128)(2,1)S(1)} %copy-done.22), kind=kLoop, calls=%fused_computation.49 | loop fusion | flops 262144 | bytes 1048576 | tf_op jit(solution)/shard_map/stack | solution.py:264
  92.3 1.3 %collective-permute-start.4 = (bf16[2,256,512]{2,1,0:T(8,128)(2,1)}, bf16[2,256,512]{2,1,0:T(8,128)(2,1)}, u32[]{:S(2)}, u32[]{:S(2)}) collective-permute-start(bf16[2,256,512]{2,1,0:T(8,128)(2,1)} %pad_maximum_fusion.2), channel_id=1, source_target_pairs={{4,0},{8,4},{12,8},{16,12},{20,16},{24,20},{28,24},{5,1},{9,5},{13... | collective-permute-start | bytes 1572872 | tf_op jit(solution)/shard_map/ppermute | solution.py:15
  93.6 1.1 fusion.69
  94.7 1.4 %all-to-all-done = f32[8,1,10240]{2,1,0:T(1,128)S(1)} async-done(((f32[8,1,10240]{2,1,0:T(1,128)}), f32[8,1,10240]{2,1,0:T(1,128)S(1)}, u32[]{:S(2)}, u32[]{:S(2)}) %all-to-all-start) | async-done | bytes 327712 | tf_op jit(solution)/shard_map/all_to_all | solution.py:82
  97.3 6.6 %all-to-all-start.1 = ((f32[8,1,10240]{2,1,0:T(1,128)}), f32[8,1,10240]{2,1,0:T(1,128)}, u32[]{:S(2)}, u32[]{:S(2)}) async-start(f32[8,1,10240]{2,1,0:T(1,128)} %broadcast_in_dim.65), calls=%async_computation.1 | async-start | bytes 655360 | tf_op jit(solution)/shard_map/all_to_all | solution.py:85
  103.9 1.3 convolution_add_fusion.4
  106.6 10.0 %all-to-all-done.1 = f32[8,1,10240]{2,1,0:T(1,128)} async-done(((f32[8,1,10240]{2,1,0:T(1,128)}), f32[8,1,10240]{2,1,0:T(1,128)}, u32[]{:S(2)}, u32[]{:S(2)}) %all-to-all-start.1) | async-done | bytes 327712 | tf_op jit(solution)/shard_map/all_to_all | solution.py:85
  117.5 1.5 %collective-permute-start.8 = (f32[1,16384]{1,0:T(1,128)S(1)}, f32[1,16384]{1,0:T(1,128)S(1)}, u32[]{:S(2)}, u32[]{:S(2)}) collective-permute-start(f32[1,16384]{1,0:T(1,128)S(1)} %bitcast.255), channel_id=1, source_target_pairs={{0,2},{1,3},{2,0},{3,1},{4,6},{5,7},{6,4},{7,5},{8,10},{9,11},{10,... | collective-permute-start | bytes 196616 | tf_op jit(solution)/shard_map/ppermute | solution.py:21
  119.0 1.4 %fusion.18 = bf16[2,256,512]{2,1,0:T(8,128)(2,1)S(1)} fusion(f32[1,256,512]{2,1,0:T(8,128)S(1)} %copy.207, f32[1,256,512]{2,1,0:T(8,128)S(1)} %copy.206, bf16[2,256,512]{2,1,0:T(8,128)(2,1)} %collective-permute-done.3, bf16[2,256,512]{2,1,0:T(8,128)(2,1)} %collective-permute-done.4), kind=kLoop, calls=%fused_computation.40 | loop fusion | flops 1572864 | bytes 2621440 | tf_op jit(solution)/shard_map/convert.3
  122.9 1.8 %reduce.3 = f32[8,10240]{1,0:T(8,128)S(1)} reduce(f32[8,1,10240]{2,1,0:T(1,128)} %all-to-all-done.1, f32[]{:T(128)} %constant.257), dimensions={1}, to_apply=%all_to_all.12.reduce_sub_computation | reduce | bytes 655364 | tf_op jit(solution)/shard_map/all_to_all | solution.py:85
  126.2 0.9 reshape_reshape.7
  (183 shorter events, 35.6 us)
Async XLA Ops:
  0.6 26.5 %copy-start = (bf16[512,512]{1,0:T(8,128)(2,1)S(1)}, bf16[512,512]{1,0:T(8,128)(2,1)}, u32[]{:S(2)}) copy-start(bf16[512,512]{1,0:T(8,128)(2,1)} %param.19) | copy-start | bytes 1572868
  2.0 12.0 %copy-start.6 = (bf16[2,256,512]{1,2,0:T(8,128)(2,1)}, bf16[2,256,512]{1,2,0:T(8,128)(2,1)S(1)}, u32[]{:S(2)}) copy-start(bf16[2,256,512]{1,2,0:T(8,128)(2,1)S(1)} %pad_maximum_fusion) | copy-start | bytes 1572868
  2.0 18.1 %collective-permute-start.1 = (bf16[2,256,512]{1,2,0:T(8,128)(2,1)S(1)}, bf16[2,256,512]{1,2,0:T(8,128)(2,1)S(1)}, u32[]{:S(2)}, u32[]{:S(2)}) collective-permute-start(bf16[2,256,512]{1,2,0:T(8,128)(2,1)S(1)} %pad_maximum_fusion), channel_id=1, source_target_pairs={{0,8},{4,12},{8,16},{12,20},{16,24},{20,28},{1,9},{5,13},{9,17},{1... | collective-permute-start | bytes 1572872 | tf_op jit(solution)/shard_map/ppermute | solution.py:15
  7.0 16.3 %collective-permute-start = (bf16[2,256,512]{1,2,0:T(8,128)(2,1)S(1)}, bf16[2,256,512]{1,2,0:T(8,128)(2,1)}, u32[]{:S(2)}, u32[]{:S(2)}) collective-permute-start(bf16[2,256,512]{1,2,0:T(8,128)(2,1)S(1)} %pad_maximum_fusion), channel_id=1, source_target_pairs={{0,4},{4,8},{8,12},{12,16},{16,20},{20,24},{24,28},{1,5},{5,9},{9,... | collective-permute-start | bytes 1572872 | tf_op jit(solution)/shard_map/ppermute | solution.py:15
  11.3 1.6 %copy-start.37 = (s32[1,6]{1,0:T(1,128)S(1)}, s32[1,6]{1,0:T(1,128)}, u32[]{:S(2)}) copy-start(s32[1,6]{1,0:T(1,128)} %param.16) | copy-start | bytes 76
  11.4 2.7 %copy-start.28 = (bf16[1,256,512]{2,1,0:T(8,128)(2,1)S(1)}, bf16[1,256,512]{2,1,0:T(8,128)(2,1)}, u32[]{:S(2)}) copy-start(bf16[1,256,512]{2,1,0:T(8,128)(2,1)} %param.10) | copy-start | bytes 786436
  14.9 4.5 %copy-start.32 = (s32[1,256]{1,0:T(1,128)}, s32[1,256]{1,0:T(1,128)S(1)}, u32[]{:S(2)}) copy-start(s32[1,256]{1,0:T(1,128)S(1)} %get-tuple-element.78) | copy-start | bytes 3076
  24.4 1.5 %copy-start.18 = (bf16[1,256,512]{1,2,0:T(8,128)(2,1)}, bf16[1,256,512]{1,2,0:T(8,128)(2,1)S(1)}, u32[]{:S(2)}) copy-start(bf16[1,256,512]{1,2,0:T(8,128)(2,1)S(1)} %get-tuple-element.66) | copy-start | bytes 786436
  24.4 1.5 %copy-start.20 = (bf16[1,256,512]{1,2,0:T(8,128)(2,1)}, bf16[1,256,512]{1,2,0:T(8,128)(2,1)S(1)}, u32[]{:S(2)}) copy-start(bf16[1,256,512]{1,2,0:T(8,128)(2,1)S(1)} %get-tuple-element.65) | copy-start | bytes 786436
  24.5 1.5 %copy-start.14 = (f32[256,4,128]{0,2,1:T(8,128)S(1)}, f32[256,4,128]{0,2,1:T(8,128)}, u32[]{:S(2)}) copy-start(f32[256,4,128]{0,2,1:T(8,128)} %convolution_bitcast_fusion.2) | copy-start | bytes 1572868
  29.3 3.3 %copy-start.15 = (bf16[256,512]{1,0:T(8,128)(2,1)}, bf16[256,512]{1,0:T(8,128)(2,1)S(1)}, u32[]{:S(2)}) copy-start(bf16[256,512]{1,0:T(8,128)(2,1)S(1)} %get-tuple-element.54) | copy-start | bytes 786436
  29.3 1.2 copy-start.12
  29.4 2.0 %copy-start.1 = (bf16[256,512]{0,1:T(8,128)(2,1)}, bf16[256,512]{0,1:T(8,128)(2,1)S(1)}, u32[]{:S(2)}) copy-start(bf16[256,512]{0,1:T(8,128)(2,1)S(1)} %copy.257) | copy-start | bytes 786436
  31.4 1.4 %copy-start.40 = (f32[4,256,256]{2,1,0:T(8,128)S(1)}, f32[4,256,256]{2,1,0:T(8,128)}, u32[]{:S(2)}) copy-start(f32[4,256,256]{2,1,0:T(8,128)} %get-tuple-element.88) | copy-start | bytes 3145732
  38.2 1.8 %copy-start.39 = (f32[4,256,256]{2,1,0:T(8,128)S(1)}, f32[4,256,256]{2,1,0:T(8,128)}, u32[]{:S(2)}) copy-start(f32[4,256,256]{2,1,0:T(8,128)} %get-tuple-element.84) | copy-start | bytes 3145732
  38.6 1.4 %copy-start.16 = (bf16[256,512]{1,0:T(8,128)(2,1)S(1)}, bf16[256,512]{1,0:T(8,128)(2,1)}, u32[]{:S(2)}) copy-start(bf16[256,512]{1,0:T(8,128)(2,1)} %copy-done.15) | copy-start | bytes 786436
  38.6 2.0 %collective-permute-start.2 = (f32[2,65536]{1,0:T(2,128)S(1)}, f32[2,65536]{1,0:T(2,128)S(1)}, u32[]{:S(2)}, u32[]{:S(2)}) collective-permute-start(f32[2,65536]{1,0:T(2,128)S(1)} %bitcast.253), channel_id=1, source_target_pairs={{0,1},{1,0},{2,3},{3,2},{4,5},{5,4},{6,7},{7,6},{8,9},{9,8},{10,11... | collective-permute-start | bytes 1572872 | tf_op jit(solution)/shard_map/ppermute | solution.py:21
  44.0 24.0 %collective-permute-start.3 = (bf16[2,256,512]{2,1,0:T(8,128)(2,1)}, bf16[2,256,512]{2,1,0:T(8,128)(2,1)}, u32[]{:S(2)}, u32[]{:S(2)}) collective-permute-start(bf16[2,256,512]{2,1,0:T(8,128)(2,1)} %pad_maximum_fusion.1), channel_id=1, source_target_pairs={{8,0},{12,4},{16,8},{20,12},{24,16},{28,20},{9,1},{13,5},{17,9},{2... | collective-permute-start | bytes 1572872 | tf_op jit(solution)/shard_map/ppermute | solution.py:15
  47.6 20.4 %copy-start.7 = (bf16[2,256,512]{1,2,0:T(8,128)(2,1)S(1)}, bf16[2,256,512]{1,2,0:T(8,128)(2,1)}, u32[]{:S(2)}) copy-start(bf16[2,256,512]{1,2,0:T(8,128)(2,1)} %copy-done.6) | copy-start | bytes 1572868
  47.6 21.1 %copy-start.38 = (f32[4,256,256]{2,1,0:T(8,128)S(1)}, f32[4,256,256]{2,1,0:T(8,128)}, u32[]{:S(2)}) copy-start(f32[4,256,256]{2,1,0:T(8,128)} %get-tuple-element.86) | copy-start | bytes 3145732
  71.1 2.5 %collective-permute-start.6 = (f32[2,16384]{1,0:T(2,128)S(1)}, f32[2,16384]{1,0:T(2,128)S(1)}, u32[]{:S(2)}, u32[]{:S(2)}) collective-permute-start(f32[2,16384]{1,0:T(2,128)S(1)} %bitcast.260), channel_id=1, source_target_pairs={{0,1},{1,0},{2,3},{3,2},{4,5},{5,4},{6,7},{7,6},{8,9},{9,8},{10,11... | collective-permute-start | bytes 393224 | tf_op jit(solution)/shard_map/ppermute | solution.py:21
  72.0 8.9 %collective-permute-start.5 = (f32[1,65536]{1,0:T(1,128)S(1)}, f32[1,65536]{1,0:T(1,128)S(1)}, u32[]{:S(2)}, u32[]{:S(2)}) collective-permute-start(f32[1,65536]{1,0:T(1,128)S(1)} %constant_dynamic-slice_fusion.3), channel_id=1, source_target_pairs={{0,2},{1,3},{2,0},{3,1},{4,6},{5,7},{6,4},{7,5},{8,10},{9,11},{10,... | collective-permute-start | bytes 786440 | tf_op jit(solution)/shard_map/ppermute | solution.py:21
  73.8 7.8 %collective-permute-start.7 = (f32[1,16384]{1,0:T(1,128)S(1)}, f32[1,16384]{1,0:T(1,128)S(1)}, u32[]{:S(2)}, u32[]{:S(2)}) collective-permute-start(f32[1,16384]{1,0:T(1,128)S(1)} %constant_dynamic-slice_fusion), channel_id=1, source_target_pairs={{0,2},{1,3},{2,0},{3,1},{4,6},{5,7},{6,4},{7,5},{8,10},{9,11},{10,... | collective-permute-start | bytes 196616 | tf_op jit(solution)/shard_map/ppermute | solution.py:21
  82.5 4.2 %copy-start.2 = (bf16[256,512]{0,1:T(8,128)(2,1)S(1)}, bf16[256,512]{0,1:T(8,128)(2,1)}, u32[]{:S(2)}) copy-start(bf16[256,512]{0,1:T(8,128)(2,1)} %copy-done.1) | copy-start | bytes 786436
  82.5 13.7 %all-to-all-start = ((f32[8,1,10240]{2,1,0:T(1,128)}), f32[8,1,10240]{2,1,0:T(1,128)S(1)}, u32[]{:S(2)}, u32[]{:S(2)}) async-start(f32[8,1,10240]{2,1,0:T(1,128)} %bitcast.238), calls=%async_computation | async-start | bytes 655360 | tf_op jit(solution)/shard_map/all_to_all | solution.py:82
  88.6 1.8 %copy-start.22 = (bf16[1,256,512]{2,1,0:T(8,128)(2,1)S(1)}, bf16[1,256,512]{2,1,0:T(8,128)(2,1)}, u32[]{:S(2)}) copy-start(bf16[1,256,512]{2,1,0:T(8,128)(2,1)} %copy.210) | copy-start | bytes 786436
  90.4 3.2 %copy-start.19 = (bf16[1,256,512]{1,2,0:T(8,128)(2,1)S(1)}, bf16[1,256,512]{1,2,0:T(8,128)(2,1)}, u32[]{:S(2)}) copy-start(bf16[1,256,512]{1,2,0:T(8,128)(2,1)} %copy-done.18) | copy-start | bytes 786436
  92.3 26.7 %collective-permute-start.4 = (bf16[2,256,512]{2,1,0:T(8,128)(2,1)}, bf16[2,256,512]{2,1,0:T(8,128)(2,1)}, u32[]{:S(2)}, u32[]{:S(2)}) collective-permute-start(bf16[2,256,512]{2,1,0:T(8,128)(2,1)} %pad_maximum_fusion.2), channel_id=1, source_target_pairs={{4,0},{8,4},{12,8},{16,12},{20,16},{24,20},{28,24},{5,1},{9,5},{13... | collective-permute-start | bytes 1572872 | tf_op jit(solution)/shard_map/ppermute | solution.py:15
  96.4 7.5 %copy-start.5 = (f32[4,128,256]{2,1,0:T(8,128)S(1)}, f32[4,128,256]{2,1,0:T(8,128)}, u32[]{:S(2)}) copy-start(f32[4,128,256]{2,1,0:T(8,128)} %fusion.69) | copy-start | bytes 1572868
  97.3 19.4 %all-to-all-start.1 = ((f32[8,1,10240]{2,1,0:T(1,128)}), f32[8,1,10240]{2,1,0:T(1,128)}, u32[]{:S(2)}, u32[]{:S(2)}) async-start(f32[8,1,10240]{2,1,0:T(1,128)} %broadcast_in_dim.65), calls=%async_computation.1 | async-start | bytes 655360 | tf_op jit(solution)/shard_map/all_to_all | solution.py:85
  117.5 4.3 %collective-permute-start.8 = (f32[1,16384]{1,0:T(1,128)S(1)}, f32[1,16384]{1,0:T(1,128)S(1)}, u32[]{:S(2)}, u32[]{:S(2)}) collective-permute-start(f32[1,16384]{1,0:T(1,128)S(1)} %bitcast.255), channel_id=1, source_target_pairs={{0,2},{1,3},{2,0},{3,1},{4,6},{5,7},{6,4},{7,5},{8,10},{9,11},{10,... | collective-permute-start | bytes 196616 | tf_op jit(solution)/shard_map/ppermute | solution.py:21
  122.0 3.5 %collective-permute-start.9 = (f32[2,16384]{1,0:T(2,128)S(1)}, f32[2,16384]{1,0:T(2,128)S(1)}, u32[]{:S(2)}, u32[]{:S(2)}) collective-permute-start(f32[2,16384]{1,0:T(2,128)S(1)} %maximum_bitcast_fusion), channel_id=1, source_target_pairs={{0,1},{1,0},{2,3},{3,2},{4,5},{5,4},{6,7},{7,6},{8,9},{9,8},{10,11... | collective-permute-start | bytes 393224 | tf_op jit(solution)/shard_map/ppermute | solution.py:21
  (21 other events, 19.4 us)

commit v9 on v5

--- a/solution.py
+++ b/solution.py
@@ -213,14 +213,18 @@
     )
     weight_plan = [("split", "dp", mask) for mask in axis_bits("dp")]
     weight_plan.append(("exchange", "ctx", 0))
+    weight_plan += [("skip", "ctx", 0), ("skip", "ctx", 0), ("tie", "ctx", 0)]
     weight_state = [weight_term.reshape(dp_size, -1), 0]
 
     def slot(anchor):
         blocks, done = weight_state
         if done < len(weight_plan):
-            blocks, anchor = lax.optimization_barrier((blocks, anchor))
             kind, axis, mask = weight_plan[done]
-            if kind == "exchange":
+            if kind != "skip":
+                blocks, anchor = lax.optimization_barrier((blocks, anchor))
+            if kind in ("skip", "tie"):
+                weight_state[0] = blocks
+            elif kind == "exchange":
                 weight_state[0] = summed_by_exchange(blocks.reshape(-1), (axis,))
             else:
                 weight_state[0] = plan_step(blocks, kind, axis, mask)

time: 123 us -> 124 us (level)
  waiting for transfers between devices: 27.2 us -> 35.2 us
  starting transfers between devices: 39.8 us -> 34 us
    all_to_all x2, starting transfers between devices: 19.7 us -> 14.3 us  [summed_by_exchange(): pieces = lax.all_to_all(flat.reshape(size, -1), axes, 0, 0, tiled=True)]
    all_to_all x2, waiting for transfers between devices: 13.5 us -> 18 us  [summed_by_exchange(): return lax.all_to_all(spread, axes, 0, 0, tiled=True).reshape(flat.shape)]
    all_to_all x2, waiting for transfers between devices: 9.8 us -> 13.5 us  [summed_by_exchange(): pieces = lax.all_to_all(flat.reshape(size, -1), axes, 0, 0, tiled=True)]
    unnamed x80 -> x78, local copies, waits for them, and re-layouts: 9.88 us -> 9.51 us
  transfers between devices with their start and end apart: 10 -> 10, of which waited for: 6 -> 6; matrix products, arithmetic and copies ran while one was open for 26% -> 25% of each run, Pallas kernels for 0% -> 0%
where the time goes in v9:
time: 124 us; the launch traced here: 123 us
  waiting for transfers between devices  35.2 us (28%)
  starting transfers between devices  34 us (27%)
  local copies, waits for them, and re-layouts  26.2 us (21%)
  matrix products  16.1 us (13%)
  other arithmetic  10 us (8%)
  between operations  1.47 us (1%)
    all_to_all x2, waiting for transfers between devices, summed_by_exchange(): return lax.all_to_all(spread, axes, 0, 0, tiled=True).reshape(flat.shape)  18 us
    all_to_all x2, starting transfers between devices, summed_by_exchange(): pieces = lax.all_to_all(flat.reshape(size, -1), axes, 0, 0, tiled=True)  14.3 us
    all_to_all x2, waiting for transfers between devices, summed_by_exchange(): pieces = lax.all_to_all(flat.reshape(size, -1), axes, 0, 0, tiled=True)  13.5 us
    ppermute x4, starting transfers between devices, passed_along(): return lax.ppermute(value, axis, pairs)  12.1 us
    unnamed x78, local copies, waits for them, and re-layouts  9.51 us
    all_to_all x2, starting transfers between devices, summed_by_exchange(): return lax.all_to_all(spread, axes, 0, 0, tiled=True).reshape(flat.shape)  6.01 us
    ppermute x2, waiting for transfers between devices, exchanged(): return lax.ppermute(value, axis, pairs)  3.66 us
    dot_general x3, matrix products, shards(): jnp.einsum('ihd,jhd->hij', query_heads, forward_key_heads, preferred_elem...  3.37 us
  transfers between devices with their start and end apart: 10, of which 6 were waited for; matrix products, arithmetic and copies ran while one was open for 25% of the time, Pallas kernels for 0%

profile of v9, /device:TPU:0, one launch (start us, length us, event | category | flops | bytes accessed | tf_op | source)
XLA Modules:
  0.0 122.9 jit_solution(17213937357479244647)
XLA Ops:
  0.7 1.2 copy.179
  2.0 5.8 %collective-permute-start.1 = (bf16[2,256,512]{1,2,0:T(8,128)(2,1)S(1)}, bf16[2,256,512]{1,2,0:T(8,128)(2,1)}, u32[]{:S(2)}, u32[]{:S(2)}) collective-permute-start(bf16[2,256,512]{1,2,0:T(8,128)(2,1)S(1)} %pad_maximum_fusion), channel_id=1, source_target_pairs={{0,8},{4,12},{8,16},{12,20},{16,24},{20,28},{1,9},{5,13},{9,17},{1... | collective-permute-start | bytes 1572872 | tf_op jit(solution)/shard_map/ppermute | solution.py:15
  7.8 3.4 %collective-permute-start = (bf16[2,256,512]{1,2,0:T(8,128)(2,1)S(1)}, bf16[2,256,512]{1,2,0:T(8,128)(2,1)S(1)}, u32[]{:S(2)}, u32[]{:S(2)}) collective-permute-start(bf16[2,256,512]{1,2,0:T(8,128)(2,1)S(1)} %pad_maximum_fusion), channel_id=1, source_target_pairs={{0,4},{4,8},{8,12},{12,16},{16,20},{20,24},{24,28},{1,5},{5,9},{9,... | collective-permute-start | bytes 1572872 | tf_op jit(solution)/shard_map/ppermute | solution.py:15
  15.7 1.5 %select_convert_fusion.2 = (bf16[4,256,256]{2,1,0:T(8,128)(2,1)S(1)}, f32[4,256,256]{2,1,0:T(8,128)}) fusion(pred[256,256]{1,0:T(8,128)(4,1)S(1)} %copy.130, f32[4,256,256]{2,1,0:T(8,128)S(1)} %convolution_multiply_fusion.5, bf16[4,256,128]{2,1,0:T(8,128)(2,1)S(1)} %fusion.16, s32[256]{0:T(256)S(1)} %bitcast.248), kind=kOutput, calls=%fused_computation.45 | convolution fusion | flops 68976640 | bytes 2950144 | tf_op jit(solution)/shard_map/vqx,px->vqp/dot_general | solution.py:160
  18.0 1.1 convolution_bitcast_fusion.2
  21.0 1.1 fusion.66
  22.1 1.5 %select_convert_fusion = (bf16[4,256,256]{2,1,0:T(8,128)(2,1)S(1)}, f32[4,256,256]{2,1,0:T(8,128)}) fusion(pred[256,256]{1,0:T(8,128)(4,1)S(1)} %copy.143, f32[4,256,256]{2,1,0:T(8,128)S(1)} %fusion.48, bf16[256,4,128]{0,2,1:T(8,128)(2,1)S(1)} %bitcast.210, bf16[256,4,128]{0,2,1:T(8,128)(2,1)S(1)} %bitcast.239), kind=kOutput, calls=%fused_computation.41 | convolution fusion | flops 69206016 | bytes 3211264 | tf_op jit(solution)/shard_map/ihd,jhd->hij/dot_general | solution.py:175
  25.2 1.5 %select_convert_fusion.1 = (bf16[4,256,256]{2,1,0:T(8,128)(2,1)S(1)}, f32[4,256,256]{2,1,0:T(8,128)}) fusion(pred[256,256]{1,0:T(8,128)(4,1)S(1)} %copy.138, f32[4,256,256]{2,1,0:T(8,128)S(1)} %fusion.44, bf16[256,4,128]{0,2,1:T(8,128)(2,1)S(1)} %bitcast.211, bf16[256,4,128]{0,2,1:T(8,128)(2,1)S(1)} %bitcast.240), kind=kOutput, calls=%fused_computation.43 | convolution fusion | flops 69206016 | bytes 3211264 | tf_op jit(solution)/shard_map/ihd,jhd->hij/dot_general | solution.py:175
  28.6 0.9 fusion.19
  30.3 0.9 convolution_convert_fusion
  31.3 0.9 convolution_convert_fusion.1
  32.7 1.0 copy.162
  37.4 0.9 constant_dynamic-slice_fusion.2
  38.9 1.1 fusion.63
  41.6 1.6 %collective-permute-start.3 = (f32[1,65536]{1,0:T(1,128)S(1)}, f32[1,65536]{1,0:T(1,128)}, u32[]{:S(2)}, u32[]{:S(2)}) collective-permute-start(f32[1,65536]{1,0:T(1,128)S(1)} %constant_dynamic-slice_fusion), channel_id=1, source_target_pairs={{0,2},{1,3},{2,0},{3,1},{4,6},{5,7},{6,4},{7,5},{8,10},{9,11},{10,... | collective-permute-start | bytes 786440 | tf_op jit(solution)/shard_map/ppermute | solution.py:21
  45.2 1.6 %collective-permute-start.4 = (bf16[2,256,512]{2,1,0:T(8,128)(2,1)}, bf16[2,256,512]{2,1,0:T(8,128)(2,1)}, u32[]{:S(2)}, u32[]{:S(2)}) collective-permute-start(bf16[2,256,512]{2,1,0:T(8,128)(2,1)} %pad_maximum_fusion.1), channel_id=1, source_target_pairs={{8,0},{12,4},{16,8},{20,12},{24,16},{28,20},{9,1},{13,5},{17,9},{2... | collective-permute-start | bytes 1572872 | tf_op jit(solution)/shard_map/ppermute | solution.py:15
  46.8 3.4 %collective-permute-done.3 = f32[1,65536]{1,0:T(1,128)} collective-permute-done((f32[1,65536]{1,0:T(1,128)S(1)}, f32[1,65536]{1,0:T(1,128)}, u32[]{:S(2)}, u32[]{:S(2)}) %collective-permute-start.3) | collective-permute-done | bytes 262176 | tf_op jit(solution)/shard_map/ppermute | solution.py:21
  50.2 2.0 %dynamic-slice_add_fusion = f32[1,65536]{1,0:T(1,128)} fusion(f32[1,65536]{1,0:T(1,128)} %collective-permute-done.3, f32[2,65536]{1,0:T(2,128)S(1)} %bitcast_add_fusion, s32[]{:T(128)S(6)} %select_n.144), kind=kLoop, calls=%fused_computation.68 | loop fusion | flops 65536 | bytes 786436 | tf_op jit(solution)/shard_map/add | solution.py:71
  53.5 0.9 fusion.15
  54.8 11.7 %all-to-all-start = ((f32[8,1,8192]{2,1,0:T(1,128)}), f32[8,1,8192]{2,1,0:T(1,128)}, u32[]{:S(2)}, u32[]{:S(2)}) async-start(f32[8,1,8192]{2,1,0:T(1,128)} %bitcast.42), calls=%async_computation | async-start | bytes 524288 | tf_op jit(solution)/shard_map/all_to_all | solution.py:82
  66.9 1.1 copy.165
  68.9 1.3 %collective-permute-start.5 = (bf16[2,256,512]{2,1,0:T(8,128)(2,1)}, bf16[2,256,512]{2,1,0:T(8,128)(2,1)}, u32[]{:S(2)}, u32[]{:S(2)}) collective-permute-start(bf16[2,256,512]{2,1,0:T(8,128)(2,1)} %pad_maximum_fusion.2), channel_id=1, source_target_pairs={{4,0},{8,4},{12,8},{16,12},{20,16},{24,20},{28,24},{5,1},{9,5},{13... | collective-permute-start | bytes 1572872 | tf_op jit(solution)/shard_map/ppermute | solution.py:15
  70.8 4.6 %all-to-all-done = f32[8,1,8192]{2,1,0:T(1,128)} async-done(((f32[8,1,8192]{2,1,0:T(1,128)}), f32[8,1,8192]{2,1,0:T(1,128)}, u32[]{:S(2)}, u32[]{:S(2)}) %all-to-all-start) | async-done | bytes 262176 | tf_op jit(solution)/shard_map/all_to_all | solution.py:82
  75.4 1.1 reduce_sum.92
  77.4 3.4 %all-to-all-start.1 = ((f32[8,1,8192]{2,1,0:T(1,128)}), f32[8,1,8192]{2,1,0:T(1,128)S(1)}, u32[]{:S(2)}, u32[]{:S(2)}) async-start(f32[8,1,8192]{2,1,0:T(1,128)} %broadcast_in_dim.64), calls=%async_computation.1 | async-start | bytes 524288 | tf_op jit(solution)/shard_map/all_to_all | solution.py:85
  80.9 1.2 copy-done.32
  82.6 9.7 %all-to-all-done.1 = f32[8,1,8192]{2,1,0:T(1,128)S(1)} async-done(((f32[8,1,8192]{2,1,0:T(1,128)}), f32[8,1,8192]{2,1,0:T(1,128)S(1)}, u32[]{:S(2)}, u32[]{:S(2)}) %all-to-all-start.1) | async-done | bytes 262176 | tf_op jit(solution)/shard_map/all_to_all | solution.py:85
  94.9 2.6 %all-to-all-start.2 = ((f32[32,1,2048]{2,1,0:T(1,128)}), f32[32,1,2048]{2,1,0:T(1,128)S(1)}, u32[]{:S(2)}, u32[]{:S(2)}) async-start(f32[32,1,2048]{2,1,0:T(1,128)} %bitcast.57), calls=%async_computation.2 | async-start | bytes 524288 | tf_op jit(solution)/shard_map/all_to_all | solution.py:82
  99.1 9.0 %all-to-all-done.2 = f32[32,1,2048]{2,1,0:T(1,128)S(1)} async-done(((f32[32,1,2048]{2,1,0:T(1,128)}), f32[32,1,2048]{2,1,0:T(1,128)S(1)}, u32[]{:S(2)}, u32[]{:S(2)}) %all-to-all-start.2) | async-done | bytes 262176 | tf_op jit(solution)/shard_map/all_to_all | solution.py:82
  109.0 2.6 %all-to-all-start.3 = ((f32[32,1,2048]{2,1,0:T(1,128)}), f32[32,1,2048]{2,1,0:T(1,128)S(1)}, u32[]{:S(2)}, u32[]{:S(2)}) async-start(f32[32,1,2048]{2,1,0:T(1,128)} %broadcast_in_dim.66), calls=%async_computation.3 | async-start | bytes 524288 | tf_op jit(solution)/shard_map/all_to_all | solution.py:85
  111.7 1.4 %fusion.18 = bf16[2,256,512]{2,1,0:T(8,128)(2,1)S(1)} fusion(f32[1,256,512]{2,1,0:T(8,128)S(1)} %copy-done.2, f32[1,256,512]{2,1,0:T(8,128)S(1)} %copy.161, bf16[2,256,512]{2,1,0:T(8,128)(2,1)} %collective-permute-done.4, bf16[2,256,512]{2,1,0:T(8,128)(2,1)} %collective-permute-done.5), kind=kLoop, calls=%fused_computation.40 | loop fusion | flops 1572864 | bytes 2621440 | tf_op jit(solution)/shard_map/convert.3
  113.9 8.3 %all-to-all-done.3 = f32[32,1,2048]{2,1,0:T(1,128)S(1)} async-done(((f32[32,1,2048]{2,1,0:T(1,128)}), f32[32,1,2048]{2,1,0:T(1,128)S(1)}, u32[]{:S(2)}, u32[]{:S(2)}) %all-to-all-start.3) | async-done | bytes 262176 | tf_op jit(solution)/shard_map/all_to_all | solution.py:85
  (154 shorter events, 31.2 us)
Async XLA Ops:
  0.6 26.8 %copy-start = (bf16[512,512]{1,0:T(8,128)(2,1)S(1)}, bf16[512,512]{1,0:T(8,128)(2,1)}, u32[]{:S(2)}) copy-start(bf16[512,512]{1,0:T(8,128)(2,1)} %param.19) | copy-start | bytes 1572868
  0.6 1.2 copy-start.14
  2.0 12.1 %copy-start.3 = (bf16[2,256,512]{1,2,0:T(8,128)(2,1)}, bf16[2,256,512]{1,2,0:T(8,128)(2,1)S(1)}, u32[]{:S(2)}) copy-start(bf16[2,256,512]{1,2,0:T(8,128)(2,1)S(1)} %pad_maximum_fusion) | copy-start | bytes 1572868
  2.0 18.9 %collective-permute-start.1 = (bf16[2,256,512]{1,2,0:T(8,128)(2,1)S(1)}, bf16[2,256,512]{1,2,0:T(8,128)(2,1)}, u32[]{:S(2)}, u32[]{:S(2)}) collective-permute-start(bf16[2,256,512]{1,2,0:T(8,128)(2,1)S(1)} %pad_maximum_fusion), channel_id=1, source_target_pairs={{0,8},{4,12},{8,16},{12,20},{16,24},{20,28},{1,9},{5,13},{9,17},{1... | collective-permute-start | bytes 1572872 | tf_op jit(solution)/shard_map/ppermute | solution.py:15
  7.8 16.6 %collective-permute-start = (bf16[2,256,512]{1,2,0:T(8,128)(2,1)S(1)}, bf16[2,256,512]{1,2,0:T(8,128)(2,1)S(1)}, u32[]{:S(2)}, u32[]{:S(2)}) collective-permute-start(bf16[2,256,512]{1,2,0:T(8,128)(2,1)S(1)} %pad_maximum_fusion), channel_id=1, source_target_pairs={{0,4},{4,8},{8,12},{12,16},{16,20},{20,24},{24,28},{1,5},{5,9},{9,... | collective-permute-start | bytes 1572872 | tf_op jit(solution)/shard_map/ppermute | solution.py:15
  11.4 1.6 %copy-start.31 = (s32[1,6]{1,0:T(1,128)S(1)}, s32[1,6]{1,0:T(1,128)}, u32[]{:S(2)}) copy-start(s32[1,6]{1,0:T(1,128)} %param.16) | copy-start | bytes 76
  11.4 2.7 %copy-start.22 = (bf16[1,256,512]{2,1,0:T(8,128)(2,1)S(1)}, bf16[1,256,512]{2,1,0:T(8,128)(2,1)}, u32[]{:S(2)}) copy-start(bf16[1,256,512]{2,1,0:T(8,128)(2,1)} %param.10) | copy-start | bytes 786436
  14.9 5.3 %copy-start.26 = (s32[1,256]{1,0:T(1,128)}, s32[1,256]{1,0:T(1,128)S(1)}, u32[]{:S(2)}) copy-start(s32[1,256]{1,0:T(1,128)S(1)} %get-tuple-element.77) | copy-start | bytes 3076
  20.1 2.0 %copy-start.24 = (pred[256,256]{1,0:T(8,128)(4,1)}, pred[256,256]{1,0:T(8,128)(4,1)S(1)}, u32[]{:S(2)}) copy-start(pred[256,256]{1,0:T(8,128)(4,1)S(1)} %copy.143) | copy-start | bytes 196612
  25.2 1.5 %copy-start.11 = (f32[256,4,128]{0,2,1:T(8,128)S(1)}, f32[256,4,128]{0,2,1:T(8,128)}, u32[]{:S(2)}) copy-start(f32[256,4,128]{0,2,1:T(8,128)} %convolution_bitcast_fusion.2) | copy-start | bytes 1572868
  30.3 1.0 copy-start.10
  31.3 1.0 copy-start.8
  38.4 1.6 %copy-start.34 = (f32[4,256,256]{2,1,0:T(8,128)S(1)}, f32[4,256,256]{2,1,0:T(8,128)}, u32[]{:S(2)}) copy-start(f32[4,256,256]{2,1,0:T(8,128)} %get-tuple-element.82) | copy-start | bytes 3145732
  38.8 1.2 copy-start.13
  38.8 1.2 copy-start.25
  38.8 2.0 %collective-permute-start.2 = (f32[2,65536]{1,0:T(2,128)S(1)}, f32[2,65536]{1,0:T(2,128)S(1)}, u32[]{:S(2)}, u32[]{:S(2)}) collective-permute-start(f32[2,65536]{1,0:T(2,128)S(1)} %bitcast.235), channel_id=1, source_target_pairs={{0,1},{1,0},{2,3},{3,2},{4,5},{5,4},{6,7},{7,6},{8,9},{9,8},{10,11... | collective-permute-start | bytes 1572872 | tf_op jit(solution)/shard_map/ppermute | solution.py:21
  41.6 8.6 %collective-permute-start.3 = (f32[1,65536]{1,0:T(1,128)S(1)}, f32[1,65536]{1,0:T(1,128)}, u32[]{:S(2)}, u32[]{:S(2)}) collective-permute-start(f32[1,65536]{1,0:T(1,128)S(1)} %constant_dynamic-slice_fusion), channel_id=1, source_target_pairs={{0,2},{1,3},{2,0},{3,1},{4,6},{5,7},{6,4},{7,5},{8,10},{9,11},{10,... | collective-permute-start | bytes 786440 | tf_op jit(solution)/shard_map/ppermute | solution.py:21
  45.2 7.0 %copy-start.6 = (bf16[2,256,512]{1,2,0:T(8,128)(2,1)S(1)}, bf16[2,256,512]{1,2,0:T(8,128)(2,1)}, u32[]{:S(2)}) copy-start(bf16[2,256,512]{1,2,0:T(8,128)(2,1)} %copy-done.5) | copy-start | bytes 1572868
  45.2 7.7 %copy-start.33 = (f32[4,256,256]{2,1,0:T(8,128)S(1)}, f32[4,256,256]{2,1,0:T(8,128)}, u32[]{:S(2)}) copy-start(f32[4,256,256]{2,1,0:T(8,128)} %get-tuple-element.86) | copy-start | bytes 3145732
  45.2 25.6 %collective-permute-start.4 = (bf16[2,256,512]{2,1,0:T(8,128)(2,1)}, bf16[2,256,512]{2,1,0:T(8,128)(2,1)}, u32[]{:S(2)}, u32[]{:S(2)}) collective-permute-start(bf16[2,256,512]{2,1,0:T(8,128)(2,1)} %pad_maximum_fusion.1), channel_id=1, source_target_pairs={{8,0},{12,4},{16,8},{20,12},{24,16},{28,20},{9,1},{13,5},{17,9},{2... | collective-permute-start | bytes 1572872 | tf_op jit(solution)/shard_map/ppermute | solution.py:15
  54.8 11.7 %copy-start.27 = (s32[1,256]{1,0:T(1,128)S(1)}, s32[1,256]{1,0:T(1,128)}, u32[]{:S(2)}) copy-start(s32[1,256]{1,0:T(1,128)} %copy-done.26) | copy-start | bytes 3076
  54.8 20.6 %all-to-all-start = ((f32[8,1,8192]{2,1,0:T(1,128)}), f32[8,1,8192]{2,1,0:T(1,128)}, u32[]{:S(2)}, u32[]{:S(2)}) async-start(f32[8,1,8192]{2,1,0:T(1,128)} %bitcast.42), calls=%async_computation | async-start | bytes 524288 | tf_op jit(solution)/shard_map/all_to_all | solution.py:82
  66.9 1.2 copy-start.16
  68.0 2.1 %copy-start.15 = (bf16[1,256,512]{1,2,0:T(8,128)(2,1)S(1)}, bf16[1,256,512]{1,2,0:T(8,128)(2,1)}, u32[]{:S(2)}) copy-start(bf16[1,256,512]{1,2,0:T(8,128)(2,1)} %get-tuple-element.66) | copy-start | bytes 786436
  68.9 42.8 %collective-permute-start.5 = (bf16[2,256,512]{2,1,0:T(8,128)(2,1)}, bf16[2,256,512]{2,1,0:T(8,128)(2,1)}, u32[]{:S(2)}, u32[]{:S(2)}) collective-permute-start(bf16[2,256,512]{2,1,0:T(8,128)(2,1)} %pad_maximum_fusion.2), channel_id=1, source_target_pairs={{4,0},{8,4},{12,8},{16,12},{20,16},{24,20},{28,24},{5,1},{9,5},{13... | collective-permute-start | bytes 1572872 | tf_op jit(solution)/shard_map/ppermute | solution.py:15
  70.8 10.0 %copy-start.4 = (bf16[2,256,512]{1,2,0:T(8,128)(2,1)S(1)}, bf16[2,256,512]{1,2,0:T(8,128)(2,1)}, u32[]{:S(2)}) copy-start(bf16[2,256,512]{1,2,0:T(8,128)(2,1)} %copy-done.3) | copy-start | bytes 1572868
  77.4 14.9 %all-to-all-start.1 = ((f32[8,1,8192]{2,1,0:T(1,128)}), f32[8,1,8192]{2,1,0:T(1,128)S(1)}, u32[]{:S(2)}, u32[]{:S(2)}) async-start(f32[8,1,8192]{2,1,0:T(1,128)} %broadcast_in_dim.64), calls=%async_computation.1 | async-start | bytes 524288 | tf_op jit(solution)/shard_map/all_to_all | solution.py:85
  80.8 1.2 copy-start.32
  82.6 9.7 %copy-start.29 = (s32[1,256]{1,0:T(1,128)S(1)}, s32[1,256]{1,0:T(1,128)}, u32[]{:S(2)}) copy-start(s32[1,256]{1,0:T(1,128)} %copy-done.28) | copy-start | bytes 3076
  94.9 13.2 %all-to-all-start.2 = ((f32[32,1,2048]{2,1,0:T(1,128)}), f32[32,1,2048]{2,1,0:T(1,128)S(1)}, u32[]{:S(2)}, u32[]{:S(2)}) async-start(f32[32,1,2048]{2,1,0:T(1,128)} %bitcast.57), calls=%async_computation.2 | async-start | bytes 524288 | tf_op jit(solution)/shard_map/all_to_all | solution.py:82
  99.1 12.6 %copy-start.2 = (f32[1,256,512]{2,1,0:T(8,128)S(1)}, f32[1,256,512]{2,1,0:T(8,128)}, u32[]{:S(2)}) copy-start(f32[1,256,512]{2,1,0:T(8,128)} %copy.162) | copy-start | bytes 1572868
  109.0 13.2 %all-to-all-start.3 = ((f32[32,1,2048]{2,1,0:T(1,128)}), f32[32,1,2048]{2,1,0:T(1,128)S(1)}, u32[]{:S(2)}, u32[]{:S(2)}) async-start(f32[32,1,2048]{2,1,0:T(1,128)} %broadcast_in_dim.66), calls=%async_computation.3 | async-start | bytes 524288 | tf_op jit(solution)/shard_map/all_to_all | solution.py:85
  (13 other events, 11.3 us)

commit v10 on v5

--- a/solution.py
+++ b/solution.py
@@ -221,7 +221,7 @@
             blocks, anchor = lax.optimization_barrier((blocks, anchor))
             kind, axis, mask = weight_plan[done]
             if kind == "exchange":
-                weight_state[0] = summed_by_exchange(blocks.reshape(-1), (axis,))
+                weight_state[0] = lax.psum(blocks.reshape(-1), axis)
             else:
                 weight_state[0] = plan_step(blocks, kind, axis, mask)
             weight_state[1] = done + 1

time: 123 us -> 152 us (1.24)
  waiting for transfers between devices: 27.2 us -> 58.2 us
  starting transfers between devices: 39.8 us -> 25.6 us
  between operations: 1.45 us -> 14.9 us
  matrix products: 17.3 us -> 15.4 us
    psum x0 -> x1, waiting for transfers between devices: none -> 29.2 us  [slot(): weight_state[0] = lax.psum(blocks.reshape(-1), axis)]
    all_to_all x2 -> x1, starting transfers between devices: 19.7 us -> 9.29 us  [summed_by_exchange(): pieces = lax.all_to_all(flat.reshape(size, -1), axes, 0, 0, tiled=True)]
    ppermute x4, waiting for transfers between devices: 0.01 us -> 6.3 us  [passed_along(): return lax.ppermute(value, axis, pairs)]
    all_to_all x2 -> x1, waiting for transfers between devices: 13.5 us -> 8.31 us  [summed_by_exchange(): return lax.all_to_all(spread, axes, 0, 0, tiled=True).reshape(flat.shape)]
    all_to_all x2 -> x1, starting transfers between devices: 6.4 us -> 2.61 us  [summed_by_exchange(): return lax.all_to_all(spread, axes, 0, 0, tiled=True).reshape(flat.shape)]
    unnamed x80 -> x77, local copies, waits for them, and re-layouts: 9.88 us -> 11.3 us
    all_to_all x2 -> x1, waiting for transfers between devices: 9.8 us -> 10.7 us  [summed_by_exchange(): pieces = lax.all_to_all(flat.reshape(size, -1), axes, 0, 0, tiled=True)]
  transfers between devices with their start and end apart: 10 -> 9, of which waited for: 6 -> 6; matrix products, arithmetic and copies ran while one was open for 26% -> 20% of each run, Pallas kernels for 0% -> 0%
where the time goes in v10:
time: 152 us; the launch traced here: 151 us
  waiting for transfers between devices  58.2 us (38%)
  local copies, waits for them, and re-layouts  27.7 us (18%)
  starting transfers between devices  25.6 us (17%)
  matrix products  15.4 us (10%)
  between operations  14.9 us (10%)
  other arithmetic  9.4 us (6%)
    psum x1, waiting for transfers between devices, slot(): weight_state[0] = lax.psum(blocks.reshape(-1), axis)  29.2 us
    ppermute x4, starting transfers between devices, passed_along(): return lax.ppermute(value, axis, pairs)  12.1 us
    unnamed x77, local copies, waits for them, and re-layouts  11.3 us
    all_to_all x1, waiting for transfers between devices, summed_by_exchange(): pieces = lax.all_to_all(flat.reshape(size, -1), axes, 0, 0, tiled=True)  10.7 us
    all_to_all x1, starting transfers between devices, summed_by_exchange(): pieces = lax.all_to_all(flat.reshape(size, -1), axes, 0, 0, tiled=True)  9.29 us
    all_to_all x1, waiting for transfers between devices, summed_by_exchange(): return lax.all_to_all(spread, axes, 0, 0, tiled=True).reshape(flat.shape)  8.31 us
    ppermute x4, waiting for transfers between devices, passed_along(): return lax.ppermute(value, axis, pairs)  6.3 us
    ppermute x2, waiting for transfers between devices, exchanged(): return lax.ppermute(value, axis, pairs)  3.68 us
  transfers between devices with their start and end apart: 9, of which 6 were waited for; matrix products, arithmetic and copies ran while one was open for 20% of the time, Pallas kernels for 0%

profile of v10, /device:TPU:0, one launch (start us, length us, event | category | flops | bytes accessed | tf_op | source)
XLA Modules:
  0.0 151.2 jit_solution(12337245786493501877)
XLA Ops:
  7.2 1.2 copy.179
  8.6 5.8 %collective-permute-start.1 = (bf16[2,256,512]{1,2,0:T(8,128)(2,1)S(1)}, bf16[2,256,512]{1,2,0:T(8,128)(2,1)}, u32[]{:S(2)}, u32[]{:S(2)}) collective-permute-start(bf16[2,256,512]{1,2,0:T(8,128)(2,1)S(1)} %pad_maximum_fusion), channel_id=1, source_target_pairs={{0,8},{4,12},{8,16},{12,20},{16,24},{20,28},{1,9},{5,13},{9,17},{1... | collective-permute-start | bytes 1572872 | tf_op jit(solution)/shard_map/ppermute | solution.py:15
  14.4 3.4 %collective-permute-start = (bf16[2,256,512]{1,2,0:T(8,128)(2,1)S(1)}, bf16[2,256,512]{1,2,0:T(8,128)(2,1)S(1)}, u32[]{:S(2)}, u32[]{:S(2)}) collective-permute-start(bf16[2,256,512]{1,2,0:T(8,128)(2,1)S(1)} %pad_maximum_fusion), channel_id=1, source_target_pairs={{0,4},{4,8},{8,12},{12,16},{16,20},{20,24},{24,28},{1,5},{5,9},{9,... | collective-permute-start | bytes 1572872 | tf_op jit(solution)/shard_map/ppermute | solution.py:15
  18.1 0.9 compare_bitcast_fusion.1
  22.3 1.5 select_convert_fusion.2
  24.6 1.1 convolution_bitcast_fusion.2
  27.6 1.1 fusion.66
  28.7 1.5 %select_convert_fusion = (bf16[4,256,256]{2,1,0:T(8,128)(2,1)S(1)}, f32[4,256,256]{2,1,0:T(8,128)}) fusion(pred[256,256]{1,0:T(8,128)(4,1)S(1)} %copy.143, f32[4,256,256]{2,1,0:T(8,128)S(1)} %fusion.48, bf16[256,4,128]{0,2,1:T(8,128)(2,1)S(1)} %bitcast.208, bf16[256,4,128]{0,2,1:T(8,128)(2,1)S(1)} %bitcast.236), kind=kOutput, calls=%fused_computation.41 | convolution fusion | flops 69206016 | bytes 3211264 | tf_op jit(solution)/shard_map/ihd,jhd->hij/dot_general | solution.py:175
  31.8 1.5 select_convert_fusion.1
  35.2 0.9 fusion.19
  37.9 0.9 convolution_convert_fusion.1
  39.3 1.0 copy.162
  40.3 0.8 copy.156
  43.9 0.9 constant_dynamic-slice_fusion.2
  45.4 1.1 fusion.63
  48.1 1.6 %collective-permute-start.3 = (f32[1,65536]{1,0:T(1,128)S(1)}, f32[1,65536]{1,0:T(1,128)}, u32[]{:S(2)}, u32[]{:S(2)}) collective-permute-start(f32[1,65536]{1,0:T(1,128)S(1)} %constant_dynamic-slice_fusion), channel_id=1, source_target_pairs={{0,2},{1,3},{2,0},{3,1},{4,6},{5,7},{6,4},{7,5},{8,10},{9,11},{10,... | collective-permute-start | bytes 786440 | tf_op jit(solution)/shard_map/ppermute | solution.py:21
  51.7 1.6 %collective-permute-start.4 = (bf16[2,256,512]{2,1,0:T(8,128)(2,1)}, bf16[2,256,512]{2,1,0:T(8,128)(2,1)}, u32[]{:S(2)}, u32[]{:S(2)}) collective-permute-start(bf16[2,256,512]{2,1,0:T(8,128)(2,1)} %pad_maximum_fusion.1), channel_id=1, source_target_pairs={{8,0},{12,4},{16,8},{20,12},{24,16},{28,20},{9,1},{13,5},{17,9},{2... | collective-permute-start | bytes 1572872 | tf_op jit(solution)/shard_map/ppermute | solution.py:15
  53.3 3.4 %collective-permute-done.3 = f32[1,65536]{1,0:T(1,128)} collective-permute-done((f32[1,65536]{1,0:T(1,128)S(1)}, f32[1,65536]{1,0:T(1,128)}, u32[]{:S(2)}, u32[]{:S(2)}) %collective-permute-start.3) | collective-permute-done | bytes 262176 | tf_op jit(solution)/shard_map/ppermute | solution.py:21
  56.7 1.3 dynamic-slice_add_fusion
  59.3 0.9 fusion.15
  61.1 1.3 reduce.6
  64.2 1.1 copy.165
  66.2 1.3 collective-permute-start.5
  68.1 6.3 %collective-permute-done.4 = bf16[2,256,512]{2,1,0:T(8,128)(2,1)} collective-permute-done((bf16[2,256,512]{2,1,0:T(8,128)(2,1)}, bf16[2,256,512]{2,1,0:T(8,128)(2,1)}, u32[]{:S(2)}, u32[]{:S(2)}) %collective-permute-start.4) | collective-permute-done | bytes 524320 | tf_op jit(solution)/shard_map/ppermute | solution.py:15
  77.0 9.3 %all-to-all-start = ((f32[32,1,2048]{2,1,0:T(1,128)}), f32[32,1,2048]{2,1,0:T(1,128)S(1)}, u32[]{:S(2)}, u32[]{:S(2)}) async-start(f32[32,1,2048]{2,1,0:T(1,128)} %bitcast.55), calls=%async_computation | async-start | bytes 524288 | tf_op jit(solution)/shard_map/all_to_all | solution.py:82
  87.0 0.8 copy.170
  87.9 10.7 %all-to-all-done = f32[32,1,2048]{2,1,0:T(1,128)S(1)} async-done(((f32[32,1,2048]{2,1,0:T(1,128)}), f32[32,1,2048]{2,1,0:T(1,128)S(1)}, u32[]{:S(2)}, u32[]{:S(2)}) %all-to-all-start) | async-done | bytes 262176 | tf_op jit(solution)/shard_map/all_to_all | solution.py:82
  99.6 2.6 %all-to-all-start.1 = ((f32[32,1,2048]{2,1,0:T(1,128)}), f32[32,1,2048]{2,1,0:T(1,128)S(1)}, u32[]{:S(2)}, u32[]{:S(2)}) async-start(f32[32,1,2048]{2,1,0:T(1,128)} %broadcast_in_dim.63), calls=%async_computation.1 | async-start | bytes 524288 | tf_op jit(solution)/shard_map/all_to_all | solution.py:85
  102.2 1.4 fusion.18
  104.5 8.3 %all-to-all-done.1 = f32[32,1,2048]{2,1,0:T(1,128)S(1)} async-done(((f32[32,1,2048]{2,1,0:T(1,128)}), f32[32,1,2048]{2,1,0:T(1,128)S(1)}, u32[]{:S(2)}, u32[]{:S(2)}) %all-to-all-start.1) | async-done | bytes 262176 | tf_op jit(solution)/shard_map/all_to_all | solution.py:85
  112.8 29.2 %all-reduce.2.cloned.1.call-done = f32[128,512]{1,0:T(8,128)} async-done(((f32[128,512]{1,0:T(8,128)}), f32[128,512]{1,0:T(8,128)}) %all-reduce.2.cloned.1.call-update) | async-done | bytes 262160 | tf_op jit(solution)/shard_map/psum | solution.py:224
  142.0 1.7 %copy.211 = f32[128,512]{1,0:T(8,128)} copy(f32[128,512]{1,0:T(8,128)} %all-reduce.2.cloned.1.call-done) | data formatting | bytes 524288
  (152 shorter events, 29.9 us)
Async XLA Ops:
  7.2 26.8 %copy-start = (bf16[512,512]{1,0:T(8,128)(2,1)S(1)}, bf16[512,512]{1,0:T(8,128)(2,1)}, u32[]{:S(2)}) copy-start(bf16[512,512]{1,0:T(8,128)(2,1)} %param.19) | copy-start | bytes 1572868
  7.2 1.2 copy-start.14
  7.2 134.8 %all-reduce.2.cloned.1.call-start = ((), (), s32[]{:S(2)}) async-start(), calls=%async_computation.2 | async-start | bytes 524288 | tf_op jit(solution)/shard_map/psum | solution.py:224
  8.6 12.1 %copy-start.3 = (bf16[2,256,512]{1,2,0:T(8,128)(2,1)}, bf16[2,256,512]{1,2,0:T(8,128)(2,1)S(1)}, u32[]{:S(2)}) copy-start(bf16[2,256,512]{1,2,0:T(8,128)(2,1)S(1)} %pad_maximum_fusion) | copy-start | bytes 1572868
  8.6 19.0 %collective-permute-start.1 = (bf16[2,256,512]{1,2,0:T(8,128)(2,1)S(1)}, bf16[2,256,512]{1,2,0:T(8,128)(2,1)}, u32[]{:S(2)}, u32[]{:S(2)}) collective-permute-start(bf16[2,256,512]{1,2,0:T(8,128)(2,1)S(1)} %pad_maximum_fusion), channel_id=1, source_target_pairs={{0,8},{4,12},{8,16},{12,20},{16,24},{20,28},{1,9},{5,13},{9,17},{1... | collective-permute-start | bytes 1572872 | tf_op jit(solution)/shard_map/ppermute | solution.py:15
  14.4 16.6 %collective-permute-start = (bf16[2,256,512]{1,2,0:T(8,128)(2,1)S(1)}, bf16[2,256,512]{1,2,0:T(8,128)(2,1)S(1)}, u32[]{:S(2)}, u32[]{:S(2)}) collective-permute-start(bf16[2,256,512]{1,2,0:T(8,128)(2,1)S(1)} %pad_maximum_fusion), channel_id=1, source_target_pairs={{0,4},{4,8},{8,12},{12,16},{16,20},{20,24},{24,28},{1,5},{5,9},{9,... | collective-permute-start | bytes 1572872 | tf_op jit(solution)/shard_map/ppermute | solution.py:15
  18.0 1.6 %copy-start.30 = (s32[1,6]{1,0:T(1,128)S(1)}, s32[1,6]{1,0:T(1,128)}, u32[]{:S(2)}) copy-start(s32[1,6]{1,0:T(1,128)} %param.16) | copy-start | bytes 76
  18.0 2.7 %copy-start.21 = (bf16[1,256,512]{2,1,0:T(8,128)(2,1)S(1)}, bf16[1,256,512]{2,1,0:T(8,128)(2,1)}, u32[]{:S(2)}) copy-start(bf16[1,256,512]{2,1,0:T(8,128)(2,1)} %param.10) | copy-start | bytes 786436
  21.5 5.3 %copy-start.25 = (s32[1,256]{1,0:T(1,128)}, s32[1,256]{1,0:T(1,128)S(1)}, u32[]{:S(2)}) copy-start(s32[1,256]{1,0:T(1,128)S(1)} %get-tuple-element.73) | copy-start | bytes 3076
  26.7 2.0 %copy-start.23 = (pred[256,256]{1,0:T(8,128)(4,1)}, pred[256,256]{1,0:T(8,128)(4,1)S(1)}, u32[]{:S(2)}) copy-start(pred[256,256]{1,0:T(8,128)(4,1)S(1)} %copy.143) | copy-start | bytes 196612
  31.8 1.5 copy-start.11
  33.8 1.0 copy-start.19
  36.9 1.0 copy-start.10
  37.9 1.0 copy-start.8
  39.3 1.0 copy-start.18
  44.9 1.6 %copy-start.33 = (f32[4,256,256]{2,1,0:T(8,128)S(1)}, f32[4,256,256]{2,1,0:T(8,128)}, u32[]{:S(2)}) copy-start(f32[4,256,256]{2,1,0:T(8,128)} %get-tuple-element.78) | copy-start | bytes 3145732
  45.3 1.2 copy-start.13
  45.3 1.2 copy-start.24
  45.3 2.0 %collective-permute-start.2 = (f32[2,65536]{1,0:T(2,128)S(1)}, f32[2,65536]{1,0:T(2,128)S(1)}, u32[]{:S(2)}, u32[]{:S(2)}) collective-permute-start(f32[2,65536]{1,0:T(2,128)S(1)} %bitcast.232), channel_id=1, source_target_pairs={{0,1},{1,0},{2,3},{3,2},{4,5},{5,4},{6,7},{7,6},{8,9},{9,8},{10,11... | collective-permute-start | bytes 1572872 | tf_op jit(solution)/shard_map/ppermute | solution.py:21
  48.1 8.6 %collective-permute-start.3 = (f32[1,65536]{1,0:T(1,128)S(1)}, f32[1,65536]{1,0:T(1,128)}, u32[]{:S(2)}, u32[]{:S(2)}) collective-permute-start(f32[1,65536]{1,0:T(1,128)S(1)} %constant_dynamic-slice_fusion), channel_id=1, source_target_pairs={{0,2},{1,3},{2,0},{3,1},{4,6},{5,7},{6,4},{7,5},{8,10},{9,11},{10,... | collective-permute-start | bytes 786440 | tf_op jit(solution)/shard_map/ppermute | solution.py:21
  49.9 1.0 copy-start.17
  51.7 6.3 %copy-start.6 = (bf16[2,256,512]{1,2,0:T(8,128)(2,1)S(1)}, bf16[2,256,512]{1,2,0:T(8,128)(2,1)}, u32[]{:S(2)}) copy-start(bf16[2,256,512]{1,2,0:T(8,128)(2,1)} %copy-done.5) | copy-start | bytes 1572868
  51.7 7.1 %copy-start.32 = (f32[4,256,256]{2,1,0:T(8,128)S(1)}, f32[4,256,256]{2,1,0:T(8,128)}, u32[]{:S(2)}) copy-start(f32[4,256,256]{2,1,0:T(8,128)} %get-tuple-element.82) | copy-start | bytes 3145732
  51.7 22.8 %collective-permute-start.4 = (bf16[2,256,512]{2,1,0:T(8,128)(2,1)}, bf16[2,256,512]{2,1,0:T(8,128)(2,1)}, u32[]{:S(2)}, u32[]{:S(2)}) collective-permute-start(bf16[2,256,512]{2,1,0:T(8,128)(2,1)} %pad_maximum_fusion.1), channel_id=1, source_target_pairs={{8,0},{12,4},{16,8},{20,12},{24,16},{28,20},{9,1},{13,5},{17,9},{2... | collective-permute-start | bytes 1572872 | tf_op jit(solution)/shard_map/ppermute | solution.py:15
  64.2 1.2 copy-start.16
  65.3 2.1 %copy-start.15 = (bf16[1,256,512]{1,2,0:T(8,128)(2,1)S(1)}, bf16[1,256,512]{1,2,0:T(8,128)(2,1)}, u32[]{:S(2)}) copy-start(bf16[1,256,512]{1,2,0:T(8,128)(2,1)} %get-tuple-element.62) | copy-start | bytes 786436
  66.2 36.0 %collective-permute-start.5 = (bf16[2,256,512]{2,1,0:T(8,128)(2,1)}, bf16[2,256,512]{2,1,0:T(8,128)(2,1)}, u32[]{:S(2)}, u32[]{:S(2)}) collective-permute-start(bf16[2,256,512]{2,1,0:T(8,128)(2,1)} %pad_maximum_fusion.2), channel_id=1, source_target_pairs={{4,0},{8,4},{12,8},{16,12},{20,16},{24,20},{28,24},{5,1},{9,5},{13... | collective-permute-start | bytes 1572872 | tf_op jit(solution)/shard_map/ppermute | solution.py:15
  67.8 6.6 %copy-start.4 = (bf16[2,256,512]{1,2,0:T(8,128)(2,1)S(1)}, bf16[2,256,512]{1,2,0:T(8,128)(2,1)}, u32[]{:S(2)}) copy-start(bf16[2,256,512]{1,2,0:T(8,128)(2,1)} %copy-done.3) | copy-start | bytes 1572868
  67.8 6.7 %copy-start.31 = (f32[4,256,256]{2,1,0:T(8,128)S(1)}, f32[4,256,256]{2,1,0:T(8,128)}, u32[]{:S(2)}) copy-start(f32[4,256,256]{2,1,0:T(8,128)} %get-tuple-element.80) | copy-start | bytes 3145732
  77.0 21.6 %all-to-all-start = ((f32[32,1,2048]{2,1,0:T(1,128)}), f32[32,1,2048]{2,1,0:T(1,128)S(1)}, u32[]{:S(2)}, u32[]{:S(2)}) async-start(f32[32,1,2048]{2,1,0:T(1,128)} %bitcast.55), calls=%async_computation | async-start | bytes 524288 | tf_op jit(solution)/shard_map/all_to_all | solution.py:82
  87.9 14.4 %copy-start.2 = (f32[1,256,512]{2,1,0:T(8,128)S(1)}, f32[1,256,512]{2,1,0:T(8,128)}, u32[]{:S(2)}) copy-start(f32[1,256,512]{2,1,0:T(8,128)} %copy.162) | copy-start | bytes 1572868
  99.6 13.2 %all-to-all-start.1 = ((f32[32,1,2048]{2,1,0:T(1,128)}), f32[32,1,2048]{2,1,0:T(1,128)S(1)}, u32[]{:S(2)}, u32[]{:S(2)}) async-start(f32[32,1,2048]{2,1,0:T(1,128)} %broadcast_in_dim.63), calls=%async_computation.1 | async-start | bytes 524288 | tf_op jit(solution)/shard_map/all_to_all | solution.py:85
  (11 other events, 8.7 us)
Sparse Core Ops, SparseCore 0:
  63.3 78.6 all-reduce.1

commit v11 on v8

--- a/solution.py
+++ b/solution.py
@@ -212,14 +212,18 @@
         mixed, grad_rows, (((0,), (0,)), ((), ())), preferred_element_type=jnp.float32
     )
     weight_plan = [("split", "dp", mask) for mask in axis_bits("dp")]
+    weight_plan += [("skip", "dp", 0), ("skip", "dp", 0), ("tie", "dp", 0)]
     weight_state = [weight_term.reshape(dp_size, -1), 0]
 
     def slot(anchor):
         blocks, done = weight_state
         if done < len(weight_plan):
-            blocks, anchor = lax.optimization_barrier((blocks, anchor))
             kind, axis, mask = weight_plan[done]
-            if kind == "exchange":
+            if kind != "skip":
+                blocks, anchor = lax.optimization_barrier((blocks, anchor))
+            if kind in ("skip", "tie"):
+                weight_state[0] = blocks
+            elif kind == "exchange":
                 weight_state[0] = summed_by_exchange(blocks.reshape(-1), (axis,))
             else:
                 weight_state[0] = plan_step(blocks, kind, axis, mask)

time: 128 us -> 124 us (0.969)
  waiting for transfers between devices: 38.9 us -> 33.8 us
  matrix products: 19.1 us -> 20.6 us
    ppermute x4, waiting for transfers between devices: 20 us -> 16.1 us  [passed_along(): return lax.ppermute(value, axis, pairs)]
    unnamed x90 -> x86, local copies, waits for them, and re-layouts: 10.8 us -> 7.49 us
  transfers between devices with their start and end apart: 12 -> 12, of which waited for: 7 -> 7; matrix products, arithmetic and copies ran while one was open for 24% -> 26% of each run, Pallas kernels for 0% -> 0%
where the time goes in v11:
time: 124 us; the launch traced here: 122 us
  waiting for transfers between devices  33.8 us (27%)
  local copies, waits for them, and re-layouts  27.6 us (22%)
  starting transfers between devices  26.7 us (22%)
  matrix products  20.6 us (17%)
  other arithmetic  12.3 us (10%)
  between operations  1.47 us (1%)
    ppermute x4, waiting for transfers between devices, passed_along(): return lax.ppermute(value, axis, pairs)  16.1 us
    ppermute x4, starting transfers between devices, passed_along(): return lax.ppermute(value, axis, pairs)  12 us
    all_to_all x1, waiting for transfers between devices, summed_by_exchange(): return lax.all_to_all(spread, axes, 0, 0, tiled=True).reshape(flat.shape)  9.28 us
    ppermute x6, waiting for transfers between devices, exchanged(): return lax.ppermute(value, axis, pairs)  7.59 us
    unnamed x86, local copies, waits for them, and re-layouts  7.49 us
    all_to_all x1, starting transfers between devices, summed_by_exchange(): return lax.all_to_all(spread, axes, 0, 0, tiled=True).reshape(flat.shape)  7.09 us
    all_to_all x1, starting transfers between devices, summed_by_exchange(): pieces = lax.all_to_all(flat.reshape(size, -1), axes, 0, 0, tiled=True)  4.01 us
    another operation x3, local copies, waits for them, and re-layouts, shards(): key_terms[distance] = jnp.stack([key_part, value_part])  3.88 us
  transfers between devices with their start and end apart: 12, of which 7 were waited for; matrix products, arithmetic and copies ran while one was open for 26% of the time, Pallas kernels for 0%

profile of v11, /device:TPU:0, one launch (start us, length us, event | category | flops | bytes accessed | tf_op | source)
XLA Modules:
  0.0 122.4 jit_solution(1458040048670833346)
XLA Ops:
  0.7 1.2 copy.225
  2.0 5.0 %collective-permute-start.1 = (bf16[2,256,512]{1,2,0:T(8,128)(2,1)S(1)}, bf16[2,256,512]{1,2,0:T(8,128)(2,1)S(1)}, u32[]{:S(2)}, u32[]{:S(2)}) collective-permute-start(bf16[2,256,512]{1,2,0:T(8,128)(2,1)S(1)} %pad_maximum_fusion), channel_id=1, source_target_pairs={{0,8},{4,12},{8,16},{12,20},{16,24},{20,28},{1,9},{5,13},{9,17},{1... | collective-permute-start | bytes 1572872 | tf_op jit(solution)/shard_map/ppermute | solution.py:15
  7.0 4.2 %collective-permute-start = (bf16[2,256,512]{1,2,0:T(8,128)(2,1)S(1)}, bf16[2,256,512]{1,2,0:T(8,128)(2,1)}, u32[]{:S(2)}, u32[]{:S(2)}) collective-permute-start(bf16[2,256,512]{1,2,0:T(8,128)(2,1)S(1)} %pad_maximum_fusion), channel_id=1, source_target_pairs={{0,4},{4,8},{8,12},{12,16},{16,20},{20,24},{24,28},{1,5},{5,9},{9,... | collective-permute-start | bytes 1572872 | tf_op jit(solution)/shard_map/ppermute | solution.py:15
  16.7 1.5 %select_convert_fusion.2 = (bf16[4,256,256]{2,1,0:T(8,128)(2,1)S(1)}, f32[4,256,256]{2,1,0:T(8,128)}) fusion(pred[256,256]{1,0:T(8,128)(4,1)S(1)} %copy-done.28, f32[4,256,256]{2,1,0:T(8,128)S(1)} %convolution_multiply_fusion.5, bf16[4,256,128]{2,1,0:T(8,128)(2,1)S(1)} %fusion.16, s32[256]{0:T(256)S(1)} %bitcast.268), kind=kOutput, calls=%fused_computation.45 | convolution fusion | flops 68976640 | bytes 2950144 | tf_op jit(solution)/shard_map/vqx,px->vqp/dot_general | solution.py:160
  21.7 1.5 %select_convert_fusion = (bf16[4,256,256]{2,1,0:T(8,128)(2,1)S(1)}, f32[4,256,256]{2,1,0:T(8,128)}) fusion(pred[256,256]{1,0:T(8,128)(4,1)S(1)} %copy-done.30, f32[4,256,256]{2,1,0:T(8,128)S(1)} %fusion.48, bf16[256,4,128]{0,2,1:T(8,128)(2,1)S(1)} %bitcast.226, bf16[256,4,128]{0,2,1:T(8,128)(2,1)S(1)} %bitcast.259), kind=kOutput, calls=%fused_computation.41 | convolution fusion | flops 69206016 | bytes 3211264 | tf_op jit(solution)/shard_map/ihd,jhd->hij/dot_general | solution.py:175
  23.6 1.1 fusion.67
  24.7 1.5 %select_convert_fusion.1 = (bf16[4,256,256]{2,1,0:T(8,128)(2,1)S(1)}, f32[4,256,256]{2,1,0:T(8,128)}) fusion(pred[256,256]{1,0:T(8,128)(4,1)S(1)} %copy.183, f32[4,256,256]{2,1,0:T(8,128)S(1)} %fusion.44, bf16[256,4,128]{0,2,1:T(8,128)(2,1)S(1)} %bitcast.227, bf16[256,4,128]{0,2,1:T(8,128)(2,1)S(1)} %bitcast.239), kind=kOutput, calls=%fused_computation.43 | convolution fusion | flops 69206016 | bytes 3211264 | tf_op jit(solution)/shard_map/ihd,jhd->hij/dot_general | solution.py:175
  28.7 0.9 fusion.19
  30.7 1.7 %fusion.8 = bf16[4,256,256]{2,1,0:T(8,128)(2,1)S(1)} fusion(bf16[256,4,128]{0,2,1:T(8,128)(2,1)S(1)} %bitcast.243, f32[4,256,256]{2,1,0:T(8,128)} %get-tuple-element.92, pred[256,256]{1,0:T(8,128)(4,1)S(1)} %copy.183, bf16[256,512]{1,0:T(8,128)(2,1)S(1)} %get-tuple-element.58), kind=kOutput, calls=%fused_computation.15 | convolution fusion | flops 69730304 | bytes 2162688 | tf_op jit(solution)/shard_map/ihd,jhd->hij/dot_general | solution.py:244
  32.5 1.2 fusion.42
  41.3 1.6 %collective-permute-start.4 = (f32[1,65536]{1,0:T(1,128)S(1)}, f32[1,65536]{1,0:T(1,128)S(1)}, u32[]{:S(2)}, u32[]{:S(2)}) collective-permute-start(f32[1,65536]{1,0:T(1,128)S(1)} %constant_dynamic-slice_fusion.3), channel_id=1, source_target_pairs={{0,2},{1,3},{2,0},{3,1},{4,6},{5,7},{6,4},{7,5},{8,10},{9,11},{10,... | collective-permute-start | bytes 786440 | tf_op jit(solution)/shard_map/ppermute | solution.py:21
  43.0 1.5 %collective-permute-start.3 = (bf16[2,256,512]{2,1,0:T(8,128)(2,1)S(1)}, bf16[2,256,512]{2,1,0:T(8,128)(2,1)S(1)}, u32[]{:S(2)}, u32[]{:S(2)}) collective-permute-start(bf16[2,256,512]{2,1,0:T(8,128)(2,1)S(1)} %pad_maximum_fusion.1), channel_id=1, source_target_pairs={{8,0},{12,4},{16,8},{20,12},{24,16},{28,20},{9,1},{13,5},{17,9},{2... | collective-permute-start | bytes 1572872 | tf_op jit(solution)/shard_map/ppermute | solution.py:15
  44.9 4.9 %collective-permute-done.4 = f32[1,65536]{1,0:T(1,128)S(1)} collective-permute-done((f32[1,65536]{1,0:T(1,128)S(1)}, f32[1,65536]{1,0:T(1,128)S(1)}, u32[]{:S(2)}, u32[]{:S(2)}) %collective-permute-start.4) | collective-permute-done | bytes 262176 | tf_op jit(solution)/shard_map/ppermute | solution.py:21
  50.1 16.0 %collective-permute-done.3 = bf16[2,256,512]{2,1,0:T(8,128)(2,1)S(1)} collective-permute-done((bf16[2,256,512]{2,1,0:T(8,128)(2,1)S(1)}, bf16[2,256,512]{2,1,0:T(8,128)(2,1)S(1)}, u32[]{:S(2)}, u32[]{:S(2)}) %collective-permute-start.3) | collective-permute-done | bytes 524320 | tf_op jit(solution)/shard_map/ppermute | solution.py:15
  70.3 1.0 fusion.70
  74.1 1.2 %copy.207 = f32[1,256,512]{2,1,0:T(8,128)S(1)} copy(f32[1,256,512]{1,2,0:T(8,128)} %bitcast.236) | data formatting | bytes 1048576 | tf_op jit(solution)/shard_map/stack;reshape | solution.py:268
  75.4 1.3 %collective-permute-done.7 = f32[1,16384]{1,0:T(1,128)} collective-permute-done((f32[1,16384]{1,0:T(1,128)}, f32[1,16384]{1,0:T(1,128)}, u32[]{:S(2)}, u32[]{:S(2)}) %collective-permute-start.7) | collective-permute-done | bytes 65568 | tf_op jit(solution)/shard_map/ppermute | solution.py:21
  76.7 0.9 dynamic-slice_add_fusion.1
  78.4 4.0 %all-to-all-start = ((f32[8,1,10240]{2,1,0:T(1,128)}), f32[8,1,10240]{2,1,0:T(1,128)S(1)}, u32[]{:S(2)}, u32[]{:S(2)}) async-start(f32[8,1,10240]{2,1,0:T(1,128)} %bitcast.238), calls=%async_computation | async-start | bytes 655360 | tf_op jit(solution)/shard_map/all_to_all | solution.py:82
  82.4 2.0 %convolution_convert_fusion = bf16[4,128,256]{2,1,0:T(8,128)(2,1)} fusion(bf16[256,4,128]{0,2,1:T(8,128)(2,1)S(1)} %bitcast.233, bf16[4,256,256]{2,1,0:T(8,128)(2,1)} %copy-done.12), kind=kOutput, calls=%fused_computation.33 | convolution fusion | flops 67239936 | bytes 1048576 | tf_op jit(solution)/shard_map/hij,ihd->jhd/dot_general | solution.py:247
  84.4 1.8 %copy.211 = bf16[1,256,512]{2,1,0:T(8,128)(2,1)} copy(bf16[1,256,512]{1,2,0:T(8,128)(2,1)} %bitcast.248) | data formatting | bytes 524288 | tf_op jit(solution)/shard_map/stack;reshape | solution.py:268
  86.2 1.9 %pad_maximum_fusion.2 = bf16[2,256,512]{2,1,0:T(8,128)(2,1)} fusion(bf16[1,256,512]{2,1,0:T(8,128)(2,1)} %copy.211, bf16[1,256,512]{2,1,0:T(8,128)(2,1)} %copy.210), kind=kLoop, calls=%fused_computation.49 | loop fusion | flops 262144 | bytes 1048576 | tf_op jit(solution)/shard_map/stack | solution.py:268
  88.1 1.3 %collective-permute-start.5 = (bf16[2,256,512]{2,1,0:T(8,128)(2,1)}, bf16[2,256,512]{2,1,0:T(8,128)(2,1)}, u32[]{:S(2)}, u32[]{:S(2)}) collective-permute-start(bf16[2,256,512]{2,1,0:T(8,128)(2,1)} %pad_maximum_fusion.2), channel_id=1, source_target_pairs={{4,0},{8,4},{12,8},{16,12},{20,16},{24,20},{28,24},{5,1},{9,5},{13... | collective-permute-start | bytes 1572872 | tf_op jit(solution)/shard_map/ppermute | solution.py:15
  89.4 1.1 fusion.69
  92.6 7.1 %all-to-all-start.1 = ((f32[8,1,10240]{2,1,0:T(1,128)}), f32[8,1,10240]{2,1,0:T(1,128)}, u32[]{:S(2)}, u32[]{:S(2)}) async-start(f32[8,1,10240]{2,1,0:T(1,128)} %broadcast_in_dim.65), calls=%async_computation.1 | async-start | bytes 655360 | tf_op jit(solution)/shard_map/all_to_all | solution.py:85
  99.7 1.3 %convolution_add_fusion.4 = f32[4,128,256]{2,1,0:T(8,128)S(1)} fusion(f32[4,128,256]{2,1,0:T(8,128)S(1)} %copy-done.4, bf16[256,4,128]{0,2,1:T(8,128)(2,1)} %bitcast.241, bf16[4,256,256]{2,1,0:T(8,128)(2,1)S(1)} %fusion.7), kind=kOutput, calls=%fused_computation.29 | convolution fusion | flops 67239936 | bytes 1835008 | tf_op jit(solution)/shard_map/hij,jhd->ihd/dot_general | solution.py:254
  101.4 1.3 %fusion.13 = bf16[4,128,256]{2,1,0:T(8,128)(2,1)S(1)} fusion(f32[4,128,256]{2,1,0:T(8,128)S(1)} %convolution_add_fusion.4, bf16[256,4,128]{0,2,1:T(8,128)(2,1)} %bitcast.252, bf16[4,256,256]{2,1,0:T(8,128)(2,1)S(1)} %fusion.9), kind=kOutput, calls=%fused_computation.30 | convolution fusion | flops 67502080 | bytes 1572864 | tf_op jit(solution)/shard_map/hij,jhd->ihd/dot_general | solution.py:254
  102.8 9.3 %all-to-all-done.1 = f32[8,1,10240]{2,1,0:T(1,128)} async-done(((f32[8,1,10240]{2,1,0:T(1,128)}), f32[8,1,10240]{2,1,0:T(1,128)}, u32[]{:S(2)}, u32[]{:S(2)}) %all-to-all-start.1) | async-done | bytes 327712 | tf_op jit(solution)/shard_map/all_to_all | solution.py:85
  113.8 1.3 %fusion.18 = bf16[2,256,512]{2,1,0:T(8,128)(2,1)S(1)} fusion(f32[1,256,512]{2,1,0:T(8,128)S(1)} %copy.207, f32[1,256,512]{2,1,0:T(8,128)S(1)} %copy.206, bf16[2,256,512]{2,1,0:T(8,128)(2,1)S(1)} %copy-done.25, bf16[2,256,512]{2,1,0:T(8,128)(2,1)} %collective-permute-done.5), kind=kLoop, calls=%fused_computation.40 | loop fusion | flops 1572864 | bytes 2621440 | tf_op jit(solution)/shard_map/convert.3
  115.9 1.3 %collective-permute-done.8 = f32[1,16384]{1,0:T(1,128)S(1)} collective-permute-done((f32[1,16384]{1,0:T(1,128)S(1)}, f32[1,16384]{1,0:T(1,128)S(1)}, u32[]{:S(2)}, u32[]{:S(2)}) %collective-permute-start.8) | collective-permute-done | bytes 65568 | tf_op jit(solution)/shard_map/ppermute | solution.py:21
  118.3 1.8 %reduce.3 = f32[8,10240]{1,0:T(8,128)S(1)} reduce(f32[8,1,10240]{2,1,0:T(1,128)} %all-to-all-done.1, f32[]{:T(128)} %constant.257), dimensions={1}, to_apply=%all_to_all.12.reduce_sub_computation | reduce | bytes 655364 | tf_op jit(solution)/shard_map/all_to_all | solution.py:85
  121.5 0.9 reshape_reshape.7
  (179 shorter events, 36.4 us)
Async XLA Ops:
  0.6 27.5 %copy-start = (bf16[512,512]{1,0:T(8,128)(2,1)S(1)}, bf16[512,512]{1,0:T(8,128)(2,1)}, u32[]{:S(2)}) copy-start(bf16[512,512]{1,0:T(8,128)(2,1)} %param.19) | copy-start | bytes 1572868
  0.6 1.2 copy-start.15
  2.0 12.6 %copy-start.5 = (bf16[2,256,512]{1,2,0:T(8,128)(2,1)}, bf16[2,256,512]{1,2,0:T(8,128)(2,1)S(1)}, u32[]{:S(2)}) copy-start(bf16[2,256,512]{1,2,0:T(8,128)(2,1)S(1)} %pad_maximum_fusion) | copy-start | bytes 1572868
  2.0 18.9 %collective-permute-start.1 = (bf16[2,256,512]{1,2,0:T(8,128)(2,1)S(1)}, bf16[2,256,512]{1,2,0:T(8,128)(2,1)S(1)}, u32[]{:S(2)}, u32[]{:S(2)}) collective-permute-start(bf16[2,256,512]{1,2,0:T(8,128)(2,1)S(1)} %pad_maximum_fusion), channel_id=1, source_target_pairs={{0,8},{4,12},{8,16},{12,20},{16,24},{20,28},{1,9},{5,13},{9,17},{1... | collective-permute-start | bytes 1572872 | tf_op jit(solution)/shard_map/ppermute | solution.py:15
  7.0 16.5 %collective-permute-start = (bf16[2,256,512]{1,2,0:T(8,128)(2,1)S(1)}, bf16[2,256,512]{1,2,0:T(8,128)(2,1)}, u32[]{:S(2)}, u32[]{:S(2)}) collective-permute-start(bf16[2,256,512]{1,2,0:T(8,128)(2,1)S(1)} %pad_maximum_fusion), channel_id=1, source_target_pairs={{0,4},{4,8},{8,12},{12,16},{16,20},{20,24},{24,28},{1,5},{5,9},{9,... | collective-permute-start | bytes 1572872 | tf_op jit(solution)/shard_map/ppermute | solution.py:15
  11.3 1.6 %copy-start.36 = (s32[1,6]{1,0:T(1,128)S(1)}, s32[1,6]{1,0:T(1,128)}, u32[]{:S(2)}) copy-start(s32[1,6]{1,0:T(1,128)} %param.16) | copy-start | bytes 76
  11.4 3.3 %copy-start.26 = (bf16[1,256,512]{2,1,0:T(8,128)(2,1)S(1)}, bf16[1,256,512]{2,1,0:T(8,128)(2,1)}, u32[]{:S(2)}) copy-start(bf16[1,256,512]{2,1,0:T(8,128)(2,1)} %param.10) | copy-start | bytes 786436
  15.5 4.7 %copy-start.31 = (s32[1,256]{1,0:T(1,128)}, s32[1,256]{1,0:T(1,128)S(1)}, u32[]{:S(2)}) copy-start(s32[1,256]{1,0:T(1,128)S(1)} %get-tuple-element.82) | copy-start | bytes 3076
  24.7 1.5 %copy-start.16 = (bf16[1,256,512]{1,2,0:T(8,128)(2,1)}, bf16[1,256,512]{1,2,0:T(8,128)(2,1)S(1)}, u32[]{:S(2)}) copy-start(bf16[1,256,512]{1,2,0:T(8,128)(2,1)S(1)} %get-tuple-element.70) | copy-start | bytes 786436
  24.7 1.5 %copy-start.18 = (bf16[1,256,512]{1,2,0:T(8,128)(2,1)}, bf16[1,256,512]{1,2,0:T(8,128)(2,1)S(1)}, u32[]{:S(2)}) copy-start(bf16[1,256,512]{1,2,0:T(8,128)(2,1)S(1)} %get-tuple-element.69) | copy-start | bytes 786436
  29.8 3.9 %copy-start.1 = (bf16[256,512]{0,1:T(8,128)(2,1)}, bf16[256,512]{0,1:T(8,128)(2,1)S(1)}, u32[]{:S(2)}) copy-start(bf16[256,512]{0,1:T(8,128)(2,1)S(1)} %copy.257) | copy-start | bytes 786436
  37.7 1.8 %copy-start.38 = (f32[4,256,256]{2,1,0:T(8,128)S(1)}, f32[4,256,256]{2,1,0:T(8,128)}, u32[]{:S(2)}) copy-start(f32[4,256,256]{2,1,0:T(8,128)} %get-tuple-element.88) | copy-start | bytes 3145732
  38.1 1.4 %copy-start.14 = (bf16[256,512]{1,0:T(8,128)(2,1)S(1)}, bf16[256,512]{1,0:T(8,128)(2,1)}, u32[]{:S(2)}) copy-start(bf16[256,512]{1,0:T(8,128)(2,1)} %copy-done.13) | copy-start | bytes 786436
  38.1 2.0 %collective-permute-start.2 = (f32[2,65536]{1,0:T(2,128)S(1)}, f32[2,65536]{1,0:T(2,128)S(1)}, u32[]{:S(2)}, u32[]{:S(2)}) collective-permute-start(f32[2,65536]{1,0:T(2,128)S(1)} %bitcast.253), channel_id=1, source_target_pairs={{0,1},{1,0},{2,3},{3,2},{4,5},{5,4},{6,7},{7,6},{8,9},{9,8},{10,11... | collective-permute-start | bytes 1572872 | tf_op jit(solution)/shard_map/ppermute | solution.py:21
  41.1 1.9 %copy-start.21 = (bf16[1,256,512]{2,1,0:T(8,128)(2,1)S(1)}, bf16[1,256,512]{2,1,0:T(8,128)(2,1)}, u32[]{:S(2)}) copy-start(bf16[1,256,512]{2,1,0:T(8,128)(2,1)} %copy.201) | copy-start | bytes 786436
  41.3 3.2 %copy-start.11 = (f32[4,256,128]{2,1,0:T(8,128)S(1)}, f32[4,256,128]{2,1,0:T(8,128)}, u32[]{:S(2)}) copy-start(f32[4,256,128]{2,1,0:T(8,128)} %fusion.42) | copy-start | bytes 1572868
  41.3 3.2 %copy-start.32 = (s32[1,256]{1,0:T(1,128)S(1)}, s32[1,256]{1,0:T(1,128)}, u32[]{:S(2)}) copy-start(s32[1,256]{1,0:T(1,128)} %copy-done.31) | copy-start | bytes 3076
  41.3 8.4 %collective-permute-start.4 = (f32[1,65536]{1,0:T(1,128)S(1)}, f32[1,65536]{1,0:T(1,128)S(1)}, u32[]{:S(2)}, u32[]{:S(2)}) collective-permute-start(f32[1,65536]{1,0:T(1,128)S(1)} %constant_dynamic-slice_fusion.3), channel_id=1, source_target_pairs={{0,2},{1,3},{2,0},{3,1},{4,6},{5,7},{6,4},{7,5},{8,10},{9,11},{10,... | collective-permute-start | bytes 786440 | tf_op jit(solution)/shard_map/ppermute | solution.py:21
  43.0 23.2 %collective-permute-start.3 = (bf16[2,256,512]{2,1,0:T(8,128)(2,1)S(1)}, bf16[2,256,512]{2,1,0:T(8,128)(2,1)S(1)}, u32[]{:S(2)}, u32[]{:S(2)}) collective-permute-start(bf16[2,256,512]{2,1,0:T(8,128)(2,1)S(1)} %pad_maximum_fusion.1), channel_id=1, source_target_pairs={{8,0},{12,4},{16,8},{20,12},{24,16},{28,20},{9,1},{13,5},{17,9},{2... | collective-permute-start | bytes 1572872 | tf_op jit(solution)/shard_map/ppermute | solution.py:15
  44.9 21.3 %copy-start.6 = (bf16[2,256,512]{1,2,0:T(8,128)(2,1)S(1)}, bf16[2,256,512]{1,2,0:T(8,128)(2,1)}, u32[]{:S(2)}) copy-start(bf16[2,256,512]{1,2,0:T(8,128)(2,1)} %copy-done.5) | copy-start | bytes 1572868
  44.9 22.2 %copy-start.37 = (f32[4,256,256]{2,1,0:T(8,128)S(1)}, f32[4,256,256]{2,1,0:T(8,128)}, u32[]{:S(2)}) copy-start(f32[4,256,256]{2,1,0:T(8,128)} %get-tuple-element.90) | copy-start | bytes 3145732
  50.1 17.0 %copy-start.29 = (pred[256,256]{1,0:T(8,128)(4,1)S(1)}, pred[256,256]{1,0:T(8,128)(4,1)}, u32[]{:S(2)}) copy-start(pred[256,256]{1,0:T(8,128)(4,1)} %copy.175) | copy-start | bytes 196612
  69.4 1.9 %collective-permute-start.6 = (f32[2,16384]{1,0:T(2,128)S(1)}, f32[2,16384]{1,0:T(2,128)S(1)}, u32[]{:S(2)}, u32[]{:S(2)}) collective-permute-start(f32[2,16384]{1,0:T(2,128)S(1)} %bitcast.260), channel_id=1, source_target_pairs={{0,1},{1,0},{2,3},{3,2},{4,5},{5,4},{6,7},{7,6},{8,9},{9,8},{10,11... | collective-permute-start | bytes 393224 | tf_op jit(solution)/shard_map/ppermute | solution.py:21
  72.1 4.6 %collective-permute-start.7 = (f32[1,16384]{1,0:T(1,128)}, f32[1,16384]{1,0:T(1,128)}, u32[]{:S(2)}, u32[]{:S(2)}) collective-permute-start(f32[1,16384]{1,0:T(1,128)} %constant_dynamic-slice_fusion), channel_id=1, source_target_pairs={{0,2},{1,3},{2,0},{3,1},{4,6},{5,7},{6,4},{7,5},{8,10},{9,11},{10,... | collective-permute-start | bytes 196616 | tf_op jit(solution)/shard_map/ppermute | solution.py:21
  78.4 13.0 %all-to-all-start = ((f32[8,1,10240]{2,1,0:T(1,128)}), f32[8,1,10240]{2,1,0:T(1,128)S(1)}, u32[]{:S(2)}, u32[]{:S(2)}) async-start(f32[8,1,10240]{2,1,0:T(1,128)} %bitcast.238), calls=%async_computation | async-start | bytes 655360 | tf_op jit(solution)/shard_map/all_to_all | solution.py:82
  86.2 3.2 %copy-start.17 = (bf16[1,256,512]{1,2,0:T(8,128)(2,1)S(1)}, bf16[1,256,512]{1,2,0:T(8,128)(2,1)}, u32[]{:S(2)}) copy-start(bf16[1,256,512]{1,2,0:T(8,128)(2,1)} %copy-done.16) | copy-start | bytes 786436
  88.1 25.6 %collective-permute-start.5 = (bf16[2,256,512]{2,1,0:T(8,128)(2,1)}, bf16[2,256,512]{2,1,0:T(8,128)(2,1)}, u32[]{:S(2)}, u32[]{:S(2)}) collective-permute-start(bf16[2,256,512]{2,1,0:T(8,128)(2,1)} %pad_maximum_fusion.2), channel_id=1, source_target_pairs={{4,0},{8,4},{12,8},{16,12},{20,16},{24,20},{28,24},{5,1},{9,5},{13... | collective-permute-start | bytes 1572872 | tf_op jit(solution)/shard_map/ppermute | solution.py:15
  91.7 8.0 %copy-start.4 = (f32[4,128,256]{2,1,0:T(8,128)S(1)}, f32[4,128,256]{2,1,0:T(8,128)}, u32[]{:S(2)}) copy-start(f32[4,128,256]{2,1,0:T(8,128)} %fusion.69) | copy-start | bytes 1572868
  92.6 19.4 %all-to-all-start.1 = ((f32[8,1,10240]{2,1,0:T(1,128)}), f32[8,1,10240]{2,1,0:T(1,128)}, u32[]{:S(2)}, u32[]{:S(2)}) async-start(f32[8,1,10240]{2,1,0:T(1,128)} %broadcast_in_dim.65), calls=%async_computation.1 | async-start | bytes 655360 | tf_op jit(solution)/shard_map/all_to_all | solution.py:85
  101.4 12.4 %copy-start.25 = (bf16[2,256,512]{2,1,0:T(8,128)(2,1)S(1)}, bf16[2,256,512]{2,1,0:T(8,128)(2,1)}, u32[]{:S(2)}) copy-start(bf16[2,256,512]{2,1,0:T(8,128)(2,1)} %copy-done.24) | copy-start | bytes 1572868
  112.9 4.3 %collective-permute-start.8 = (f32[1,16384]{1,0:T(1,128)S(1)}, f32[1,16384]{1,0:T(1,128)S(1)}, u32[]{:S(2)}, u32[]{:S(2)}) collective-permute-start(f32[1,16384]{1,0:T(1,128)S(1)} %bitcast.255), channel_id=1, source_target_pairs={{0,2},{1,3},{2,0},{3,1},{4,6},{5,7},{6,4},{7,5},{8,10},{9,11},{10,... | collective-permute-start | bytes 196616 | tf_op jit(solution)/shard_map/ppermute | solution.py:21
  117.4 3.5 %collective-permute-start.9 = (f32[2,16384]{1,0:T(2,128)S(1)}, f32[2,16384]{1,0:T(2,128)S(1)}, u32[]{:S(2)}, u32[]{:S(2)}) collective-permute-start(f32[2,16384]{1,0:T(2,128)S(1)} %maximum_bitcast_fusion), channel_id=1, source_target_pairs={{0,1},{1,0},{2,3},{3,2},{4,5},{5,4},{6,7},{7,6},{8,9},{9,8},{10,11... | collective-permute-start | bytes 393224 | tf_op jit(solution)/shard_map/ppermute | solution.py:21
  (19 other events, 16.8 us)

commit v12 on v9

--- a/solution.py
+++ b/solution.py
@@ -213,7 +213,7 @@
     )
     weight_plan = [("split", "dp", mask) for mask in axis_bits("dp")]
     weight_plan.append(("exchange", "ctx", 0))
-    weight_plan += [("skip", "ctx", 0), ("skip", "ctx", 0), ("tie", "ctx", 0)]
+    weight_plan.append(("tie", "ctx", 0))
     weight_state = [weight_term.reshape(dp_size, -1), 0]
 
     def slot(anchor):
@@ -238,8 +238,6 @@
     for distance in (2, 1, 0):
         visible, scores, weights, key_bucket_indicator = tiles[distance]
         pair = slot(window[distance])
-        if distance == 0:
-            sent[2], pair = lax.optimization_barrier((sent[2], pair))
         key_heads = pair[0].reshape(local_rows, head_count, head_dim)
         value_heads = pair[1].reshape(local_rows, head_count, head_dim)
         weight_grad = jnp.einsum(
@@ -252,6 +250,9 @@
             jnp.bfloat16
         )
         score_gradient = slot(score_gradient)
+        if distance == 1:
+            weight_state[0], held = lax.optimization_barrier((weight_state[0], held))
+            sent[2] = passed_along(held, "ctx", -2)
         query_part = jnp.einsum(
             "hij,jhd->ihd", score_gradient, key_heads, preferred_element_type=jnp.float32
         ).reshape(local_rows, width)
@@ -267,7 +268,9 @@
         share_sum = bucket_share_piece if share_sum is None else share_sum + bucket_share_piece
         query_sum = query_sum + query_part
         key_terms[distance] = jnp.stack([key_part, value_part])
-        if distance > 0:
+        if distance == 2:
+            held = key_terms[distance].astype(jnp.bfloat16)
+        elif distance == 1:
             sent[distance] = passed_along(
                 key_terms[distance].astype(jnp.bfloat16), "ctx", -distance
             )

time: 124 us -> 137 us (1.10)
  starting transfers between devices: 34 us -> 38.1 us
  matrix products: 16.1 us -> 19.9 us
  local copies, waits for them, and re-layouts: 26.2 us -> 29.7 us
    all_to_all x2, waiting for transfers between devices: 13.5 us -> 5.64 us  [summed_by_exchange(): pieces = lax.all_to_all(flat.reshape(size, -1), axes, 0, 0, tiled=True)]
    all_to_all x2, waiting for transfers between devices: 18 us -> 21.9 us  [summed_by_exchange(): return lax.all_to_all(spread, axes, 0, 0, tiled=True).reshape(flat.shape)]
    all_to_all x2, starting transfers between devices: 6.01 us -> 9.23 us  [summed_by_exchange(): return lax.all_to_all(spread, axes, 0, 0, tiled=True).reshape(flat.shape)]
    ppermute x4, waiting for transfers between devices: 0.01 us -> 2.56 us  [passed_along(): return lax.ppermute(value, axis, pairs)]
    all_to_all x2, starting transfers between devices: 14.3 us -> 16.1 us  [summed_by_exchange(): pieces = lax.all_to_all(flat.reshape(size, -1), axes, 0, 0, tiled=True)]
    ppermute x2, waiting for transfers between devices: 3.66 us -> 5.48 us  [exchanged(): return lax.ppermute(value, axis, pairs)]
    unnamed x78 -> x84, local copies, waits for them, and re-layouts: 9.51 us -> 11 us
    dot_general x3, matrix products: 1.4 us -> 2.92 us  [shards(): jnp.einsum('hij,ihd->jhd', score_gradient, query_heads, preferred_element...]
  transfers between devices with their start and end apart: 10 -> 10, of which waited for: 6 -> 7; matrix products, arithmetic and copies ran while one was open for 25% -> 21% of each run, Pallas kernels for 0% -> 0%
where the time goes in v12:
time: 137 us; the launch traced here: 135 us
  starting transfers between devices  38.1 us (28%)
  waiting for transfers between devices  35.6 us (26%)
  local copies, waits for them, and re-layouts  29.7 us (22%)
  matrix products  19.9 us (15%)
  other arithmetic  10.6 us (8%)
  between operations  1.41 us (1%)
    all_to_all x2, waiting for transfers between devices, summed_by_exchange(): return lax.all_to_all(spread, axes, 0, 0, tiled=True).reshape(flat.shape)  21.9 us
    all_to_all x2, starting transfers between devices, summed_by_exchange(): pieces = lax.all_to_all(flat.reshape(size, -1), axes, 0, 0, tiled=True)  16.1 us
    ppermute x4, starting transfers between devices, passed_along(): return lax.ppermute(value, axis, pairs)  11.1 us
    unnamed x84, local copies, waits for them, and re-layouts  11 us
    all_to_all x2, starting transfers between devices, summed_by_exchange(): return lax.all_to_all(spread, axes, 0, 0, tiled=True).reshape(flat.shape)  9.23 us
    all_to_all x2, waiting for transfers between devices, summed_by_exchange(): pieces = lax.all_to_all(flat.reshape(size, -1), axes, 0, 0, tiled=True)  5.64 us
    ppermute x2, waiting for transfers between devices, exchanged(): return lax.ppermute(value, axis, pairs)  5.48 us
    dot_general x3, matrix products, shards(): jnp.einsum('ihd,jhd->hij', query_heads, forward_key_heads, preferred_elem...  3.39 us
  transfers between devices with their start and end apart: 10, of which 7 were waited for; matrix products, arithmetic and copies ran while one was open for 21% of the time, Pallas kernels for 0%

profile of v12, /device:TPU:0, one launch (start us, length us, event | category | flops | bytes accessed | tf_op | source)
XLA Modules:
  0.0 135.4 jit_solution(9610882824166579712)
XLA Ops:
  0.7 1.2 copy.185
  2.0 5.0 %collective-permute-start.1 = (bf16[2,256,512]{1,2,0:T(8,128)(2,1)S(1)}, bf16[2,256,512]{1,2,0:T(8,128)(2,1)S(1)}, u32[]{:S(2)}, u32[]{:S(2)}) collective-permute-start(bf16[2,256,512]{1,2,0:T(8,128)(2,1)S(1)} %pad_maximum_fusion), channel_id=1, source_target_pairs={{0,8},{4,12},{8,16},{12,20},{16,24},{20,28},{1,9},{5,13},{9,17},{1... | collective-permute-start | bytes 1572872 | tf_op jit(solution)/shard_map/ppermute | solution.py:15
  7.0 3.4 %collective-permute-start = (bf16[2,256,512]{1,2,0:T(8,128)(2,1)S(1)}, bf16[2,256,512]{1,2,0:T(8,128)(2,1)S(1)}, u32[]{:S(2)}, u32[]{:S(2)}) collective-permute-start(bf16[2,256,512]{1,2,0:T(8,128)(2,1)S(1)} %pad_maximum_fusion), channel_id=1, source_target_pairs={{0,4},{4,8},{8,12},{12,16},{16,20},{20,24},{24,28},{1,5},{5,9},{9,... | collective-permute-start | bytes 1572872 | tf_op jit(solution)/shard_map/ppermute | solution.py:15
  15.0 1.5 %select_convert_fusion.2 = (bf16[4,256,256]{2,1,0:T(8,128)(2,1)S(1)}, f32[4,256,256]{2,1,0:T(8,128)}) fusion(pred[256,256]{1,0:T(8,128)(4,1)S(1)} %copy.133, f32[4,256,256]{2,1,0:T(8,128)S(1)} %convolution_multiply_fusion.5, bf16[4,256,128]{2,1,0:T(8,128)(2,1)S(1)} %fusion.18, s32[256]{0:T(256)S(1)} %bitcast.240), kind=kOutput, calls=%fused_computation.47 | convolution fusion | flops 68976640 | bytes 2950144 | tf_op jit(solution)/shard_map/vqx,px->vqp/dot_general | solution.py:160
  17.3 1.1 convolution_bitcast_fusion.3
  21.1 1.5 %select_convert_fusion = (bf16[4,256,256]{2,1,0:T(8,128)(2,1)S(1)}, f32[4,256,256]{2,1,0:T(8,128)}) fusion(pred[256,256]{1,0:T(8,128)(4,1)S(1)} %copy-done.32, f32[4,256,256]{2,1,0:T(8,128)S(1)} %fusion.45, bf16[256,4,128]{0,2,1:T(8,128)(2,1)S(1)} %bitcast.201, bf16[256,4,128]{0,2,1:T(8,128)(2,1)S(1)} %bitcast.231), kind=kOutput, calls=%fused_computation.43 | convolution fusion | flops 69206016 | bytes 3211264 | tf_op jit(solution)/shard_map/ihd,jhd->hij/dot_general | solution.py:175
  24.2 1.5 %select_convert_fusion.1 = (bf16[4,256,256]{2,1,0:T(8,128)(2,1)S(1)}, f32[4,256,256]{2,1,0:T(8,128)}) fusion(pred[256,256]{1,0:T(8,128)(4,1)S(1)} %copy.141, f32[4,256,256]{2,1,0:T(8,128)S(1)} %fusion.41, bf16[256,4,128]{0,2,1:T(8,128)(2,1)S(1)} %bitcast.202, bf16[256,4,128]{0,2,1:T(8,128)(2,1)S(1)} %bitcast.232), kind=kOutput, calls=%fused_computation.45 | convolution fusion | flops 69206016 | bytes 3211264 | tf_op jit(solution)/shard_map/ihd,jhd->hij/dot_general | solution.py:175
  31.2 1.8 %fusion.59 = (bf16[1,256,512]{1,2,0:T(8,128)(2,1)}, bf16[1,256,512]{1,2,0:T(8,128)(2,1)S(1)}) fusion(bf16[2,256,512]{1,2,0:T(8,128)(2,1)} %copy-done.9), kind=kLoop, calls=%fused_computation.141 | loop fusion | bytes 1048576 | tf_op jit(solution)/shard_map/slice | solution.py:241
  39.4 1.6 %collective-permute-start.3 = (f32[1,65536]{1,0:T(1,128)S(1)}, f32[1,65536]{1,0:T(1,128)S(1)}, u32[]{:S(2)}, u32[]{:S(2)}) collective-permute-start(f32[1,65536]{1,0:T(1,128)S(1)} %constant_dynamic-slice_fusion), channel_id=1, source_target_pairs={{0,2},{1,3},{2,0},{3,1},{4,6},{5,7},{6,4},{7,5},{8,10},{9,11},{10,... | collective-permute-start | bytes 786440 | tf_op jit(solution)/shard_map/ppermute | solution.py:21
  41.3 1.0 convolution_multiply_fusion.8
  42.3 5.5 %collective-permute-done.3 = f32[1,65536]{1,0:T(1,128)S(1)} collective-permute-done((f32[1,65536]{1,0:T(1,128)S(1)}, f32[1,65536]{1,0:T(1,128)S(1)}, u32[]{:S(2)}, u32[]{:S(2)}) %collective-permute-start.3) | collective-permute-done | bytes 262176 | tf_op jit(solution)/shard_map/ppermute | solution.py:21
  47.8 1.1 dynamic-slice_add_fusion
  48.8 12.7 %all-to-all-start = ((f32[8,1,8192]{2,1,0:T(1,128)}), f32[8,1,8192]{2,1,0:T(1,128)}, u32[]{:S(2)}, u32[]{:S(2)}) async-start(f32[8,1,8192]{2,1,0:T(1,128)} %bitcast.35), calls=%async_computation | async-start | bytes 524288 | tf_op jit(solution)/shard_map/all_to_all | solution.py:82
  62.5 1.8 %copy.166 = bf16[1,256,512]{2,1,0:T(8,128)(2,1)} copy(bf16[1,256,512]{1,2,0:T(8,128)(2,1)} %bitcast.226) | data formatting | bytes 524288 | tf_op jit(solution)/shard_map/stack;reshape | solution.py:270
  66.3 0.9 fusion.17
  67.3 1.1 copy.169
  70.1 1.1 reduce_sum.92
  72.1 5.3 %all-to-all-start.1 = ((f32[8,1,8192]{2,1,0:T(1,128)}), f32[8,1,8192]{2,1,0:T(1,128)}, u32[]{:S(2)}, u32[]{:S(2)}) async-start(f32[8,1,8192]{2,1,0:T(1,128)} %broadcast_in_dim.64), calls=%async_computation.1 | async-start | bytes 524288 | tf_op jit(solution)/shard_map/all_to_all | solution.py:85
  78.3 1.8 %fusion.8 = bf16[4,256,256]{2,1,0:T(8,128)(2,1)S(1)} fusion(bf16[256,4,128]{0,2,1:T(8,128)(2,1)S(1)} %bitcast.211, bf16[256,4,128]{0,2,1:T(8,128)(2,1)S(1)} %bitcast.230, f32[4,256,256]{2,1,0:T(8,128)} %get-tuple-element.84, pred[256,256]{1,0:T(8,128)(4,1)S(1)} %copy.141), kind=kOutput, calls=%fused_computation.15 | convolution fusion | flops 69730304 | bytes 2162688 | tf_op jit(solution)/shard_map/ihd,jhd->hij/dot_general | solution.py:243
  80.1 5.5 %all-to-all-done.1 = f32[8,1,8192]{2,1,0:T(1,128)} async-done(((f32[8,1,8192]{2,1,0:T(1,128)}), f32[8,1,8192]{2,1,0:T(1,128)}, u32[]{:S(2)}, u32[]{:S(2)}) %all-to-all-start.1) | async-done | bytes 262176 | tf_op jit(solution)/shard_map/all_to_all | solution.py:85
  86.6 1.1 fusion.39
  88.6 1.7 %reshape.737 = f32[128,512]{1,0:T(8,128)} reshape(f32[65536]{0:T(1024)} %bitcast.36) | data formatting | bytes 524288 | tf_op jit(solution)/shard_map/reshape | solution.py:284
  90.3 1.1 fusion.64
  93.7 3.4 %all-to-all-start.2 = ((f32[32,1,2048]{2,1,0:T(1,128)}), f32[32,1,2048]{2,1,0:T(1,128)}, u32[]{:S(2)}, u32[]{:S(2)}) async-start(f32[32,1,2048]{2,1,0:T(1,128)} %bitcast.55), calls=%async_computation.2 | async-start | bytes 524288 | tf_op jit(solution)/shard_map/all_to_all | solution.py:82
  97.1 1.4 %collective-permute-start.5 = (bf16[2,256,512]{2,1,0:T(8,128)(2,1)}, bf16[2,256,512]{2,1,0:T(8,128)(2,1)}, u32[]{:S(2)}, u32[]{:S(2)}) collective-permute-start(bf16[2,256,512]{2,1,0:T(8,128)(2,1)} %pad_maximum_fusion.2), channel_id=1, source_target_pairs={{8,0},{12,4},{16,8},{20,12},{24,16},{28,20},{9,1},{13,5},{17,9},{2... | collective-permute-start | bytes 1572872 | tf_op jit(solution)/shard_map/ppermute | solution.py:15
  99.4 1.3 collective-permute-start.4
  102.9 4.8 %all-to-all-done.2 = f32[32,1,2048]{2,1,0:T(1,128)} async-done(((f32[32,1,2048]{2,1,0:T(1,128)}), f32[32,1,2048]{2,1,0:T(1,128)}, u32[]{:S(2)}, u32[]{:S(2)}) %all-to-all-start.2) | async-done | bytes 262176 | tf_op jit(solution)/shard_map/all_to_all | solution.py:82
  107.7 1.1 reduce_sum.93
  109.7 4.0 %all-to-all-start.3 = ((f32[32,1,2048]{2,1,0:T(1,128)}), f32[32,1,2048]{2,1,0:T(1,128)S(1)}, u32[]{:S(2)}, u32[]{:S(2)}) async-start(f32[32,1,2048]{2,1,0:T(1,128)} %broadcast_in_dim.66), calls=%async_computation.3 | async-start | bytes 524288 | tf_op jit(solution)/shard_map/all_to_all | solution.py:85
  113.6 2.4 %collective-permute-done.5 = bf16[2,256,512]{2,1,0:T(8,128)(2,1)} collective-permute-done((bf16[2,256,512]{2,1,0:T(8,128)(2,1)}, bf16[2,256,512]{2,1,0:T(8,128)(2,1)}, u32[]{:S(2)}, u32[]{:S(2)}) %collective-permute-start.5) | collective-permute-done | bytes 524320 | tf_op jit(solution)/shard_map/ppermute | solution.py:15
  116.2 1.3 fusion.20
  118.3 16.4 %all-to-all-done.3 = f32[32,1,2048]{2,1,0:T(1,128)S(1)} async-done(((f32[32,1,2048]{2,1,0:T(1,128)}), f32[32,1,2048]{2,1,0:T(1,128)S(1)}, u32[]{:S(2)}, u32[]{:S(2)}) %all-to-all-start.3) | async-done | bytes 262176 | tf_op jit(solution)/shard_map/all_to_all | solution.py:85
  (159 shorter events, 37.4 us)
Async XLA Ops:
  0.6 27.0 %copy-start = (bf16[512,512]{1,0:T(8,128)(2,1)S(1)}, bf16[512,512]{1,0:T(8,128)(2,1)}, u32[]{:S(2)}) copy-start(bf16[512,512]{1,0:T(8,128)(2,1)} %param.19) | copy-start | bytes 1572868
  0.6 1.2 copy-start.21
  1.8 12.8 %copy-start.3 = (bf16[1,256,512]{1,2,0:T(8,128)(2,1)}, bf16[1,256,512]{1,2,0:T(8,128)(2,1)S(1)}, u32[]{:S(2)}) copy-start(bf16[1,256,512]{1,2,0:T(8,128)(2,1)S(1)} %copy.185) | copy-start | bytes 786436
  2.0 18.2 %collective-permute-start.1 = (bf16[2,256,512]{1,2,0:T(8,128)(2,1)S(1)}, bf16[2,256,512]{1,2,0:T(8,128)(2,1)S(1)}, u32[]{:S(2)}, u32[]{:S(2)}) collective-permute-start(bf16[2,256,512]{1,2,0:T(8,128)(2,1)S(1)} %pad_maximum_fusion), channel_id=1, source_target_pairs={{0,8},{4,12},{8,16},{12,20},{16,24},{20,28},{1,9},{5,13},{9,17},{1... | collective-permute-start | bytes 1572872 | tf_op jit(solution)/shard_map/ppermute | solution.py:15
  7.0 16.4 %collective-permute-start = (bf16[2,256,512]{1,2,0:T(8,128)(2,1)S(1)}, bf16[2,256,512]{1,2,0:T(8,128)(2,1)S(1)}, u32[]{:S(2)}, u32[]{:S(2)}) collective-permute-start(bf16[2,256,512]{1,2,0:T(8,128)(2,1)S(1)} %pad_maximum_fusion), channel_id=1, source_target_pairs={{0,4},{4,8},{8,12},{12,16},{16,20},{20,24},{24,28},{1,5},{5,9},{9,... | collective-permute-start | bytes 1572872 | tf_op jit(solution)/shard_map/ppermute | solution.py:15
  10.6 1.6 %copy-start.35 = (s32[1,6]{1,0:T(1,128)S(1)}, s32[1,6]{1,0:T(1,128)}, u32[]{:S(2)}) copy-start(s32[1,6]{1,0:T(1,128)} %param.16) | copy-start | bytes 76
  10.7 5.8 %copy-start.19 = (bf16[256,4,128]{2,1,0:T(4,128)(2,1)}, bf16[256,4,128]{2,1,0:T(4,128)(2,1)S(1)}, u32[]{:S(2)}) copy-start(bf16[256,4,128]{2,1,0:T(4,128)(2,1)S(1)} %reshape_squeeze_stack_squeeze.9) | copy-start | bytes 786436
  10.7 2.7 %copy-start.30 = (bf16[1,256,512]{2,1,0:T(8,128)(2,1)S(1)}, bf16[1,256,512]{2,1,0:T(8,128)(2,1)}, u32[]{:S(2)}) copy-start(bf16[1,256,512]{2,1,0:T(8,128)(2,1)} %param.10) | copy-start | bytes 786436
  20.2 2.4 %copy-start.9 = (bf16[2,256,512]{1,2,0:T(8,128)(2,1)}, bf16[2,256,512]{1,2,0:T(8,128)(2,1)S(1)}, u32[]{:S(2)}) copy-start(bf16[2,256,512]{1,2,0:T(8,128)(2,1)S(1)} %collective-permute-done.1) | copy-start | bytes 1572868
  24.2 1.5 %copy-start.16 = (f32[256,4,128]{0,2,1:T(8,128)S(1)}, f32[256,4,128]{0,2,1:T(8,128)}, u32[]{:S(2)}) copy-start(f32[256,4,128]{0,2,1:T(8,128)} %convolution_bitcast_fusion.3) | copy-start | bytes 1572868
  29.4 32.1 %copy-start.1 = (bf16[256,512]{0,1:T(8,128)(2,1)}, bf16[256,512]{0,1:T(8,128)(2,1)S(1)}, u32[]{:S(2)}) copy-start(bf16[256,512]{0,1:T(8,128)(2,1)S(1)} %copy.186) | copy-start | bytes 786436
  33.8 1.4 %copy-start.37 = (f32[4,256,256]{2,1,0:T(8,128)S(1)}, f32[4,256,256]{2,1,0:T(8,128)}, u32[]{:S(2)}) copy-start(f32[4,256,256]{2,1,0:T(8,128)} %get-tuple-element.80) | copy-start | bytes 3145732
  35.1 3.4 %collective-permute-start.2 = (f32[2,65536]{1,0:T(2,128)S(1)}, f32[2,65536]{1,0:T(2,128)S(1)}, u32[]{:S(2)}, u32[]{:S(2)}) collective-permute-start(f32[2,65536]{1,0:T(2,128)S(1)} %bitcast.228), channel_id=1, source_target_pairs={{0,1},{1,0},{2,3},{3,2},{4,5},{5,4},{6,7},{7,6},{8,9},{9,8},{10,11... | collective-permute-start | bytes 1572872 | tf_op jit(solution)/shard_map/ppermute | solution.py:21
  36.7 1.3 copy-start.36
  39.2 1.9 %copy-start.13 = (bf16[4,256,256]{2,1,0:T(8,128)(2,1)S(1)}, bf16[4,256,256]{2,1,0:T(8,128)(2,1)}, u32[]{:S(2)}) copy-start(bf16[4,256,256]{2,1,0:T(8,128)(2,1)} %copy-done.12) | copy-start | bytes 1572868
  39.4 8.4 %collective-permute-start.3 = (f32[1,65536]{1,0:T(1,128)S(1)}, f32[1,65536]{1,0:T(1,128)S(1)}, u32[]{:S(2)}, u32[]{:S(2)}) collective-permute-start(f32[1,65536]{1,0:T(1,128)S(1)} %constant_dynamic-slice_fusion), channel_id=1, source_target_pairs={{0,2},{1,3},{2,0},{3,1},{4,6},{5,7},{6,4},{7,5},{8,10},{9,11},{10,... | collective-permute-start | bytes 786440 | tf_op jit(solution)/shard_map/ppermute | solution.py:21
  42.3 19.2 %copy-start.18 = (bf16[4,256,256]{2,1,0:T(8,128)(2,1)S(1)}, bf16[4,256,256]{2,1,0:T(8,128)(2,1)}, u32[]{:S(2)}) copy-start(bf16[4,256,256]{2,1,0:T(8,128)(2,1)} %copy-done.17) | copy-start | bytes 1572868
  48.8 21.2 %all-to-all-start = ((f32[8,1,8192]{2,1,0:T(1,128)}), f32[8,1,8192]{2,1,0:T(1,128)}, u32[]{:S(2)}, u32[]{:S(2)}) async-start(f32[8,1,8192]{2,1,0:T(1,128)} %bitcast.35), calls=%async_computation | async-start | bytes 524288 | tf_op jit(solution)/shard_map/all_to_all | solution.py:82
  67.3 1.1 copy-start.27
  69.3 8.0 %copy-start.8 = (bf16[2,256,512]{1,2,0:T(8,128)(2,1)S(1)}, bf16[2,256,512]{1,2,0:T(8,128)(2,1)}, u32[]{:S(2)}) copy-start(bf16[2,256,512]{1,2,0:T(8,128)(2,1)} %copy-done.7) | copy-start | bytes 1572868
  72.1 13.6 %all-to-all-start.1 = ((f32[8,1,8192]{2,1,0:T(1,128)}), f32[8,1,8192]{2,1,0:T(1,128)}, u32[]{:S(2)}, u32[]{:S(2)}) async-start(f32[8,1,8192]{2,1,0:T(1,128)} %broadcast_in_dim.64), calls=%async_computation.1 | async-start | bytes 524288 | tf_op jit(solution)/shard_map/all_to_all | solution.py:85
  86.6 1.1 copy-start.28
  88.6 1.7 %copy-start.24 = (bf16[1,256,512]{1,2,0:T(8,128)(2,1)S(1)}, bf16[1,256,512]{1,2,0:T(8,128)(2,1)}, u32[]{:S(2)}) copy-start(bf16[1,256,512]{1,2,0:T(8,128)(2,1)} %get-tuple-element.64) | copy-start | bytes 786436
  90.3 1.1 copy-start.15
  93.7 4.9 %copy-start.25 = (bf16[1,256,512]{2,1,0:T(8,128)(2,1)S(1)}, bf16[1,256,512]{2,1,0:T(8,128)(2,1)}, u32[]{:S(2)}) copy-start(bf16[1,256,512]{2,1,0:T(8,128)(2,1)} %copy.166) | copy-start | bytes 786436
  93.7 4.9 %copy-start.26 = (bf16[1,256,512]{2,1,0:T(8,128)(2,1)S(1)}, bf16[1,256,512]{2,1,0:T(8,128)(2,1)}, u32[]{:S(2)}) copy-start(bf16[1,256,512]{2,1,0:T(8,128)(2,1)} %copy.165) | copy-start | bytes 786436
  93.7 14.0 %all-to-all-start.2 = ((f32[32,1,2048]{2,1,0:T(1,128)}), f32[32,1,2048]{2,1,0:T(1,128)}, u32[]{:S(2)}, u32[]{:S(2)}) async-start(f32[32,1,2048]{2,1,0:T(1,128)} %bitcast.55), calls=%async_computation.2 | async-start | bytes 524288 | tf_op jit(solution)/shard_map/all_to_all | solution.py:82
  97.1 3.6 %copy-start.6 = (f32[4,128,256]{2,1,0:T(8,128)S(1)}, f32[4,128,256]{2,1,0:T(8,128)}, u32[]{:S(2)}) copy-start(f32[4,128,256]{2,1,0:T(8,128)} %fusion.64) | copy-start | bytes 1572868
  97.1 3.6 %copy-start.22 = (bf16[1,256,512]{1,2,0:T(8,128)(2,1)S(1)}, bf16[1,256,512]{1,2,0:T(8,128)(2,1)}, u32[]{:S(2)}) copy-start(bf16[1,256,512]{1,2,0:T(8,128)(2,1)} %get-tuple-element.61) | copy-start | bytes 786436
  97.1 18.9 %collective-permute-start.5 = (bf16[2,256,512]{2,1,0:T(8,128)(2,1)}, bf16[2,256,512]{2,1,0:T(8,128)(2,1)}, u32[]{:S(2)}, u32[]{:S(2)}) collective-permute-start(bf16[2,256,512]{2,1,0:T(8,128)(2,1)} %pad_maximum_fusion.2), channel_id=1, source_target_pairs={{8,0},{12,4},{16,8},{20,12},{24,16},{28,20},{9,1},{13,5},{17,9},{2... | collective-permute-start | bytes 1572872 | tf_op jit(solution)/shard_map/ppermute | solution.py:15
  99.4 16.8 %collective-permute-start.4 = (bf16[2,256,512]{2,1,0:T(8,128)(2,1)}, bf16[2,256,512]{2,1,0:T(8,128)(2,1)S(1)}, u32[]{:S(2)}, u32[]{:S(2)}) collective-permute-start(bf16[2,256,512]{2,1,0:T(8,128)(2,1)} %pad_maximum_fusion.1), channel_id=1, source_target_pairs={{4,0},{8,4},{12,8},{16,12},{20,16},{24,20},{28,24},{5,1},{9,5},{13... | collective-permute-start | bytes 1572872 | tf_op jit(solution)/shard_map/ppermute | solution.py:15
  109.7 25.1 %all-to-all-start.3 = ((f32[32,1,2048]{2,1,0:T(1,128)}), f32[32,1,2048]{2,1,0:T(1,128)S(1)}, u32[]{:S(2)}, u32[]{:S(2)}) async-start(f32[32,1,2048]{2,1,0:T(1,128)} %broadcast_in_dim.66), calls=%async_computation.3 | async-start | bytes 524288 | tf_op jit(solution)/shard_map/all_to_all | solution.py:85
  (16 other events, 14.4 us)

commit v13 on v5

--- a/solution.py
+++ b/solution.py
@@ -140,7 +140,7 @@
     map_rows = lax.dynamic_slice_in_dim(block_map[0], cycle_index * blocks_here, blocks_here, 0)
     query_heads = query_rows.reshape(local_rows, head_count, head_dim)
     stacked = jnp.stack([key_rows, value_rows])
-    window = [stacked, passed_along(stacked, "ctx", 1), passed_along(stacked, "ctx", 2)]
+    window = [stacked, None, None]
     tiles = []
     attended = jnp.zeros((local_rows, head_count, head_dim), jnp.float32)
     for distance in range(3):
@@ -185,6 +185,10 @@
             "hij,jhd->ihd", forward_weights, forward_value_heads, preferred_element_type=jnp.float32
         )
         attended = attended + attended_part
+        if distance == 0:
+            shipped, attended = lax.optimization_barrier((stacked, attended))
+            window[1] = passed_along(shipped, "ctx", 1)
+            window[2] = passed_along(shipped, "ctx", 2)
         tiles.append((visible, forward_scores, forward_weights, key_bucket_indicator))
     attended = attended.reshape(local_rows, width)
     centered = attended - jnp.mean(attended, axis=1, keepdims=True)

time: 123 us -> 132 us (1.073)
  waiting for transfers between devices: 27.2 us -> 33.1 us
  starting transfers between devices: 39.8 us -> 42.4 us
  matrix products: 17.3 us -> 15.9 us
    ppermute x4, waiting for transfers between devices: 0.01 us -> 5.14 us  [passed_along(): return lax.ppermute(value, axis, pairs)]
    all_to_all x2, starting transfers between devices: 19.7 us -> 21.8 us  [summed_by_exchange(): pieces = lax.all_to_all(flat.reshape(size, -1), axes, 0, 0, tiled=True)]
    dot_general x3, matrix products: 2.11 us -> 0.7 us  [shards(): jnp.einsum('hij,ihd->jhd', weights, grad_heads, preferred_element_type=jn...]
    unnamed x80 -> x81, local copies, waits for them, and re-layouts: 9.88 us -> 10.8 us
  transfers between devices with their start and end apart: 10 -> 10, of which waited for: 6 -> 7; matrix products, arithmetic and copies ran while one was open for 26% -> 20% of each run, Pallas kernels for 0% -> 0%
where the time goes in v13:
time: 132 us; the launch traced here: 131 us
  starting transfers between devices  42.4 us (32%)
  waiting for transfers between devices  33.1 us (25%)
  local copies, waits for them, and re-layouts  27.8 us (21%)
  matrix products  15.9 us (12%)
  other arithmetic  9.84 us (7%)
  between operations  1.54 us (1%)
    all_to_all x2, starting transfers between devices, summed_by_exchange(): pieces = lax.all_to_all(flat.reshape(size, -1), axes, 0, 0, tiled=True)  21.8 us
    all_to_all x2, waiting for transfers between devices, summed_by_exchange(): return lax.all_to_all(spread, axes, 0, 0, tiled=True).reshape(flat.shape)  13.5 us
    ppermute x4, starting transfers between devices, passed_along(): return lax.ppermute(value, axis, pairs)  12.5 us
    unnamed x81, local copies, waits for them, and re-layouts  10.8 us
    all_to_all x2, waiting for transfers between devices, summed_by_exchange(): pieces = lax.all_to_all(flat.reshape(size, -1), axes, 0, 0, tiled=True)  9.75 us
    all_to_all x2, starting transfers between devices, summed_by_exchange(): return lax.all_to_all(spread, axes, 0, 0, tiled=True).reshape(flat.shape)  6.4 us
    ppermute x4, waiting for transfers between devices, passed_along(): return lax.ppermute(value, axis, pairs)  5.14 us
    ppermute x2, waiting for transfers between devices, exchanged(): return lax.ppermute(value, axis, pairs)  4.67 us
  transfers between devices with their start and end apart: 10, of which 7 were waited for; matrix products, arithmetic and copies ran while one was open for 20% of the time, Pallas kernels for 0%

profile of v13, /device:TPU:0, one launch (start us, length us, event | category | flops | bytes accessed | tf_op | source)
XLA Modules:
  0.0 130.6 jit_solution(3711592921896095899)
XLA Ops:
  0.8 1.1 reshape_squeeze_stack_squeeze.6
  3.1 0.9 compare_bitcast_fusion.1
  7.4 1.5 %select_convert_fusion.2 = (bf16[4,256,256]{2,1,0:T(8,128)(2,1)S(1)}, f32[4,256,256]{2,1,0:T(8,128)}) fusion(pred[256,256]{1,0:T(8,128)(4,1)S(1)} %copy.142, f32[4,256,256]{2,1,0:T(8,128)S(1)} %convolution_multiply_fusion.5, bf16[4,256,128]{2,1,0:T(8,128)(2,1)S(1)} %fusion.16, s32[256]{0:T(256)S(1)} %bitcast.244), kind=kOutput, calls=%fused_computation.45 | convolution fusion | flops 68976640 | bytes 2950144 | tf_op jit(solution)/shard_map/vqx,px->vqp/dot_general | solution.py:160
  8.9 1.1 convolution_bitcast_fusion.2
  10.0 5.9 %collective-permute-start.1 = (bf16[2,256,512]{1,2,0:T(8,128)(2,1)S(1)}, bf16[2,256,512]{1,2,0:T(8,128)(2,1)}, u32[]{:S(2)}, u32[]{:S(2)}) collective-permute-start(bf16[2,256,512]{1,2,0:T(8,128)(2,1)S(1)} %pad_maximum_fusion), channel_id=1, source_target_pairs={{0,8},{4,12},{8,16},{12,20},{16,24},{20,28},{1,9},{5,13},{9,17},{1... | collective-permute-start | bytes 1572872 | tf_op jit(solution)/shard_map/ppermute | solution.py:15
  15.9 3.6 %collective-permute-start = (bf16[2,256,512]{1,2,0:T(8,128)(2,1)S(1)}, bf16[2,256,512]{1,2,0:T(8,128)(2,1)S(1)}, u32[]{:S(2)}, u32[]{:S(2)}) collective-permute-start(bf16[2,256,512]{1,2,0:T(8,128)(2,1)S(1)} %pad_maximum_fusion), channel_id=1, source_target_pairs={{0,4},{4,8},{8,12},{12,16},{16,20},{20,24},{24,28},{1,5},{5,9},{9,... | collective-permute-start | bytes 1572872 | tf_op jit(solution)/shard_map/ppermute | solution.py:15
  21.6 4.6 %collective-permute-done.1 = bf16[2,256,512]{1,2,0:T(8,128)(2,1)} collective-permute-done((bf16[2,256,512]{1,2,0:T(8,128)(2,1)S(1)}, bf16[2,256,512]{1,2,0:T(8,128)(2,1)}, u32[]{:S(2)}, u32[]{:S(2)}) %collective-permute-start.1) | collective-permute-done | bytes 524320 | tf_op jit(solution)/shard_map/ppermute | solution.py:15
  26.2 1.1 fusion.67
  27.3 1.5 %select_convert_fusion = (bf16[4,256,256]{2,1,0:T(8,128)(2,1)S(1)}, f32[4,256,256]{2,1,0:T(8,128)}) fusion(pred[256,256]{1,0:T(8,128)(4,1)S(1)} %copy-done.26, f32[4,256,256]{2,1,0:T(8,128)S(1)} %fusion.49, bf16[256,4,128]{0,2,1:T(8,128)(2,1)S(1)} %bitcast.206, bf16[256,4,128]{0,2,1:T(8,128)(2,1)S(1)} %bitcast.235), kind=kOutput, calls=%fused_computation.41 | convolution fusion | flops 69206016 | bytes 3211264 | tf_op jit(solution)/shard_map/ihd,jhd->hij/dot_general | solution.py:175
  30.9 1.5 %select_convert_fusion.1 = (bf16[4,256,256]{2,1,0:T(8,128)(2,1)S(1)}, f32[4,256,256]{2,1,0:T(8,128)}) fusion(pred[256,256]{1,0:T(8,128)(4,1)S(1)} %copy.148, f32[4,256,256]{2,1,0:T(8,128)S(1)} %fusion.45, bf16[256,4,128]{0,2,1:T(8,128)(2,1)S(1)} %bitcast.207, bf16[256,4,128]{0,2,1:T(8,128)(2,1)S(1)} %bitcast.236), kind=kOutput, calls=%fused_computation.43 | convolution fusion | flops 69206016 | bytes 3211264 | tf_op jit(solution)/shard_map/ihd,jhd->hij/dot_general | solution.py:175
  35.1 0.9 fusion.19
  39.8 1.0 copy.177
  43.7 0.9 constant_dynamic-slice_fusion.2
  45.2 1.1 fusion.64
  47.9 1.6 %collective-permute-start.3 = (f32[1,65536]{1,0:T(1,128)S(1)}, f32[1,65536]{1,0:T(1,128)}, u32[]{:S(2)}, u32[]{:S(2)}) collective-permute-start(f32[1,65536]{1,0:T(1,128)S(1)} %constant_dynamic-slice_fusion), channel_id=1, source_target_pairs={{0,2},{1,3},{2,0},{3,1},{4,6},{5,7},{6,4},{7,5},{8,10},{9,11},{10,... | collective-permute-start | bytes 786440 | tf_op jit(solution)/shard_map/ppermute | solution.py:21
  50.7 1.4 %collective-permute-start.4 = (bf16[2,256,512]{2,1,0:T(8,128)(2,1)}, bf16[2,256,512]{2,1,0:T(8,128)(2,1)}, u32[]{:S(2)}, u32[]{:S(2)}) collective-permute-start(bf16[2,256,512]{2,1,0:T(8,128)(2,1)} %pad_maximum_fusion.1), channel_id=1, source_target_pairs={{8,0},{12,4},{16,8},{20,12},{24,16},{28,20},{9,1},{13,5},{17,9},{2... | collective-permute-start | bytes 1572872 | tf_op jit(solution)/shard_map/ppermute | solution.py:15
  52.1 4.4 %collective-permute-done.3 = f32[1,65536]{1,0:T(1,128)} collective-permute-done((f32[1,65536]{1,0:T(1,128)S(1)}, f32[1,65536]{1,0:T(1,128)}, u32[]{:S(2)}, u32[]{:S(2)}) %collective-permute-start.3) | collective-permute-done | bytes 262176 | tf_op jit(solution)/shard_map/ppermute | solution.py:21
  56.5 2.0 %dynamic-slice_add_fusion = f32[1,65536]{1,0:T(1,128)} fusion(f32[1,65536]{1,0:T(1,128)} %collective-permute-done.3, f32[2,65536]{1,0:T(2,128)S(1)} %bitcast_add_fusion, s32[]{:T(128)S(6)} %select_n.144), kind=kLoop, calls=%fused_computation.69 | loop fusion | flops 65536 | bytes 786436 | tf_op jit(solution)/shard_map/add | solution.py:71
  58.5 14.0 %all-to-all-start = ((f32[8,1,8192]{2,1,0:T(1,128)}), f32[8,1,8192]{2,1,0:T(1,128)S(1)}, u32[]{:S(2)}, u32[]{:S(2)}) async-start(f32[8,1,8192]{2,1,0:T(1,128)} %bitcast.53), calls=%async_computation | async-start | bytes 524288 | tf_op jit(solution)/shard_map/all_to_all | solution.py:82
  72.6 1.7 %fusion.8 = bf16[4,256,256]{2,1,0:T(8,128)(2,1)S(1)} fusion(bf16[256,4,128]{0,2,1:T(8,128)(2,1)S(1)} %bitcast.232, f32[4,256,256]{2,1,0:T(8,128)} %get-tuple-element.86, pred[256,256]{1,0:T(8,128)(4,1)S(1)} %copy.148, bf16[256,512]{1,0:T(8,128)(2,1)S(1)} %copy-done.15), kind=kOutput, calls=%fused_computation.15 | convolution fusion | flops 69730304 | bytes 2162688 | tf_op jit(solution)/shard_map/ihd,jhd->hij/dot_general | solution.py:245
  74.3 0.9 fusion.15
  75.3 1.1 copy.180
  76.4 0.8 pad_maximum_fusion.2
  77.3 1.6 %collective-permute-start.5 = (bf16[2,256,512]{2,1,0:T(8,128)(2,1)}, bf16[2,256,512]{2,1,0:T(8,128)(2,1)}, u32[]{:S(2)}, u32[]{:S(2)}) collective-permute-start(bf16[2,256,512]{2,1,0:T(8,128)(2,1)} %pad_maximum_fusion.2), channel_id=1, source_target_pairs={{4,0},{8,4},{12,8},{16,12},{20,16},{24,20},{28,24},{5,1},{9,5},{13... | collective-permute-start | bytes 1572872 | tf_op jit(solution)/shard_map/ppermute | solution.py:15
  83.6 7.8 %all-to-all-start.2 = ((f32[32,1,2048]{2,1,0:T(1,128)}), f32[32,1,2048]{2,1,0:T(1,128)S(1)}, u32[]{:S(2)}, u32[]{:S(2)}) async-start(f32[32,1,2048]{2,1,0:T(1,128)} %bitcast.221), calls=%async_computation.2 | async-start | bytes 524288 | tf_op jit(solution)/shard_map/all_to_all | solution.py:82
  92.2 9.7 %all-to-all-done.2 = f32[32,1,2048]{2,1,0:T(1,128)S(1)} async-done(((f32[32,1,2048]{2,1,0:T(1,128)}), f32[32,1,2048]{2,1,0:T(1,128)S(1)}, u32[]{:S(2)}, u32[]{:S(2)}) %all-to-all-start.2) | async-done | bytes 262176 | tf_op jit(solution)/shard_map/all_to_all | solution.py:82
  102.8 3.4 %all-to-all-start.1 = ((f32[8,1,8192]{2,1,0:T(1,128)}), f32[8,1,8192]{2,1,0:T(1,128)S(1)}, u32[]{:S(2)}, u32[]{:S(2)}) async-start(f32[8,1,8192]{2,1,0:T(1,128)} %broadcast_in_dim.65), calls=%async_computation.1 | async-start | bytes 524288 | tf_op jit(solution)/shard_map/all_to_all | solution.py:85
  107.8 0.8 copy.185
  108.9 6.6 %all-to-all-done.1 = f32[8,1,8192]{2,1,0:T(1,128)S(1)} async-done(((f32[8,1,8192]{2,1,0:T(1,128)}), f32[8,1,8192]{2,1,0:T(1,128)S(1)}, u32[]{:S(2)}, u32[]{:S(2)}) %all-to-all-start.1) | async-done | bytes 262176 | tf_op jit(solution)/shard_map/all_to_all | solution.py:85
  116.3 3.0 %all-to-all-start.3 = ((f32[32,1,2048]{2,1,0:T(1,128)}), f32[32,1,2048]{2,1,0:T(1,128)S(1)}, u32[]{:S(2)}, u32[]{:S(2)}) async-start(f32[32,1,2048]{2,1,0:T(1,128)} %broadcast_in_dim.66), calls=%async_computation.3 | async-start | bytes 524288 | tf_op jit(solution)/shard_map/all_to_all | solution.py:85
  119.3 1.4 %fusion.18 = bf16[2,256,512]{2,1,0:T(8,128)(2,1)S(1)} fusion(f32[1,256,512]{2,1,0:T(8,128)S(1)} %copy-done.2, f32[1,256,512]{2,1,0:T(8,128)S(1)} %copy.176, bf16[2,256,512]{2,1,0:T(8,128)(2,1)} %collective-permute-done.4, bf16[2,256,512]{2,1,0:T(8,128)(2,1)} %collective-permute-done.5), kind=kLoop, calls=%fused_computation.40 | loop fusion | flops 1572864 | bytes 2621440 | tf_op jit(solution)/shard_map/convert.3
  122.9 6.9 %all-to-all-done.3 = f32[32,1,2048]{2,1,0:T(1,128)S(1)} async-done(((f32[32,1,2048]{2,1,0:T(1,128)}), f32[32,1,2048]{2,1,0:T(1,128)S(1)}, u32[]{:S(2)}, u32[]{:S(2)}) %all-to-all-start.3) | async-done | bytes 262176 | tf_op jit(solution)/shard_map/all_to_all | solution.py:85
  (161 shorter events, 32.9 us)
Async XLA Ops:
  0.6 33.2 %copy-start = (bf16[512,512]{1,0:T(8,128)(2,1)S(1)}, bf16[512,512]{1,0:T(8,128)(2,1)}, u32[]{:S(2)}) copy-start(bf16[512,512]{1,0:T(8,128)(2,1)} %param.19) | copy-start | bytes 1572868
  0.8 1.1 copy-start.16
  2.9 1.7 %copy-start.33 = (s32[1,6]{1,0:T(1,128)S(1)}, s32[1,6]{1,0:T(1,128)}, u32[]{:S(2)}) copy-start(s32[1,6]{1,0:T(1,128)} %param.16) | copy-start | bytes 76
  3.1 2.7 %copy-start.24 = (bf16[1,256,512]{2,1,0:T(8,128)(2,1)S(1)}, bf16[1,256,512]{2,1,0:T(8,128)(2,1)}, u32[]{:S(2)}) copy-start(bf16[1,256,512]{2,1,0:T(8,128)(2,1)} %param.10) | copy-start | bytes 786436
  6.5 14.3 %copy-start.28 = (s32[1,256]{1,0:T(1,128)}, s32[1,256]{1,0:T(1,128)S(1)}, u32[]{:S(2)}) copy-start(s32[1,256]{1,0:T(1,128)S(1)} %get-tuple-element.77) | copy-start | bytes 3076
  7.0 8.8 %copy-start.3 = (bf16[2,256,512]{1,2,0:T(8,128)(2,1)}, bf16[2,256,512]{1,2,0:T(8,128)(2,1)S(1)}, u32[]{:S(2)}) copy-start(bf16[2,256,512]{1,2,0:T(8,128)(2,1)S(1)} %pad_maximum_fusion) | copy-start | bytes 1572868
  8.9 1.1 copy-start.7
  10.0 10.5 %copy-start.1 = (bf16[1,256,512]{2,1,0:T(8,128)(2,1)S(1)}, bf16[1,256,512]{2,1,0:T(8,128)(2,1)}, u32[]{:S(2)}) copy-start(bf16[1,256,512]{2,1,0:T(8,128)(2,1)} %param.13) | copy-start | bytes 786436
  10.0 16.2 %collective-permute-start.1 = (bf16[2,256,512]{1,2,0:T(8,128)(2,1)S(1)}, bf16[2,256,512]{1,2,0:T(8,128)(2,1)}, u32[]{:S(2)}, u32[]{:S(2)}) collective-permute-start(bf16[2,256,512]{1,2,0:T(8,128)(2,1)S(1)} %pad_maximum_fusion), channel_id=1, source_target_pairs={{0,8},{4,12},{8,16},{12,20},{16,24},{20,28},{1,9},{5,13},{9,17},{1... | collective-permute-start | bytes 1572872 | tf_op jit(solution)/shard_map/ppermute | solution.py:15
  15.9 14.3 %collective-permute-start = (bf16[2,256,512]{1,2,0:T(8,128)(2,1)S(1)}, bf16[2,256,512]{1,2,0:T(8,128)(2,1)S(1)}, u32[]{:S(2)}, u32[]{:S(2)}) collective-permute-start(bf16[2,256,512]{1,2,0:T(8,128)(2,1)S(1)} %pad_maximum_fusion), channel_id=1, source_target_pairs={{0,4},{4,8},{8,12},{12,16},{16,20},{20,24},{24,28},{1,5},{5,9},{9,... | collective-permute-start | bytes 1572872 | tf_op jit(solution)/shard_map/ppermute | solution.py:15
  21.6 5.7 %copy-start.26 = (pred[256,256]{1,0:T(8,128)(4,1)S(1)}, pred[256,256]{1,0:T(8,128)(4,1)}, u32[]{:S(2)}) copy-start(pred[256,256]{1,0:T(8,128)(4,1)} %copy.154) | copy-start | bytes 196612
  30.9 1.5 %copy-start.11 = (f32[256,4,128]{2,0,1:T(8,128)S(1)}, f32[256,4,128]{2,0,1:T(8,128)}, u32[]{:S(2)}) copy-start(f32[256,4,128]{2,0,1:T(8,128)} %convolution_bitcast_fusion.2) | copy-start | bytes 1572868
  36.0 1.1 copy-start.13
  37.2 1.0 copy-start.10
  38.2 1.0 copy-start.8
  44.7 1.6 %copy-start.35 = (f32[4,256,256]{2,1,0:T(8,128)S(1)}, f32[4,256,256]{2,1,0:T(8,128)}, u32[]{:S(2)}) copy-start(f32[4,256,256]{2,1,0:T(8,128)} %get-tuple-element.84) | copy-start | bytes 3145732
  45.1 1.2 copy-start.15
  45.1 1.2 copy-start.27
  45.1 2.0 %collective-permute-start.2 = (f32[2,65536]{1,0:T(2,128)S(1)}, f32[2,65536]{1,0:T(2,128)S(1)}, u32[]{:S(2)}, u32[]{:S(2)}) collective-permute-start(f32[2,65536]{1,0:T(2,128)S(1)} %bitcast.231), channel_id=1, source_target_pairs={{0,1},{1,0},{2,3},{3,2},{4,5},{5,4},{6,7},{7,6},{8,9},{9,8},{10,11... | collective-permute-start | bytes 1572872 | tf_op jit(solution)/shard_map/ppermute | solution.py:21
  47.9 8.6 %collective-permute-start.3 = (f32[1,65536]{1,0:T(1,128)S(1)}, f32[1,65536]{1,0:T(1,128)}, u32[]{:S(2)}, u32[]{:S(2)}) collective-permute-start(f32[1,65536]{1,0:T(1,128)S(1)} %constant_dynamic-slice_fusion), channel_id=1, source_target_pairs={{0,2},{1,3},{2,0},{3,1},{4,6},{5,7},{6,4},{7,5},{8,10},{9,11},{10,... | collective-permute-start | bytes 786440 | tf_op jit(solution)/shard_map/ppermute | solution.py:21
  50.7 7.8 %copy-start.6 = (bf16[2,256,512]{1,2,0:T(8,128)(2,1)S(1)}, bf16[2,256,512]{1,2,0:T(8,128)(2,1)}, u32[]{:S(2)}) copy-start(bf16[2,256,512]{1,2,0:T(8,128)(2,1)} %copy-done.5) | copy-start | bytes 1572868
  50.7 29.0 %collective-permute-start.4 = (bf16[2,256,512]{2,1,0:T(8,128)(2,1)}, bf16[2,256,512]{2,1,0:T(8,128)(2,1)}, u32[]{:S(2)}, u32[]{:S(2)}) collective-permute-start(bf16[2,256,512]{2,1,0:T(8,128)(2,1)} %pad_maximum_fusion.1), channel_id=1, source_target_pairs={{8,0},{12,4},{16,8},{20,12},{24,16},{28,20},{9,1},{13,5},{17,9},{2... | collective-permute-start | bytes 1572872 | tf_op jit(solution)/shard_map/ppermute | solution.py:15
  58.5 25.1 %all-to-all-start = ((f32[8,1,8192]{2,1,0:T(1,128)}), f32[8,1,8192]{2,1,0:T(1,128)S(1)}, u32[]{:S(2)}, u32[]{:S(2)}) async-start(f32[8,1,8192]{2,1,0:T(1,128)} %bitcast.53), calls=%async_computation | async-start | bytes 524288 | tf_op jit(solution)/shard_map/all_to_all | solution.py:82
  75.3 1.1 copy-start.20
  77.3 2.0 %copy-start.29 = (s32[1,256]{1,0:T(1,128)S(1)}, s32[1,256]{1,0:T(1,128)}, u32[]{:S(2)}) copy-start(s32[1,256]{1,0:T(1,128)} %copy-done.28) | copy-start | bytes 3076
  77.3 42.0 %collective-permute-start.5 = (bf16[2,256,512]{2,1,0:T(8,128)(2,1)}, bf16[2,256,512]{2,1,0:T(8,128)(2,1)}, u32[]{:S(2)}, u32[]{:S(2)}) collective-permute-start(bf16[2,256,512]{2,1,0:T(8,128)(2,1)} %pad_maximum_fusion.2), channel_id=1, source_target_pairs={{4,0},{8,4},{12,8},{16,12},{20,16},{24,20},{28,24},{5,1},{9,5},{13... | collective-permute-start | bytes 1572872 | tf_op jit(solution)/shard_map/ppermute | solution.py:15
  79.3 1.0 copy-start.4
  79.3 1.8 %copy-start.34 = (f32[4,256,256]{2,1,0:T(8,128)S(1)}, f32[4,256,256]{2,1,0:T(8,128)}, u32[]{:S(2)}) copy-start(f32[4,256,256]{2,1,0:T(8,128)} %get-tuple-element.82) | copy-start | bytes 3145732
  83.6 18.4 %all-to-all-start.2 = ((f32[32,1,2048]{2,1,0:T(1,128)}), f32[32,1,2048]{2,1,0:T(1,128)S(1)}, u32[]{:S(2)}, u32[]{:S(2)}) async-start(f32[32,1,2048]{2,1,0:T(1,128)} %bitcast.221), calls=%async_computation.2 | async-start | bytes 524288 | tf_op jit(solution)/shard_map/all_to_all | solution.py:82
  102.8 12.6 %all-to-all-start.1 = ((f32[8,1,8192]{2,1,0:T(1,128)}), f32[8,1,8192]{2,1,0:T(1,128)S(1)}, u32[]{:S(2)}, u32[]{:S(2)}) async-start(f32[8,1,8192]{2,1,0:T(1,128)} %broadcast_in_dim.65), calls=%async_computation.1 | async-start | bytes 524288 | tf_op jit(solution)/shard_map/all_to_all | solution.py:85
  108.7 10.6 %copy-start.2 = (f32[1,256,512]{2,1,0:T(8,128)S(1)}, f32[1,256,512]{2,1,0:T(8,128)}, u32[]{:S(2)}) copy-start(f32[1,256,512]{2,1,0:T(8,128)} %copy.177) | copy-start | bytes 1572868
  116.3 13.6 %all-to-all-start.3 = ((f32[32,1,2048]{2,1,0:T(1,128)}), f32[32,1,2048]{2,1,0:T(1,128)S(1)}, u32[]{:S(2)}, u32[]{:S(2)}) async-start(f32[32,1,2048]{2,1,0:T(1,128)} %broadcast_in_dim.66), calls=%async_computation.3 | async-start | bytes 524288 | tf_op jit(solution)/shard_map/all_to_all | solution.py:85
  (14 other events, 11.8 us)

commit v14 on v5

--- a/solution.py
+++ b/solution.py
@@ -81,8 +81,9 @@
         size *= lax.axis_size(axis)
     pieces = lax.all_to_all(flat.reshape(size, -1), axes, 0, 0, tiled=True)
     total = jnp.sum(pieces, axis=0, keepdims=True)
-    spread = jnp.broadcast_to(total, pieces.shape)
-    return lax.all_to_all(spread, axes, 0, 0, tiled=True).reshape(flat.shape)
+    spread = jnp.broadcast_to(total.astype(jnp.bfloat16), pieces.shape)
+    gathered = lax.all_to_all(spread, axes, 0, 0, tiled=True)
+    return gathered.astype(flat.dtype).reshape(flat.shape)
 
 
 def silu_slope(scores):

time: 123 us -> 117 us (0.951)
  waiting for transfers between devices: 27.2 us -> 18.8 us
  other arithmetic: 9.68 us -> 14.5 us
  starting transfers between devices: 39.8 us -> 38.4 us
    all_to_all x2, waiting for transfers between devices: 13.5 us -> 9.17 us  [summed_by_exchange(): gathered = lax.all_to_all(spread, axes, 0, 0, tiled=True)]
    all_to_all x2, waiting for transfers between devices: 9.8 us -> 5.96 us  [summed_by_exchange(): pieces = lax.all_to_all(flat.reshape(size, -1), axes, 0, 0, tiled=True)]
    broadcast_in_dim x0 -> x2, other arithmetic: none -> 2.79 us  [summed_by_exchange(): spread = jnp.broadcast_to(total.astype(jnp.bfloat16), pieces.shape)]
    convert_element_type x0 -> x2, other arithmetic: none -> 1.69 us  [summed_by_exchange(): return gathered.astype(flat.dtype).reshape(flat.shape)]
    unnamed x80 -> x81, local copies, waits for them, and re-layouts: 9.88 us -> 10.4 us
  transfers between devices with their start and end apart: 10 -> 10, of which waited for: 6 -> 6; matrix products, arithmetic and copies ran while one was open for 26% -> 30% of each run, Pallas kernels for 0% -> 0%
where the time goes in v14:
time: 117 us; the launch traced here: 115 us
  starting transfers between devices  38.4 us (33%)
  local copies, waits for them, and re-layouts  26.1 us (22%)
  waiting for transfers between devices  18.8 us (16%)
  matrix products  16.1 us (14%)
  other arithmetic  14.5 us (12%)
  between operations  1.5 us (1%)
    all_to_all x2, starting transfers between devices, summed_by_exchange(): pieces = lax.all_to_all(flat.reshape(size, -1), axes, 0, 0, tiled=True)  18.7 us
    ppermute x4, starting transfers between devices, passed_along(): return lax.ppermute(value, axis, pairs)  12.1 us
    unnamed x81, local copies, waits for them, and re-layouts  10.4 us
    all_to_all x2, waiting for transfers between devices, summed_by_exchange(): gathered = lax.all_to_all(spread, axes, 0, 0, tiled=True)  9.17 us
    all_to_all x2, waiting for transfers between devices, summed_by_exchange(): pieces = lax.all_to_all(flat.reshape(size, -1), axes, 0, 0, tiled=True)  5.96 us
    all_to_all x2, starting transfers between devices, summed_by_exchange(): gathered = lax.all_to_all(spread, axes, 0, 0, tiled=True)  5.95 us
    ppermute x2, waiting for transfers between devices, exchanged(): return lax.ppermute(value, axis, pairs)  3.65 us
    dot_general x3, matrix products, shards(): jnp.einsum('ihd,jhd->hij', query_heads, forward_key_heads, preferred_elem...  3.37 us
  transfers between devices with their start and end apart: 10, of which 6 were waited for; matrix products, arithmetic and copies ran while one was open for 30% of the time, Pallas kernels for 0%

profile of v14, /device:TPU:0, one launch (start us, length us, event | category | flops | bytes accessed | tf_op | source)
XLA Modules:
  0.0 115.5 jit_solution(5318205266564126551)
XLA Ops:
  0.7 1.2 copy.179
  2.0 5.8 %collective-permute-start.1 = (bf16[2,256,512]{1,2,0:T(8,128)(2,1)S(1)}, bf16[2,256,512]{1,2,0:T(8,128)(2,1)}, u32[]{:S(2)}, u32[]{:S(2)}) collective-permute-start(bf16[2,256,512]{1,2,0:T(8,128)(2,1)S(1)} %pad_maximum_fusion), channel_id=1, source_target_pairs={{0,8},{4,12},{8,16},{12,20},{16,24},{20,28},{1,9},{5,13},{9,17},{1... | collective-permute-start | bytes 1572872 | tf_op jit(solution)/shard_map/ppermute | solution.py:15
  7.8 3.4 %collective-permute-start = (bf16[2,256,512]{1,2,0:T(8,128)(2,1)S(1)}, bf16[2,256,512]{1,2,0:T(8,128)(2,1)S(1)}, u32[]{:S(2)}, u32[]{:S(2)}) collective-permute-start(bf16[2,256,512]{1,2,0:T(8,128)(2,1)S(1)} %pad_maximum_fusion), channel_id=1, source_target_pairs={{0,4},{4,8},{8,12},{12,16},{16,20},{20,24},{24,28},{1,5},{5,9},{9,... | collective-permute-start | bytes 1572872 | tf_op jit(solution)/shard_map/ppermute | solution.py:15
  15.7 1.5 %select_convert_fusion.2 = (bf16[4,256,256]{2,1,0:T(8,128)(2,1)S(1)}, f32[4,256,256]{2,1,0:T(8,128)}) fusion(pred[256,256]{1,0:T(8,128)(4,1)S(1)} %copy.130, f32[4,256,256]{2,1,0:T(8,128)S(1)} %convolution_multiply_fusion.5, bf16[4,256,128]{2,1,0:T(8,128)(2,1)S(1)} %fusion.16, s32[256]{0:T(256)S(1)} %bitcast.246), kind=kOutput, calls=%fused_computation.45 | convolution fusion | flops 68976640 | bytes 2950144 | tf_op jit(solution)/shard_map/vqx,px->vqp/dot_general | solution.py:161
  18.0 1.1 convolution_bitcast_fusion.2
  21.0 1.1 fusion.66
  22.1 1.5 %select_convert_fusion = (bf16[4,256,256]{2,1,0:T(8,128)(2,1)S(1)}, f32[4,256,256]{2,1,0:T(8,128)}) fusion(pred[256,256]{1,0:T(8,128)(4,1)S(1)} %copy.143, f32[4,256,256]{2,1,0:T(8,128)S(1)} %fusion.48, bf16[256,4,128]{0,2,1:T(8,128)(2,1)S(1)} %bitcast.209, bf16[256,4,128]{0,2,1:T(8,128)(2,1)S(1)} %bitcast.237), kind=kOutput, calls=%fused_computation.41 | convolution fusion | flops 69206016 | bytes 3211264 | tf_op jit(solution)/shard_map/ihd,jhd->hij/dot_general | solution.py:176
  25.2 1.5 %select_convert_fusion.1 = (bf16[4,256,256]{2,1,0:T(8,128)(2,1)S(1)}, f32[4,256,256]{2,1,0:T(8,128)}) fusion(pred[256,256]{1,0:T(8,128)(4,1)S(1)} %copy.138, f32[4,256,256]{2,1,0:T(8,128)S(1)} %fusion.44, bf16[256,4,128]{0,2,1:T(8,128)(2,1)S(1)} %bitcast.210, bf16[256,4,128]{0,2,1:T(8,128)(2,1)S(1)} %bitcast.238), kind=kOutput, calls=%fused_computation.43 | convolution fusion | flops 69206016 | bytes 3211264 | tf_op jit(solution)/shard_map/ihd,jhd->hij/dot_general | solution.py:176
  30.3 0.9 convolution_convert_fusion
  31.3 0.9 convolution_convert_fusion.1
  32.7 1.0 copy.162
  38.8 1.1 fusion.63
  41.5 1.6 %collective-permute-start.3 = (f32[1,65536]{1,0:T(1,128)S(1)}, f32[1,65536]{1,0:T(1,128)}, u32[]{:S(2)}, u32[]{:S(2)}) collective-permute-start(f32[1,65536]{1,0:T(1,128)S(1)} %constant_dynamic-slice_fusion), channel_id=1, source_target_pairs={{0,2},{1,3},{2,0},{3,1},{4,6},{5,7},{6,4},{7,5},{8,10},{9,11},{10,... | collective-permute-start | bytes 786440 | tf_op jit(solution)/shard_map/ppermute | solution.py:21
  45.2 1.6 %collective-permute-start.4 = (bf16[2,256,512]{2,1,0:T(8,128)(2,1)}, bf16[2,256,512]{2,1,0:T(8,128)(2,1)}, u32[]{:S(2)}, u32[]{:S(2)}) collective-permute-start(bf16[2,256,512]{2,1,0:T(8,128)(2,1)} %pad_maximum_fusion.1), channel_id=1, source_target_pairs={{8,0},{12,4},{16,8},{20,12},{24,16},{28,20},{9,1},{13,5},{17,9},{2... | collective-permute-start | bytes 1572872 | tf_op jit(solution)/shard_map/ppermute | solution.py:15
  46.8 3.4 %collective-permute-done.3 = f32[1,65536]{1,0:T(1,128)} collective-permute-done((f32[1,65536]{1,0:T(1,128)S(1)}, f32[1,65536]{1,0:T(1,128)}, u32[]{:S(2)}, u32[]{:S(2)}) %collective-permute-start.3) | collective-permute-done | bytes 262176 | tf_op jit(solution)/shard_map/ppermute | solution.py:21
  50.1 2.0 %dynamic-slice_add_fusion = f32[1,65536]{1,0:T(1,128)} fusion(f32[1,65536]{1,0:T(1,128)} %collective-permute-done.3, f32[2,65536]{1,0:T(2,128)S(1)} %bitcast_add_fusion, s32[]{:T(128)S(6)} %select_n.144), kind=kLoop, calls=%fused_computation.69 | loop fusion | flops 65536 | bytes 786436 | tf_op jit(solution)/shard_map/add | solution.py:71
  53.4 0.9 fusion.15
  54.7 11.7 %all-to-all-start = ((f32[8,1,8192]{2,1,0:T(1,128)}), f32[8,1,8192]{2,1,0:T(1,128)}, u32[]{:S(2)}, u32[]{:S(2)}) async-start(f32[8,1,8192]{2,1,0:T(1,128)} %bitcast.54), calls=%async_computation | async-start | bytes 524288 | tf_op jit(solution)/shard_map/all_to_all | solution.py:82
  66.9 1.1 copy.165
  68.9 1.3 %collective-permute-start.5 = (bf16[2,256,512]{2,1,0:T(8,128)(2,1)}, bf16[2,256,512]{2,1,0:T(8,128)(2,1)}, u32[]{:S(2)}, u32[]{:S(2)}) collective-permute-start(bf16[2,256,512]{2,1,0:T(8,128)(2,1)} %pad_maximum_fusion.2), channel_id=1, source_target_pairs={{4,0},{8,4},{12,8},{16,12},{20,16},{24,20},{28,24},{5,1},{9,5},{13... | collective-permute-start | bytes 1572872 | tf_op jit(solution)/shard_map/ppermute | solution.py:15
  74.4 1.0 all-to-all-done
  75.4 7.0 %all-to-all-start.2 = ((f32[32,1,2048]{2,1,0:T(1,128)}), f32[32,1,2048]{2,1,0:T(1,128)S(1)}, u32[]{:S(2)}, u32[]{:S(2)}) async-start(f32[32,1,2048]{2,1,0:T(1,128)} %bitcast.56), calls=%async_computation.2 | async-start | bytes 524288 | tf_op jit(solution)/shard_map/all_to_all | solution.py:82
  84.0 1.2 reduce_sum.92
  85.8 1.4 %reduce.6 = bf16[8,8192]{1,0:T(8,128)(2,1)S(1)} reduce(bf16[8,1,8192]{2,1,0:T(2,128)(2,1)S(1)} %broadcast_in_dim.65, bf16[]{:T(256)} %broadcast.604), dimensions={1}, to_apply=%broadcast_in_dim.65.reduce_sub_computation | reduce | bytes 262146 | tf_op jit(solution)/shard_map/broadcast_in_dim | solution.py:84
  88.0 5.0 %all-to-all-done.2 = f32[32,1,2048]{2,1,0:T(1,128)S(1)} async-done(((f32[32,1,2048]{2,1,0:T(1,128)}), f32[32,1,2048]{2,1,0:T(1,128)S(1)}, u32[]{:S(2)}, u32[]{:S(2)}) %all-to-all-start.2) | async-done | bytes 262176 | tf_op jit(solution)/shard_map/all_to_all | solution.py:82
  93.0 3.4 %all-to-all-start.1 = ((bf16[8,2,4096]{2,1,0:T(2,128)(2,1)}), bf16[8,2,4096]{2,1,0:T(2,128)(2,1)S(1)}, u32[]{:S(2)}, u32[]{:S(2)}) async-start(bf16[8,2,4096]{2,1,0:T(2,128)(2,1)} %reshape.751), calls=%async_computation.1 | async-start | bytes 262144 | tf_op jit(solution)/shard_map/all_to_all | solution.py:85
  96.4 1.4 %fusion.18 = bf16[2,256,512]{2,1,0:T(8,128)(2,1)S(1)} fusion(f32[1,256,512]{2,1,0:T(8,128)S(1)} %copy-done.2, f32[1,256,512]{2,1,0:T(8,128)S(1)} %copy.161, bf16[2,256,512]{2,1,0:T(8,128)(2,1)} %collective-permute-done.4, bf16[2,256,512]{2,1,0:T(8,128)(2,1)} %collective-permute-done.5), kind=kLoop, calls=%fused_computation.40 | loop fusion | flops 1572864 | bytes 2621440 | tf_op jit(solution)/shard_map/convert.5
  98.1 1.4 %reduce.7 = bf16[32,2048]{1,0:T(8,128)(2,1)S(1)} reduce(bf16[32,1,2048]{2,1,0:T(2,128)(2,1)S(1)} %broadcast_in_dim.66, bf16[]{:T(256)} %broadcast.604), dimensions={1}, to_apply=%broadcast_in_dim.66.reduce_sub_computation | reduce | bytes 262146 | tf_op jit(solution)/shard_map/broadcast_in_dim | solution.py:84
  100.2 3.4 %all-to-all-done.1 = bf16[8,2,4096]{2,1,0:T(2,128)(2,1)S(1)} async-done(((bf16[8,2,4096]{2,1,0:T(2,128)(2,1)}), bf16[8,2,4096]{2,1,0:T(2,128)(2,1)S(1)}, u32[]{:S(2)}, u32[]{:S(2)}) %all-to-all-start.1) | async-done | bytes 131104 | tf_op jit(solution)/shard_map/all_to_all | solution.py:85
  103.6 2.6 %all-to-all-start.3 = ((bf16[32,2,1024]{2,1,0:T(2,128)(2,1)}), bf16[32,2,1024]{2,1,0:T(2,128)(2,1)S(1)}, u32[]{:S(2)}, u32[]{:S(2)}) async-start(bf16[32,2,1024]{2,1,0:T(2,128)(2,1)} %reshape.753), calls=%async_computation.3 | async-start | bytes 262144 | tf_op jit(solution)/shard_map/all_to_all | solution.py:85
  108.7 5.8 %all-to-all-done.3 = bf16[32,2,1024]{2,1,0:T(2,128)(2,1)S(1)} async-done(((bf16[32,2,1024]{2,1,0:T(2,128)(2,1)}), bf16[32,2,1024]{2,1,0:T(2,128)(2,1)S(1)}, u32[]{:S(2)}, u32[]{:S(2)}) %all-to-all-start.3) | async-done | bytes 131104 | tf_op jit(solution)/shard_map/all_to_all | solution.py:85
  114.5 1.0 convert_element_type.147
  (162 shorter events, 35.0 us)
Async XLA Ops:
  0.6 26.8 %copy-start = (bf16[512,512]{1,0:T(8,128)(2,1)S(1)}, bf16[512,512]{1,0:T(8,128)(2,1)}, u32[]{:S(2)}) copy-start(bf16[512,512]{1,0:T(8,128)(2,1)} %param.19) | copy-start | bytes 1572868
  0.6 1.2 %copy-start.14 = (bf16[1,256,512]{2,1,0:T(8,128)(2,1)S(1)}, bf16[1,256,512]{2,1,0:T(8,128)(2,1)}, u32[]{:S(2)}) copy-start(bf16[1,256,512]{2,1,0:T(8,128)(2,1)} %param.11) | copy-start | bytes 786436
  2.0 12.1 %copy-start.3 = (bf16[2,256,512]{1,2,0:T(8,128)(2,1)}, bf16[2,256,512]{1,2,0:T(8,128)(2,1)S(1)}, u32[]{:S(2)}) copy-start(bf16[2,256,512]{1,2,0:T(8,128)(2,1)S(1)} %pad_maximum_fusion) | copy-start | bytes 1572868
  2.0 19.0 %collective-permute-start.1 = (bf16[2,256,512]{1,2,0:T(8,128)(2,1)S(1)}, bf16[2,256,512]{1,2,0:T(8,128)(2,1)}, u32[]{:S(2)}, u32[]{:S(2)}) collective-permute-start(bf16[2,256,512]{1,2,0:T(8,128)(2,1)S(1)} %pad_maximum_fusion), channel_id=1, source_target_pairs={{0,8},{4,12},{8,16},{12,20},{16,24},{20,28},{1,9},{5,13},{9,17},{1... | collective-permute-start | bytes 1572872 | tf_op jit(solution)/shard_map/ppermute | solution.py:15
  7.8 16.6 %collective-permute-start = (bf16[2,256,512]{1,2,0:T(8,128)(2,1)S(1)}, bf16[2,256,512]{1,2,0:T(8,128)(2,1)S(1)}, u32[]{:S(2)}, u32[]{:S(2)}) collective-permute-start(bf16[2,256,512]{1,2,0:T(8,128)(2,1)S(1)} %pad_maximum_fusion), channel_id=1, source_target_pairs={{0,4},{4,8},{8,12},{12,16},{16,20},{20,24},{24,28},{1,5},{5,9},{9,... | collective-permute-start | bytes 1572872 | tf_op jit(solution)/shard_map/ppermute | solution.py:15
  11.4 1.6 %copy-start.31 = (s32[1,6]{1,0:T(1,128)S(1)}, s32[1,6]{1,0:T(1,128)}, u32[]{:S(2)}) copy-start(s32[1,6]{1,0:T(1,128)} %param.16) | copy-start | bytes 76
  11.5 2.7 %copy-start.22 = (bf16[1,256,512]{2,1,0:T(8,128)(2,1)S(1)}, bf16[1,256,512]{2,1,0:T(8,128)(2,1)}, u32[]{:S(2)}) copy-start(bf16[1,256,512]{2,1,0:T(8,128)(2,1)} %param.10) | copy-start | bytes 786436
  14.9 5.3 %copy-start.26 = (s32[1,256]{1,0:T(1,128)}, s32[1,256]{1,0:T(1,128)S(1)}, u32[]{:S(2)}) copy-start(s32[1,256]{1,0:T(1,128)S(1)} %get-tuple-element.73) | copy-start | bytes 3076
  20.1 2.0 %copy-start.24 = (pred[256,256]{1,0:T(8,128)(4,1)}, pred[256,256]{1,0:T(8,128)(4,1)S(1)}, u32[]{:S(2)}) copy-start(pred[256,256]{1,0:T(8,128)(4,1)S(1)} %copy.143) | copy-start | bytes 196612
  25.2 1.5 %copy-start.11 = (f32[256,4,128]{0,2,1:T(8,128)S(1)}, f32[256,4,128]{0,2,1:T(8,128)}, u32[]{:S(2)}) copy-start(f32[256,4,128]{0,2,1:T(8,128)} %convolution_bitcast_fusion.2) | copy-start | bytes 1572868
  30.2 1.0 copy-start.10
  31.3 1.0 copy-start.8
  32.7 1.0 copy-start.19
  38.3 1.6 %copy-start.34 = (f32[4,256,256]{2,1,0:T(8,128)S(1)}, f32[4,256,256]{2,1,0:T(8,128)}, u32[]{:S(2)}) copy-start(f32[4,256,256]{2,1,0:T(8,128)} %get-tuple-element.78) | copy-start | bytes 3145732
  38.7 1.2 %copy-start.13 = (bf16[256,512]{1,0:T(8,128)(2,1)S(1)}, bf16[256,512]{1,0:T(8,128)(2,1)}, u32[]{:S(2)}) copy-start(bf16[256,512]{1,0:T(8,128)(2,1)} %copy-done.12) | copy-start | bytes 786436
  38.7 1.2 %copy-start.25 = (pred[256,256]{1,0:T(8,128)(4,1)S(1)}, pred[256,256]{1,0:T(8,128)(4,1)}, u32[]{:S(2)}) copy-start(pred[256,256]{1,0:T(8,128)(4,1)} %copy-done.24) | copy-start | bytes 196612
  38.8 2.0 %collective-permute-start.2 = (f32[2,65536]{1,0:T(2,128)S(1)}, f32[2,65536]{1,0:T(2,128)S(1)}, u32[]{:S(2)}, u32[]{:S(2)}) collective-permute-start(f32[2,65536]{1,0:T(2,128)S(1)} %bitcast.232), channel_id=1, source_target_pairs={{0,1},{1,0},{2,3},{3,2},{4,5},{5,4},{6,7},{7,6},{8,9},{9,8},{10,11... | collective-permute-start | bytes 1572872 | tf_op jit(solution)/shard_map/ppermute | solution.py:21
  41.5 8.6 %collective-permute-start.3 = (f32[1,65536]{1,0:T(1,128)S(1)}, f32[1,65536]{1,0:T(1,128)}, u32[]{:S(2)}, u32[]{:S(2)}) collective-permute-start(f32[1,65536]{1,0:T(1,128)S(1)} %constant_dynamic-slice_fusion), channel_id=1, source_target_pairs={{0,2},{1,3},{2,0},{3,1},{4,6},{5,7},{6,4},{7,5},{8,10},{9,11},{10,... | collective-permute-start | bytes 786440 | tf_op jit(solution)/shard_map/ppermute | solution.py:21
  45.2 7.0 %copy-start.6 = (bf16[2,256,512]{1,2,0:T(8,128)(2,1)S(1)}, bf16[2,256,512]{1,2,0:T(8,128)(2,1)}, u32[]{:S(2)}) copy-start(bf16[2,256,512]{1,2,0:T(8,128)(2,1)} %copy-done.5) | copy-start | bytes 1572868
  45.2 7.7 %copy-start.33 = (f32[4,256,256]{2,1,0:T(8,128)S(1)}, f32[4,256,256]{2,1,0:T(8,128)}, u32[]{:S(2)}) copy-start(f32[4,256,256]{2,1,0:T(8,128)} %get-tuple-element.82) | copy-start | bytes 3145732
  45.2 25.7 %collective-permute-start.4 = (bf16[2,256,512]{2,1,0:T(8,128)(2,1)}, bf16[2,256,512]{2,1,0:T(8,128)(2,1)}, u32[]{:S(2)}, u32[]{:S(2)}) collective-permute-start(bf16[2,256,512]{2,1,0:T(8,128)(2,1)} %pad_maximum_fusion.1), channel_id=1, source_target_pairs={{8,0},{12,4},{16,8},{20,12},{24,16},{28,20},{9,1},{13,5},{17,9},{2... | collective-permute-start | bytes 1572872 | tf_op jit(solution)/shard_map/ppermute | solution.py:15
  54.7 11.7 %copy-start.27 = (s32[1,256]{1,0:T(1,128)S(1)}, s32[1,256]{1,0:T(1,128)}, u32[]{:S(2)}) copy-start(s32[1,256]{1,0:T(1,128)} %copy-done.26) | copy-start | bytes 3076
  54.7 20.6 %all-to-all-start = ((f32[8,1,8192]{2,1,0:T(1,128)}), f32[8,1,8192]{2,1,0:T(1,128)}, u32[]{:S(2)}, u32[]{:S(2)}) async-start(f32[8,1,8192]{2,1,0:T(1,128)} %bitcast.54), calls=%async_computation | async-start | bytes 524288 | tf_op jit(solution)/shard_map/all_to_all | solution.py:82
  66.8 1.2 copy-start.16
  68.0 2.2 %copy-start.15 = (bf16[1,256,512]{1,2,0:T(8,128)(2,1)S(1)}, bf16[1,256,512]{1,2,0:T(8,128)(2,1)}, u32[]{:S(2)}) copy-start(bf16[1,256,512]{1,2,0:T(8,128)(2,1)} %get-tuple-element.62) | copy-start | bytes 786436
  68.9 27.5 %collective-permute-start.5 = (bf16[2,256,512]{2,1,0:T(8,128)(2,1)}, bf16[2,256,512]{2,1,0:T(8,128)(2,1)}, u32[]{:S(2)}, u32[]{:S(2)}) collective-permute-start(bf16[2,256,512]{2,1,0:T(8,128)(2,1)} %pad_maximum_fusion.2), channel_id=1, source_target_pairs={{4,0},{8,4},{12,8},{16,12},{20,16},{24,20},{28,24},{5,1},{9,5},{13... | collective-permute-start | bytes 1572872 | tf_op jit(solution)/shard_map/ppermute | solution.py:15
  70.5 1.0 copy-start.4
  70.5 1.4 %copy-start.32 = (f32[4,256,256]{2,1,0:T(8,128)S(1)}, f32[4,256,256]{2,1,0:T(8,128)}, u32[]{:S(2)}) copy-start(f32[4,256,256]{2,1,0:T(8,128)} %get-tuple-element.80) | copy-start | bytes 3145732
  75.4 17.6 %all-to-all-start.2 = ((f32[32,1,2048]{2,1,0:T(1,128)}), f32[32,1,2048]{2,1,0:T(1,128)S(1)}, u32[]{:S(2)}, u32[]{:S(2)}) async-start(f32[32,1,2048]{2,1,0:T(1,128)} %bitcast.56), calls=%async_computation.2 | async-start | bytes 524288 | tf_op jit(solution)/shard_map/all_to_all | solution.py:82
  85.3 11.1 %copy-start.2 = (f32[1,256,512]{2,1,0:T(8,128)S(1)}, f32[1,256,512]{2,1,0:T(8,128)}, u32[]{:S(2)}) copy-start(f32[1,256,512]{2,1,0:T(8,128)} %copy.162) | copy-start | bytes 1572868
  93.0 10.7 %all-to-all-start.1 = ((bf16[8,2,4096]{2,1,0:T(2,128)(2,1)}), bf16[8,2,4096]{2,1,0:T(2,128)(2,1)S(1)}, u32[]{:S(2)}, u32[]{:S(2)}) async-start(bf16[8,2,4096]{2,1,0:T(2,128)(2,1)} %reshape.751), calls=%async_computation.1 | async-start | bytes 262144 | tf_op jit(solution)/shard_map/all_to_all | solution.py:85
  103.6 10.8 %all-to-all-start.3 = ((bf16[32,2,1024]{2,1,0:T(2,128)(2,1)}), bf16[32,2,1024]{2,1,0:T(2,128)(2,1)S(1)}, u32[]{:S(2)}, u32[]{:S(2)}) async-start(bf16[32,2,1024]{2,1,0:T(2,128)(2,1)} %reshape.753), calls=%async_computation.3 | async-start | bytes 262144 | tf_op jit(solution)/shard_map/all_to_all | solution.py:85
  (13 other events, 10.9 us)

commit v15 on v14

--- a/solution.py
+++ b/solution.py
@@ -228,6 +228,7 @@
             weight_state[1] = done + 1
         return anchor
 
+    grad_heads = slot(grad_heads)
     query_sum = jnp.zeros((local_rows, width), jnp.float32)
     share_sum = None
     key_terms = [None, None, None]

time: 117 us -> 137 us (1.17)
  waiting for transfers between devices: 18.8 us -> 31.8 us
  matrix products: 16.1 us -> 19 us
  local copies, waits for them, and re-layouts: 26.1 us -> 28.7 us
  other arithmetic: 14.5 us -> 16.3 us
    all_to_all x2, waiting for transfers between devices: 5.96 us -> 12.1 us  [summed_by_exchange(): pieces = lax.all_to_all(flat.reshape(size, -1), axes, 0, 0, tiled=True)]
    ppermute x4, waiting for transfers between devices: 0.01 us -> 6.02 us  [passed_along(): return lax.ppermute(value, axis, pairs)]
    ppermute x2, waiting for transfers between devices: 3.65 us -> 6.3 us  [exchanged(): return lax.ppermute(value, axis, pairs)]
    unnamed x81 -> x91, local copies, waits for them, and re-layouts: 10.4 us -> 12.9 us
    all_to_all x2, waiting for transfers between devices: 9.17 us -> 7.39 us  [summed_by_exchange(): gathered = lax.all_to_all(spread, axes, 0, 0, tiled=True)]
  transfers between devices with their start and end apart: 10 -> 10, of which waited for: 6 -> 6; matrix products, arithmetic and copies ran while one was open for 30% -> 28% of each run, Pallas kernels for 0% -> 0%
where the time goes in v15:
time: 137 us; the launch traced here: 135 us
  starting transfers between devices  38.3 us (28%)
  waiting for transfers between devices  31.8 us (23%)
  local copies, waits for them, and re-layouts  28.7 us (21%)
  matrix products  19 us (14%)
  other arithmetic  16.3 us (12%)
  between operations  1.37 us (1%)
    all_to_all x2, starting transfers between devices, summed_by_exchange(): pieces = lax.all_to_all(flat.reshape(size, -1), axes, 0, 0, tiled=True)  18.6 us
    unnamed x91, local copies, waits for them, and re-layouts  12.9 us
    ppermute x4, starting transfers between devices, passed_along(): return lax.ppermute(value, axis, pairs)  12.2 us
    all_to_all x2, waiting for transfers between devices, summed_by_exchange(): pieces = lax.all_to_all(flat.reshape(size, -1), axes, 0, 0, tiled=True)  12.1 us
    all_to_all x2, waiting for transfers between devices, summed_by_exchange(): gathered = lax.all_to_all(spread, axes, 0, 0, tiled=True)  7.39 us
    ppermute x2, waiting for transfers between devices, exchanged(): return lax.ppermute(value, axis, pairs)  6.3 us
    ppermute x4, waiting for transfers between devices, passed_along(): return lax.ppermute(value, axis, pairs)  6.02 us
    all_to_all x2, starting transfers between devices, summed_by_exchange(): gathered = lax.all_to_all(spread, axes, 0, 0, tiled=True)  5.95 us
  transfers between devices with their start and end apart: 10, of which 6 were waited for; matrix products, arithmetic and copies ran while one was open for 28% of the time, Pallas kernels for 0%

profile of v15, /device:TPU:0, one launch (start us, length us, event | category | flops | bytes accessed | tf_op | source)
XLA Modules:
  0.0 135.4 jit_solution(9548736280211642604)
XLA Ops:
  0.7 1.2 copy.180
  2.0 5.0 %collective-permute-start.1 = (bf16[2,256,512]{1,2,0:T(8,128)(2,1)S(1)}, bf16[2,256,512]{1,2,0:T(8,128)(2,1)S(1)}, u32[]{:S(2)}, u32[]{:S(2)}) collective-permute-start(bf16[2,256,512]{1,2,0:T(8,128)(2,1)S(1)} %pad_maximum_fusion), channel_id=1, source_target_pairs={{0,8},{4,12},{8,16},{12,20},{16,24},{20,28},{1,9},{5,13},{9,17},{1... | collective-permute-start | bytes 1572872 | tf_op jit(solution)/shard_map/ppermute | solution.py:15
  7.0 4.2 %collective-permute-start = (bf16[2,256,512]{1,2,0:T(8,128)(2,1)S(1)}, bf16[2,256,512]{1,2,0:T(8,128)(2,1)}, u32[]{:S(2)}, u32[]{:S(2)}) collective-permute-start(bf16[2,256,512]{1,2,0:T(8,128)(2,1)S(1)} %pad_maximum_fusion), channel_id=1, source_target_pairs={{0,4},{4,8},{8,12},{12,16},{16,20},{20,24},{24,28},{1,5},{5,9},{9,... | collective-permute-start | bytes 1572872 | tf_op jit(solution)/shard_map/ppermute | solution.py:15
  15.6 1.5 %select_convert_fusion.2 = (bf16[4,256,256]{2,1,0:T(8,128)(2,1)S(1)}, f32[4,256,256]{2,1,0:T(8,128)}) fusion(pred[256,256]{1,0:T(8,128)(4,1)S(1)} %copy.131, f32[4,256,256]{2,1,0:T(8,128)S(1)} %convolution_multiply_fusion.5, bf16[4,256,128]{2,1,0:T(8,128)(2,1)S(1)} %fusion.16, s32[256]{0:T(256)S(1)} %bitcast.223), kind=kOutput, calls=%fused_computation.45 | convolution fusion | flops 68976640 | bytes 2950144 | tf_op jit(solution)/shard_map/vqx,px->vqp/dot_general | solution.py:161
  17.9 1.1 convolution_bitcast_fusion.2
  21.7 1.5 %select_convert_fusion = (bf16[4,256,256]{2,1,0:T(8,128)(2,1)S(1)}, f32[4,256,256]{2,1,0:T(8,128)}) fusion(pred[256,256]{1,0:T(8,128)(4,1)S(1)} %copy.144, f32[4,256,256]{2,1,0:T(8,128)S(1)} %fusion.45, bf16[256,4,128]{0,2,1:T(8,128)(2,1)S(1)} %bitcast.189, bf16[256,4,128]{0,2,1:T(8,128)(2,1)S(1)} %bitcast.215), kind=kOutput, calls=%fused_computation.41 | convolution fusion | flops 69206016 | bytes 3211264 | tf_op jit(solution)/shard_map/ihd,jhd->hij/dot_general | solution.py:176
  25.1 1.5 %select_convert_fusion.1 = (bf16[4,256,256]{2,1,0:T(8,128)(2,1)S(1)}, f32[4,256,256]{2,1,0:T(8,128)}) fusion(pred[256,256]{1,0:T(8,128)(4,1)S(1)} %copy.139, f32[4,256,256]{2,1,0:T(8,128)S(1)} %fusion.41, bf16[256,4,128]{0,2,1:T(8,128)(2,1)S(1)} %bitcast.190, bf16[256,4,128]{0,2,1:T(8,128)(2,1)S(1)} %bitcast.198), kind=kOutput, calls=%fused_computation.43 | convolution fusion | flops 69206016 | bytes 3211264 | tf_op jit(solution)/shard_map/ihd,jhd->hij/dot_general | solution.py:176
  37.9 1.1 copy.167
  39.4 1.7 %constant_dynamic-slice_fusion.2 = (f32[2,1,65536]{2,1,0:T(1,128)}, f32[2,1,65536]{2,1,0:T(1,128)S(1)}) fusion(f32[2,2,65536]{2,1,0:T(2,128)S(1)} %reshape.741, s32[]{:T(128)S(6)} %select_n.139, s32[]{:T(128)S(6)} %select_n.140), kind=kLoop, calls=%fused_computation.104 | loop fusion | bytes 2097160 | tf_op jit(solution)/shard_map/jit(dynamic_index_in_dim)/dynamic_slice | solution.py:69
  41.1 1.2 copy.200
  45.4 1.6 %collective-permute-start.5 = (bf16[2,256,512]{2,1,0:T(8,128)(2,1)}, bf16[2,256,512]{2,1,0:T(8,128)(2,1)}, u32[]{:S(2)}, u32[]{:S(2)}) collective-permute-start(bf16[2,256,512]{2,1,0:T(8,128)(2,1)} %pad_maximum_fusion.2), channel_id=1, source_target_pairs={{4,0},{8,4},{12,8},{16,12},{20,16},{24,20},{28,24},{5,1},{9,5},{13... | collective-permute-start | bytes 1572872 | tf_op jit(solution)/shard_map/ppermute | solution.py:15
  48.4 1.6 %bitcast_add_fusion = f32[2,65536]{1,0:T(2,128)S(1)} fusion(f32[2,65536]{1,0:T(2,128)} %collective-permute-done.2, f32[2,1,65536]{2,1,0:T(1,128)S(1)} %copy-done.10), kind=kLoop, calls=%fused_computation.51 | loop fusion | flops 131072 | bytes 1572864 | tf_op jit(solution)/shard_map/add | solution.py:71
  51.0 1.6 %collective-permute-start.3 = (f32[1,65536]{1,0:T(1,128)S(1)}, f32[1,65536]{1,0:T(1,128)S(1)}, u32[]{:S(2)}, u32[]{:S(2)}) collective-permute-start(f32[1,65536]{1,0:T(1,128)S(1)} %constant_dynamic-slice_fusion), channel_id=1, source_target_pairs={{0,2},{1,3},{2,0},{3,1},{4,6},{5,7},{6,4},{7,5},{8,10},{9,11},{10,... | collective-permute-start | bytes 786440 | tf_op jit(solution)/shard_map/ppermute | solution.py:21
  53.1 6.3 %collective-permute-done.3 = f32[1,65536]{1,0:T(1,128)S(1)} collective-permute-done((f32[1,65536]{1,0:T(1,128)S(1)}, f32[1,65536]{1,0:T(1,128)S(1)}, u32[]{:S(2)}, u32[]{:S(2)}) %collective-permute-start.3) | collective-permute-done | bytes 262176 | tf_op jit(solution)/shard_map/ppermute | solution.py:21
  60.5 14.6 %all-to-all-start = ((f32[8,1,8192]{2,1,0:T(1,128)}), f32[8,1,8192]{2,1,0:T(1,128)}, u32[]{:S(2)}, u32[]{:S(2)}) async-start(f32[8,1,8192]{2,1,0:T(1,128)} %bitcast.207), calls=%async_computation | async-start | bytes 524288 | tf_op jit(solution)/shard_map/all_to_all | solution.py:82
  76.0 1.1 copy.156
  78.0 1.4 %collective-permute-start.4 = (bf16[2,256,512]{2,1,0:T(8,128)(2,1)}, bf16[2,256,512]{2,1,0:T(8,128)(2,1)}, u32[]{:S(2)}, u32[]{:S(2)}) collective-permute-start(bf16[2,256,512]{2,1,0:T(8,128)(2,1)} %pad_maximum_fusion.1), channel_id=1, source_target_pairs={{8,0},{12,4},{16,8},{20,12},{24,16},{28,20},{9,1},{13,5},{17,9},{2... | collective-permute-start | bytes 1572872 | tf_op jit(solution)/shard_map/ppermute | solution.py:15
  79.4 1.2 convolution_add_fusion.2
  80.9 3.0 %all-to-all-done = f32[8,1,8192]{2,1,0:T(1,128)} async-done(((f32[8,1,8192]{2,1,0:T(1,128)}), f32[8,1,8192]{2,1,0:T(1,128)}, u32[]{:S(2)}, u32[]{:S(2)}) %all-to-all-start) | async-done | bytes 262176 | tf_op jit(solution)/shard_map/all_to_all | solution.py:82
  84.0 1.2 reduce_sum.92
  85.8 1.4 %reduce.6 = bf16[8,8192]{1,0:T(8,128)(2,1)S(1)} reduce(bf16[8,1,8192]{2,1,0:T(2,128)(2,1)S(1)} %broadcast_in_dim.65, bf16[]{:T(256)} %broadcast.604), dimensions={1}, to_apply=%broadcast_in_dim.65.reduce_sub_computation | reduce | bytes 262146 | tf_op jit(solution)/shard_map/broadcast_in_dim | solution.py:84
  87.9 6.0 %collective-permute-done.4 = bf16[2,256,512]{2,1,0:T(8,128)(2,1)} collective-permute-done((bf16[2,256,512]{2,1,0:T(8,128)(2,1)}, bf16[2,256,512]{2,1,0:T(8,128)(2,1)}, u32[]{:S(2)}, u32[]{:S(2)}) %collective-permute-start.4) | collective-permute-done | bytes 524320 | tf_op jit(solution)/shard_map/ppermute | solution.py:15
  94.7 1.8 %fusion.9 = bf16[4,256,256]{2,1,0:T(8,128)(2,1)S(1)} fusion(bf16[256,4,128]{0,2,1:T(8,128)(2,1)S(1)} %bitcast.214, f32[4,256,256]{2,1,0:T(8,128)} %get-tuple-element.78, pred[256,256]{1,0:T(8,128)(4,1)S(1)} %copy.131, bf16[256,4,128]{2,1,0:T(4,128)(2,1)S(1)} %copy-done.20), kind=kOutput, calls=%fused_computation.16 | convolution fusion | flops 69730304 | bytes 2162688 | tf_op jit(solution)/shard_map/ihd,jhd->hij/dot_general | solution.py:243
  98.4 4.0 %all-to-all-start.2 = ((f32[32,1,2048]{2,1,0:T(1,128)}), f32[32,1,2048]{2,1,0:T(1,128)}, u32[]{:S(2)}, u32[]{:S(2)}) async-start(f32[32,1,2048]{2,1,0:T(1,128)} %bitcast.54), calls=%async_computation.2 | async-start | bytes 524288 | tf_op jit(solution)/shard_map/all_to_all | solution.py:82
  103.8 9.0 %all-to-all-done.2 = f32[32,1,2048]{2,1,0:T(1,128)} async-done(((f32[32,1,2048]{2,1,0:T(1,128)}), f32[32,1,2048]{2,1,0:T(1,128)}, u32[]{:S(2)}, u32[]{:S(2)}) %all-to-all-start.2) | async-done | bytes 262176 | tf_op jit(solution)/shard_map/all_to_all | solution.py:82
  112.9 3.4 %all-to-all-start.1 = ((bf16[8,2,4096]{2,1,0:T(2,128)(2,1)}), bf16[8,2,4096]{2,1,0:T(2,128)(2,1)S(1)}, u32[]{:S(2)}, u32[]{:S(2)}) async-start(bf16[8,2,4096]{2,1,0:T(2,128)(2,1)} %reshape.751), calls=%async_computation.1 | async-start | bytes 262144 | tf_op jit(solution)/shard_map/all_to_all | solution.py:85
  116.3 1.4 %fusion.18 = bf16[2,256,512]{2,1,0:T(8,128)(2,1)S(1)} fusion(f32[1,256,512]{2,1,0:T(8,128)S(1)} %copy.163, f32[1,256,512]{2,1,0:T(8,128)S(1)} %copy.162, bf16[2,256,512]{2,1,0:T(8,128)(2,1)} %collective-permute-done.4, bf16[2,256,512]{2,1,0:T(8,128)(2,1)} %collective-permute-done.5), kind=kLoop, calls=%fused_computation.40 | loop fusion | flops 1572864 | bytes 2621440 | tf_op jit(solution)/shard_map/convert.5
  117.7 1.1 reduce_sum.93
  119.0 1.4 %reduce.7 = bf16[32,2048]{1,0:T(8,128)(2,1)S(1)} reduce(bf16[32,1,2048]{2,1,0:T(2,128)(2,1)S(1)} %broadcast_in_dim.66, bf16[]{:T(256)} %broadcast.604), dimensions={1}, to_apply=%broadcast_in_dim.66.reduce_sub_computation | reduce | bytes 262146 | tf_op jit(solution)/shard_map/broadcast_in_dim | solution.py:84
  121.1 2.5 %all-to-all-done.1 = bf16[8,2,4096]{2,1,0:T(2,128)(2,1)S(1)} async-done(((bf16[8,2,4096]{2,1,0:T(2,128)(2,1)}), bf16[8,2,4096]{2,1,0:T(2,128)(2,1)S(1)}, u32[]{:S(2)}, u32[]{:S(2)}) %all-to-all-start.1) | async-done | bytes 131104 | tf_op jit(solution)/shard_map/all_to_all | solution.py:85
  123.6 2.6 %all-to-all-start.3 = ((bf16[32,2,1024]{2,1,0:T(2,128)(2,1)}), bf16[32,2,1024]{2,1,0:T(2,128)(2,1)S(1)}, u32[]{:S(2)}, u32[]{:S(2)}) async-start(bf16[32,2,1024]{2,1,0:T(2,128)(2,1)} %reshape.753), calls=%async_computation.3 | async-start | bytes 262144 | tf_op jit(solution)/shard_map/all_to_all | solution.py:85
  129.4 4.9 %all-to-all-done.3 = bf16[32,2,1024]{2,1,0:T(2,128)(2,1)S(1)} async-done(((bf16[32,2,1024]{2,1,0:T(2,128)(2,1)}), bf16[32,2,1024]{2,1,0:T(2,128)(2,1)S(1)}, u32[]{:S(2)}, u32[]{:S(2)}) %all-to-all-start.3) | async-done | bytes 131104 | tf_op jit(solution)/shard_map/all_to_all | solution.py:85
  (172 shorter events, 41.0 us)
Async XLA Ops:
  0.6 28.0 %copy-start = (bf16[512,512]{1,0:T(8,128)(2,1)S(1)}, bf16[512,512]{1,0:T(8,128)(2,1)}, u32[]{:S(2)}) copy-start(bf16[512,512]{1,0:T(8,128)(2,1)} %param.19) | copy-start | bytes 1572868
  0.6 1.2 copy-start.16
  2.0 12.0 %copy-start.2 = (bf16[2,256,512]{1,2,0:T(8,128)(2,1)}, bf16[2,256,512]{1,2,0:T(8,128)(2,1)S(1)}, u32[]{:S(2)}) copy-start(bf16[2,256,512]{1,2,0:T(8,128)(2,1)S(1)} %pad_maximum_fusion) | copy-start | bytes 1572868
  2.0 18.9 %collective-permute-start.1 = (bf16[2,256,512]{1,2,0:T(8,128)(2,1)S(1)}, bf16[2,256,512]{1,2,0:T(8,128)(2,1)S(1)}, u32[]{:S(2)}, u32[]{:S(2)}) collective-permute-start(bf16[2,256,512]{1,2,0:T(8,128)(2,1)S(1)} %pad_maximum_fusion), channel_id=1, source_target_pairs={{0,8},{4,12},{8,16},{12,20},{16,24},{20,28},{1,9},{5,13},{9,17},{1... | collective-permute-start | bytes 1572872 | tf_op jit(solution)/shard_map/ppermute | solution.py:15
  7.0 17.0 %collective-permute-start = (bf16[2,256,512]{1,2,0:T(8,128)(2,1)S(1)}, bf16[2,256,512]{1,2,0:T(8,128)(2,1)}, u32[]{:S(2)}, u32[]{:S(2)}) collective-permute-start(bf16[2,256,512]{1,2,0:T(8,128)(2,1)S(1)} %pad_maximum_fusion), channel_id=1, source_target_pairs={{0,4},{4,8},{8,12},{12,16},{16,20},{20,24},{24,28},{1,5},{5,9},{9,... | collective-permute-start | bytes 1572872 | tf_op jit(solution)/shard_map/ppermute | solution.py:15
  11.3 1.6 %copy-start.37 = (s32[1,6]{1,0:T(1,128)S(1)}, s32[1,6]{1,0:T(1,128)}, u32[]{:S(2)}) copy-start(s32[1,6]{1,0:T(1,128)} %param.16) | copy-start | bytes 76
  11.4 2.7 %copy-start.32 = (bf16[1,256,512]{2,1,0:T(8,128)(2,1)S(1)}, bf16[1,256,512]{2,1,0:T(8,128)(2,1)}, u32[]{:S(2)}) copy-start(bf16[1,256,512]{2,1,0:T(8,128)(2,1)} %param.10) | copy-start | bytes 786436
  20.0 5.1 %copy-start.34 = (pred[256,256]{1,0:T(8,128)(4,1)}, pred[256,256]{1,0:T(8,128)(4,1)S(1)}, u32[]{:S(2)}) copy-start(pred[256,256]{1,0:T(8,128)(4,1)S(1)} %copy.139) | copy-start | bytes 196612
  25.1 1.6 %copy-start.21 = (bf16[1,256,512]{1,2,0:T(8,128)(2,1)}, bf16[1,256,512]{1,2,0:T(8,128)(2,1)S(1)}, u32[]{:S(2)}) copy-start(bf16[1,256,512]{1,2,0:T(8,128)(2,1)S(1)} %get-tuple-element.64) | copy-start | bytes 786436
  25.1 1.6 %copy-start.23 = (bf16[1,256,512]{1,2,0:T(8,128)(2,1)}, bf16[1,256,512]{1,2,0:T(8,128)(2,1)S(1)}, u32[]{:S(2)}) copy-start(bf16[1,256,512]{1,2,0:T(8,128)(2,1)S(1)} %get-tuple-element.63) | copy-start | bytes 786436
  25.1 1.5 %copy-start.12 = (f32[256,4,128]{0,2,1:T(8,128)S(1)}, f32[256,4,128]{0,2,1:T(8,128)}, u32[]{:S(2)}) copy-start(f32[256,4,128]{0,2,1:T(8,128)} %convolution_bitcast_fusion.2) | copy-start | bytes 1572868
  30.2 1.1 copy-start.31
  30.2 2.1 %copy-start.17 = (bf16[256,4,128]{2,1,0:T(4,128)(2,1)}, bf16[256,4,128]{2,1,0:T(4,128)(2,1)S(1)}, u32[]{:S(2)}) copy-start(bf16[256,4,128]{2,1,0:T(4,128)(2,1)S(1)} %reshape.740) | copy-start | bytes 786436
  34.4 2.1 %copy-start.39 = (f32[4,256,256]{2,1,0:T(8,128)S(1)}, f32[4,256,256]{2,1,0:T(8,128)}, u32[]{:S(2)}) copy-start(f32[4,256,256]{2,1,0:T(8,128)} %get-tuple-element.80) | copy-start | bytes 3145732
  42.3 1.2 copy-start.11
  42.3 5.3 %collective-permute-start.2 = (f32[2,65536]{1,0:T(2,128)}, f32[2,65536]{1,0:T(2,128)}, u32[]{:S(2)}, u32[]{:S(2)}) collective-permute-start(f32[2,65536]{1,0:T(2,128)} %bitcast.185), channel_id=1, source_target_pairs={{0,1},{1,0},{2,3},{3,2},{4,5},{5,4},{6,7},{7,6},{8,9},{9,8},{10,11... | collective-permute-start | bytes 1572872 | tf_op jit(solution)/shard_map/ppermute | solution.py:21
  45.4 2.0 %copy-start.22 = (bf16[1,256,512]{1,2,0:T(8,128)(2,1)S(1)}, bf16[1,256,512]{1,2,0:T(8,128)(2,1)}, u32[]{:S(2)}) copy-start(bf16[1,256,512]{1,2,0:T(8,128)(2,1)} %copy-done.21) | copy-start | bytes 786436
  45.4 70.9 %collective-permute-start.5 = (bf16[2,256,512]{2,1,0:T(8,128)(2,1)}, bf16[2,256,512]{2,1,0:T(8,128)(2,1)}, u32[]{:S(2)}, u32[]{:S(2)}) collective-permute-start(bf16[2,256,512]{2,1,0:T(8,128)(2,1)} %pad_maximum_fusion.2), channel_id=1, source_target_pairs={{4,0},{8,4},{12,8},{16,12},{20,16},{24,20},{28,24},{5,1},{9,5},{13... | collective-permute-start | bytes 1572872 | tf_op jit(solution)/shard_map/ppermute | solution.py:15
  48.4 1.6 %copy-start.5 = (bf16[2,256,512]{1,2,0:T(8,128)(2,1)S(1)}, bf16[2,256,512]{1,2,0:T(8,128)(2,1)}, u32[]{:S(2)}) copy-start(bf16[2,256,512]{1,2,0:T(8,128)(2,1)} %copy-done.4) | copy-start | bytes 1572868
  50.0 2.6 %copy-start.38 = (f32[4,256,256]{2,1,0:T(8,128)S(1)}, f32[4,256,256]{2,1,0:T(8,128)}, u32[]{:S(2)}) copy-start(f32[4,256,256]{2,1,0:T(8,128)} %get-tuple-element.76) | copy-start | bytes 3145732
  50.8 1.8 %copy-start.19 = (bf16[256,4,128]{2,1,0:T(4,128)(2,1)S(1)}, bf16[256,4,128]{2,1,0:T(4,128)(2,1)}, u32[]{:S(2)}) copy-start(bf16[256,4,128]{2,1,0:T(4,128)(2,1)} %copy-done.17) | copy-start | bytes 786436
  51.0 8.4 %collective-permute-start.3 = (f32[1,65536]{1,0:T(1,128)S(1)}, f32[1,65536]{1,0:T(1,128)S(1)}, u32[]{:S(2)}, u32[]{:S(2)}) collective-permute-start(f32[1,65536]{1,0:T(1,128)S(1)} %constant_dynamic-slice_fusion), channel_id=1, source_target_pairs={{0,2},{1,3},{2,0},{3,1},{4,6},{5,7},{6,4},{7,5},{8,10},{9,11},{10,... | collective-permute-start | bytes 786440 | tf_op jit(solution)/shard_map/ppermute | solution.py:21
  60.5 23.5 %all-to-all-start = ((f32[8,1,8192]{2,1,0:T(1,128)}), f32[8,1,8192]{2,1,0:T(1,128)}, u32[]{:S(2)}, u32[]{:S(2)}) async-start(f32[8,1,8192]{2,1,0:T(1,128)} %bitcast.207), calls=%async_computation | async-start | bytes 524288 | tf_op jit(solution)/shard_map/all_to_all | solution.py:82
  76.0 1.1 copy-start.27
  78.0 2.6 %copy-start.25 = (bf16[1,256,512]{1,2,0:T(8,128)(2,1)S(1)}, bf16[1,256,512]{1,2,0:T(8,128)(2,1)}, u32[]{:S(2)}) copy-start(bf16[1,256,512]{1,2,0:T(8,128)(2,1)} %get-tuple-element.60) | copy-start | bytes 786436
  78.0 15.9 %collective-permute-start.4 = (bf16[2,256,512]{2,1,0:T(8,128)(2,1)}, bf16[2,256,512]{2,1,0:T(8,128)(2,1)}, u32[]{:S(2)}, u32[]{:S(2)}) collective-permute-start(bf16[2,256,512]{2,1,0:T(8,128)(2,1)} %pad_maximum_fusion.1), channel_id=1, source_target_pairs={{8,0},{12,4},{16,8},{20,12},{24,16},{28,20},{9,1},{13,5},{17,9},{2... | collective-permute-start | bytes 1572872 | tf_op jit(solution)/shard_map/ppermute | solution.py:15
  85.1 8.8 %copy-start.3 = (bf16[2,256,512]{1,2,0:T(8,128)(2,1)S(1)}, bf16[2,256,512]{1,2,0:T(8,128)(2,1)}, u32[]{:S(2)}) copy-start(bf16[2,256,512]{1,2,0:T(8,128)(2,1)} %copy-done.2) | copy-start | bytes 1572868
  87.9 6.8 %copy-start.20 = (bf16[256,4,128]{2,1,0:T(4,128)(2,1)S(1)}, bf16[256,4,128]{2,1,0:T(4,128)(2,1)}, u32[]{:S(2)}) copy-start(bf16[256,4,128]{2,1,0:T(4,128)(2,1)} %copy-done.17) | copy-start | bytes 786436
  94.7 1.8 %copy-start.15 = (f32[4,256,128]{2,1,0:T(8,128)S(1)}, f32[4,256,128]{2,1,0:T(8,128)}, u32[]{:S(2)}) copy-start(f32[4,256,128]{2,1,0:T(8,128)} %convolution_add_fusion.2) | copy-start | bytes 1572868
  98.4 14.5 %all-to-all-start.2 = ((f32[32,1,2048]{2,1,0:T(1,128)}), f32[32,1,2048]{2,1,0:T(1,128)}, u32[]{:S(2)}, u32[]{:S(2)}) async-start(f32[32,1,2048]{2,1,0:T(1,128)} %bitcast.54), calls=%async_computation.2 | async-start | bytes 524288 | tf_op jit(solution)/shard_map/all_to_all | solution.py:82
  112.9 10.7 %all-to-all-start.1 = ((bf16[8,2,4096]{2,1,0:T(2,128)(2,1)}), bf16[8,2,4096]{2,1,0:T(2,128)(2,1)S(1)}, u32[]{:S(2)}, u32[]{:S(2)}) async-start(bf16[8,2,4096]{2,1,0:T(2,128)(2,1)} %reshape.751), calls=%async_computation.1 | async-start | bytes 262144 | tf_op jit(solution)/shard_map/all_to_all | solution.py:85
  123.6 10.8 %all-to-all-start.3 = ((bf16[32,2,1024]{2,1,0:T(2,128)(2,1)}), bf16[32,2,1024]{2,1,0:T(2,128)(2,1)S(1)}, u32[]{:S(2)}, u32[]{:S(2)}) async-start(bf16[32,2,1024]{2,1,0:T(2,128)(2,1)} %reshape.753), calls=%async_computation.3 | async-start | bytes 262144 | tf_op jit(solution)/shard_map/all_to_all | solution.py:85
  (18 other events, 17.0 us)

commit v16 on v14

--- a/solution.py
+++ b/solution.py
@@ -79,8 +79,9 @@
     size = 1
     for axis in axes:
         size *= lax.axis_size(axis)
-    pieces = lax.all_to_all(flat.reshape(size, -1), axes, 0, 0, tiled=True)
-    total = jnp.sum(pieces, axis=0, keepdims=True)
+    outgoing = flat.reshape(size, -1).astype(jnp.bfloat16)
+    pieces = lax.all_to_all(outgoing, axes, 0, 0, tiled=True)
+    total = jnp.sum(pieces.astype(flat.dtype), axis=0, keepdims=True)
     spread = jnp.broadcast_to(total.astype(jnp.bfloat16), pieces.shape)
     gathered = lax.all_to_all(spread, axes, 0, 0, tiled=True)
     return gathered.astype(flat.dtype).reshape(flat.shape)

time: 117 us -> 120 us (1.026)
  waiting for transfers between devices: 18.8 us -> 16.2 us
  starting transfers between devices: 38.4 us -> 40.9 us
  other arithmetic: 14.5 us -> 16.8 us
  matrix products: 16.1 us -> 17.9 us
    all_to_all x2, starting transfers between devices: 5.95 us -> 10.5 us  [summed_by_exchange(): gathered = lax.all_to_all(spread, axes, 0, 0, tiled=True)]
    convert_element_type x0 -> x2, other arithmetic: none -> 2.75 us  [summed_by_exchange(): outgoing = flat.reshape(size, -1).astype(jnp.bfloat16)]
    dot_general x3, matrix products: 1.56 us -> 4.01 us  [shards(): jnp.einsum('ihd,jhd->hij', grad_heads, value_heads, preferred_element_typ...]
    all_to_all x2, waiting for transfers between devices: 9.17 us -> 7.05 us  [summed_by_exchange(): gathered = lax.all_to_all(spread, axes, 0, 0, tiled=True)]
    all_to_all x2, starting transfers between devices: 18.7 us -> 16.8 us  [summed_by_exchange(): pieces = lax.all_to_all(outgoing, axes, 0, 0, tiled=True)]
    unnamed x81 -> x75, local copies, waits for them, and re-layouts: 10.4 us -> 11.8 us
  transfers between devices with their start and end apart: 10 -> 10, of which waited for: 6 -> 5; matrix products, arithmetic and copies ran while one was open for 30% -> 33% of each run, Pallas kernels for 0% -> 0%
where the time goes in v16:
time: 120 us; the launch traced here: 119 us
  starting transfers between devices  40.9 us (34%)
  local copies, waits for them, and re-layouts  26 us (22%)
  matrix products  17.9 us (15%)
  other arithmetic  16.8 us (14%)
  waiting for transfers between devices  16.2 us (14%)
  between operations  1.52 us (1%)
    all_to_all x2, starting transfers between devices, summed_by_exchange(): pieces = lax.all_to_all(outgoing, axes, 0, 0, tiled=True)  16.8 us
    ppermute x4, starting transfers between devices, passed_along(): return lax.ppermute(value, axis, pairs)  11.9 us
    unnamed x75, local copies, waits for them, and re-layouts  11.8 us
    all_to_all x2, starting transfers between devices, summed_by_exchange(): gathered = lax.all_to_all(spread, axes, 0, 0, tiled=True)  10.5 us
    all_to_all x2, waiting for transfers between devices, summed_by_exchange(): gathered = lax.all_to_all(spread, axes, 0, 0, tiled=True)  7.05 us
    all_to_all x2, waiting for transfers between devices, summed_by_exchange(): pieces = lax.all_to_all(outgoing, axes, 0, 0, tiled=True)  5.31 us
    dot_general x3, matrix products, shards(): jnp.einsum('ihd,jhd->hij', grad_heads, value_heads, preferred_element_typ...  4.01 us
    ppermute x2, waiting for transfers between devices, exchanged(): return lax.ppermute(value, axis, pairs)  3.79 us
  transfers between devices with their start and end apart: 10, of which 5 were waited for; matrix products, arithmetic and copies ran while one was open for 33% of the time, Pallas kernels for 0%

profile of v16, /device:TPU:0, one launch (start us, length us, event | category | flops | bytes accessed | tf_op | source)
XLA Modules:
  0.0 119.1 jit_solution(970763672961820898)
XLA Ops:
  0.7 1.2 copy.179
  2.0 5.7 %collective-permute-start.1 = (bf16[2,256,512]{1,2,0:T(8,128)(2,1)S(1)}, bf16[2,256,512]{1,2,0:T(8,128)(2,1)}, u32[]{:S(2)}, u32[]{:S(2)}) collective-permute-start(bf16[2,256,512]{1,2,0:T(8,128)(2,1)S(1)} %pad_maximum_fusion), channel_id=1, source_target_pairs={{0,8},{4,12},{8,16},{12,20},{16,24},{20,28},{1,9},{5,13},{9,17},{1... | collective-permute-start | bytes 1572872 | tf_op jit(solution)/shard_map/ppermute | solution.py:15
  7.8 3.4 %collective-permute-start = (bf16[2,256,512]{1,2,0:T(8,128)(2,1)S(1)}, bf16[2,256,512]{1,2,0:T(8,128)(2,1)S(1)}, u32[]{:S(2)}, u32[]{:S(2)}) collective-permute-start(bf16[2,256,512]{1,2,0:T(8,128)(2,1)S(1)} %pad_maximum_fusion), channel_id=1, source_target_pairs={{0,4},{4,8},{8,12},{12,16},{16,20},{20,24},{24,28},{1,5},{5,9},{9,... | collective-permute-start | bytes 1572872 | tf_op jit(solution)/shard_map/ppermute | solution.py:15
  15.7 1.5 %select_convert_fusion.2 = (bf16[4,256,256]{2,1,0:T(8,128)(2,1)S(1)}, f32[4,256,256]{2,1,0:T(8,128)}) fusion(pred[256,256]{1,0:T(8,128)(4,1)S(1)} %copy.130, f32[4,256,256]{2,1,0:T(8,128)S(1)} %convolution_multiply_fusion.5, bf16[4,256,128]{2,1,0:T(8,128)(2,1)S(1)} %fusion.16, s32[256]{0:T(256)S(1)} %bitcast.246), kind=kOutput, calls=%fused_computation.46 | convolution fusion | flops 68976640 | bytes 2950144 | tf_op jit(solution)/shard_map/vqx,px->vqp/dot_general | solution.py:162
  18.0 1.1 convolution_bitcast_fusion.2
  21.0 1.1 fusion.67
  22.1 1.5 %select_convert_fusion = (bf16[4,256,256]{2,1,0:T(8,128)(2,1)S(1)}, f32[4,256,256]{2,1,0:T(8,128)}) fusion(pred[256,256]{1,0:T(8,128)(4,1)S(1)} %copy.143, f32[4,256,256]{2,1,0:T(8,128)S(1)} %fusion.49, bf16[256,4,128]{0,2,1:T(8,128)(2,1)S(1)} %bitcast.208, bf16[256,4,128]{0,2,1:T(8,128)(2,1)S(1)} %bitcast.237), kind=kOutput, calls=%fused_computation.42 | convolution fusion | flops 69206016 | bytes 3211264 | tf_op jit(solution)/shard_map/ihd,jhd->hij/dot_general | solution.py:177
  25.2 1.5 %select_convert_fusion.1 = (bf16[4,256,256]{2,1,0:T(8,128)(2,1)S(1)}, f32[4,256,256]{2,1,0:T(8,128)}) fusion(pred[256,256]{1,0:T(8,128)(4,1)S(1)} %copy.138, f32[4,256,256]{2,1,0:T(8,128)S(1)} %fusion.45, bf16[256,4,128]{0,2,1:T(8,128)(2,1)S(1)} %bitcast.209, bf16[256,4,128]{0,2,1:T(8,128)(2,1)S(1)} %bitcast.238), kind=kOutput, calls=%fused_computation.44 | convolution fusion | flops 69206016 | bytes 3211264 | tf_op jit(solution)/shard_map/ihd,jhd->hij/dot_general | solution.py:177
  31.3 0.9 convolution_convert_fusion.1
  32.7 1.0 copy.162
  38.8 1.1 fusion.64
  41.5 1.6 %collective-permute-start.3 = (f32[1,65536]{1,0:T(1,128)S(1)}, f32[1,65536]{1,0:T(1,128)}, u32[]{:S(2)}, u32[]{:S(2)}) collective-permute-start(f32[1,65536]{1,0:T(1,128)S(1)} %constant_dynamic-slice_fusion), channel_id=1, source_target_pairs={{0,2},{1,3},{2,0},{3,1},{4,6},{5,7},{6,4},{7,5},{8,10},{9,11},{10,... | collective-permute-start | bytes 786440 | tf_op jit(solution)/shard_map/ppermute | solution.py:21
  45.1 1.5 %collective-permute-start.4 = (bf16[2,256,512]{2,1,0:T(8,128)(2,1)}, bf16[2,256,512]{2,1,0:T(8,128)(2,1)}, u32[]{:S(2)}, u32[]{:S(2)}) collective-permute-start(bf16[2,256,512]{2,1,0:T(8,128)(2,1)} %pad_maximum_fusion.1), channel_id=1, source_target_pairs={{8,0},{12,4},{16,8},{20,12},{24,16},{28,20},{9,1},{13,5},{17,9},{2... | collective-permute-start | bytes 1572872 | tf_op jit(solution)/shard_map/ppermute | solution.py:15
  46.6 3.5 %collective-permute-done.3 = f32[1,65536]{1,0:T(1,128)} collective-permute-done((f32[1,65536]{1,0:T(1,128)S(1)}, f32[1,65536]{1,0:T(1,128)}, u32[]{:S(2)}, u32[]{:S(2)}) %collective-permute-start.3) | collective-permute-done | bytes 262176 | tf_op jit(solution)/shard_map/ppermute | solution.py:21
  50.1 1.3 %dynamic-slice_add_fusion = bf16[1,65536]{1,0:T(2,128)(2,1)S(1)} fusion(f32[1,65536]{1,0:T(1,128)} %collective-permute-done.3, f32[2,65536]{1,0:T(2,128)S(1)} %bitcast_add_fusion, s32[]{:T(128)S(6)} %select_n.144), kind=kLoop, calls=%fused_computation.70 | loop fusion | flops 131072 | bytes 655364 | tf_op jit(solution)/shard_map/add | solution.py:71
  52.0 1.4 %reduce.8 = bf16[8,8192]{1,0:T(8,128)(2,1)S(1)} reduce(bf16[8,1,8192]{2,1,0:T(2,128)(2,1)S(1)} %bitcast.228, bf16[]{:T(256)} %broadcast.602), dimensions={1}, to_apply=%bitcast.54.reduce_sub_computation | reduce | bytes 262146 | tf_op jit(solution)/shard_map/convert_element_type | solution.py:82
  54.1 11.9 %all-to-all-start = ((bf16[8,2,4096]{2,1,0:T(2,128)(2,1)}), bf16[8,2,4096]{2,1,0:T(2,128)(2,1)S(1)}, u32[]{:S(2)}, u32[]{:S(2)}) async-start(bf16[8,2,4096]{2,1,0:T(2,128)(2,1)} %reshape.771), calls=%async_computation | async-start | bytes 262144 | tf_op jit(solution)/shard_map/all_to_all | solution.py:83
  66.0 1.7 %fusion.8 = bf16[4,256,256]{2,1,0:T(8,128)(2,1)S(1)} fusion(bf16[256,4,128]{0,2,1:T(8,128)(2,1)S(1)} %bitcast.234, f32[4,256,256]{2,1,0:T(8,128)} %get-tuple-element.82, pred[256,256]{1,0:T(8,128)(4,1)S(1)} %copy-done.26, bf16[256,512]{1,0:T(8,128)(2,1)S(1)} %copy-done.13), kind=kOutput, calls=%fused_computation.15 | convolution fusion | flops 69730304 | bytes 2162688 | tf_op jit(solution)/shard_map/ihd,jhd->hij/dot_general | solution.py:243
  69.3 1.8 %pad_maximum_fusion.2 = bf16[2,256,512]{2,1,0:T(8,128)(2,1)} fusion(bf16[1,256,512]{2,1,0:T(8,128)(2,1)S(1)} %copy-done.15, bf16[1,256,512]{2,1,0:T(8,128)(2,1)} %copy.165), kind=kLoop, calls=%fused_computation.50 | loop fusion | flops 262144 | bytes 1048576 | tf_op jit(solution)/shard_map/stack | solution.py:267
  71.1 1.3 %collective-permute-start.5 = (bf16[2,256,512]{2,1,0:T(8,128)(2,1)}, bf16[2,256,512]{2,1,0:T(8,128)(2,1)}, u32[]{:S(2)}, u32[]{:S(2)}) collective-permute-start(bf16[2,256,512]{2,1,0:T(8,128)(2,1)} %pad_maximum_fusion.2), channel_id=1, source_target_pairs={{4,0},{8,4},{12,8},{16,12},{20,16},{24,20},{28,24},{5,1},{9,5},{13... | collective-permute-start | bytes 1572872 | tf_op jit(solution)/shard_map/ppermute | solution.py:15
  74.0 1.4 %reduce.9 = bf16[8,8192]{1,0:T(8,128)(2,1)S(1)} reduce(bf16[8,1,8192]{2,1,0:T(2,128)(2,1)S(1)} %broadcast_in_dim.65, bf16[]{:T(256)} %broadcast.602), dimensions={1}, to_apply=%broadcast_in_dim.65.reduce_sub_computation | reduce | bytes 262146 | tf_op jit(solution)/shard_map/broadcast_in_dim | solution.py:85
  76.2 8.0 %all-to-all-start.1 = ((bf16[8,2,4096]{2,1,0:T(2,128)(2,1)}), bf16[8,2,4096]{2,1,0:T(2,128)(2,1)S(1)}, u32[]{:S(2)}, u32[]{:S(2)}) async-start(bf16[8,2,4096]{2,1,0:T(2,128)(2,1)} %reshape.773), calls=%async_computation.1 | async-start | bytes 262144 | tf_op jit(solution)/shard_map/all_to_all | solution.py:86
  85.0 1.7 %fusion.9 = bf16[4,256,256]{2,1,0:T(8,128)(2,1)S(1)} fusion(bf16[256,4,128]{0,2,1:T(8,128)(2,1)S(1)} %bitcast.235, f32[4,256,256]{2,1,0:T(8,128)} %get-tuple-element.80, pred[256,256]{1,0:T(8,128)(4,1)S(1)} %copy-done.24, bf16[256,512]{1,0:T(8,128)(2,1)S(1)} %copy-done.13), kind=kOutput, calls=%fused_computation.16 | convolution fusion | flops 69730304 | bytes 2162688 | tf_op jit(solution)/shard_map/ihd,jhd->hij/dot_general | solution.py:243
  88.3 1.4 %reduce.10 = bf16[32,2048]{1,0:T(8,128)(2,1)S(1)} reduce(bf16[32,1,2048]{2,1,0:T(2,128)(2,1)S(1)} %convert_element_type.178, bf16[]{:T(256)} %broadcast.602), dimensions={1}, to_apply=%convert_element_type.178.reduce_sub_computation | reduce | bytes 262146 | tf_op jit(solution)/shard_map/convert_element_type | solution.py:82
  90.4 1.1 all-to-all-done.1
  91.5 4.9 %all-to-all-start.2 = ((bf16[32,2,1024]{2,1,0:T(2,128)(2,1)}), bf16[32,2,1024]{2,1,0:T(2,128)(2,1)S(1)}, u32[]{:S(2)}, u32[]{:S(2)}) async-start(bf16[32,2,1024]{2,1,0:T(2,128)(2,1)} %reshape.775), calls=%async_computation.2 | async-start | bytes 262144 | tf_op jit(solution)/shard_map/all_to_all | solution.py:83
  99.3 5.3 %all-to-all-done.2 = bf16[32,2,1024]{2,1,0:T(2,128)(2,1)S(1)} async-done(((bf16[32,2,1024]{2,1,0:T(2,128)(2,1)}), bf16[32,2,1024]{2,1,0:T(2,128)(2,1)S(1)}, u32[]{:S(2)}, u32[]{:S(2)}) %all-to-all-start.2) | async-done | bytes 131104 | tf_op jit(solution)/shard_map/all_to_all | solution.py:83
  105.1 1.4 %reduce.11 = bf16[32,2048]{1,0:T(8,128)(2,1)S(1)} reduce(bf16[32,1,2048]{2,1,0:T(2,128)(2,1)S(1)} %broadcast_in_dim.66, bf16[]{:T(256)} %broadcast.602), dimensions={1}, to_apply=%broadcast_in_dim.66.reduce_sub_computation | reduce | bytes 262146 | tf_op jit(solution)/shard_map/broadcast_in_dim | solution.py:85
  107.3 2.6 %all-to-all-start.3 = ((bf16[32,2,1024]{2,1,0:T(2,128)(2,1)}), bf16[32,2,1024]{2,1,0:T(2,128)(2,1)S(1)}, u32[]{:S(2)}, u32[]{:S(2)}) async-start(bf16[32,2,1024]{2,1,0:T(2,128)(2,1)} %reshape.777), calls=%async_computation.3 | async-start | bytes 262144 | tf_op jit(solution)/shard_map/all_to_all | solution.py:86
  109.9 1.4 %fusion.19 = bf16[2,256,512]{2,1,0:T(8,128)(2,1)S(1)} fusion(f32[1,256,512]{2,1,0:T(8,128)S(1)} %copy-done.2, f32[1,256,512]{2,1,0:T(8,128)S(1)} %copy.161, bf16[2,256,512]{2,1,0:T(8,128)(2,1)} %collective-permute-done.4, bf16[2,256,512]{2,1,0:T(8,128)(2,1)} %collective-permute-done.5), kind=kLoop, calls=%fused_computation.41 | loop fusion | flops 1572864 | bytes 2621440 | tf_op jit(solution)/shard_map/convert.7
  112.1 5.9 %all-to-all-done.3 = bf16[32,2,1024]{2,1,0:T(2,128)(2,1)S(1)} async-done(((bf16[32,2,1024]{2,1,0:T(2,128)(2,1)}), bf16[32,2,1024]{2,1,0:T(2,128)(2,1)S(1)}, u32[]{:S(2)}, u32[]{:S(2)}) %all-to-all-start.3) | async-done | bytes 131104 | tf_op jit(solution)/shard_map/all_to_all | solution.py:86
  118.2 1.0 convert_element_type.177
  (159 shorter events, 35.5 us)
Async XLA Ops:
  0.6 26.8 %copy-start = (bf16[512,512]{1,0:T(8,128)(2,1)S(1)}, bf16[512,512]{1,0:T(8,128)(2,1)}, u32[]{:S(2)}) copy-start(bf16[512,512]{1,0:T(8,128)(2,1)} %param.19) | copy-start | bytes 1572868
  0.6 1.2 copy-start.14
  2.0 12.1 %copy-start.3 = (bf16[2,256,512]{1,2,0:T(8,128)(2,1)}, bf16[2,256,512]{1,2,0:T(8,128)(2,1)S(1)}, u32[]{:S(2)}) copy-start(bf16[2,256,512]{1,2,0:T(8,128)(2,1)S(1)} %pad_maximum_fusion) | copy-start | bytes 1572868
  2.0 19.0 %collective-permute-start.1 = (bf16[2,256,512]{1,2,0:T(8,128)(2,1)S(1)}, bf16[2,256,512]{1,2,0:T(8,128)(2,1)}, u32[]{:S(2)}, u32[]{:S(2)}) collective-permute-start(bf16[2,256,512]{1,2,0:T(8,128)(2,1)S(1)} %pad_maximum_fusion), channel_id=1, source_target_pairs={{0,8},{4,12},{8,16},{12,20},{16,24},{20,28},{1,9},{5,13},{9,17},{1... | collective-permute-start | bytes 1572872 | tf_op jit(solution)/shard_map/ppermute | solution.py:15
  7.8 16.6 %collective-permute-start = (bf16[2,256,512]{1,2,0:T(8,128)(2,1)S(1)}, bf16[2,256,512]{1,2,0:T(8,128)(2,1)S(1)}, u32[]{:S(2)}, u32[]{:S(2)}) collective-permute-start(bf16[2,256,512]{1,2,0:T(8,128)(2,1)S(1)} %pad_maximum_fusion), channel_id=1, source_target_pairs={{0,4},{4,8},{8,12},{12,16},{16,20},{20,24},{24,28},{1,5},{5,9},{9,... | collective-permute-start | bytes 1572872 | tf_op jit(solution)/shard_map/ppermute | solution.py:15
  11.3 1.6 %copy-start.28 = (s32[1,6]{1,0:T(1,128)S(1)}, s32[1,6]{1,0:T(1,128)}, u32[]{:S(2)}) copy-start(s32[1,6]{1,0:T(1,128)} %param.16) | copy-start | bytes 76
  11.4 2.7 %copy-start.21 = (bf16[1,256,512]{2,1,0:T(8,128)(2,1)S(1)}, bf16[1,256,512]{2,1,0:T(8,128)(2,1)}, u32[]{:S(2)}) copy-start(bf16[1,256,512]{2,1,0:T(8,128)(2,1)} %param.10) | copy-start | bytes 786436
  14.1 1.6 %copy-start.23 = (pred[256,256]{1,0:T(8,128)(4,1)}, pred[256,256]{1,0:T(8,128)(4,1)S(1)}, u32[]{:S(2)}) copy-start(pred[256,256]{1,0:T(8,128)(4,1)S(1)} %copy.130) | copy-start | bytes 196612
  19.1 0.9 copy-start.1
  19.3 5.9 %copy-start.25 = (pred[256,256]{1,0:T(8,128)(4,1)}, pred[256,256]{1,0:T(8,128)(4,1)S(1)}, u32[]{:S(2)}) copy-start(pred[256,256]{1,0:T(8,128)(4,1)S(1)} %copy.138) | copy-start | bytes 196612
  25.2 1.5 %copy-start.11 = (f32[256,4,128]{0,2,1:T(8,128)S(1)}, f32[256,4,128]{0,2,1:T(8,128)}, u32[]{:S(2)}) copy-start(f32[256,4,128]{0,2,1:T(8,128)} %convolution_bitcast_fusion.2) | copy-start | bytes 1572868
  27.2 1.0 copy-start.19
  30.2 1.0 copy-start.10
  31.3 1.0 copy-start.8
  32.7 1.0 copy-start.18
  33.7 1.0 copy-start.17
  38.3 1.6 %copy-start.29 = (f32[4,256,256]{2,1,0:T(8,128)S(1)}, f32[4,256,256]{2,1,0:T(8,128)}, u32[]{:S(2)}) copy-start(f32[4,256,256]{2,1,0:T(8,128)} %get-tuple-element.78) | copy-start | bytes 3145732
  38.7 1.2 copy-start.13
  38.7 2.0 %collective-permute-start.2 = (f32[2,65536]{1,0:T(2,128)S(1)}, f32[2,65536]{1,0:T(2,128)S(1)}, u32[]{:S(2)}, u32[]{:S(2)}) collective-permute-start(f32[2,65536]{1,0:T(2,128)S(1)} %bitcast.232), channel_id=1, source_target_pairs={{0,1},{1,0},{2,3},{3,2},{4,5},{5,4},{6,7},{7,6},{8,9},{9,8},{10,11... | collective-permute-start | bytes 1572872 | tf_op jit(solution)/shard_map/ppermute | solution.py:21
  41.5 8.6 %collective-permute-start.3 = (f32[1,65536]{1,0:T(1,128)S(1)}, f32[1,65536]{1,0:T(1,128)}, u32[]{:S(2)}, u32[]{:S(2)}) collective-permute-start(f32[1,65536]{1,0:T(1,128)S(1)} %constant_dynamic-slice_fusion), channel_id=1, source_target_pairs={{0,2},{1,3},{2,0},{3,1},{4,6},{5,7},{6,4},{7,5},{8,10},{9,11},{10,... | collective-permute-start | bytes 786440 | tf_op jit(solution)/shard_map/ppermute | solution.py:21
  43.3 1.0 copy-start.16
  45.1 39.0 %collective-permute-start.4 = (bf16[2,256,512]{2,1,0:T(8,128)(2,1)}, bf16[2,256,512]{2,1,0:T(8,128)(2,1)}, u32[]{:S(2)}, u32[]{:S(2)}) collective-permute-start(bf16[2,256,512]{2,1,0:T(8,128)(2,1)} %pad_maximum_fusion.1), channel_id=1, source_target_pairs={{8,0},{12,4},{16,8},{20,12},{24,16},{28,20},{9,1},{13,5},{17,9},{2... | collective-permute-start | bytes 1572872 | tf_op jit(solution)/shard_map/ppermute | solution.py:15
  51.4 2.7 %copy-start.6 = (bf16[2,256,512]{1,2,0:T(8,128)(2,1)S(1)}, bf16[2,256,512]{1,2,0:T(8,128)(2,1)}, u32[]{:S(2)}) copy-start(bf16[2,256,512]{1,2,0:T(8,128)(2,1)} %copy-done.5) | copy-start | bytes 1572868
  54.1 11.9 %copy-start.26 = (pred[256,256]{1,0:T(8,128)(4,1)S(1)}, pred[256,256]{1,0:T(8,128)(4,1)}, u32[]{:S(2)}) copy-start(pred[256,256]{1,0:T(8,128)(4,1)} %copy-done.25) | copy-start | bytes 196612
  54.1 19.3 %all-to-all-start = ((bf16[8,2,4096]{2,1,0:T(2,128)(2,1)}), bf16[8,2,4096]{2,1,0:T(2,128)(2,1)S(1)}, u32[]{:S(2)}, u32[]{:S(2)}) async-start(bf16[8,2,4096]{2,1,0:T(2,128)(2,1)} %reshape.771), calls=%async_computation | async-start | bytes 262144 | tf_op jit(solution)/shard_map/all_to_all | solution.py:83
  68.3 1.0 copy-start.15
  71.1 38.8 %collective-permute-start.5 = (bf16[2,256,512]{2,1,0:T(8,128)(2,1)}, bf16[2,256,512]{2,1,0:T(8,128)(2,1)}, u32[]{:S(2)}, u32[]{:S(2)}) collective-permute-start(bf16[2,256,512]{2,1,0:T(8,128)(2,1)} %pad_maximum_fusion.2), channel_id=1, source_target_pairs={{4,0},{8,4},{12,8},{16,12},{20,16},{24,20},{28,24},{5,1},{9,5},{13... | collective-permute-start | bytes 1572872 | tf_op jit(solution)/shard_map/ppermute | solution.py:15
  74.0 10.2 %copy-start.4 = (bf16[2,256,512]{1,2,0:T(8,128)(2,1)S(1)}, bf16[2,256,512]{1,2,0:T(8,128)(2,1)}, u32[]{:S(2)}) copy-start(bf16[2,256,512]{1,2,0:T(8,128)(2,1)} %copy-done.3) | copy-start | bytes 1572868
  76.2 15.3 %all-to-all-start.1 = ((bf16[8,2,4096]{2,1,0:T(2,128)(2,1)}), bf16[8,2,4096]{2,1,0:T(2,128)(2,1)S(1)}, u32[]{:S(2)}, u32[]{:S(2)}) async-start(bf16[8,2,4096]{2,1,0:T(2,128)(2,1)} %reshape.773), calls=%async_computation.1 | async-start | bytes 262144 | tf_op jit(solution)/shard_map/all_to_all | solution.py:86
  91.5 13.1 %all-to-all-start.2 = ((bf16[32,2,1024]{2,1,0:T(2,128)(2,1)}), bf16[32,2,1024]{2,1,0:T(2,128)(2,1)S(1)}, u32[]{:S(2)}, u32[]{:S(2)}) async-start(bf16[32,2,1024]{2,1,0:T(2,128)(2,1)} %reshape.775), calls=%async_computation.2 | async-start | bytes 262144 | tf_op jit(solution)/shard_map/all_to_all | solution.py:83
  105.1 4.8 %copy-start.2 = (f32[1,256,512]{2,1,0:T(8,128)S(1)}, f32[1,256,512]{2,1,0:T(8,128)}, u32[]{:S(2)}) copy-start(f32[1,256,512]{2,1,0:T(8,128)} %copy.162) | copy-start | bytes 1572868
  107.3 10.8 %all-to-all-start.3 = ((bf16[32,2,1024]{2,1,0:T(2,128)(2,1)}), bf16[32,2,1024]{2,1,0:T(2,128)(2,1)S(1)}, u32[]{:S(2)}, u32[]{:S(2)}) async-start(bf16[32,2,1024]{2,1,0:T(2,128)(2,1)} %reshape.777), calls=%async_computation.3 | async-start | bytes 262144 | tf_op jit(solution)/shard_map/all_to_all | solution.py:86
  (8 other events, 6.5 us)

commit v17 on v14

--- a/solution.py
+++ b/solution.py
@@ -213,15 +213,19 @@
         mixed, grad_rows, (((0,), (0,)), ((), ())), preferred_element_type=jnp.float32
     )
     weight_plan = [("split", "dp", mask) for mask in axis_bits("dp")]
+    weight_plan.append(("skip", "ctx", 0))
     weight_plan.append(("exchange", "ctx", 0))
     weight_state = [weight_term.reshape(dp_size, -1), 0]
 
     def slot(anchor):
         blocks, done = weight_state
         if done < len(weight_plan):
-            blocks, anchor = lax.optimization_barrier((blocks, anchor))
             kind, axis, mask = weight_plan[done]
-            if kind == "exchange":
+            if kind != "skip":
+                blocks, anchor = lax.optimization_barrier((blocks, anchor))
+            if kind == "skip":
+                weight_state[0] = blocks
+            elif kind == "exchange":
                 weight_state[0] = summed_by_exchange(blocks.reshape(-1), (axis,))
             else:
                 weight_state[0] = plan_step(blocks, kind, axis, mask)

time: 117 us -> 119 us (1.017)
  waiting for transfers between devices: 18.8 us -> 20.6 us
  local copies, waits for them, and re-layouts: 26.1 us -> 27.7 us
    all_to_all x2, waiting for transfers between devices: 5.96 us -> 8.24 us  [summed_by_exchange(): pieces = lax.all_to_all(flat.reshape(size, -1), axes, 0, 0, tiled=True)]
    unnamed x81 -> x91, local copies, waits for them, and re-layouts: 10.4 us -> 11.6 us
  transfers between devices with their start and end apart: 10 -> 10, of which waited for: 6 -> 6; matrix products, arithmetic and copies ran while one was open for 30% -> 28% of each run, Pallas kernels for 0% -> 0%
where the time goes in v17:
time: 119 us; the launch traced here: 118 us
  starting transfers between devices  37.4 us (31%)
  local copies, waits for them, and re-layouts  27.7 us (23%)
  waiting for transfers between devices  20.6 us (17%)
  matrix products  17 us (14%)
  other arithmetic  14.3 us (12%)
  between operations  1.4 us (1%)
    all_to_all x2, starting transfers between devices, summed_by_exchange(): pieces = lax.all_to_all(flat.reshape(size, -1), axes, 0, 0, tiled=True)  18 us
    ppermute x4, starting transfers between devices, passed_along(): return lax.ppermute(value, axis, pairs)  11.9 us
    unnamed x91, local copies, waits for them, and re-layouts  11.6 us
    all_to_all x2, waiting for transfers between devices, summed_by_exchange(): gathered = lax.all_to_all(spread, axes, 0, 0, tiled=True)  9.18 us
    all_to_all x2, waiting for transfers between devices, summed_by_exchange(): pieces = lax.all_to_all(flat.reshape(size, -1), axes, 0, 0, tiled=True)  8.24 us
    all_to_all x2, starting transfers between devices, summed_by_exchange(): gathered = lax.all_to_all(spread, axes, 0, 0, tiled=True)  5.93 us
    dot_general x3, matrix products, shards(): jnp.einsum('ihd,jhd->hij', query_heads, forward_key_heads, preferred_elem...  3.35 us
    ppermute x2, waiting for transfers between devices, exchanged(): return lax.ppermute(value, axis, pairs)  3.12 us
  transfers between devices with their start and end apart: 10, of which 6 were waited for; matrix products, arithmetic and copies ran while one was open for 28% of the time, Pallas kernels for 0%

profile of v17, /device:TPU:0, one launch (start us, length us, event | category | flops | bytes accessed | tf_op | source)
XLA Modules:
  0.0 118.5 jit_solution(14875657019770705692)
XLA Ops:
  0.7 1.2 copy.180
  2.0 5.0 %collective-permute-start.1 = (bf16[2,256,512]{1,2,0:T(8,128)(2,1)S(1)}, bf16[2,256,512]{1,2,0:T(8,128)(2,1)S(1)}, u32[]{:S(2)}, u32[]{:S(2)}) collective-permute-start(bf16[2,256,512]{1,2,0:T(8,128)(2,1)S(1)} %pad_maximum_fusion), channel_id=1, source_target_pairs={{0,8},{4,12},{8,16},{12,20},{16,24},{20,28},{1,9},{5,13},{9,17},{1... | collective-permute-start | bytes 1572872 | tf_op jit(solution)/shard_map/ppermute | solution.py:15
  7.0 4.2 %collective-permute-start = (bf16[2,256,512]{1,2,0:T(8,128)(2,1)S(1)}, bf16[2,256,512]{1,2,0:T(8,128)(2,1)}, u32[]{:S(2)}, u32[]{:S(2)}) collective-permute-start(bf16[2,256,512]{1,2,0:T(8,128)(2,1)S(1)} %pad_maximum_fusion), channel_id=1, source_target_pairs={{0,4},{4,8},{8,12},{12,16},{16,20},{20,24},{24,28},{1,5},{5,9},{9,... | collective-permute-start | bytes 1572872 | tf_op jit(solution)/shard_map/ppermute | solution.py:15
  15.7 1.5 %select_convert_fusion.2 = (bf16[4,256,256]{2,1,0:T(8,128)(2,1)S(1)}, f32[4,256,256]{2,1,0:T(8,128)}) fusion(pred[256,256]{1,0:T(8,128)(4,1)S(1)} %copy.131, f32[4,256,256]{2,1,0:T(8,128)S(1)} %convolution_multiply_fusion.5, bf16[4,256,128]{2,1,0:T(8,128)(2,1)S(1)} %fusion.16, s32[256]{0:T(256)S(1)} %bitcast.244), kind=kOutput, calls=%fused_computation.45 | convolution fusion | flops 68976640 | bytes 2950144 | tf_op jit(solution)/shard_map/vqx,px->vqp/dot_general | solution.py:161
  18.0 1.1 convolution_bitcast_fusion.2
  21.8 1.5 %select_convert_fusion = (bf16[4,256,256]{2,1,0:T(8,128)(2,1)S(1)}, f32[4,256,256]{2,1,0:T(8,128)}) fusion(pred[256,256]{1,0:T(8,128)(4,1)S(1)} %copy.144, f32[4,256,256]{2,1,0:T(8,128)S(1)} %fusion.48, bf16[256,4,128]{0,2,1:T(8,128)(2,1)S(1)} %bitcast.207, bf16[256,4,128]{0,2,1:T(8,128)(2,1)S(1)} %bitcast.236), kind=kOutput, calls=%fused_computation.41 | convolution fusion | flops 69206016 | bytes 3211264 | tf_op jit(solution)/shard_map/ihd,jhd->hij/dot_general | solution.py:176
  23.6 1.1 fusion.64
  24.7 1.5 %select_convert_fusion.1 = (bf16[4,256,256]{2,1,0:T(8,128)(2,1)S(1)}, f32[4,256,256]{2,1,0:T(8,128)}) fusion(pred[256,256]{1,0:T(8,128)(4,1)S(1)} %copy.139, f32[4,256,256]{2,1,0:T(8,128)S(1)} %fusion.44, bf16[256,4,128]{0,2,1:T(8,128)(2,1)S(1)} %bitcast.208, bf16[256,4,128]{0,2,1:T(8,128)(2,1)S(1)} %bitcast.219), kind=kOutput, calls=%fused_computation.43 | convolution fusion | flops 69206016 | bytes 3211264 | tf_op jit(solution)/shard_map/ihd,jhd->hij/dot_general | solution.py:176
  29.6 1.0 copy-done.11
  30.6 0.9 convolution_convert_fusion
  31.6 0.9 convolution_convert_fusion.1
  34.6 1.0 copy.163
  44.2 1.5 %collective-permute-start.3 = (f32[1,65536]{1,0:T(1,128)}, f32[1,65536]{1,0:T(1,128)}, u32[]{:S(2)}, u32[]{:S(2)}) collective-permute-start(f32[1,65536]{1,0:T(1,128)} %constant_dynamic-slice_fusion), channel_id=1, source_target_pairs={{0,2},{1,3},{2,0},{3,1},{4,6},{5,7},{6,4},{7,5},{8,10},{9,11},{10,... | collective-permute-start | bytes 786440 | tf_op jit(solution)/shard_map/ppermute | solution.py:21
  45.7 0.9 fusion.14
  46.7 1.1 copy.156
  48.6 1.5 %collective-permute-start.4 = (bf16[2,256,512]{2,1,0:T(8,128)(2,1)}, bf16[2,256,512]{2,1,0:T(8,128)(2,1)}, u32[]{:S(2)}, u32[]{:S(2)}) collective-permute-start(bf16[2,256,512]{2,1,0:T(8,128)(2,1)} %pad_maximum_fusion.1), channel_id=1, source_target_pairs={{8,0},{12,4},{16,8},{20,12},{24,16},{28,20},{9,1},{13,5},{17,9},{2... | collective-permute-start | bytes 1572872 | tf_op jit(solution)/shard_map/ppermute | solution.py:15
  50.1 2.7 %collective-permute-done.3 = f32[1,65536]{1,0:T(1,128)} collective-permute-done((f32[1,65536]{1,0:T(1,128)}, f32[1,65536]{1,0:T(1,128)}, u32[]{:S(2)}, u32[]{:S(2)}) %collective-permute-start.3) | collective-permute-done | bytes 262176 | tf_op jit(solution)/shard_map/ppermute | solution.py:21
  52.9 2.0 %dynamic-slice_add_fusion = f32[1,65536]{1,0:T(1,128)} fusion(f32[1,65536]{1,0:T(1,128)} %collective-permute-done.3, f32[2,65536]{1,0:T(2,128)S(1)} %bitcast_add_fusion, s32[]{:T(128)S(6)} %select_n.144), kind=kLoop, calls=%fused_computation.69 | loop fusion | flops 65536 | bytes 786436 | tf_op jit(solution)/shard_map/add | solution.py:71
  55.5 12.7 %all-to-all-start = ((f32[8,1,8192]{2,1,0:T(1,128)}), f32[8,1,8192]{2,1,0:T(1,128)S(1)}, u32[]{:S(2)}, u32[]{:S(2)}) async-start(f32[8,1,8192]{2,1,0:T(1,128)} %bitcast.52), calls=%async_computation | async-start | bytes 524288 | tf_op jit(solution)/shard_map/all_to_all | solution.py:82
  70.9 1.3 %collective-permute-start.5 = (bf16[2,256,512]{2,1,0:T(8,128)(2,1)}, bf16[2,256,512]{2,1,0:T(8,128)(2,1)}, u32[]{:S(2)}, u32[]{:S(2)}) collective-permute-start(bf16[2,256,512]{2,1,0:T(8,128)(2,1)} %pad_maximum_fusion.2), channel_id=1, source_target_pairs={{4,0},{8,4},{12,8},{16,12},{20,16},{24,20},{28,24},{5,1},{9,5},{13... | collective-permute-start | bytes 1572872 | tf_op jit(solution)/shard_map/ppermute | solution.py:15
  76.8 2.7 %all-to-all-done = f32[8,1,8192]{2,1,0:T(1,128)S(1)} async-done(((f32[8,1,8192]{2,1,0:T(1,128)}), f32[8,1,8192]{2,1,0:T(1,128)S(1)}, u32[]{:S(2)}, u32[]{:S(2)}) %all-to-all-start) | async-done | bytes 262176 | tf_op jit(solution)/shard_map/all_to_all | solution.py:82
  79.5 5.3 %all-to-all-start.2 = ((f32[32,1,2048]{2,1,0:T(1,128)}), f32[32,1,2048]{2,1,0:T(1,128)S(1)}, u32[]{:S(2)}, u32[]{:S(2)}) async-start(f32[32,1,2048]{2,1,0:T(1,128)} %bitcast.54), calls=%async_computation.2 | async-start | bytes 524288 | tf_op jit(solution)/shard_map/all_to_all | solution.py:82
  85.3 1.3 %fusion.13 = bf16[4,128,256]{2,1,0:T(8,128)(2,1)S(1)} fusion(f32[4,128,256]{2,1,0:T(8,128)S(1)} %convolution_add_fusion.4, bf16[256,4,128]{0,2,1:T(8,128)(2,1)} %bitcast.231, bf16[4,256,256]{2,1,0:T(8,128)(2,1)S(1)} %fusion.9), kind=kOutput, calls=%fused_computation.30 | convolution fusion | flops 67502080 | bytes 1572864 | tf_op jit(solution)/shard_map/hij,jhd->ihd/dot_general | solution.py:256
  88.3 1.4 %reduce.6 = bf16[8,8192]{1,0:T(8,128)(2,1)S(1)} reduce(bf16[8,1,8192]{2,1,0:T(2,128)(2,1)S(1)} %broadcast_in_dim.65, bf16[]{:T(256)} %broadcast.604), dimensions={1}, to_apply=%broadcast_in_dim.65.reduce_sub_computation | reduce | bytes 262146 | tf_op jit(solution)/shard_map/broadcast_in_dim | solution.py:84
  90.4 5.6 %all-to-all-done.2 = f32[32,1,2048]{2,1,0:T(1,128)S(1)} async-done(((f32[32,1,2048]{2,1,0:T(1,128)}), f32[32,1,2048]{2,1,0:T(1,128)S(1)}, u32[]{:S(2)}, u32[]{:S(2)}) %all-to-all-start.2) | async-done | bytes 262176 | tf_op jit(solution)/shard_map/all_to_all | solution.py:82
  96.0 3.4 %all-to-all-start.1 = ((bf16[8,2,4096]{2,1,0:T(2,128)(2,1)}), bf16[8,2,4096]{2,1,0:T(2,128)(2,1)S(1)}, u32[]{:S(2)}, u32[]{:S(2)}) async-start(bf16[8,2,4096]{2,1,0:T(2,128)(2,1)} %reshape.751), calls=%async_computation.1 | async-start | bytes 262144 | tf_op jit(solution)/shard_map/all_to_all | solution.py:85
  99.4 1.4 %fusion.18 = bf16[2,256,512]{2,1,0:T(8,128)(2,1)S(1)} fusion(f32[1,256,512]{2,1,0:T(8,128)S(1)} %copy-done.2, f32[1,256,512]{2,1,0:T(8,128)S(1)} %copy.162, bf16[2,256,512]{2,1,0:T(8,128)(2,1)} %collective-permute-done.4, bf16[2,256,512]{2,1,0:T(8,128)(2,1)} %collective-permute-done.5), kind=kLoop, calls=%fused_computation.40 | loop fusion | flops 1572864 | bytes 2621440 | tf_op jit(solution)/shard_map/convert.5
  101.1 1.4 %reduce.7 = bf16[32,2048]{1,0:T(8,128)(2,1)S(1)} reduce(bf16[32,1,2048]{2,1,0:T(2,128)(2,1)S(1)} %broadcast_in_dim.66, bf16[]{:T(256)} %broadcast.604), dimensions={1}, to_apply=%broadcast_in_dim.66.reduce_sub_computation | reduce | bytes 262146 | tf_op jit(solution)/shard_map/broadcast_in_dim | solution.py:84
  103.2 3.4 %all-to-all-done.1 = bf16[8,2,4096]{2,1,0:T(2,128)(2,1)S(1)} async-done(((bf16[8,2,4096]{2,1,0:T(2,128)(2,1)}), bf16[8,2,4096]{2,1,0:T(2,128)(2,1)S(1)}, u32[]{:S(2)}, u32[]{:S(2)}) %all-to-all-start.1) | async-done | bytes 131104 | tf_op jit(solution)/shard_map/all_to_all | solution.py:85
  106.6 2.6 %all-to-all-start.3 = ((bf16[32,2,1024]{2,1,0:T(2,128)(2,1)}), bf16[32,2,1024]{2,1,0:T(2,128)(2,1)S(1)}, u32[]{:S(2)}, u32[]{:S(2)}) async-start(bf16[32,2,1024]{2,1,0:T(2,128)(2,1)} %reshape.753), calls=%async_computation.3 | async-start | bytes 262144 | tf_op jit(solution)/shard_map/all_to_all | solution.py:85
  111.6 5.8 %all-to-all-done.3 = bf16[32,2,1024]{2,1,0:T(2,128)(2,1)S(1)} async-done(((bf16[32,2,1024]{2,1,0:T(2,128)(2,1)}), bf16[32,2,1024]{2,1,0:T(2,128)(2,1)S(1)}, u32[]{:S(2)}, u32[]{:S(2)}) %all-to-all-start.3) | async-done | bytes 131104 | tf_op jit(solution)/shard_map/all_to_all | solution.py:85
  117.5 1.0 convert_element_type.147
  (171 shorter events, 37.3 us)
Async XLA Ops:
  0.6 26.7 %copy-start = (bf16[512,512]{1,0:T(8,128)(2,1)S(1)}, bf16[512,512]{1,0:T(8,128)(2,1)}, u32[]{:S(2)}) copy-start(bf16[512,512]{1,0:T(8,128)(2,1)} %param.19) | copy-start | bytes 1572868
  0.6 1.2 copy-start.14
  2.0 12.0 %copy-start.3 = (bf16[2,256,512]{1,2,0:T(8,128)(2,1)}, bf16[2,256,512]{1,2,0:T(8,128)(2,1)S(1)}, u32[]{:S(2)}) copy-start(bf16[2,256,512]{1,2,0:T(8,128)(2,1)S(1)} %pad_maximum_fusion) | copy-start | bytes 1572868
  2.0 18.9 %collective-permute-start.1 = (bf16[2,256,512]{1,2,0:T(8,128)(2,1)S(1)}, bf16[2,256,512]{1,2,0:T(8,128)(2,1)S(1)}, u32[]{:S(2)}, u32[]{:S(2)}) collective-permute-start(bf16[2,256,512]{1,2,0:T(8,128)(2,1)S(1)} %pad_maximum_fusion), channel_id=1, source_target_pairs={{0,8},{4,12},{8,16},{12,20},{16,24},{20,28},{1,9},{5,13},{9,17},{1... | collective-permute-start | bytes 1572872 | tf_op jit(solution)/shard_map/ppermute | solution.py:15
  7.0 16.5 %collective-permute-start = (bf16[2,256,512]{1,2,0:T(8,128)(2,1)S(1)}, bf16[2,256,512]{1,2,0:T(8,128)(2,1)}, u32[]{:S(2)}, u32[]{:S(2)}) collective-permute-start(bf16[2,256,512]{1,2,0:T(8,128)(2,1)S(1)} %pad_maximum_fusion), channel_id=1, source_target_pairs={{0,4},{4,8},{8,12},{12,16},{16,20},{20,24},{24,28},{1,5},{5,9},{9,... | collective-permute-start | bytes 1572872 | tf_op jit(solution)/shard_map/ppermute | solution.py:15
  11.3 1.6 %copy-start.36 = (s32[1,6]{1,0:T(1,128)S(1)}, s32[1,6]{1,0:T(1,128)}, u32[]{:S(2)}) copy-start(s32[1,6]{1,0:T(1,128)} %param.16) | copy-start | bytes 76
  11.4 2.7 %copy-start.27 = (bf16[1,256,512]{2,1,0:T(8,128)(2,1)S(1)}, bf16[1,256,512]{2,1,0:T(8,128)(2,1)}, u32[]{:S(2)}) copy-start(bf16[1,256,512]{2,1,0:T(8,128)(2,1)} %param.10) | copy-start | bytes 786436
  14.9 5.3 %copy-start.31 = (s32[1,256]{1,0:T(1,128)}, s32[1,256]{1,0:T(1,128)S(1)}, u32[]{:S(2)}) copy-start(s32[1,256]{1,0:T(1,128)S(1)} %get-tuple-element.71) | copy-start | bytes 3076
  19.2 5.4 %copy-start.29 = (pred[256,256]{1,0:T(8,128)(4,1)}, pred[256,256]{1,0:T(8,128)(4,1)S(1)}, u32[]{:S(2)}) copy-start(pred[256,256]{1,0:T(8,128)(4,1)S(1)} %copy.139) | copy-start | bytes 196612
  24.6 1.6 %copy-start.15 = (bf16[1,256,512]{1,2,0:T(8,128)(2,1)}, bf16[1,256,512]{1,2,0:T(8,128)(2,1)S(1)}, u32[]{:S(2)}) copy-start(bf16[1,256,512]{1,2,0:T(8,128)(2,1)S(1)} %get-tuple-element.62) | copy-start | bytes 786436
  24.6 1.6 %copy-start.17 = (bf16[1,256,512]{1,2,0:T(8,128)(2,1)}, bf16[1,256,512]{1,2,0:T(8,128)(2,1)S(1)}, u32[]{:S(2)}) copy-start(bf16[1,256,512]{1,2,0:T(8,128)(2,1)S(1)} %get-tuple-element.61) | copy-start | bytes 786436
  24.7 1.5 %copy-start.9 = (f32[256,4,128]{0,2,1:T(8,128)S(1)}, f32[256,4,128]{0,2,1:T(8,128)}, u32[]{:S(2)}) copy-start(f32[256,4,128]{0,2,1:T(8,128)} %convolution_bitcast_fusion.2) | copy-start | bytes 1572868
  29.5 4.2 %copy-start.12 = (bf16[256,512]{1,0:T(8,128)(2,1)}, bf16[256,512]{1,0:T(8,128)(2,1)S(1)}, u32[]{:S(2)}) copy-start(bf16[256,512]{1,0:T(8,128)(2,1)S(1)} %get-tuple-element.52) | copy-start | bytes 786436
  29.5 1.1 copy-start.11
  32.6 1.2 %copy-start.39 = (f32[4,256,256]{2,1,0:T(8,128)S(1)}, f32[4,256,256]{2,1,0:T(8,128)}, u32[]{:S(2)}) copy-start(f32[4,256,256]{2,1,0:T(8,128)} %get-tuple-element.80) | copy-start | bytes 3145732
  32.8 1.2 copy-start.18
  32.9 1.2 copy-start.30
  40.3 1.0 copy-start.6
  40.3 1.4 %copy-start.38 = (f32[4,256,256]{2,1,0:T(8,128)S(1)}, f32[4,256,256]{2,1,0:T(8,128)}, u32[]{:S(2)}) copy-start(f32[4,256,256]{2,1,0:T(8,128)} %get-tuple-element.76) | copy-start | bytes 3145732
  40.7 1.1 copy-start.13
  40.7 2.0 %collective-permute-start.2 = (f32[2,65536]{1,0:T(2,128)S(1)}, f32[2,65536]{1,0:T(2,128)S(1)}, u32[]{:S(2)}, u32[]{:S(2)}) collective-permute-start(f32[2,65536]{1,0:T(2,128)S(1)} %bitcast.232), channel_id=1, source_target_pairs={{0,1},{1,0},{2,3},{3,2},{4,5},{5,4},{6,7},{7,6},{8,9},{9,8},{10,11... | collective-permute-start | bytes 1572872 | tf_op jit(solution)/shard_map/ppermute | solution.py:21
  44.2 8.7 %collective-permute-start.3 = (f32[1,65536]{1,0:T(1,128)}, f32[1,65536]{1,0:T(1,128)}, u32[]{:S(2)}, u32[]{:S(2)}) collective-permute-start(f32[1,65536]{1,0:T(1,128)} %constant_dynamic-slice_fusion), channel_id=1, source_target_pairs={{0,2},{1,3},{2,0},{3,1},{4,6},{5,7},{6,4},{7,5},{8,10},{9,11},{10,... | collective-permute-start | bytes 786440 | tf_op jit(solution)/shard_map/ppermute | solution.py:21
  46.7 1.1 copy-start.21
  48.6 24.2 %collective-permute-start.4 = (bf16[2,256,512]{2,1,0:T(8,128)(2,1)}, bf16[2,256,512]{2,1,0:T(8,128)(2,1)}, u32[]{:S(2)}, u32[]{:S(2)}) collective-permute-start(bf16[2,256,512]{2,1,0:T(8,128)(2,1)} %pad_maximum_fusion.1), channel_id=1, source_target_pairs={{8,0},{12,4},{16,8},{20,12},{24,16},{28,20},{9,1},{13,5},{17,9},{2... | collective-permute-start | bytes 1572872 | tf_op jit(solution)/shard_map/ppermute | solution.py:15
  55.5 24.0 %all-to-all-start = ((f32[8,1,8192]{2,1,0:T(1,128)}), f32[8,1,8192]{2,1,0:T(1,128)S(1)}, u32[]{:S(2)}, u32[]{:S(2)}) async-start(f32[8,1,8192]{2,1,0:T(1,128)} %bitcast.52), calls=%async_computation | async-start | bytes 524288 | tf_op jit(solution)/shard_map/all_to_all | solution.py:82
  70.0 2.2 %copy-start.16 = (bf16[1,256,512]{1,2,0:T(8,128)(2,1)S(1)}, bf16[1,256,512]{1,2,0:T(8,128)(2,1)}, u32[]{:S(2)}) copy-start(bf16[1,256,512]{1,2,0:T(8,128)(2,1)} %copy-done.15) | copy-start | bytes 786436
  70.9 28.4 %collective-permute-start.5 = (bf16[2,256,512]{2,1,0:T(8,128)(2,1)}, bf16[2,256,512]{2,1,0:T(8,128)(2,1)}, u32[]{:S(2)}, u32[]{:S(2)}) collective-permute-start(bf16[2,256,512]{2,1,0:T(8,128)(2,1)} %pad_maximum_fusion.2), channel_id=1, source_target_pairs={{4,0},{8,4},{12,8},{16,12},{20,16},{24,20},{28,24},{5,1},{9,5},{13... | collective-permute-start | bytes 1572872 | tf_op jit(solution)/shard_map/ppermute | solution.py:15
  72.5 1.8 %copy-start.37 = (f32[4,256,256]{2,1,0:T(8,128)S(1)}, f32[4,256,256]{2,1,0:T(8,128)}, u32[]{:S(2)}) copy-start(f32[4,256,256]{2,1,0:T(8,128)} %get-tuple-element.78) | copy-start | bytes 3145732
  79.5 16.5 %all-to-all-start.2 = ((f32[32,1,2048]{2,1,0:T(1,128)}), f32[32,1,2048]{2,1,0:T(1,128)S(1)}, u32[]{:S(2)}, u32[]{:S(2)}) async-start(f32[32,1,2048]{2,1,0:T(1,128)} %bitcast.54), calls=%async_computation.2 | async-start | bytes 524288 | tf_op jit(solution)/shard_map/all_to_all | solution.py:82
  87.7 11.6 %copy-start.2 = (f32[1,256,512]{2,1,0:T(8,128)S(1)}, f32[1,256,512]{2,1,0:T(8,128)}, u32[]{:S(2)}) copy-start(f32[1,256,512]{2,1,0:T(8,128)} %copy.163) | copy-start | bytes 1572868
  96.0 10.7 %all-to-all-start.1 = ((bf16[8,2,4096]{2,1,0:T(2,128)(2,1)}), bf16[8,2,4096]{2,1,0:T(2,128)(2,1)S(1)}, u32[]{:S(2)}, u32[]{:S(2)}) async-start(bf16[8,2,4096]{2,1,0:T(2,128)(2,1)} %reshape.751), calls=%async_computation.1 | async-start | bytes 262144 | tf_op jit(solution)/shard_map/all_to_all | solution.py:85
  106.6 10.8 %all-to-all-start.3 = ((bf16[32,2,1024]{2,1,0:T(2,128)(2,1)}), bf16[32,2,1024]{2,1,0:T(2,128)(2,1)S(1)}, u32[]{:S(2)}, u32[]{:S(2)}) async-start(bf16[32,2,1024]{2,1,0:T(2,128)(2,1)} %reshape.753), calls=%async_computation.3 | async-start | bytes 262144 | tf_op jit(solution)/shard_map/all_to_all | solution.py:85
  (18 other events, 16.3 us)

commit v18 on v17

--- a/solution.py
+++ b/solution.py
@@ -213,8 +213,8 @@
         mixed, grad_rows, (((0,), (0,)), ((), ())), preferred_element_type=jnp.float32
     )
     weight_plan = [("split", "dp", mask) for mask in axis_bits("dp")]
-    weight_plan.append(("skip", "ctx", 0))
     weight_plan.append(("exchange", "ctx", 0))
+    weight_plan += [("skip", "ctx", 0), ("tie", "ctx", 0)]
     weight_state = [weight_term.reshape(dp_size, -1), 0]
 
     def slot(anchor):
@@ -223,7 +223,7 @@
             kind, axis, mask = weight_plan[done]
             if kind != "skip":
                 blocks, anchor = lax.optimization_barrier((blocks, anchor))
-            if kind == "skip":
+            if kind in ("skip", "tie"):
                 weight_state[0] = blocks
             elif kind == "exchange":
                 weight_state[0] = summed_by_exchange(blocks.reshape(-1), (axis,))

time: 119 us -> 123 us (1.034)
  waiting for transfers between devices: 20.6 us -> 28 us
  starting transfers between devices: 37.4 us -> 34.6 us
  local copies, waits for them, and re-layouts: 27.7 us -> 26.2 us
    all_to_all x2, waiting for transfers between devices: 8.24 us -> 12.9 us  [summed_by_exchange(): pieces = lax.all_to_all(flat.reshape(size, -1), axes, 0, 0, tiled=True)]
    all_to_all x2, starting transfers between devices: 18 us -> 14.2 us  [summed_by_exchange(): pieces = lax.all_to_all(flat.reshape(size, -1), axes, 0, 0, tiled=True)]
    all_to_all x2, waiting for transfers between devices: 9.18 us -> 11.3 us  [summed_by_exchange(): gathered = lax.all_to_all(spread, axes, 0, 0, tiled=True)]
    unnamed x91 -> x83, local copies, waits for them, and re-layouts: 11.6 us -> 10.5 us
  transfers between devices with their start and end apart: 10 -> 10, of which waited for: 6 -> 6; matrix products, arithmetic and copies ran while one was open for 28% -> 29% of each run, Pallas kernels for 0% -> 0%
where the time goes in v18:
time: 123 us; the launch traced here: 122 us
  starting transfers between devices  34.6 us (28%)
  waiting for transfers between devices  28 us (23%)
  local copies, waits for them, and re-layouts  26.2 us (21%)
  matrix products  17.3 us (14%)
  other arithmetic  13.9 us (11%)
  between operations  1.47 us (1%)
    all_to_all x2, starting transfers between devices, summed_by_exchange(): pieces = lax.all_to_all(flat.reshape(size, -1), axes, 0, 0, tiled=True)  14.2 us
    all_to_all x2, waiting for transfers between devices, summed_by_exchange(): pieces = lax.all_to_all(flat.reshape(size, -1), axes, 0, 0, tiled=True)  12.9 us
    ppermute x4, starting transfers between devices, passed_along(): return lax.ppermute(value, axis, pairs)  11.9 us
    all_to_all x2, waiting for transfers between devices, summed_by_exchange(): gathered = lax.all_to_all(spread, axes, 0, 0, tiled=True)  11.3 us
    unnamed x83, local copies, waits for them, and re-layouts  10.5 us
    all_to_all x2, starting transfers between devices, summed_by_exchange(): gathered = lax.all_to_all(spread, axes, 0, 0, tiled=True)  6.82 us
    ppermute x2, waiting for transfers between devices, exchanged(): return lax.ppermute(value, axis, pairs)  3.83 us
    dot_general x3, matrix products, shards(): jnp.einsum('ihd,jhd->hij', query_heads, forward_key_heads, preferred_elem...  3.35 us
  transfers between devices with their start and end apart: 10, of which 6 were waited for; matrix products, arithmetic and copies ran while one was open for 29% of the time, Pallas kernels for 0%

profile of v18, /device:TPU:0, one launch (start us, length us, event | category | flops | bytes accessed | tf_op | source)
XLA Modules:
  0.0 121.5 jit_solution(18138562814558212942)
XLA Ops:
  0.7 1.2 copy.179
  2.0 5.8 %collective-permute-start.1 = (bf16[2,256,512]{1,2,0:T(8,128)(2,1)S(1)}, bf16[2,256,512]{1,2,0:T(8,128)(2,1)}, u32[]{:S(2)}, u32[]{:S(2)}) collective-permute-start(bf16[2,256,512]{1,2,0:T(8,128)(2,1)S(1)} %pad_maximum_fusion), channel_id=1, source_target_pairs={{0,8},{4,12},{8,16},{12,20},{16,24},{20,28},{1,9},{5,13},{9,17},{1... | collective-permute-start | bytes 1572872 | tf_op jit(solution)/shard_map/ppermute | solution.py:15
  7.8 3.4 %collective-permute-start = (bf16[2,256,512]{1,2,0:T(8,128)(2,1)S(1)}, bf16[2,256,512]{1,2,0:T(8,128)(2,1)S(1)}, u32[]{:S(2)}, u32[]{:S(2)}) collective-permute-start(bf16[2,256,512]{1,2,0:T(8,128)(2,1)S(1)} %pad_maximum_fusion), channel_id=1, source_target_pairs={{0,4},{4,8},{8,12},{12,16},{16,20},{20,24},{24,28},{1,5},{5,9},{9,... | collective-permute-start | bytes 1572872 | tf_op jit(solution)/shard_map/ppermute | solution.py:15
  15.8 1.5 %select_convert_fusion.2 = (bf16[4,256,256]{2,1,0:T(8,128)(2,1)S(1)}, f32[4,256,256]{2,1,0:T(8,128)}) fusion(pred[256,256]{1,0:T(8,128)(4,1)S(1)} %copy.130, f32[4,256,256]{2,1,0:T(8,128)S(1)} %convolution_multiply_fusion.5, bf16[4,256,128]{2,1,0:T(8,128)(2,1)S(1)} %fusion.16, s32[256]{0:T(256)S(1)} %bitcast.248), kind=kOutput, calls=%fused_computation.45 | convolution fusion | flops 68976640 | bytes 2950144 | tf_op jit(solution)/shard_map/vqx,px->vqp/dot_general | solution.py:161
  18.1 1.1 convolution_bitcast_fusion.2
  21.1 1.1 fusion.66
  22.1 1.5 %select_convert_fusion = (bf16[4,256,256]{2,1,0:T(8,128)(2,1)S(1)}, f32[4,256,256]{2,1,0:T(8,128)}) fusion(pred[256,256]{1,0:T(8,128)(4,1)S(1)} %copy.143, f32[4,256,256]{2,1,0:T(8,128)S(1)} %fusion.48, bf16[256,4,128]{0,2,1:T(8,128)(2,1)S(1)} %bitcast.210, bf16[256,4,128]{0,2,1:T(8,128)(2,1)S(1)} %bitcast.239), kind=kOutput, calls=%fused_computation.41 | convolution fusion | flops 69206016 | bytes 3211264 | tf_op jit(solution)/shard_map/ihd,jhd->hij/dot_general | solution.py:176
  25.3 1.5 %select_convert_fusion.1 = (bf16[4,256,256]{2,1,0:T(8,128)(2,1)S(1)}, f32[4,256,256]{2,1,0:T(8,128)}) fusion(pred[256,256]{1,0:T(8,128)(4,1)S(1)} %copy.138, f32[4,256,256]{2,1,0:T(8,128)S(1)} %fusion.44, bf16[256,4,128]{0,2,1:T(8,128)(2,1)S(1)} %bitcast.211, bf16[256,4,128]{0,2,1:T(8,128)(2,1)S(1)} %bitcast.240), kind=kOutput, calls=%fused_computation.43 | convolution fusion | flops 69206016 | bytes 3211264 | tf_op jit(solution)/shard_map/ihd,jhd->hij/dot_general | solution.py:176
  31.4 0.9 convolution_convert_fusion.1
  32.7 1.0 copy.162
  38.9 1.1 fusion.63
  41.6 1.6 %collective-permute-start.3 = (f32[1,65536]{1,0:T(1,128)S(1)}, f32[1,65536]{1,0:T(1,128)}, u32[]{:S(2)}, u32[]{:S(2)}) collective-permute-start(f32[1,65536]{1,0:T(1,128)S(1)} %constant_dynamic-slice_fusion), channel_id=1, source_target_pairs={{0,2},{1,3},{2,0},{3,1},{4,6},{5,7},{6,4},{7,5},{8,10},{9,11},{10,... | collective-permute-start | bytes 786440 | tf_op jit(solution)/shard_map/ppermute | solution.py:21
  45.2 1.4 %collective-permute-start.4 = (bf16[2,256,512]{2,1,0:T(8,128)(2,1)}, bf16[2,256,512]{2,1,0:T(8,128)(2,1)}, u32[]{:S(2)}, u32[]{:S(2)}) collective-permute-start(bf16[2,256,512]{2,1,0:T(8,128)(2,1)} %pad_maximum_fusion.1), channel_id=1, source_target_pairs={{8,0},{12,4},{16,8},{20,12},{24,16},{28,20},{9,1},{13,5},{17,9},{2... | collective-permute-start | bytes 1572872 | tf_op jit(solution)/shard_map/ppermute | solution.py:15
  46.6 3.6 %collective-permute-done.3 = f32[1,65536]{1,0:T(1,128)} collective-permute-done((f32[1,65536]{1,0:T(1,128)S(1)}, f32[1,65536]{1,0:T(1,128)}, u32[]{:S(2)}, u32[]{:S(2)}) %collective-permute-start.3) | collective-permute-done | bytes 262176 | tf_op jit(solution)/shard_map/ppermute | solution.py:21
  50.2 2.0 %dynamic-slice_add_fusion = f32[1,65536]{1,0:T(1,128)} fusion(f32[1,65536]{1,0:T(1,128)} %collective-permute-done.3, f32[2,65536]{1,0:T(2,128)S(1)} %bitcast_add_fusion, s32[]{:T(128)S(6)} %select_n.144), kind=kLoop, calls=%fused_computation.68 | loop fusion | flops 65536 | bytes 786436 | tf_op jit(solution)/shard_map/add | solution.py:71
  52.3 11.7 %all-to-all-start = ((f32[8,1,8192]{2,1,0:T(1,128)}), f32[8,1,8192]{2,1,0:T(1,128)S(1)}, u32[]{:S(2)}, u32[]{:S(2)}) async-start(f32[8,1,8192]{2,1,0:T(1,128)} %bitcast.41), calls=%async_computation | async-start | bytes 524288 | tf_op jit(solution)/shard_map/all_to_all | solution.py:82
  63.9 1.7 %fusion.8 = bf16[4,256,256]{2,1,0:T(8,128)(2,1)S(1)} fusion(bf16[256,4,128]{0,2,1:T(8,128)(2,1)S(1)} %bitcast.236, f32[4,256,256]{2,1,0:T(8,128)} %get-tuple-element.86, pred[256,256]{1,0:T(8,128)(4,1)S(1)} %copy.138, bf16[256,512]{1,0:T(8,128)(2,1)S(1)} %copy-done.13), kind=kOutput, calls=%fused_computation.15 | convolution fusion | flops 69730304 | bytes 2162688 | tf_op jit(solution)/shard_map/ihd,jhd->hij/dot_general | solution.py:246
  65.7 0.9 fusion.15
  66.9 1.1 copy.165
  68.9 1.3 %collective-permute-start.5 = (bf16[2,256,512]{2,1,0:T(8,128)(2,1)}, bf16[2,256,512]{2,1,0:T(8,128)(2,1)}, u32[]{:S(2)}, u32[]{:S(2)}) collective-permute-start(bf16[2,256,512]{2,1,0:T(8,128)(2,1)} %pad_maximum_fusion.2), channel_id=1, source_target_pairs={{4,0},{8,4},{12,8},{16,12},{20,16},{24,20},{28,24},{5,1},{9,5},{13... | collective-permute-start | bytes 1572872 | tf_op jit(solution)/shard_map/ppermute | solution.py:15
  70.9 3.9 %all-to-all-done = f32[8,1,8192]{2,1,0:T(1,128)S(1)} async-done(((f32[8,1,8192]{2,1,0:T(1,128)}), f32[8,1,8192]{2,1,0:T(1,128)S(1)}, u32[]{:S(2)}, u32[]{:S(2)}) %all-to-all-start) | async-done | bytes 262176 | tf_op jit(solution)/shard_map/all_to_all | solution.py:82
  75.6 1.4 %reduce.4 = bf16[8,8192]{1,0:T(8,128)(2,1)S(1)} reduce(bf16[8,1,8192]{2,1,0:T(2,128)(2,1)S(1)} %broadcast_in_dim.64, bf16[]{:T(256)} %broadcast.603), dimensions={1}, to_apply=%broadcast_in_dim.64.reduce_sub_computation | reduce | bytes 262146 | tf_op jit(solution)/shard_map/broadcast_in_dim | solution.py:84
  77.7 4.2 %all-to-all-start.1 = ((bf16[8,2,4096]{2,1,0:T(2,128)(2,1)}), bf16[8,2,4096]{2,1,0:T(2,128)(2,1)S(1)}, u32[]{:S(2)}, u32[]{:S(2)}) async-start(bf16[8,2,4096]{2,1,0:T(2,128)(2,1)} %reshape.755), calls=%async_computation.1 | async-start | bytes 262144 | tf_op jit(solution)/shard_map/all_to_all | solution.py:85
  82.4 7.0 %all-to-all-done.1 = bf16[8,2,4096]{2,1,0:T(2,128)(2,1)S(1)} async-done(((bf16[8,2,4096]{2,1,0:T(2,128)(2,1)}), bf16[8,2,4096]{2,1,0:T(2,128)(2,1)S(1)}, u32[]{:S(2)}, u32[]{:S(2)}) %all-to-all-start.1) | async-done | bytes 131104 | tf_op jit(solution)/shard_map/all_to_all | solution.py:85
  89.5 1.0 convert_element_type.146
  94.0 2.6 %all-to-all-start.2 = ((f32[32,1,2048]{2,1,0:T(1,128)}), f32[32,1,2048]{2,1,0:T(1,128)S(1)}, u32[]{:S(2)}, u32[]{:S(2)}) async-start(f32[32,1,2048]{2,1,0:T(1,128)} %bitcast.57), calls=%async_computation.2 | async-start | bytes 524288 | tf_op jit(solution)/shard_map/all_to_all | solution.py:82
  98.1 9.1 %all-to-all-done.2 = f32[32,1,2048]{2,1,0:T(1,128)S(1)} async-done(((f32[32,1,2048]{2,1,0:T(1,128)}), f32[32,1,2048]{2,1,0:T(1,128)S(1)}, u32[]{:S(2)}, u32[]{:S(2)}) %all-to-all-start.2) | async-done | bytes 262176 | tf_op jit(solution)/shard_map/all_to_all | solution.py:82
  107.5 1.4 %reduce.5 = bf16[32,2048]{1,0:T(8,128)(2,1)S(1)} reduce(bf16[32,1,2048]{2,1,0:T(2,128)(2,1)S(1)} %broadcast_in_dim.66, bf16[]{:T(256)} %broadcast.603), dimensions={1}, to_apply=%broadcast_in_dim.66.reduce_sub_computation | reduce | bytes 262146 | tf_op jit(solution)/shard_map/broadcast_in_dim | solution.py:84
  109.7 2.6 %all-to-all-start.3 = ((bf16[32,2,1024]{2,1,0:T(2,128)(2,1)}), bf16[32,2,1024]{2,1,0:T(2,128)(2,1)S(1)}, u32[]{:S(2)}, u32[]{:S(2)}) async-start(bf16[32,2,1024]{2,1,0:T(2,128)(2,1)} %reshape.757), calls=%async_computation.3 | async-start | bytes 262144 | tf_op jit(solution)/shard_map/all_to_all | solution.py:85
  112.3 1.5 %fusion.18 = bf16[2,256,512]{2,1,0:T(8,128)(2,1)S(1)} fusion(f32[1,256,512]{2,1,0:T(8,128)S(1)} %copy-done.2, f32[1,256,512]{2,1,0:T(8,128)S(1)} %copy.161, bf16[2,256,512]{2,1,0:T(8,128)(2,1)} %collective-permute-done.4, bf16[2,256,512]{2,1,0:T(8,128)(2,1)} %collective-permute-done.5), kind=kLoop, calls=%fused_computation.40 | loop fusion | flops 1572864 | bytes 2621440 | tf_op jit(solution)/shard_map/convert.5
  116.2 4.3 %all-to-all-done.3 = bf16[32,2,1024]{2,1,0:T(2,128)(2,1)S(1)} async-done(((bf16[32,2,1024]{2,1,0:T(2,128)(2,1)}), bf16[32,2,1024]{2,1,0:T(2,128)(2,1)S(1)}, u32[]{:S(2)}, u32[]{:S(2)}) %all-to-all-start.3) | async-done | bytes 131104 | tf_op jit(solution)/shard_map/all_to_all | solution.py:85
  120.6 1.0 convert_element_type.147
  (164 shorter events, 34.9 us)
Async XLA Ops:
  0.6 26.8 %copy-start = (bf16[512,512]{1,0:T(8,128)(2,1)S(1)}, bf16[512,512]{1,0:T(8,128)(2,1)}, u32[]{:S(2)}) copy-start(bf16[512,512]{1,0:T(8,128)(2,1)} %param.19) | copy-start | bytes 1572868
  0.6 1.2 copy-start.15
  2.0 12.1 %copy-start.3 = (bf16[2,256,512]{1,2,0:T(8,128)(2,1)}, bf16[2,256,512]{1,2,0:T(8,128)(2,1)S(1)}, u32[]{:S(2)}) copy-start(bf16[2,256,512]{1,2,0:T(8,128)(2,1)S(1)} %pad_maximum_fusion) | copy-start | bytes 1572868
  2.0 19.0 %collective-permute-start.1 = (bf16[2,256,512]{1,2,0:T(8,128)(2,1)S(1)}, bf16[2,256,512]{1,2,0:T(8,128)(2,1)}, u32[]{:S(2)}, u32[]{:S(2)}) collective-permute-start(bf16[2,256,512]{1,2,0:T(8,128)(2,1)S(1)} %pad_maximum_fusion), channel_id=1, source_target_pairs={{0,8},{4,12},{8,16},{12,20},{16,24},{20,28},{1,9},{5,13},{9,17},{1... | collective-permute-start | bytes 1572872 | tf_op jit(solution)/shard_map/ppermute | solution.py:15
  7.8 16.7 %collective-permute-start = (bf16[2,256,512]{1,2,0:T(8,128)(2,1)S(1)}, bf16[2,256,512]{1,2,0:T(8,128)(2,1)S(1)}, u32[]{:S(2)}, u32[]{:S(2)}) collective-permute-start(bf16[2,256,512]{1,2,0:T(8,128)(2,1)S(1)} %pad_maximum_fusion), channel_id=1, source_target_pairs={{0,4},{4,8},{8,12},{12,16},{16,20},{20,24},{24,28},{1,5},{5,9},{9,... | collective-permute-start | bytes 1572872 | tf_op jit(solution)/shard_map/ppermute | solution.py:15
  11.4 1.6 %copy-start.33 = (s32[1,6]{1,0:T(1,128)S(1)}, s32[1,6]{1,0:T(1,128)}, u32[]{:S(2)}) copy-start(s32[1,6]{1,0:T(1,128)} %param.16) | copy-start | bytes 76
  11.5 2.7 %copy-start.24 = (bf16[1,256,512]{2,1,0:T(8,128)(2,1)S(1)}, bf16[1,256,512]{2,1,0:T(8,128)(2,1)}, u32[]{:S(2)}) copy-start(bf16[1,256,512]{2,1,0:T(8,128)(2,1)} %param.10) | copy-start | bytes 786436
  14.2 1.6 %copy-start.26 = (pred[256,256]{1,0:T(8,128)(4,1)}, pred[256,256]{1,0:T(8,128)(4,1)S(1)}, u32[]{:S(2)}) copy-start(pred[256,256]{1,0:T(8,128)(4,1)S(1)} %copy.130) | copy-start | bytes 196612
  15.0 5.3 %copy-start.28 = (s32[1,256]{1,0:T(1,128)}, s32[1,256]{1,0:T(1,128)S(1)}, u32[]{:S(2)}) copy-start(s32[1,256]{1,0:T(1,128)S(1)} %get-tuple-element.77) | copy-start | bytes 3076
  25.3 1.5 %copy-start.11 = (f32[256,4,128]{0,2,1:T(8,128)S(1)}, f32[256,4,128]{0,2,1:T(8,128)}, u32[]{:S(2)}) copy-start(f32[256,4,128]{0,2,1:T(8,128)} %convolution_bitcast_fusion.2) | copy-start | bytes 1572868
  30.3 1.0 copy-start.10
  31.3 1.0 copy-start.8
  32.7 1.0 copy-start.20
  38.4 1.6 %copy-start.35 = (f32[4,256,256]{2,1,0:T(8,128)S(1)}, f32[4,256,256]{2,1,0:T(8,128)}, u32[]{:S(2)}) copy-start(f32[4,256,256]{2,1,0:T(8,128)} %get-tuple-element.82) | copy-start | bytes 3145732
  38.8 1.2 copy-start.13
  38.8 2.0 %collective-permute-start.2 = (f32[2,65536]{1,0:T(2,128)S(1)}, f32[2,65536]{1,0:T(2,128)S(1)}, u32[]{:S(2)}, u32[]{:S(2)}) collective-permute-start(f32[2,65536]{1,0:T(2,128)S(1)} %bitcast.234), channel_id=1, source_target_pairs={{0,1},{1,0},{2,3},{3,2},{4,5},{5,4},{6,7},{7,6},{8,9},{9,8},{10,11... | collective-permute-start | bytes 1572872 | tf_op jit(solution)/shard_map/ppermute | solution.py:21
  41.6 8.6 %collective-permute-start.3 = (f32[1,65536]{1,0:T(1,128)S(1)}, f32[1,65536]{1,0:T(1,128)}, u32[]{:S(2)}, u32[]{:S(2)}) collective-permute-start(f32[1,65536]{1,0:T(1,128)S(1)} %constant_dynamic-slice_fusion), channel_id=1, source_target_pairs={{0,2},{1,3},{2,0},{3,1},{4,6},{5,7},{6,4},{7,5},{8,10},{9,11},{10,... | collective-permute-start | bytes 786440 | tf_op jit(solution)/shard_map/ppermute | solution.py:21
  45.2 7.0 %copy-start.6 = (bf16[2,256,512]{1,2,0:T(8,128)(2,1)S(1)}, bf16[2,256,512]{1,2,0:T(8,128)(2,1)}, u32[]{:S(2)}) copy-start(bf16[2,256,512]{1,2,0:T(8,128)(2,1)} %copy-done.5) | copy-start | bytes 1572868
  45.2 45.2 %collective-permute-start.4 = (bf16[2,256,512]{2,1,0:T(8,128)(2,1)}, bf16[2,256,512]{2,1,0:T(8,128)(2,1)}, u32[]{:S(2)}, u32[]{:S(2)}) collective-permute-start(bf16[2,256,512]{2,1,0:T(8,128)(2,1)} %pad_maximum_fusion.1), channel_id=1, source_target_pairs={{8,0},{12,4},{16,8},{20,12},{24,16},{28,20},{9,1},{13,5},{17,9},{2... | collective-permute-start | bytes 1572872 | tf_op jit(solution)/shard_map/ppermute | solution.py:15
  52.3 22.5 %all-to-all-start = ((f32[8,1,8192]{2,1,0:T(1,128)}), f32[8,1,8192]{2,1,0:T(1,128)S(1)}, u32[]{:S(2)}, u32[]{:S(2)}) async-start(f32[8,1,8192]{2,1,0:T(1,128)} %bitcast.41), calls=%async_computation | async-start | bytes 524288 | tf_op jit(solution)/shard_map/all_to_all | solution.py:82
  66.9 1.2 copy-start.17
  68.9 43.4 %collective-permute-start.5 = (bf16[2,256,512]{2,1,0:T(8,128)(2,1)}, bf16[2,256,512]{2,1,0:T(8,128)(2,1)}, u32[]{:S(2)}, u32[]{:S(2)}) collective-permute-start(bf16[2,256,512]{2,1,0:T(8,128)(2,1)} %pad_maximum_fusion.2), channel_id=1, source_target_pairs={{4,0},{8,4},{12,8},{16,12},{20,16},{24,20},{28,24},{5,1},{9,5},{13... | collective-permute-start | bytes 1572872 | tf_op jit(solution)/shard_map/ppermute | solution.py:15
  77.7 4.2 %copy-start.29 = (s32[1,256]{1,0:T(1,128)S(1)}, s32[1,256]{1,0:T(1,128)}, u32[]{:S(2)}) copy-start(s32[1,256]{1,0:T(1,128)} %copy-done.28) | copy-start | bytes 3076
  77.7 11.6 %all-to-all-start.1 = ((bf16[8,2,4096]{2,1,0:T(2,128)(2,1)}), bf16[8,2,4096]{2,1,0:T(2,128)(2,1)S(1)}, u32[]{:S(2)}, u32[]{:S(2)}) async-start(bf16[8,2,4096]{2,1,0:T(2,128)(2,1)} %reshape.755), calls=%async_computation.1 | async-start | bytes 262144 | tf_op jit(solution)/shard_map/all_to_all | solution.py:85
  82.4 8.1 %copy-start.4 = (bf16[2,256,512]{1,2,0:T(8,128)(2,1)S(1)}, bf16[2,256,512]{1,2,0:T(8,128)(2,1)}, u32[]{:S(2)}) copy-start(bf16[2,256,512]{1,2,0:T(8,128)(2,1)} %copy-done.3) | copy-start | bytes 1572868
  89.5 1.7 %copy-start.34 = (f32[4,256,256]{2,1,0:T(8,128)S(1)}, f32[4,256,256]{2,1,0:T(8,128)}, u32[]{:S(2)}) copy-start(f32[4,256,256]{2,1,0:T(8,128)} %get-tuple-element.84) | copy-start | bytes 3145732
  90.4 1.0 copy-start.14
  90.5 1.1 copy-start.27
  94.0 13.2 %all-to-all-start.2 = ((f32[32,1,2048]{2,1,0:T(1,128)}), f32[32,1,2048]{2,1,0:T(1,128)S(1)}, u32[]{:S(2)}, u32[]{:S(2)}) async-start(f32[32,1,2048]{2,1,0:T(1,128)} %bitcast.57), calls=%async_computation.2 | async-start | bytes 524288 | tf_op jit(solution)/shard_map/all_to_all | solution.py:82
  107.5 4.8 %copy-start.2 = (f32[1,256,512]{2,1,0:T(8,128)S(1)}, f32[1,256,512]{2,1,0:T(8,128)}, u32[]{:S(2)}) copy-start(f32[1,256,512]{2,1,0:T(8,128)} %copy.162) | copy-start | bytes 1572868
  109.7 10.8 %all-to-all-start.3 = ((bf16[32,2,1024]{2,1,0:T(2,128)(2,1)}), bf16[32,2,1024]{2,1,0:T(2,128)(2,1)S(1)}, u32[]{:S(2)}, u32[]{:S(2)}) async-start(bf16[32,2,1024]{2,1,0:T(2,128)(2,1)} %reshape.757), calls=%async_computation.3 | async-start | bytes 262144 | tf_op jit(solution)/shard_map/all_to_all | solution.py:85
  112.2 1.5 %copy-start.16 = (f32[8,1,8192]{2,1,0:T(1,128)S(1)}, f32[8,1,8192]{2,1,0:T(1,128)}, u32[]{:S(2)}) copy-start(f32[8,1,8192]{2,1,0:T(1,128)} %convert_element_type.146) | copy-start | bytes 786436
  (14 other events, 11.9 us)

commit v19 on v7

--- a/solution.py
+++ b/solution.py
@@ -75,14 +75,25 @@
     return jnp.concatenate([low, high], axis=1)
 
 
+def collected_by_exchange(chunk, axis):
+    size = lax.axis_size(axis)
+    depth = len(axis_bits(axis))
+    spread = jnp.broadcast_to(chunk.astype(jnp.bfloat16)[None], (size, chunk.shape[0]))
+    gathered = lax.all_to_all(spread, axis, 0, 0, tiled=True)
+    gathered = gathered.reshape([2] * depth + [chunk.shape[0]])
+    gathered = gathered.transpose(list(reversed(range(depth))) + [depth])
+    return gathered.reshape(-1).astype(chunk.dtype)
+
+
 def summed_by_exchange(flat, axes):
     size = 1
     for axis in axes:
         size *= lax.axis_size(axis)
     pieces = lax.all_to_all(flat.reshape(size, -1), axes, 0, 0, tiled=True)
     total = jnp.sum(pieces, axis=0, keepdims=True)
-    spread = jnp.broadcast_to(total, pieces.shape)
-    return lax.all_to_all(spread, axes, 0, 0, tiled=True).reshape(flat.shape)
+    spread = jnp.broadcast_to(total.astype(jnp.bfloat16), pieces.shape)
+    gathered = lax.all_to_all(spread, axes, 0, 0, tiled=True)
+    return gathered.astype(flat.dtype).reshape(flat.shape)
 
 
 def silu_slope(scores):
@@ -213,7 +224,7 @@
     )
     weight_plan = [("split", "dp", mask) for mask in axis_bits("dp")]
     weight_plan += [("split", "ctx", mask) for mask in axis_bits("ctx")]
-    weight_plan += [("join", "ctx", mask) for mask in reversed(axis_bits("ctx"))]
+    weight_plan.append(("collect", "ctx", 0))
     weight_state = [weight_term.reshape(dp_size, -1), 0]
 
     def slot(anchor, tied=True):
@@ -222,7 +233,9 @@
             if tied:
                 blocks, anchor = lax.optimization_barrier((blocks, anchor))
             kind, axis, mask = weight_plan[done]
-            if kind == "exchange":
+            if kind == "collect":
+                weight_state[0] = collected_by_exchange(blocks.reshape(-1), axis)
+            elif kind == "exchange":
                 weight_state[0] = summed_by_exchange(blocks.reshape(-1), (axis,))
             else:
                 weight_state[0] = plan_step(blocks, kind, axis, mask)

time: 126 us -> 124 us (0.984)
  waiting for transfers between devices: 28.7 us -> 23.6 us
  other arithmetic: 13.5 us -> 16.9 us
  starting transfers between devices: 39.8 us -> 37.9 us
  local copies, waits for them, and re-layouts: 25.2 us -> 26.7 us
    ppermute x8 -> x5, waiting for transfers between devices: 19.5 us -> 5.35 us  [exchanged(): return lax.ppermute(value, axis, pairs)]
    all_to_all x1, waiting for transfers between devices: 0.97 us -> 6.8 us  [summed_by_exchange(): pieces = lax.all_to_all(flat.reshape(size, -1), axes, 0, 0, tiled=True)]
    ppermute x8 -> x5, starting transfers between devices: 20.2 us -> 15.1 us  [exchanged(): return lax.ppermute(value, axis, pairs)]
    all_to_all x1 -> x2, starting transfers between devices: 4.17 us -> 8.18 us  [the longest x1 5.6 us: collected_by_exchange(): gathered = lax.all_to_all(spread, axis, 0, 0, tiled=True)]
    all_to_all x1 -> x2, waiting for transfers between devices: 8.31 us -> 11.4 us  [the longest x1 5.94 us: summed_by_exchange(): gathered = lax.all_to_all(spread, axes, 0, 0, tiled=True)]
    broadcast_in_dim x0 -> x2, other arithmetic: none -> 2.84 us  [the longest x1 1.44 us: summed_by_exchange(): spread = jnp.broadcast_to(total.astype(jnp.bfloat16), pieces.shape)]
    convert_element_type x0 -> x2, other arithmetic: none -> 1.69 us  [the longest x1 0.97 us: summed_by_exchange(): return gathered.astype(flat.dtype).reshape(flat.shape)]
    convert_element_type x0 -> x4, local copies, waits for them, and re-layouts: none -> 1.39 us  [the longest x3 1.3 us: collected_by_exchange(): return gathered.reshape(-1).astype(chunk.dtype)]
  transfers between devices with their start and end apart: 14 -> 12, of which waited for: 8 -> 7; matrix products, arithmetic and copies ran while one was open for 27% -> 31% of each run, Pallas kernels for 0% -> 0%
where the time goes in v19:
time: 124 us; the launch traced here: 123 us
  starting transfers between devices  37.9 us (31%)
  local copies, waits for them, and re-layouts  26.7 us (22%)
  waiting for transfers between devices  23.6 us (19%)
  other arithmetic  16.9 us (14%)
  matrix products  16.6 us (13%)
  between operations  1.66 us (1%)
    ppermute x5, starting transfers between devices, exchanged(): return lax.ppermute(value, axis, pairs)  15.1 us
    ppermute x4, starting transfers between devices, passed_along(): return lax.ppermute(value, axis, pairs)  12.1 us
    unnamed x77, local copies, waits for them, and re-layouts  10.4 us
    all_to_all x1, waiting for transfers between devices, summed_by_exchange(): pieces = lax.all_to_all(flat.reshape(size, -1), axes, 0, 0, tiled=True)  6.8 us
    all_to_all x1, waiting for transfers between devices, summed_by_exchange(): gathered = lax.all_to_all(spread, axes, 0, 0, tiled=True)  5.94 us
    all_to_all x1, starting transfers between devices, collected_by_exchange(): gathered = lax.all_to_all(spread, axis, 0, 0, tiled=True)  5.6 us
    all_to_all x1, waiting for transfers between devices, collected_by_exchange(): gathered = lax.all_to_all(spread, axis, 0, 0, tiled=True)  5.47 us
    ppermute x5, waiting for transfers between devices, exchanged(): return lax.ppermute(value, axis, pairs)  5.35 us
  transfers between devices with their start and end apart: 12, of which 7 were waited for; matrix products, arithmetic and copies ran while one was open for 31% of the time, Pallas kernels for 0%

profile of v19, /device:TPU:0, one launch (start us, length us, event | category | flops | bytes accessed | tf_op | source)
XLA Modules:
  0.0 123.4 jit_solution(6932445185769484904)
XLA Ops:
  0.7 1.2 copy.223
  2.0 5.8 %collective-permute-start.1 = (bf16[2,256,512]{1,2,0:T(8,128)(2,1)S(1)}, bf16[2,256,512]{1,2,0:T(8,128)(2,1)}, u32[]{:S(2)}, u32[]{:S(2)}) collective-permute-start(bf16[2,256,512]{1,2,0:T(8,128)(2,1)S(1)} %pad_maximum_fusion), channel_id=1, source_target_pairs={{0,8},{4,12},{8,16},{12,20},{16,24},{20,28},{1,9},{5,13},{9,17},{1... | collective-permute-start | bytes 1572872 | tf_op jit(solution)/shard_map/ppermute | solution.py:15
  7.8 3.4 %collective-permute-start = (bf16[2,256,512]{1,2,0:T(8,128)(2,1)S(1)}, bf16[2,256,512]{1,2,0:T(8,128)(2,1)S(1)}, u32[]{:S(2)}, u32[]{:S(2)}) collective-permute-start(bf16[2,256,512]{1,2,0:T(8,128)(2,1)S(1)} %pad_maximum_fusion), channel_id=1, source_target_pairs={{0,4},{4,8},{8,12},{12,16},{16,20},{20,24},{24,28},{1,5},{5,9},{9,... | collective-permute-start | bytes 1572872 | tf_op jit(solution)/shard_map/ppermute | solution.py:15
  15.8 1.5 %select_convert_fusion.2 = (bf16[4,256,256]{2,1,0:T(8,128)(2,1)S(1)}, f32[4,256,256]{2,1,0:T(8,128)}) fusion(pred[256,256]{1,0:T(8,128)(4,1)S(1)} %copy.173, f32[4,256,256]{2,1,0:T(8,128)S(1)} %convolution_multiply_fusion.5, bf16[4,256,128]{2,1,0:T(8,128)(2,1)S(1)} %fusion.16, s32[256]{0:T(256)S(1)} %bitcast.259), kind=kOutput, calls=%fused_computation.45 | convolution fusion | flops 68976640 | bytes 2950144 | tf_op jit(solution)/shard_map/vqx,px->vqp/dot_general | solution.py:171
  18.1 1.1 convolution_bitcast_fusion.2
  21.1 1.1 fusion.66
  22.2 1.5 %select_convert_fusion = (bf16[4,256,256]{2,1,0:T(8,128)(2,1)S(1)}, f32[4,256,256]{2,1,0:T(8,128)}) fusion(pred[256,256]{1,0:T(8,128)(4,1)S(1)} %copy.186, f32[4,256,256]{2,1,0:T(8,128)S(1)} %fusion.48, bf16[256,4,128]{0,2,1:T(8,128)(2,1)S(1)} %bitcast.221, bf16[256,4,128]{0,2,1:T(8,128)(2,1)S(1)} %bitcast.250), kind=kOutput, calls=%fused_computation.41 | convolution fusion | flops 69206016 | bytes 3211264 | tf_op jit(solution)/shard_map/ihd,jhd->hij/dot_general | solution.py:186
  25.3 1.5 %select_convert_fusion.1 = (bf16[4,256,256]{2,1,0:T(8,128)(2,1)S(1)}, f32[4,256,256]{2,1,0:T(8,128)}) fusion(pred[256,256]{1,0:T(8,128)(4,1)S(1)} %copy.181, f32[4,256,256]{2,1,0:T(8,128)S(1)} %fusion.44, bf16[256,4,128]{0,2,1:T(8,128)(2,1)S(1)} %bitcast.222, bf16[256,4,128]{0,2,1:T(8,128)(2,1)S(1)} %bitcast.251), kind=kOutput, calls=%fused_computation.43 | convolution fusion | flops 69206016 | bytes 3211264 | tf_op jit(solution)/shard_map/ihd,jhd->hij/dot_general | solution.py:186
  32.7 1.0 copy.205
  38.9 1.1 fusion.63
  41.6 1.6 %collective-permute-start.3 = (f32[1,65536]{1,0:T(1,128)S(1)}, f32[1,65536]{1,0:T(1,128)}, u32[]{:S(2)}, u32[]{:S(2)}) collective-permute-start(f32[1,65536]{1,0:T(1,128)S(1)} %constant_dynamic-slice_fusion), channel_id=1, source_target_pairs={{0,2},{1,3},{2,0},{3,1},{4,6},{5,7},{6,4},{7,5},{8,10},{9,11},{10,... | collective-permute-start | bytes 786440 | tf_op jit(solution)/shard_map/ppermute | solution.py:21
  45.2 1.6 %collective-permute-start.5 = (bf16[2,256,512]{2,1,0:T(8,128)(2,1)}, bf16[2,256,512]{2,1,0:T(8,128)(2,1)}, u32[]{:S(2)}, u32[]{:S(2)}) collective-permute-start(bf16[2,256,512]{2,1,0:T(8,128)(2,1)} %pad_maximum_fusion.1), channel_id=1, source_target_pairs={{8,0},{12,4},{16,8},{20,12},{24,16},{28,20},{9,1},{13,5},{17,9},{2... | collective-permute-start | bytes 1572872 | tf_op jit(solution)/shard_map/ppermute | solution.py:15
  46.8 3.4 %collective-permute-done.3 = f32[1,65536]{1,0:T(1,128)} collective-permute-done((f32[1,65536]{1,0:T(1,128)S(1)}, f32[1,65536]{1,0:T(1,128)}, u32[]{:S(2)}, u32[]{:S(2)}) %collective-permute-start.3) | collective-permute-done | bytes 262176 | tf_op jit(solution)/shard_map/ppermute | solution.py:21
  50.2 1.3 %dynamic-slice_add_fusion = f32[1,65536]{1,0:T(1,128)S(1)} fusion(f32[1,65536]{1,0:T(1,128)} %collective-permute-done.3, f32[2,65536]{1,0:T(2,128)S(1)} %bitcast_add_fusion, s32[]{:T(128)S(6)} %select_n.184), kind=kLoop, calls=%fused_computation.69 | loop fusion | flops 65536 | bytes 786436 | tf_op jit(solution)/shard_map/add | solution.py:71
  52.1 1.3 %reduce.16 = f32[65536]{0:T(1024)S(1)} reduce(f32[1,65536]{1,0:T(1,128)S(1)} %dynamic-slice_add_fusion, f32[]{:T(128)} %broadcast.619), dimensions={0}, to_apply=%get-tuple-element.25.reduce_sub_computation.3 | reduce | bytes 524292 | tf_op jit(solution)/shard_map/optimization_barrier | solution.py:234
  53.6 6.5 %collective-permute-start.4 = (f32[1,32768]{1,0:T(1,128)S(1)}, f32[1,32768]{1,0:T(1,128)S(1)}, u32[]{:S(2)}, u32[]{:S(2)}) collective-permute-start(f32[1,32768]{1,0:T(1,128)S(1)} %dynamic-slice_bitcast_fusion), channel_id=1, source_target_pairs={{0,4},{4,0},{8,12},{12,8},{16,20},{20,16},{24,28},{28,24},{1,5},{5... | collective-permute-start | bytes 393224 | tf_op jit(solution)/shard_map/ppermute | solution.py:21
  60.1 1.7 %fusion.8 = bf16[4,256,256]{2,1,0:T(8,128)(2,1)S(1)} fusion(bf16[256,4,128]{0,2,1:T(8,128)(2,1)S(1)} %bitcast.247, f32[4,256,256]{2,1,0:T(8,128)} %get-tuple-element.100, pred[256,256]{1,0:T(8,128)(4,1)S(1)} %copy.181, bf16[256,512]{1,0:T(8,128)(2,1)S(1)} %copy-done.13), kind=kOutput, calls=%fused_computation.15 | convolution fusion | flops 69730304 | bytes 2162688 | tf_op jit(solution)/shard_map/ihd,jhd->hij/dot_general | solution.py:256
  61.9 1.3 %collective-permute-done.4 = f32[1,32768]{1,0:T(1,128)S(1)} collective-permute-done((f32[1,32768]{1,0:T(1,128)S(1)}, f32[1,32768]{1,0:T(1,128)S(1)}, u32[]{:S(2)}, u32[]{:S(2)}) %collective-permute-start.4) | collective-permute-done | bytes 131104 | tf_op jit(solution)/shard_map/ppermute | solution.py:21
  63.3 1.0 reduce.17
  65.1 3.8 %collective-permute-start.6 = (f32[1,16384]{1,0:T(1,128)}, f32[1,16384]{1,0:T(1,128)}, u32[]{:S(2)}, u32[]{:S(2)}) collective-permute-start(f32[1,16384]{1,0:T(1,128)} %dynamic-slice_bitcast_fusion.1), channel_id=1, source_target_pairs={{0,8},{4,12},{8,0},{12,4},{16,24},{20,28},{24,16},{28,20},{1,9},{5... | collective-permute-start | bytes 196616 | tf_op jit(solution)/shard_map/ppermute | solution.py:21
  73.3 3.1 %collective-permute-start.7 = (f32[1,8192]{1,0:T(1,128)S(1)}, f32[1,8192]{1,0:T(1,128)S(1)}, u32[]{:S(2)}, u32[]{:S(2)}) collective-permute-start(f32[1,8192]{1,0:T(1,128)S(1)} %dynamic-slice_bitcast_fusion.2), channel_id=1, source_target_pairs={{0,16},{4,20},{8,24},{12,28},{16,0},{20,4},{24,8},{28,12},{1,17},{... | collective-permute-start | bytes 98312 | tf_op jit(solution)/shard_map/ppermute | solution.py:21
  77.3 1.3 %collective-permute-start.8 = (bf16[2,256,512]{2,1,0:T(8,128)(2,1)}, bf16[2,256,512]{2,1,0:T(8,128)(2,1)}, u32[]{:S(2)}, u32[]{:S(2)}) collective-permute-start(bf16[2,256,512]{2,1,0:T(8,128)(2,1)} %pad_maximum_fusion.2), channel_id=1, source_target_pairs={{4,0},{8,4},{12,8},{16,12},{20,16},{24,20},{28,24},{5,1},{9,5},{13... | collective-permute-start | bytes 1572872 | tf_op jit(solution)/shard_map/ppermute | solution.py:15
  80.8 1.4 %reduce.19 = bf16[8,8192]{1,0:T(8,128)(2,1)S(1)} reduce(bf16[8,1,8192]{2,1,0:T(2,128)(2,1)S(1)} %broadcast_in_dim.65, bf16[]{:T(256)} %broadcast.622), dimensions={1}, to_apply=%broadcast_in_dim.65.reduce_sub_computation | reduce | bytes 262146 | tf_op jit(solution)/shard_map/broadcast_in_dim | solution.py:81
  82.9 5.6 %all-to-all-start = ((bf16[8,2,4096]{2,1,0:T(2,128)(2,1)}), bf16[8,2,4096]{2,1,0:T(2,128)(2,1)S(1)}, u32[]{:S(2)}, u32[]{:S(2)}) async-start(bf16[8,2,4096]{2,1,0:T(2,128)(2,1)} %reshape.776), calls=%async_computation | async-start | bytes 262144 | tf_op jit(solution)/shard_map/all_to_all | solution.py:82
  90.4 5.5 %all-to-all-done = bf16[8,2,4096]{2,1,0:T(2,128)(2,1)S(1)} async-done(((bf16[8,2,4096]{2,1,0:T(2,128)(2,1)}), bf16[8,2,4096]{2,1,0:T(2,128)(2,1)S(1)}, u32[]{:S(2)}, u32[]{:S(2)}) %all-to-all-start) | async-done | bytes 131104 | tf_op jit(solution)/shard_map/all_to_all | solution.py:82
  95.9 2.6 %all-to-all-start.1 = ((f32[32,1,2048]{2,1,0:T(1,128)}), f32[32,1,2048]{2,1,0:T(1,128)S(1)}, u32[]{:S(2)}, u32[]{:S(2)}) async-start(f32[32,1,2048]{2,1,0:T(1,128)} %bitcast.62), calls=%async_computation.1 | async-start | bytes 524288 | tf_op jit(solution)/shard_map/all_to_all | solution.py:92
  102.2 6.8 %all-to-all-done.1 = f32[32,1,2048]{2,1,0:T(1,128)S(1)} async-done(((f32[32,1,2048]{2,1,0:T(1,128)}), f32[32,1,2048]{2,1,0:T(1,128)S(1)}, u32[]{:S(2)}, u32[]{:S(2)}) %all-to-all-start.1) | async-done | bytes 262176 | tf_op jit(solution)/shard_map/all_to_all | solution.py:92
  109.4 1.4 %reduce.20 = bf16[32,2048]{1,0:T(8,128)(2,1)S(1)} reduce(bf16[32,1,2048]{2,1,0:T(2,128)(2,1)S(1)} %broadcast_in_dim.66, bf16[]{:T(256)} %broadcast.622), dimensions={1}, to_apply=%broadcast_in_dim.66.reduce_sub_computation | reduce | bytes 262146 | tf_op jit(solution)/shard_map/broadcast_in_dim | solution.py:94
  111.5 2.6 %all-to-all-start.2 = ((bf16[32,2,1024]{2,1,0:T(2,128)(2,1)}), bf16[32,2,1024]{2,1,0:T(2,128)(2,1)S(1)}, u32[]{:S(2)}, u32[]{:S(2)}) async-start(bf16[32,2,1024]{2,1,0:T(2,128)(2,1)} %reshape.778), calls=%async_computation.2 | async-start | bytes 262144 | tf_op jit(solution)/shard_map/all_to_all | solution.py:95
  114.1 1.4 %fusion.18 = bf16[2,256,512]{2,1,0:T(8,128)(2,1)S(1)} fusion(f32[1,256,512]{2,1,0:T(8,128)S(1)} %copy-done.2, f32[1,256,512]{2,1,0:T(8,128)S(1)} %copy.204, bf16[2,256,512]{2,1,0:T(8,128)(2,1)} %collective-permute-done.5, bf16[2,256,512]{2,1,0:T(8,128)(2,1)} %collective-permute-done.8), kind=kLoop, calls=%fused_computation.40 | loop fusion | flops 1572864 | bytes 2621440 | tf_op jit(solution)/shard_map/convert.7
  116.4 5.9 %all-to-all-done.2 = bf16[32,2,1024]{2,1,0:T(2,128)(2,1)S(1)} async-done(((bf16[32,2,1024]{2,1,0:T(2,128)(2,1)}), bf16[32,2,1024]{2,1,0:T(2,128)(2,1)S(1)}, u32[]{:S(2)}, u32[]{:S(2)}) %all-to-all-start.2) | async-done | bytes 131104 | tf_op jit(solution)/shard_map/all_to_all | solution.py:95
  122.4 1.0 convert_element_type.154
  (177 shorter events, 40.6 us)
Async XLA Ops:
  0.6 26.8 %copy-start = (bf16[512,512]{1,0:T(8,128)(2,1)S(1)}, bf16[512,512]{1,0:T(8,128)(2,1)}, u32[]{:S(2)}) copy-start(bf16[512,512]{1,0:T(8,128)(2,1)} %param.19) | copy-start | bytes 1572868
  0.6 1.2 copy-start.14
  2.0 12.1 %copy-start.3 = (bf16[2,256,512]{1,2,0:T(8,128)(2,1)}, bf16[2,256,512]{1,2,0:T(8,128)(2,1)S(1)}, u32[]{:S(2)}) copy-start(bf16[2,256,512]{1,2,0:T(8,128)(2,1)S(1)} %pad_maximum_fusion) | copy-start | bytes 1572868
  2.0 19.0 %collective-permute-start.1 = (bf16[2,256,512]{1,2,0:T(8,128)(2,1)S(1)}, bf16[2,256,512]{1,2,0:T(8,128)(2,1)}, u32[]{:S(2)}, u32[]{:S(2)}) collective-permute-start(bf16[2,256,512]{1,2,0:T(8,128)(2,1)S(1)} %pad_maximum_fusion), channel_id=1, source_target_pairs={{0,8},{4,12},{8,16},{12,20},{16,24},{20,28},{1,9},{5,13},{9,17},{1... | collective-permute-start | bytes 1572872 | tf_op jit(solution)/shard_map/ppermute | solution.py:15
  7.8 16.7 %collective-permute-start = (bf16[2,256,512]{1,2,0:T(8,128)(2,1)S(1)}, bf16[2,256,512]{1,2,0:T(8,128)(2,1)S(1)}, u32[]{:S(2)}, u32[]{:S(2)}) collective-permute-start(bf16[2,256,512]{1,2,0:T(8,128)(2,1)S(1)} %pad_maximum_fusion), channel_id=1, source_target_pairs={{0,4},{4,8},{8,12},{12,16},{16,20},{20,24},{24,28},{1,5},{5,9},{9,... | collective-permute-start | bytes 1572872 | tf_op jit(solution)/shard_map/ppermute | solution.py:15
  11.4 1.6 %copy-start.30 = (s32[1,6]{1,0:T(1,128)S(1)}, s32[1,6]{1,0:T(1,128)}, u32[]{:S(2)}) copy-start(s32[1,6]{1,0:T(1,128)} %param.16) | copy-start | bytes 76
  11.5 2.7 %copy-start.21 = (bf16[1,256,512]{2,1,0:T(8,128)(2,1)S(1)}, bf16[1,256,512]{2,1,0:T(8,128)(2,1)}, u32[]{:S(2)}) copy-start(bf16[1,256,512]{2,1,0:T(8,128)(2,1)} %param.10) | copy-start | bytes 786436
  14.2 1.6 %copy-start.23 = (pred[256,256]{1,0:T(8,128)(4,1)}, pred[256,256]{1,0:T(8,128)(4,1)S(1)}, u32[]{:S(2)}) copy-start(pred[256,256]{1,0:T(8,128)(4,1)S(1)} %copy.173) | copy-start | bytes 196612
  15.0 5.4 %copy-start.25 = (s32[1,256]{1,0:T(1,128)}, s32[1,256]{1,0:T(1,128)S(1)}, u32[]{:S(2)}) copy-start(s32[1,256]{1,0:T(1,128)S(1)} %get-tuple-element.91) | copy-start | bytes 3076
  25.3 1.5 %copy-start.11 = (f32[256,4,128]{0,2,1:T(8,128)S(1)}, f32[256,4,128]{0,2,1:T(8,128)}, u32[]{:S(2)}) copy-start(f32[256,4,128]{0,2,1:T(8,128)} %convolution_bitcast_fusion.2) | copy-start | bytes 1572868
  27.2 1.0 copy-start.19
  30.3 1.0 copy-start.10
  31.4 1.0 copy-start.8
  32.7 1.0 copy-start.18
  38.4 1.6 %copy-start.32 = (f32[4,256,256]{2,1,0:T(8,128)S(1)}, f32[4,256,256]{2,1,0:T(8,128)}, u32[]{:S(2)}) copy-start(f32[4,256,256]{2,1,0:T(8,128)} %get-tuple-element.96) | copy-start | bytes 3145732
  38.8 1.2 copy-start.13
  38.8 2.0 %collective-permute-start.2 = (f32[2,65536]{1,0:T(2,128)S(1)}, f32[2,65536]{1,0:T(2,128)S(1)}, u32[]{:S(2)}, u32[]{:S(2)}) collective-permute-start(f32[2,65536]{1,0:T(2,128)S(1)} %bitcast.245), channel_id=1, source_target_pairs={{0,1},{1,0},{2,3},{3,2},{4,5},{5,4},{6,7},{7,6},{8,9},{9,8},{10,11... | collective-permute-start | bytes 1572872 | tf_op jit(solution)/shard_map/ppermute | solution.py:21
  41.6 8.6 %collective-permute-start.3 = (f32[1,65536]{1,0:T(1,128)S(1)}, f32[1,65536]{1,0:T(1,128)}, u32[]{:S(2)}, u32[]{:S(2)}) collective-permute-start(f32[1,65536]{1,0:T(1,128)S(1)} %constant_dynamic-slice_fusion), channel_id=1, source_target_pairs={{0,2},{1,3},{2,0},{3,1},{4,6},{5,7},{6,4},{7,5},{8,10},{9,11},{10,... | collective-permute-start | bytes 786440 | tf_op jit(solution)/shard_map/ppermute | solution.py:21
  45.2 6.3 %copy-start.6 = (bf16[2,256,512]{1,2,0:T(8,128)(2,1)S(1)}, bf16[2,256,512]{1,2,0:T(8,128)(2,1)}, u32[]{:S(2)}) copy-start(bf16[2,256,512]{1,2,0:T(8,128)(2,1)} %copy-done.5) | copy-start | bytes 1572868
  45.2 33.4 %collective-permute-start.5 = (bf16[2,256,512]{2,1,0:T(8,128)(2,1)}, bf16[2,256,512]{2,1,0:T(8,128)(2,1)}, u32[]{:S(2)}, u32[]{:S(2)}) collective-permute-start(bf16[2,256,512]{2,1,0:T(8,128)(2,1)} %pad_maximum_fusion.1), channel_id=1, source_target_pairs={{8,0},{12,4},{16,8},{20,12},{24,16},{28,20},{9,1},{13,5},{17,9},{2... | collective-permute-start | bytes 1572872 | tf_op jit(solution)/shard_map/ppermute | solution.py:15
  53.6 9.5 %collective-permute-start.4 = (f32[1,32768]{1,0:T(1,128)S(1)}, f32[1,32768]{1,0:T(1,128)S(1)}, u32[]{:S(2)}, u32[]{:S(2)}) collective-permute-start(f32[1,32768]{1,0:T(1,128)S(1)} %dynamic-slice_bitcast_fusion), channel_id=1, source_target_pairs={{0,4},{4,0},{8,12},{12,8},{16,20},{20,16},{24,28},{28,24},{1,5},{5... | collective-permute-start | bytes 393224 | tf_op jit(solution)/shard_map/ppermute | solution.py:21
  65.1 6.4 %collective-permute-start.6 = (f32[1,16384]{1,0:T(1,128)}, f32[1,16384]{1,0:T(1,128)}, u32[]{:S(2)}, u32[]{:S(2)}) collective-permute-start(f32[1,16384]{1,0:T(1,128)} %dynamic-slice_bitcast_fusion.1), channel_id=1, source_target_pairs={{0,8},{4,12},{8,0},{12,4},{16,24},{20,28},{24,16},{28,20},{1,9},{5... | collective-permute-start | bytes 196616 | tf_op jit(solution)/shard_map/ppermute | solution.py:21
  71.0 5.4 %copy-start.15 = (bf16[1,256,512]{2,1,0:T(8,128)(2,1)S(1)}, bf16[1,256,512]{2,1,0:T(8,128)(2,1)}, u32[]{:S(2)}) copy-start(bf16[1,256,512]{2,1,0:T(8,128)(2,1)} %copy.209) | copy-start | bytes 786436
  73.3 5.4 %copy-start.4 = (bf16[2,256,512]{1,2,0:T(8,128)(2,1)S(1)}, bf16[2,256,512]{1,2,0:T(8,128)(2,1)}, u32[]{:S(2)}) copy-start(bf16[2,256,512]{1,2,0:T(8,128)(2,1)} %copy-done.3) | copy-start | bytes 1572868
  73.3 5.4 %copy-start.31 = (f32[4,256,256]{2,1,0:T(8,128)S(1)}, f32[4,256,256]{2,1,0:T(8,128)}, u32[]{:S(2)}) copy-start(f32[4,256,256]{2,1,0:T(8,128)} %get-tuple-element.98) | copy-start | bytes 3145732
  73.3 5.3 %collective-permute-start.7 = (f32[1,8192]{1,0:T(1,128)S(1)}, f32[1,8192]{1,0:T(1,128)S(1)}, u32[]{:S(2)}, u32[]{:S(2)}) collective-permute-start(f32[1,8192]{1,0:T(1,128)S(1)} %dynamic-slice_bitcast_fusion.2), channel_id=1, source_target_pairs={{0,16},{4,20},{8,24},{12,28},{16,0},{20,4},{24,8},{28,12},{1,17},{... | collective-permute-start | bytes 98312 | tf_op jit(solution)/shard_map/ppermute | solution.py:21
  77.3 36.8 %collective-permute-start.8 = (bf16[2,256,512]{2,1,0:T(8,128)(2,1)}, bf16[2,256,512]{2,1,0:T(8,128)(2,1)}, u32[]{:S(2)}, u32[]{:S(2)}) collective-permute-start(bf16[2,256,512]{2,1,0:T(8,128)(2,1)} %pad_maximum_fusion.2), channel_id=1, source_target_pairs={{4,0},{8,4},{12,8},{16,12},{20,16},{24,20},{28,24},{5,1},{9,5},{13... | collective-permute-start | bytes 1572872 | tf_op jit(solution)/shard_map/ppermute | solution.py:15
  82.9 5.6 %copy-start.28 = (s32[1,256]{1,0:T(1,128)S(1)}, s32[1,256]{1,0:T(1,128)}, u32[]{:S(2)}) copy-start(s32[1,256]{1,0:T(1,128)} %copy-done.27) | copy-start | bytes 3076
  82.9 12.9 %all-to-all-start = ((bf16[8,2,4096]{2,1,0:T(2,128)(2,1)}), bf16[8,2,4096]{2,1,0:T(2,128)(2,1)S(1)}, u32[]{:S(2)}, u32[]{:S(2)}) async-start(bf16[8,2,4096]{2,1,0:T(2,128)(2,1)} %reshape.776), calls=%async_computation | async-start | bytes 262144 | tf_op jit(solution)/shard_map/all_to_all | solution.py:82
  95.9 13.2 %all-to-all-start.1 = ((f32[32,1,2048]{2,1,0:T(1,128)}), f32[32,1,2048]{2,1,0:T(1,128)S(1)}, u32[]{:S(2)}, u32[]{:S(2)}) async-start(f32[32,1,2048]{2,1,0:T(1,128)} %bitcast.62), calls=%async_computation.1 | async-start | bytes 524288 | tf_op jit(solution)/shard_map/all_to_all | solution.py:92
  109.3 4.8 %copy-start.2 = (f32[1,256,512]{2,1,0:T(8,128)S(1)}, f32[1,256,512]{2,1,0:T(8,128)}, u32[]{:S(2)}) copy-start(f32[1,256,512]{2,1,0:T(8,128)} %copy.205) | copy-start | bytes 1572868
  111.5 10.8 %all-to-all-start.2 = ((bf16[32,2,1024]{2,1,0:T(2,128)(2,1)}), bf16[32,2,1024]{2,1,0:T(2,128)(2,1)S(1)}, u32[]{:S(2)}, u32[]{:S(2)}) async-start(bf16[32,2,1024]{2,1,0:T(2,128)(2,1)} %reshape.778), calls=%async_computation.2 | async-start | bytes 262144 | tf_op jit(solution)/shard_map/all_to_all | solution.py:95
  (13 other events, 10.9 us)

commit v20 on v14

--- a/solution.py
+++ b/solution.py
@@ -268,8 +268,9 @@
             sent[distance] = passed_along(
                 key_terms[distance].astype(jnp.bfloat16), "ctx", -distance
             )
+    indicator_heads = jnp.broadcast_to(indicator_float[None], (head_count,) + indicator_float.shape)
     table_local = jnp.einsum(
-        "qp,cqk->cpk", indicator_float, share_sum, precision=lax.Precision.HIGHEST
+        "cqp,cqk->cpk", indicator_heads, share_sum, precision=lax.Precision.HIGHEST
     )
     gathered = key_terms[0] + sent[1].astype(jnp.float32) + sent[2].astype(jnp.float32)
     query_grad = (query_sum * scale).astype(jnp.bfloat16)

time: 117 us -> 116 us (level)
  local copies, waits for them, and re-layouts: 26.1 us -> 24.6 us
    unnamed x81 -> x85, local copies, waits for them, and re-layouts: 10.4 us -> 9.6 us
where the time goes in v20:
time: 116 us; the launch traced here: 115 us
  starting transfers between devices  38.7 us (33%)
  local copies, waits for them, and re-layouts  24.6 us (21%)
  waiting for transfers between devices  19.1 us (16%)
  matrix products  16.8 us (14%)
  other arithmetic  14.6 us (13%)
  between operations  1.58 us (1%)
    all_to_all x2, starting transfers between devices, summed_by_exchange(): pieces = lax.all_to_all(flat.reshape(size, -1), axes, 0, 0, tiled=True)  19 us
    ppermute x4, starting transfers between devices, passed_along(): return lax.ppermute(value, axis, pairs)  12.1 us
    unnamed x85, local copies, waits for them, and re-layouts  9.6 us
    all_to_all x2, waiting for transfers between devices, summed_by_exchange(): gathered = lax.all_to_all(spread, axes, 0, 0, tiled=True)  9.17 us
    all_to_all x2, waiting for transfers between devices, summed_by_exchange(): pieces = lax.all_to_all(flat.reshape(size, -1), axes, 0, 0, tiled=True)  6.25 us
    all_to_all x2, starting transfers between devices, summed_by_exchange(): gathered = lax.all_to_all(spread, axes, 0, 0, tiled=True)  5.95 us
    ppermute x2, waiting for transfers between devices, exchanged(): return lax.ppermute(value, axis, pairs)  3.64 us
    dot_general x3, matrix products, shards(): jnp.einsum('ihd,jhd->hij', query_heads, forward_key_heads, preferred_elem...  3.38 us
  transfers between devices with their start and end apart: 10, of which 6 were waited for; matrix products, arithmetic and copies ran while one was open for 30% of the time, Pallas kernels for 0%

profile of v20, /device:TPU:0, one launch (start us, length us, event | category | flops | bytes accessed | tf_op | source)
XLA Modules:
  0.0 115.3 jit_solution(18179420014465012563)
XLA Ops:
  0.7 1.2 copy.177
  2.0 5.8 %collective-permute-start.1 = (bf16[2,256,512]{1,2,0:T(8,128)(2,1)S(1)}, bf16[2,256,512]{1,2,0:T(8,128)(2,1)}, u32[]{:S(2)}, u32[]{:S(2)}) collective-permute-start(bf16[2,256,512]{1,2,0:T(8,128)(2,1)S(1)} %pad_maximum_fusion), channel_id=1, source_target_pairs={{0,8},{4,12},{8,16},{12,20},{16,24},{20,28},{1,9},{5,13},{9,17},{1... | collective-permute-start | bytes 1572872 | tf_op jit(solution)/shard_map/ppermute | solution.py:15
  7.8 3.4 %collective-permute-start = (bf16[2,256,512]{1,2,0:T(8,128)(2,1)S(1)}, bf16[2,256,512]{1,2,0:T(8,128)(2,1)S(1)}, u32[]{:S(2)}, u32[]{:S(2)}) collective-permute-start(bf16[2,256,512]{1,2,0:T(8,128)(2,1)S(1)} %pad_maximum_fusion), channel_id=1, source_target_pairs={{0,4},{4,8},{8,12},{12,16},{16,20},{20,24},{24,28},{1,5},{5,9},{9,... | collective-permute-start | bytes 1572872 | tf_op jit(solution)/shard_map/ppermute | solution.py:15
  15.8 1.5 %select_convert_fusion.2 = (bf16[4,256,256]{2,1,0:T(8,128)(2,1)S(1)}, f32[4,256,256]{2,1,0:T(8,128)}) fusion(pred[256,256]{1,0:T(8,128)(4,1)S(1)} %copy.130, f32[4,256,256]{2,1,0:T(8,128)S(1)} %convolution_multiply_fusion.5, bf16[4,256,128]{2,1,0:T(8,128)(2,1)S(1)} %fusion.16, s32[256]{0:T(256)S(1)} %bitcast.243), kind=kOutput, calls=%fused_computation.44 | convolution fusion | flops 68976640 | bytes 2950144 | tf_op jit(solution)/shard_map/vqx,px->vqp/dot_general | solution.py:161
  17.3 1.1 convolution_bitcast_fusion.2
  20.4 1.1 fusion.68
  21.5 1.5 %select_convert_fusion = (bf16[4,256,256]{2,1,0:T(8,128)(2,1)S(1)}, f32[4,256,256]{2,1,0:T(8,128)}) fusion(pred[256,256]{1,0:T(8,128)(4,1)S(1)} %copy.143, f32[4,256,256]{2,1,0:T(8,128)S(1)} %fusion.50, bf16[256,4,128]{0,2,1:T(8,128)(2,1)S(1)} %bitcast.206, bf16[256,4,128]{0,2,1:T(8,128)(2,1)S(1)} %bitcast.234), kind=kOutput, calls=%fused_computation.40 | convolution fusion | flops 69206016 | bytes 3211264 | tf_op jit(solution)/shard_map/ihd,jhd->hij/dot_general | solution.py:176
  24.7 1.5 %select_convert_fusion.1 = (bf16[4,256,256]{2,1,0:T(8,128)(2,1)S(1)}, f32[4,256,256]{2,1,0:T(8,128)}) fusion(pred[256,256]{1,0:T(8,128)(4,1)S(1)} %copy.138, f32[4,256,256]{2,1,0:T(8,128)S(1)} %fusion.46, bf16[256,4,128]{0,2,1:T(8,128)(2,1)S(1)} %bitcast.207, bf16[256,4,128]{0,2,1:T(8,128)(2,1)S(1)} %bitcast.235), kind=kOutput, calls=%fused_computation.42 | convolution fusion | flops 69206016 | bytes 3211264 | tf_op jit(solution)/shard_map/ihd,jhd->hij/dot_general | solution.py:176
  30.7 0.9 convolution_convert_fusion.1
  32.1 1.0 copy.162
  38.3 1.1 fusion.65
  41.0 1.6 %collective-permute-start.3 = (f32[1,65536]{1,0:T(1,128)S(1)}, f32[1,65536]{1,0:T(1,128)}, u32[]{:S(2)}, u32[]{:S(2)}) collective-permute-start(f32[1,65536]{1,0:T(1,128)S(1)} %constant_dynamic-slice_fusion), channel_id=1, source_target_pairs={{0,2},{1,3},{2,0},{3,1},{4,6},{5,7},{6,4},{7,5},{8,10},{9,11},{10,... | collective-permute-start | bytes 786440 | tf_op jit(solution)/shard_map/ppermute | solution.py:21
  44.6 1.6 %collective-permute-start.4 = (bf16[2,256,512]{2,1,0:T(8,128)(2,1)}, bf16[2,256,512]{2,1,0:T(8,128)(2,1)}, u32[]{:S(2)}, u32[]{:S(2)}) collective-permute-start(bf16[2,256,512]{2,1,0:T(8,128)(2,1)} %pad_maximum_fusion.1), channel_id=1, source_target_pairs={{8,0},{12,4},{16,8},{20,12},{24,16},{28,20},{9,1},{13,5},{17,9},{2... | collective-permute-start | bytes 1572872 | tf_op jit(solution)/shard_map/ppermute | solution.py:15
  46.2 3.4 %collective-permute-done.3 = f32[1,65536]{1,0:T(1,128)} collective-permute-done((f32[1,65536]{1,0:T(1,128)S(1)}, f32[1,65536]{1,0:T(1,128)}, u32[]{:S(2)}, u32[]{:S(2)}) %collective-permute-start.3) | collective-permute-done | bytes 262176 | tf_op jit(solution)/shard_map/ppermute | solution.py:21
  49.6 2.0 %dynamic-slice_add_fusion = f32[1,65536]{1,0:T(1,128)} fusion(f32[1,65536]{1,0:T(1,128)} %collective-permute-done.3, f32[2,65536]{1,0:T(2,128)S(1)} %bitcast_add_fusion, s32[]{:T(128)S(6)} %select_n.144), kind=kLoop, calls=%fused_computation.70 | loop fusion | flops 65536 | bytes 786436 | tf_op jit(solution)/shard_map/add | solution.py:71
  53.0 0.9 fusion.15
  54.3 12.3 %all-to-all-start = ((f32[8,1,8192]{2,1,0:T(1,128)}), f32[8,1,8192]{2,1,0:T(1,128)}, u32[]{:S(2)}, u32[]{:S(2)}) async-start(f32[8,1,8192]{2,1,0:T(1,128)} %bitcast.54), calls=%async_computation | async-start | bytes 524288 | tf_op jit(solution)/shard_map/all_to_all | solution.py:82
  67.0 1.1 copy.165
  69.0 1.3 %collective-permute-start.5 = (bf16[2,256,512]{2,1,0:T(8,128)(2,1)}, bf16[2,256,512]{2,1,0:T(8,128)(2,1)}, u32[]{:S(2)}, u32[]{:S(2)}) collective-permute-start(bf16[2,256,512]{2,1,0:T(8,128)(2,1)} %pad_maximum_fusion.2), channel_id=1, source_target_pairs={{4,0},{8,4},{12,8},{16,12},{20,16},{24,20},{28,24},{5,1},{9,5},{13... | collective-permute-start | bytes 1572872 | tf_op jit(solution)/shard_map/ppermute | solution.py:15
  73.0 1.3 %fusion.28 = f32[4,128,128]{2,1,0:T(8,128)} fusion(f32[4,256,128]{2,1,0:T(8,128)S(1)} %convolution_add_fusion.1, f32[256,128]{0,1:T(8,128)S(1)} %copy.167), kind=kOutput, calls=%fused_computation.68 | convolution fusion | flops 201326592 | bytes 917504 | tf_op jit(solution)/shard_map/cqp,cqk->cpk/dot_general | solution.py:272
  74.3 1.3 %all-to-all-done = f32[8,1,8192]{2,1,0:T(1,128)} async-done(((f32[8,1,8192]{2,1,0:T(1,128)}), f32[8,1,8192]{2,1,0:T(1,128)}, u32[]{:S(2)}, u32[]{:S(2)}) %all-to-all-start) | async-done | bytes 262176 | tf_op jit(solution)/shard_map/all_to_all | solution.py:82
  75.5 6.7 %all-to-all-start.2 = ((f32[32,1,2048]{2,1,0:T(1,128)}), f32[32,1,2048]{2,1,0:T(1,128)S(1)}, u32[]{:S(2)}, u32[]{:S(2)}) async-start(f32[32,1,2048]{2,1,0:T(1,128)} %bitcast.55), calls=%async_computation.2 | async-start | bytes 524288 | tf_op jit(solution)/shard_map/all_to_all | solution.py:82
  83.9 1.2 reduce_sum.92
  85.7 1.4 %reduce.6 = bf16[8,8192]{1,0:T(8,128)(2,1)S(1)} reduce(bf16[8,1,8192]{2,1,0:T(2,128)(2,1)S(1)} %broadcast_in_dim.67, bf16[]{:T(256)} %broadcast.614), dimensions={1}, to_apply=%broadcast_in_dim.67.reduce_sub_computation | reduce | bytes 262146 | tf_op jit(solution)/shard_map/broadcast_in_dim | solution.py:84
  87.8 5.0 %all-to-all-done.2 = f32[32,1,2048]{2,1,0:T(1,128)S(1)} async-done(((f32[32,1,2048]{2,1,0:T(1,128)}), f32[32,1,2048]{2,1,0:T(1,128)S(1)}, u32[]{:S(2)}, u32[]{:S(2)}) %all-to-all-start.2) | async-done | bytes 262176 | tf_op jit(solution)/shard_map/all_to_all | solution.py:82
  92.8 3.4 %all-to-all-start.1 = ((bf16[8,2,4096]{2,1,0:T(2,128)(2,1)}), bf16[8,2,4096]{2,1,0:T(2,128)(2,1)S(1)}, u32[]{:S(2)}, u32[]{:S(2)}) async-start(bf16[8,2,4096]{2,1,0:T(2,128)(2,1)} %reshape.772), calls=%async_computation.1 | async-start | bytes 262144 | tf_op jit(solution)/shard_map/all_to_all | solution.py:85
  96.2 1.4 %fusion.18 = bf16[2,256,512]{2,1,0:T(8,128)(2,1)S(1)} fusion(f32[1,256,512]{2,1,0:T(8,128)S(1)} %copy-done.2, f32[1,256,512]{2,1,0:T(8,128)S(1)} %copy.161, bf16[2,256,512]{2,1,0:T(8,128)(2,1)} %collective-permute-done.4, bf16[2,256,512]{2,1,0:T(8,128)(2,1)} %collective-permute-done.5), kind=kLoop, calls=%fused_computation.39 | loop fusion | flops 1572864 | bytes 2621440 | tf_op jit(solution)/shard_map/convert.5
  98.0 1.4 %reduce.7 = bf16[32,2048]{1,0:T(8,128)(2,1)S(1)} reduce(bf16[32,1,2048]{2,1,0:T(2,128)(2,1)S(1)} %broadcast_in_dim.69, bf16[]{:T(256)} %broadcast.614), dimensions={1}, to_apply=%broadcast_in_dim.69.reduce_sub_computation | reduce | bytes 262146 | tf_op jit(solution)/shard_map/broadcast_in_dim | solution.py:84
  100.1 3.4 %all-to-all-done.1 = bf16[8,2,4096]{2,1,0:T(2,128)(2,1)S(1)} async-done(((bf16[8,2,4096]{2,1,0:T(2,128)(2,1)}), bf16[8,2,4096]{2,1,0:T(2,128)(2,1)S(1)}, u32[]{:S(2)}, u32[]{:S(2)}) %all-to-all-start.1) | async-done | bytes 131104 | tf_op jit(solution)/shard_map/all_to_all | solution.py:85
  103.5 2.6 %all-to-all-start.3 = ((bf16[32,2,1024]{2,1,0:T(2,128)(2,1)}), bf16[32,2,1024]{2,1,0:T(2,128)(2,1)S(1)}, u32[]{:S(2)}, u32[]{:S(2)}) async-start(bf16[32,2,1024]{2,1,0:T(2,128)(2,1)} %reshape.774), calls=%async_computation.3 | async-start | bytes 262144 | tf_op jit(solution)/shard_map/all_to_all | solution.py:85
  108.5 5.8 %all-to-all-done.3 = bf16[32,2,1024]{2,1,0:T(2,128)(2,1)S(1)} async-done(((bf16[32,2,1024]{2,1,0:T(2,128)(2,1)}), bf16[32,2,1024]{2,1,0:T(2,128)(2,1)S(1)}, u32[]{:S(2)}, u32[]{:S(2)}) %all-to-all-start.3) | async-done | bytes 131104 | tf_op jit(solution)/shard_map/all_to_all | solution.py:85
  114.4 1.0 convert_element_type.161
  (167 shorter events, 33.8 us)
Async XLA Ops:
  0.6 26.2 %copy-start = (bf16[512,512]{1,0:T(8,128)(2,1)S(1)}, bf16[512,512]{1,0:T(8,128)(2,1)}, u32[]{:S(2)}) copy-start(bf16[512,512]{1,0:T(8,128)(2,1)} %param.19) | copy-start | bytes 1572868
  0.6 1.2 %copy-start.14 = (bf16[1,256,512]{2,1,0:T(8,128)(2,1)S(1)}, bf16[1,256,512]{2,1,0:T(8,128)(2,1)}, u32[]{:S(2)}) copy-start(bf16[1,256,512]{2,1,0:T(8,128)(2,1)} %param.11) | copy-start | bytes 786436
  2.0 12.1 %copy-start.3 = (bf16[2,256,512]{1,2,0:T(8,128)(2,1)}, bf16[2,256,512]{1,2,0:T(8,128)(2,1)S(1)}, u32[]{:S(2)}) copy-start(bf16[2,256,512]{1,2,0:T(8,128)(2,1)S(1)} %pad_maximum_fusion) | copy-start | bytes 1572868
  2.0 18.4 %collective-permute-start.1 = (bf16[2,256,512]{1,2,0:T(8,128)(2,1)S(1)}, bf16[2,256,512]{1,2,0:T(8,128)(2,1)}, u32[]{:S(2)}, u32[]{:S(2)}) collective-permute-start(bf16[2,256,512]{1,2,0:T(8,128)(2,1)S(1)} %pad_maximum_fusion), channel_id=1, source_target_pairs={{0,8},{4,12},{8,16},{12,20},{16,24},{20,28},{1,9},{5,13},{9,17},{1... | collective-permute-start | bytes 1572872 | tf_op jit(solution)/shard_map/ppermute | solution.py:15
  7.8 16.0 %collective-permute-start = (bf16[2,256,512]{1,2,0:T(8,128)(2,1)S(1)}, bf16[2,256,512]{1,2,0:T(8,128)(2,1)S(1)}, u32[]{:S(2)}, u32[]{:S(2)}) collective-permute-start(bf16[2,256,512]{1,2,0:T(8,128)(2,1)S(1)} %pad_maximum_fusion), channel_id=1, source_target_pairs={{0,4},{4,8},{8,12},{12,16},{16,20},{20,24},{24,28},{1,5},{5,9},{9,... | collective-permute-start | bytes 1572872 | tf_op jit(solution)/shard_map/ppermute | solution.py:15
  11.4 1.6 %copy-start.33 = (s32[1,6]{1,0:T(1,128)S(1)}, s32[1,6]{1,0:T(1,128)}, u32[]{:S(2)}) copy-start(s32[1,6]{1,0:T(1,128)} %param.16) | copy-start | bytes 76
  11.5 2.7 %copy-start.22 = (bf16[1,256,512]{2,1,0:T(8,128)(2,1)S(1)}, bf16[1,256,512]{2,1,0:T(8,128)(2,1)}, u32[]{:S(2)}) copy-start(bf16[1,256,512]{2,1,0:T(8,128)(2,1)} %param.10) | copy-start | bytes 786436
  14.2 1.6 %copy-start.24 = (pred[256,256]{1,0:T(8,128)(4,1)}, pred[256,256]{1,0:T(8,128)(4,1)S(1)}, u32[]{:S(2)}) copy-start(pred[256,256]{1,0:T(8,128)(4,1)S(1)} %copy.130) | copy-start | bytes 196612
  17.3 1.1 copy-start.7
  18.8 5.8 %copy-start.26 = (pred[256,256]{1,0:T(8,128)(4,1)}, pred[256,256]{1,0:T(8,128)(4,1)S(1)}, u32[]{:S(2)}) copy-start(pred[256,256]{1,0:T(8,128)(4,1)S(1)} %copy.138) | copy-start | bytes 196612
  19.5 2.0 %copy-start.28 = (pred[256,256]{1,0:T(8,128)(4,1)}, pred[256,256]{1,0:T(8,128)(4,1)S(1)}, u32[]{:S(2)}) copy-start(pred[256,256]{1,0:T(8,128)(4,1)S(1)} %copy.143) | copy-start | bytes 196612
  24.7 1.5 %copy-start.11 = (f32[256,4,128]{0,2,1:T(8,128)S(1)}, f32[256,4,128]{0,2,1:T(8,128)}, u32[]{:S(2)}) copy-start(f32[256,4,128]{0,2,1:T(8,128)} %convolution_bitcast_fusion.2) | copy-start | bytes 1572868
  29.7 1.0 copy-start.10
  37.8 1.6 %copy-start.36 = (f32[4,256,256]{2,1,0:T(8,128)S(1)}, f32[4,256,256]{2,1,0:T(8,128)}, u32[]{:S(2)}) copy-start(f32[4,256,256]{2,1,0:T(8,128)} %get-tuple-element.78) | copy-start | bytes 3145732
  38.2 1.2 %copy-start.13 = (bf16[256,512]{1,0:T(8,128)(2,1)S(1)}, bf16[256,512]{1,0:T(8,128)(2,1)}, u32[]{:S(2)}) copy-start(bf16[256,512]{1,0:T(8,128)(2,1)} %copy-done.12) | copy-start | bytes 786436
  38.2 1.2 %copy-start.29 = (pred[256,256]{1,0:T(8,128)(4,1)S(1)}, pred[256,256]{1,0:T(8,128)(4,1)}, u32[]{:S(2)}) copy-start(pred[256,256]{1,0:T(8,128)(4,1)} %copy-done.28) | copy-start | bytes 196612
  38.2 2.0 %collective-permute-start.2 = (f32[2,65536]{1,0:T(2,128)S(1)}, f32[2,65536]{1,0:T(2,128)S(1)}, u32[]{:S(2)}, u32[]{:S(2)}) collective-permute-start(f32[2,65536]{1,0:T(2,128)S(1)} %bitcast.229), channel_id=1, source_target_pairs={{0,1},{1,0},{2,3},{3,2},{4,5},{5,4},{6,7},{7,6},{8,9},{9,8},{10,11... | collective-permute-start | bytes 1572872 | tf_op jit(solution)/shard_map/ppermute | solution.py:21
  41.0 8.6 %collective-permute-start.3 = (f32[1,65536]{1,0:T(1,128)S(1)}, f32[1,65536]{1,0:T(1,128)}, u32[]{:S(2)}, u32[]{:S(2)}) collective-permute-start(f32[1,65536]{1,0:T(1,128)S(1)} %constant_dynamic-slice_fusion), channel_id=1, source_target_pairs={{0,2},{1,3},{2,0},{3,1},{4,6},{5,7},{6,4},{7,5},{8,10},{9,11},{10,... | collective-permute-start | bytes 786440 | tf_op jit(solution)/shard_map/ppermute | solution.py:21
  44.6 7.0 %copy-start.6 = (bf16[2,256,512]{1,2,0:T(8,128)(2,1)S(1)}, bf16[2,256,512]{1,2,0:T(8,128)(2,1)}, u32[]{:S(2)}) copy-start(bf16[2,256,512]{1,2,0:T(8,128)(2,1)} %copy-done.5) | copy-start | bytes 1572868
  44.6 7.7 %copy-start.35 = (f32[4,256,256]{2,1,0:T(8,128)S(1)}, f32[4,256,256]{2,1,0:T(8,128)}, u32[]{:S(2)}) copy-start(f32[4,256,256]{2,1,0:T(8,128)} %get-tuple-element.82) | copy-start | bytes 3145732
  44.6 26.3 %collective-permute-start.4 = (bf16[2,256,512]{2,1,0:T(8,128)(2,1)}, bf16[2,256,512]{2,1,0:T(8,128)(2,1)}, u32[]{:S(2)}, u32[]{:S(2)}) collective-permute-start(bf16[2,256,512]{2,1,0:T(8,128)(2,1)} %pad_maximum_fusion.1), channel_id=1, source_target_pairs={{8,0},{12,4},{16,8},{20,12},{24,16},{28,20},{9,1},{13,5},{17,9},{2... | collective-permute-start | bytes 1572872 | tf_op jit(solution)/shard_map/ppermute | solution.py:15
  54.3 21.2 %all-to-all-start = ((f32[8,1,8192]{2,1,0:T(1,128)}), f32[8,1,8192]{2,1,0:T(1,128)}, u32[]{:S(2)}, u32[]{:S(2)}) async-start(f32[8,1,8192]{2,1,0:T(1,128)} %bitcast.54), calls=%async_computation | async-start | bytes 524288 | tf_op jit(solution)/shard_map/all_to_all | solution.py:82
  66.9 1.2 %copy-start.16 = (bf16[1,256,512]{2,1,0:T(8,128)(2,1)S(1)}, bf16[1,256,512]{2,1,0:T(8,128)(2,1)}, u32[]{:S(2)}) copy-start(bf16[1,256,512]{2,1,0:T(8,128)(2,1)} %copy.166) | copy-start | bytes 786436
  68.1 2.1 %copy-start.15 = (bf16[1,256,512]{1,2,0:T(8,128)(2,1)S(1)}, bf16[1,256,512]{1,2,0:T(8,128)(2,1)}, u32[]{:S(2)}) copy-start(bf16[1,256,512]{1,2,0:T(8,128)(2,1)} %get-tuple-element.62) | copy-start | bytes 786436
  69.0 27.2 %collective-permute-start.5 = (bf16[2,256,512]{2,1,0:T(8,128)(2,1)}, bf16[2,256,512]{2,1,0:T(8,128)(2,1)}, u32[]{:S(2)}, u32[]{:S(2)}) collective-permute-start(bf16[2,256,512]{2,1,0:T(8,128)(2,1)} %pad_maximum_fusion.2), channel_id=1, source_target_pairs={{4,0},{8,4},{12,8},{16,12},{20,16},{24,20},{28,24},{5,1},{9,5},{13... | collective-permute-start | bytes 1572872 | tf_op jit(solution)/shard_map/ppermute | solution.py:15
  70.6 1.0 copy-start.4
  70.6 1.4 %copy-start.34 = (f32[4,256,256]{2,1,0:T(8,128)S(1)}, f32[4,256,256]{2,1,0:T(8,128)}, u32[]{:S(2)}) copy-start(f32[4,256,256]{2,1,0:T(8,128)} %get-tuple-element.80) | copy-start | bytes 3145732
  70.9 1.1 copy-start.25
  75.5 17.3 %all-to-all-start.2 = ((f32[32,1,2048]{2,1,0:T(1,128)}), f32[32,1,2048]{2,1,0:T(1,128)S(1)}, u32[]{:S(2)}, u32[]{:S(2)}) async-start(f32[32,1,2048]{2,1,0:T(1,128)} %bitcast.55), calls=%async_computation.2 | async-start | bytes 524288 | tf_op jit(solution)/shard_map/all_to_all | solution.py:82
  85.2 11.1 %copy-start.2 = (f32[1,256,512]{2,1,0:T(8,128)S(1)}, f32[1,256,512]{2,1,0:T(8,128)}, u32[]{:S(2)}) copy-start(f32[1,256,512]{2,1,0:T(8,128)} %copy.162) | copy-start | bytes 1572868
  92.8 10.7 %all-to-all-start.1 = ((bf16[8,2,4096]{2,1,0:T(2,128)(2,1)}), bf16[8,2,4096]{2,1,0:T(2,128)(2,1)S(1)}, u32[]{:S(2)}, u32[]{:S(2)}) async-start(bf16[8,2,4096]{2,1,0:T(2,128)(2,1)} %reshape.772), calls=%async_computation.1 | async-start | bytes 262144 | tf_op jit(solution)/shard_map/all_to_all | solution.py:85
  103.5 10.8 %all-to-all-start.3 = ((bf16[32,2,1024]{2,1,0:T(2,128)(2,1)}), bf16[32,2,1024]{2,1,0:T(2,128)(2,1)S(1)}, u32[]{:S(2)}, u32[]{:S(2)}) async-start(bf16[32,2,1024]{2,1,0:T(2,128)(2,1)} %reshape.774), calls=%async_computation.3 | async-start | bytes 262144 | tf_op jit(solution)/shard_map/all_to_all | solution.py:85
  (15 other events, 13.0 us)

commit v21 on v20

--- a/solution.py
+++ b/solution.py
@@ -140,7 +140,7 @@
     ).astype(jnp.bfloat16)
     map_rows = lax.dynamic_slice_in_dim(block_map[0], cycle_index * blocks_here, blocks_here, 0)
     query_heads = query_rows.reshape(local_rows, head_count, head_dim)
-    stacked = jnp.stack([key_rows, value_rows])
+    stacked = jnp.concatenate([key_rows, value_rows], axis=0)
     window = [stacked, passed_along(stacked, "ctx", 1), passed_along(stacked, "ctx", 2)]
     tiles = []
     attended = jnp.zeros((local_rows, head_count, head_dim), jnp.float32)
@@ -170,8 +170,8 @@
             key_bucket_indicator,
         )
         forward_pair = window[distance]
-        forward_key_heads = forward_pair[0].reshape(local_rows, head_count, head_dim)
-        forward_value_heads = forward_pair[1].reshape(local_rows, head_count, head_dim)
+        forward_key_heads = forward_pair[:local_rows].reshape(local_rows, head_count, head_dim)
+        forward_value_heads = forward_pair[local_rows:].reshape(local_rows, head_count, head_dim)
         forward_scores = (
             jnp.einsum(
                 "ihd,jhd->hij", query_heads, forward_key_heads, preferred_element_type=jnp.float32
@@ -237,8 +237,8 @@
         pair = slot(window[distance])
         if distance == 0:
             sent[2], pair = lax.optimization_barrier((sent[2], pair))
-        key_heads = pair[0].reshape(local_rows, head_count, head_dim)
-        value_heads = pair[1].reshape(local_rows, head_count, head_dim)
+        key_heads = pair[:local_rows].reshape(local_rows, head_count, head_dim)
+        value_heads = pair[local_rows:].reshape(local_rows, head_count, head_dim)
         weight_grad = jnp.einsum(
             "ihd,jhd->hij", grad_heads, value_heads, preferred_element_type=jnp.float32
         )
@@ -263,7 +263,7 @@
         )
         share_sum = bucket_share_piece if share_sum is None else share_sum + bucket_share_piece
         query_sum = query_sum + query_part
-        key_terms[distance] = jnp.stack([key_part, value_part])
+        key_terms[distance] = jnp.concatenate([key_part, value_part], axis=0)
         if distance > 0:
             sent[distance] = passed_along(
                 key_terms[distance].astype(jnp.bfloat16), "ctx", -distance
@@ -274,8 +274,8 @@
     )
     gathered = key_terms[0] + sent[1].astype(jnp.float32) + sent[2].astype(jnp.float32)
     query_grad = (query_sum * scale).astype(jnp.bfloat16)
-    key_grad = gathered[0].astype(jnp.bfloat16)
-    value_grad = gathered[1].astype(jnp.bfloat16)
+    key_grad = gathered[:local_rows].astype(jnp.bfloat16)
+    value_grad = gathered[local_rows:].astype(jnp.bfloat16)
     projection_grad = weight_state[0].reshape(width // dp_size, width)
     table_grad = summed_by_exchange(table_local.reshape(-1), ("ctx", "dp")).reshape(
         table_local.shape

time: 116 us -> 116 us (level)
    another operation x5 -> x2, local copies, waits for them, and re-layouts: 3.9 us -> 1.22 us  [the longest x1 1.15 us: shards(): forward_pair[local_rows:].reshape(local_rows, head_count, head_dim)]
    reshape x0 -> x3, local copies, waits for them, and re-layouts: none -> 2.68 us  [shards(): value_part = jnp.einsum('hij,ihd->jhd', weights, grad_heads, preferred_el...]
    another operation x5 -> x2, other arithmetic: 3.36 us -> 1.59 us  [the longest x2 1.71 us: shards(): key_terms[distance] = jnp.stack([key_part, value_part])]
    concatenate x0 -> x3, other arithmetic: none -> 1.73 us  [the longest x2 1.69 us: shards(): key_terms[distance] = jnp.concatenate([key_part, value_part], axis=0)]
    slice x6 -> x5, local copies, waits for them, and re-layouts: 3.76 us -> 2.94 us  [the longest x2 1.1 us: shards(): forward_pair[:local_rows].reshape(local_rows, head_count, head_dim)]
where the time goes in v21:
time: 116 us; the launch traced here: 115 us
  starting transfers between devices  38.7 us (33%)
  local copies, waits for them, and re-layouts  24.6 us (21%)
  waiting for transfers between devices  19.1 us (16%)
  matrix products  16.7 us (14%)
  other arithmetic  14.6 us (13%)
  between operations  1.58 us (1%)
    all_to_all x2, starting transfers between devices, summed_by_exchange(): pieces = lax.all_to_all(flat.reshape(size, -1), axes, 0, 0, tiled=True)  19 us
    ppermute x4, starting transfers between devices, passed_along(): return lax.ppermute(value, axis, pairs)  12.1 us
    unnamed x85, local copies, waits for them, and re-layouts  9.6 us
    all_to_all x2, waiting for transfers between devices, summed_by_exchange(): gathered = lax.all_to_all(spread, axes, 0, 0, tiled=True)  9.17 us
    all_to_all x2, waiting for transfers between devices, summed_by_exchange(): pieces = lax.all_to_all(flat.reshape(size, -1), axes, 0, 0, tiled=True)  6.25 us
    all_to_all x2, starting transfers between devices, summed_by_exchange(): gathered = lax.all_to_all(spread, axes, 0, 0, tiled=True)  5.95 us
    ppermute x2, waiting for transfers between devices, exchanged(): return lax.ppermute(value, axis, pairs)  3.65 us
    dot_general x3, matrix products, shards(): jnp.einsum('ihd,jhd->hij', query_heads, forward_key_heads, preferred_elem...  3.38 us
  transfers between devices with their start and end apart: 10, of which 6 were waited for; matrix products, arithmetic and copies ran while one was open for 30% of the time, Pallas kernels for 0%

profile of v21, /device:TPU:0, one launch (start us, length us, event | category | flops | bytes accessed | tf_op | source)
XLA Modules:
  0.0 115.3 jit_solution(3784464970152738462)
XLA Ops:
  0.7 1.2 copy.177
  2.0 5.8 %collective-permute-start.1 = (bf16[512,512]{0,1:T(8,128)(2,1)S(1)}, bf16[512,512]{0,1:T(8,128)(2,1)}, u32[]{:S(2)}, u32[]{:S(2)}) collective-permute-start(bf16[512,512]{0,1:T(8,128)(2,1)S(1)} %pad_maximum_fusion), channel_id=1, source_target_pairs={{0,8},{4,12},{8,16},{12,20},{16,24},{20,28},{1,9},{5,13},{9,17},{1... | collective-permute-start | bytes 1572872 | tf_op jit(solution)/shard_map/ppermute | solution.py:15
  7.8 3.4 %collective-permute-start = (bf16[512,512]{0,1:T(8,128)(2,1)S(1)}, bf16[512,512]{0,1:T(8,128)(2,1)S(1)}, u32[]{:S(2)}, u32[]{:S(2)}) collective-permute-start(bf16[512,512]{0,1:T(8,128)(2,1)S(1)} %pad_maximum_fusion), channel_id=1, source_target_pairs={{0,4},{4,8},{8,12},{12,16},{16,20},{20,24},{24,28},{1,5},{5,9},{9,... | collective-permute-start | bytes 1572872 | tf_op jit(solution)/shard_map/ppermute | solution.py:15
  15.8 1.5 %select_convert_fusion.2 = (bf16[4,256,256]{2,1,0:T(8,128)(2,1)S(1)}, f32[4,256,256]{2,1,0:T(8,128)}) fusion(pred[256,256]{1,0:T(8,128)(4,1)S(1)} %copy.130, f32[4,256,256]{2,1,0:T(8,128)S(1)} %convolution_multiply_fusion.5, bf16[4,256,128]{2,1,0:T(8,128)(2,1)S(1)} %fusion.16, s32[256]{0:T(256)S(1)} %bitcast.251), kind=kOutput, calls=%fused_computation.44 | convolution fusion | flops 68976640 | bytes 2950144 | tf_op jit(solution)/shard_map/vqx,px->vqp/dot_general | solution.py:161
  17.3 1.1 convolution_bitcast_fusion.2
  20.4 1.1 fusion.67
  21.5 1.5 %select_convert_fusion = (bf16[4,256,256]{2,1,0:T(8,128)(2,1)S(1)}, f32[4,256,256]{2,1,0:T(8,128)}) fusion(pred[256,256]{1,0:T(8,128)(4,1)S(1)} %copy.143, f32[4,256,256]{2,1,0:T(8,128)S(1)} %fusion.50, bf16[256,4,128]{0,2,1:T(8,128)(2,1)S(1)} %bitcast.212, bf16[256,4,128]{0,2,1:T(8,128)(2,1)S(1)} %bitcast.242), kind=kOutput, calls=%fused_computation.40 | convolution fusion | flops 69206016 | bytes 3211264 | tf_op jit(solution)/shard_map/ihd,jhd->hij/dot_general | solution.py:176
  24.6 1.5 %select_convert_fusion.1 = (bf16[4,256,256]{2,1,0:T(8,128)(2,1)S(1)}, f32[4,256,256]{2,1,0:T(8,128)}) fusion(pred[256,256]{1,0:T(8,128)(4,1)S(1)} %copy.138, f32[4,256,256]{2,1,0:T(8,128)S(1)} %fusion.46, bf16[256,4,128]{0,2,1:T(8,128)(2,1)S(1)} %bitcast.213, bf16[256,4,128]{0,2,1:T(8,128)(2,1)S(1)} %bitcast.243), kind=kOutput, calls=%fused_computation.42 | convolution fusion | flops 69206016 | bytes 3211264 | tf_op jit(solution)/shard_map/ihd,jhd->hij/dot_general | solution.py:176
  30.7 0.9 convolution_convert_fusion.1
  32.1 1.0 copy.162
  38.3 1.1 fusion.64
  41.0 1.6 %collective-permute-start.3 = (f32[1,65536]{1,0:T(1,128)S(1)}, f32[1,65536]{1,0:T(1,128)}, u32[]{:S(2)}, u32[]{:S(2)}) collective-permute-start(f32[1,65536]{1,0:T(1,128)S(1)} %constant_dynamic-slice_fusion), channel_id=1, source_target_pairs={{0,2},{1,3},{2,0},{3,1},{4,6},{5,7},{6,4},{7,5},{8,10},{9,11},{10,... | collective-permute-start | bytes 786440 | tf_op jit(solution)/shard_map/ppermute | solution.py:21
  44.6 1.6 %collective-permute-start.4 = (bf16[512,512]{1,0:T(8,128)(2,1)}, bf16[512,512]{1,0:T(8,128)(2,1)}, u32[]{:S(2)}, u32[]{:S(2)}) collective-permute-start(bf16[512,512]{1,0:T(8,128)(2,1)} %pad_maximum_fusion.1), channel_id=1, source_target_pairs={{8,0},{12,4},{16,8},{20,12},{24,16},{28,20},{9,1},{13,5},{17,9},{2... | collective-permute-start | bytes 1572872 | tf_op jit(solution)/shard_map/ppermute | solution.py:15
  46.2 3.4 %collective-permute-done.3 = f32[1,65536]{1,0:T(1,128)} collective-permute-done((f32[1,65536]{1,0:T(1,128)S(1)}, f32[1,65536]{1,0:T(1,128)}, u32[]{:S(2)}, u32[]{:S(2)}) %collective-permute-start.3) | collective-permute-done | bytes 262176 | tf_op jit(solution)/shard_map/ppermute | solution.py:21
  49.6 2.0 %dynamic-slice_add_fusion = f32[1,65536]{1,0:T(1,128)} fusion(f32[1,65536]{1,0:T(1,128)} %collective-permute-done.3, f32[2,65536]{1,0:T(2,128)S(1)} %bitcast_add_fusion, s32[]{:T(128)S(6)} %select_n.144), kind=kLoop, calls=%fused_computation.72 | loop fusion | flops 65536 | bytes 786436 | tf_op jit(solution)/shard_map/add | solution.py:71
  53.0 0.9 fusion.15
  54.3 12.3 %all-to-all-start = ((f32[8,1,8192]{2,1,0:T(1,128)}), f32[8,1,8192]{2,1,0:T(1,128)}, u32[]{:S(2)}, u32[]{:S(2)}) async-start(f32[8,1,8192]{2,1,0:T(1,128)} %bitcast.58), calls=%async_computation | async-start | bytes 524288 | tf_op jit(solution)/shard_map/all_to_all | solution.py:82
  66.9 1.1 copy.165
  68.9 1.3 %collective-permute-start.5 = (bf16[512,512]{1,0:T(8,128)(2,1)}, bf16[512,512]{1,0:T(8,128)(2,1)}, u32[]{:S(2)}, u32[]{:S(2)}) collective-permute-start(bf16[512,512]{1,0:T(8,128)(2,1)} %pad_maximum_fusion.2), channel_id=1, source_target_pairs={{4,0},{8,4},{12,8},{16,12},{20,16},{24,20},{28,24},{5,1},{9,5},{13... | collective-permute-start | bytes 1572872 | tf_op jit(solution)/shard_map/ppermute | solution.py:15
  72.9 1.3 %fusion.28 = f32[4,128,128]{2,1,0:T(8,128)} fusion(f32[4,256,128]{2,1,0:T(8,128)S(1)} %convolution_add_fusion.1, f32[256,128]{0,1:T(8,128)S(1)} %copy.167), kind=kOutput, calls=%fused_computation.70 | convolution fusion | flops 201326592 | bytes 917504 | tf_op jit(solution)/shard_map/cqp,cqk->cpk/dot_general | solution.py:272
  74.2 1.3 %all-to-all-done = f32[8,1,8192]{2,1,0:T(1,128)} async-done(((f32[8,1,8192]{2,1,0:T(1,128)}), f32[8,1,8192]{2,1,0:T(1,128)}, u32[]{:S(2)}, u32[]{:S(2)}) %all-to-all-start) | async-done | bytes 262176 | tf_op jit(solution)/shard_map/all_to_all | solution.py:82
  75.5 6.7 %all-to-all-start.2 = ((f32[32,1,2048]{2,1,0:T(1,128)}), f32[32,1,2048]{2,1,0:T(1,128)S(1)}, u32[]{:S(2)}, u32[]{:S(2)}) async-start(f32[32,1,2048]{2,1,0:T(1,128)} %bitcast.59), calls=%async_computation.2 | async-start | bytes 524288 | tf_op jit(solution)/shard_map/all_to_all | solution.py:82
  83.8 1.2 reduce_sum.92
  85.7 1.4 %reduce.6 = bf16[8,8192]{1,0:T(8,128)(2,1)S(1)} reduce(bf16[8,1,8192]{2,1,0:T(2,128)(2,1)S(1)} %broadcast_in_dim.73, bf16[]{:T(256)} %broadcast.593), dimensions={1}, to_apply=%broadcast_in_dim.73.reduce_sub_computation | reduce | bytes 262146 | tf_op jit(solution)/shard_map/broadcast_in_dim | solution.py:84
  87.8 5.0 %all-to-all-done.2 = f32[32,1,2048]{2,1,0:T(1,128)S(1)} async-done(((f32[32,1,2048]{2,1,0:T(1,128)}), f32[32,1,2048]{2,1,0:T(1,128)S(1)}, u32[]{:S(2)}, u32[]{:S(2)}) %all-to-all-start.2) | async-done | bytes 262176 | tf_op jit(solution)/shard_map/all_to_all | solution.py:82
  92.8 3.4 %all-to-all-start.1 = ((bf16[8,2,4096]{2,1,0:T(2,128)(2,1)}), bf16[8,2,4096]{2,1,0:T(2,128)(2,1)S(1)}, u32[]{:S(2)}, u32[]{:S(2)}) async-start(bf16[8,2,4096]{2,1,0:T(2,128)(2,1)} %reshape.796), calls=%async_computation.1 | async-start | bytes 262144 | tf_op jit(solution)/shard_map/all_to_all | solution.py:85
  96.2 1.4 %fusion.18 = bf16[512,512]{1,0:T(8,128)(2,1)S(1)} fusion(f32[256,512]{1,0:T(8,128)S(1)} %copy-done.2, f32[256,512]{1,0:T(8,128)S(1)} %copy.161, bf16[512,512]{1,0:T(8,128)(2,1)} %collective-permute-done.4, bf16[512,512]{1,0:T(8,128)(2,1)} %collective-permute-done.5), kind=kLoop, calls=%fused_computation.39 | loop fusion | flops 1572864 | bytes 2621440 | tf_op jit(solution)/shard_map/convert.5
  97.9 1.4 %reduce.7 = bf16[32,2048]{1,0:T(8,128)(2,1)S(1)} reduce(bf16[32,1,2048]{2,1,0:T(2,128)(2,1)S(1)} %broadcast_in_dim.75, bf16[]{:T(256)} %broadcast.593), dimensions={1}, to_apply=%broadcast_in_dim.75.reduce_sub_computation | reduce | bytes 262146 | tf_op jit(solution)/shard_map/broadcast_in_dim | solution.py:84
  100.1 3.4 %all-to-all-done.1 = bf16[8,2,4096]{2,1,0:T(2,128)(2,1)S(1)} async-done(((bf16[8,2,4096]{2,1,0:T(2,128)(2,1)}), bf16[8,2,4096]{2,1,0:T(2,128)(2,1)S(1)}, u32[]{:S(2)}, u32[]{:S(2)}) %all-to-all-start.1) | async-done | bytes 131104 | tf_op jit(solution)/shard_map/all_to_all | solution.py:85
  103.5 2.6 %all-to-all-start.3 = ((bf16[32,2,1024]{2,1,0:T(2,128)(2,1)}), bf16[32,2,1024]{2,1,0:T(2,128)(2,1)S(1)}, u32[]{:S(2)}, u32[]{:S(2)}) async-start(bf16[32,2,1024]{2,1,0:T(2,128)(2,1)} %reshape.798), calls=%async_computation.3 | async-start | bytes 262144 | tf_op jit(solution)/shard_map/all_to_all | solution.py:85
  108.5 5.8 %all-to-all-done.3 = bf16[32,2,1024]{2,1,0:T(2,128)(2,1)S(1)} async-done(((bf16[32,2,1024]{2,1,0:T(2,128)(2,1)}), bf16[32,2,1024]{2,1,0:T(2,128)(2,1)S(1)}, u32[]{:S(2)}, u32[]{:S(2)}) %all-to-all-start.3) | async-done | bytes 131104 | tf_op jit(solution)/shard_map/all_to_all | solution.py:85
  114.4 1.0 convert_element_type.159
  (167 shorter events, 33.8 us)
Async XLA Ops:
  0.6 26.2 %copy-start = (bf16[512,512]{1,0:T(8,128)(2,1)S(1)}, bf16[512,512]{1,0:T(8,128)(2,1)}, u32[]{:S(2)}) copy-start(bf16[512,512]{1,0:T(8,128)(2,1)} %param.19) | copy-start | bytes 1572868
  0.6 1.2 %copy-start.14 = (bf16[1,256,512]{2,1,0:T(8,128)(2,1)S(1)}, bf16[1,256,512]{2,1,0:T(8,128)(2,1)}, u32[]{:S(2)}) copy-start(bf16[1,256,512]{2,1,0:T(8,128)(2,1)} %param.11) | copy-start | bytes 786436
  2.0 12.1 %copy-start.3 = (bf16[512,512]{0,1:T(8,128)(2,1)}, bf16[512,512]{0,1:T(8,128)(2,1)S(1)}, u32[]{:S(2)}) copy-start(bf16[512,512]{0,1:T(8,128)(2,1)S(1)} %pad_maximum_fusion) | copy-start | bytes 1572868
  2.0 18.4 %collective-permute-start.1 = (bf16[512,512]{0,1:T(8,128)(2,1)S(1)}, bf16[512,512]{0,1:T(8,128)(2,1)}, u32[]{:S(2)}, u32[]{:S(2)}) collective-permute-start(bf16[512,512]{0,1:T(8,128)(2,1)S(1)} %pad_maximum_fusion), channel_id=1, source_target_pairs={{0,8},{4,12},{8,16},{12,20},{16,24},{20,28},{1,9},{5,13},{9,17},{1... | collective-permute-start | bytes 1572872 | tf_op jit(solution)/shard_map/ppermute | solution.py:15
  7.8 16.0 %collective-permute-start = (bf16[512,512]{0,1:T(8,128)(2,1)S(1)}, bf16[512,512]{0,1:T(8,128)(2,1)S(1)}, u32[]{:S(2)}, u32[]{:S(2)}) collective-permute-start(bf16[512,512]{0,1:T(8,128)(2,1)S(1)} %pad_maximum_fusion), channel_id=1, source_target_pairs={{0,4},{4,8},{8,12},{12,16},{16,20},{20,24},{24,28},{1,5},{5,9},{9,... | collective-permute-start | bytes 1572872 | tf_op jit(solution)/shard_map/ppermute | solution.py:15
  11.4 1.6 %copy-start.33 = (s32[1,6]{1,0:T(1,128)S(1)}, s32[1,6]{1,0:T(1,128)}, u32[]{:S(2)}) copy-start(s32[1,6]{1,0:T(1,128)} %param.16) | copy-start | bytes 76
  11.5 2.7 %copy-start.22 = (bf16[1,256,512]{2,1,0:T(8,128)(2,1)S(1)}, bf16[1,256,512]{2,1,0:T(8,128)(2,1)}, u32[]{:S(2)}) copy-start(bf16[1,256,512]{2,1,0:T(8,128)(2,1)} %param.10) | copy-start | bytes 786436
  14.2 1.6 %copy-start.24 = (pred[256,256]{1,0:T(8,128)(4,1)}, pred[256,256]{1,0:T(8,128)(4,1)S(1)}, u32[]{:S(2)}) copy-start(pred[256,256]{1,0:T(8,128)(4,1)S(1)} %copy.130) | copy-start | bytes 196612
  17.3 1.1 copy-start.7
  18.8 5.8 %copy-start.26 = (pred[256,256]{1,0:T(8,128)(4,1)}, pred[256,256]{1,0:T(8,128)(4,1)S(1)}, u32[]{:S(2)}) copy-start(pred[256,256]{1,0:T(8,128)(4,1)S(1)} %copy.138) | copy-start | bytes 196612
  19.5 2.0 %copy-start.28 = (pred[256,256]{1,0:T(8,128)(4,1)}, pred[256,256]{1,0:T(8,128)(4,1)S(1)}, u32[]{:S(2)}) copy-start(pred[256,256]{1,0:T(8,128)(4,1)S(1)} %copy.143) | copy-start | bytes 196612
  24.6 1.5 %copy-start.11 = (f32[256,4,128]{0,2,1:T(8,128)S(1)}, f32[256,4,128]{0,2,1:T(8,128)}, u32[]{:S(2)}) copy-start(f32[256,4,128]{0,2,1:T(8,128)} %convolution_bitcast_fusion.2) | copy-start | bytes 1572868
  29.7 1.0 copy-start.10
  37.7 1.6 %copy-start.36 = (f32[4,256,256]{2,1,0:T(8,128)S(1)}, f32[4,256,256]{2,1,0:T(8,128)}, u32[]{:S(2)}) copy-start(f32[4,256,256]{2,1,0:T(8,128)} %get-tuple-element.78) | copy-start | bytes 3145732
  38.2 1.2 %copy-start.13 = (bf16[256,512]{1,0:T(8,128)(2,1)S(1)}, bf16[256,512]{1,0:T(8,128)(2,1)}, u32[]{:S(2)}) copy-start(bf16[256,512]{1,0:T(8,128)(2,1)} %copy-done.12) | copy-start | bytes 786436
  38.2 1.2 %copy-start.29 = (pred[256,256]{1,0:T(8,128)(4,1)S(1)}, pred[256,256]{1,0:T(8,128)(4,1)}, u32[]{:S(2)}) copy-start(pred[256,256]{1,0:T(8,128)(4,1)} %copy-done.28) | copy-start | bytes 196612
  38.2 2.0 %collective-permute-start.2 = (f32[2,65536]{1,0:T(2,128)S(1)}, f32[2,65536]{1,0:T(2,128)S(1)}, u32[]{:S(2)}, u32[]{:S(2)}) collective-permute-start(f32[2,65536]{1,0:T(2,128)S(1)} %bitcast.237), channel_id=1, source_target_pairs={{0,1},{1,0},{2,3},{3,2},{4,5},{5,4},{6,7},{7,6},{8,9},{9,8},{10,11... | collective-permute-start | bytes 1572872 | tf_op jit(solution)/shard_map/ppermute | solution.py:21
  41.0 8.6 %collective-permute-start.3 = (f32[1,65536]{1,0:T(1,128)S(1)}, f32[1,65536]{1,0:T(1,128)}, u32[]{:S(2)}, u32[]{:S(2)}) collective-permute-start(f32[1,65536]{1,0:T(1,128)S(1)} %constant_dynamic-slice_fusion), channel_id=1, source_target_pairs={{0,2},{1,3},{2,0},{3,1},{4,6},{5,7},{6,4},{7,5},{8,10},{9,11},{10,... | collective-permute-start | bytes 786440 | tf_op jit(solution)/shard_map/ppermute | solution.py:21
  44.6 7.0 %copy-start.6 = (bf16[512,512]{0,1:T(8,128)(2,1)S(1)}, bf16[512,512]{0,1:T(8,128)(2,1)}, u32[]{:S(2)}) copy-start(bf16[512,512]{0,1:T(8,128)(2,1)} %copy-done.5) | copy-start | bytes 1572868
  44.6 7.7 %copy-start.35 = (f32[4,256,256]{2,1,0:T(8,128)S(1)}, f32[4,256,256]{2,1,0:T(8,128)}, u32[]{:S(2)}) copy-start(f32[4,256,256]{2,1,0:T(8,128)} %get-tuple-element.82) | copy-start | bytes 3145732
  44.6 26.3 %collective-permute-start.4 = (bf16[512,512]{1,0:T(8,128)(2,1)}, bf16[512,512]{1,0:T(8,128)(2,1)}, u32[]{:S(2)}, u32[]{:S(2)}) collective-permute-start(bf16[512,512]{1,0:T(8,128)(2,1)} %pad_maximum_fusion.1), channel_id=1, source_target_pairs={{8,0},{12,4},{16,8},{20,12},{24,16},{28,20},{9,1},{13,5},{17,9},{2... | collective-permute-start | bytes 1572872 | tf_op jit(solution)/shard_map/ppermute | solution.py:15
  54.3 21.2 %all-to-all-start = ((f32[8,1,8192]{2,1,0:T(1,128)}), f32[8,1,8192]{2,1,0:T(1,128)}, u32[]{:S(2)}, u32[]{:S(2)}) async-start(f32[8,1,8192]{2,1,0:T(1,128)} %bitcast.58), calls=%async_computation | async-start | bytes 524288 | tf_op jit(solution)/shard_map/all_to_all | solution.py:82
  66.9 1.2 %copy-start.16 = (bf16[256,512]{1,0:T(8,128)(2,1)S(1)}, bf16[256,512]{1,0:T(8,128)(2,1)}, u32[]{:S(2)}) copy-start(bf16[256,512]{1,0:T(8,128)(2,1)} %copy.166) | copy-start | bytes 786436
  68.1 2.1 %copy-start.15 = (bf16[256,512]{0,1:T(8,128)(2,1)S(1)}, bf16[256,512]{0,1:T(8,128)(2,1)}, u32[]{:S(2)}) copy-start(bf16[256,512]{0,1:T(8,128)(2,1)} %get-tuple-element.62) | copy-start | bytes 786436
  68.9 27.2 %collective-permute-start.5 = (bf16[512,512]{1,0:T(8,128)(2,1)}, bf16[512,512]{1,0:T(8,128)(2,1)}, u32[]{:S(2)}, u32[]{:S(2)}) collective-permute-start(bf16[512,512]{1,0:T(8,128)(2,1)} %pad_maximum_fusion.2), channel_id=1, source_target_pairs={{4,0},{8,4},{12,8},{16,12},{20,16},{24,20},{28,24},{5,1},{9,5},{13... | collective-permute-start | bytes 1572872 | tf_op jit(solution)/shard_map/ppermute | solution.py:15
  70.5 1.0 copy-start.4
  70.6 1.4 %copy-start.34 = (f32[4,256,256]{2,1,0:T(8,128)S(1)}, f32[4,256,256]{2,1,0:T(8,128)}, u32[]{:S(2)}) copy-start(f32[4,256,256]{2,1,0:T(8,128)} %get-tuple-element.80) | copy-start | bytes 3145732
  70.9 1.1 copy-start.25
  75.5 17.3 %all-to-all-start.2 = ((f32[32,1,2048]{2,1,0:T(1,128)}), f32[32,1,2048]{2,1,0:T(1,128)S(1)}, u32[]{:S(2)}, u32[]{:S(2)}) async-start(f32[32,1,2048]{2,1,0:T(1,128)} %bitcast.59), calls=%async_computation.2 | async-start | bytes 524288 | tf_op jit(solution)/shard_map/all_to_all | solution.py:82
  85.1 11.1 %copy-start.2 = (f32[256,512]{1,0:T(8,128)S(1)}, f32[256,512]{1,0:T(8,128)}, u32[]{:S(2)}) copy-start(f32[256,512]{1,0:T(8,128)} %copy.162) | copy-start | bytes 1572868
  92.8 10.7 %all-to-all-start.1 = ((bf16[8,2,4096]{2,1,0:T(2,128)(2,1)}), bf16[8,2,4096]{2,1,0:T(2,128)(2,1)S(1)}, u32[]{:S(2)}, u32[]{:S(2)}) async-start(bf16[8,2,4096]{2,1,0:T(2,128)(2,1)} %reshape.796), calls=%async_computation.1 | async-start | bytes 262144 | tf_op jit(solution)/shard_map/all_to_all | solution.py:85
  103.5 10.8 %all-to-all-start.3 = ((bf16[32,2,1024]{2,1,0:T(2,128)(2,1)}), bf16[32,2,1024]{2,1,0:T(2,128)(2,1)S(1)}, u32[]{:S(2)}, u32[]{:S(2)}) async-start(bf16[32,2,1024]{2,1,0:T(2,128)(2,1)} %reshape.798), calls=%async_computation.3 | async-start | bytes 262144 | tf_op jit(solution)/shard_map/all_to_all | solution.py:85
  (15 other events, 13.0 us)

commit v22 on v21

--- a/solution.py
+++ b/solution.py
@@ -268,10 +268,19 @@
             sent[distance] = passed_along(
                 key_terms[distance].astype(jnp.bfloat16), "ctx", -distance
             )
-    indicator_heads = jnp.broadcast_to(indicator_float[None], (head_count,) + indicator_float.shape)
-    table_local = jnp.einsum(
-        "cqp,cqk->cpk", indicator_heads, share_sum, precision=lax.Precision.HIGHEST
-    )
+    indicator_heads = jnp.broadcast_to(
+        query_bucket_indicator[None], (head_count,) + query_bucket_indicator.shape
+    )
+    share_high = share_sum.astype(jnp.bfloat16)
+    share_rest = share_sum - share_high.astype(jnp.float32)
+    share_mid = share_rest.astype(jnp.bfloat16)
+    share_low = (share_rest - share_mid.astype(jnp.float32)).astype(jnp.bfloat16)
+    table_local = None
+    for share_part in (share_low, share_mid, share_high):
+        term = jnp.einsum(
+            "cqp,cqk->cpk", indicator_heads, share_part, preferred_element_type=jnp.float32
+        )
+        table_local = term if table_local is None else table_local + term
     gathered = key_terms[0] + sent[1].astype(jnp.float32) + sent[2].astype(jnp.float32)
     query_grad = (query_sum * scale).astype(jnp.bfloat16)
     key_grad = gathered[:local_rows].astype(jnp.bfloat16)

time: 116 us -> 117 us (level)
  local copies, waits for them, and re-layouts: 24.6 us -> 26.4 us
  waiting for transfers between devices: 19.1 us -> 17.8 us
    all_to_all x2, waiting for transfers between devices: 6.25 us -> 4.96 us  [summed_by_exchange(): pieces = lax.all_to_all(flat.reshape(size, -1), axes, 0, 0, tiled=True)]
    unnamed x85 -> x83, local copies, waits for them, and re-layouts: 9.6 us -> 10.7 us
  transfers between devices with their start and end apart: 10 -> 10, of which waited for: 6 -> 6; matrix products, arithmetic and copies ran while one was open for 30% -> 31% of each run, Pallas kernels for 0% -> 0%
where the time goes in v22:
time: 117 us; the launch traced here: 116 us
  starting transfers between devices  38.7 us (33%)
  local copies, waits for them, and re-layouts  26.4 us (23%)
  waiting for transfers between devices  17.8 us (15%)
  matrix products  16.8 us (14%)
  other arithmetic  14.6 us (12%)
  between operations  1.57 us (1%)
    all_to_all x2, starting transfers between devices, summed_by_exchange(): pieces = lax.all_to_all(flat.reshape(size, -1), axes, 0, 0, tiled=True)  19 us
    ppermute x4, starting transfers between devices, passed_along(): return lax.ppermute(value, axis, pairs)  12.1 us
    unnamed x83, local copies, waits for them, and re-layouts  10.7 us
    all_to_all x2, waiting for transfers between devices, summed_by_exchange(): gathered = lax.all_to_all(spread, axes, 0, 0, tiled=True)  9.17 us
    all_to_all x2, starting transfers between devices, summed_by_exchange(): gathered = lax.all_to_all(spread, axes, 0, 0, tiled=True)  5.94 us
    all_to_all x2, waiting for transfers between devices, summed_by_exchange(): pieces = lax.all_to_all(flat.reshape(size, -1), axes, 0, 0, tiled=True)  4.96 us
    ppermute x2, waiting for transfers between devices, exchanged(): return lax.ppermute(value, axis, pairs)  3.66 us
    dot_general x3, matrix products, shards(): jnp.einsum('ihd,jhd->hij', query_heads, forward_key_heads, preferred_elem...  3.36 us
  transfers between devices with their start and end apart: 10, of which 6 were waited for; matrix products, arithmetic and copies ran while one was open for 31% of the time, Pallas kernels for 0%

profile of v22, /device:TPU:0, one launch (start us, length us, event | category | flops | bytes accessed | tf_op | source)
XLA Modules:
  0.0 115.8 jit_solution(16606612445575415417)
XLA Ops:
  0.7 1.2 copy.177
  2.0 5.8 %collective-permute-start.1 = (bf16[512,512]{0,1:T(8,128)(2,1)S(1)}, bf16[512,512]{0,1:T(8,128)(2,1)}, u32[]{:S(2)}, u32[]{:S(2)}) collective-permute-start(bf16[512,512]{0,1:T(8,128)(2,1)S(1)} %pad_maximum_fusion), channel_id=1, source_target_pairs={{0,8},{4,12},{8,16},{12,20},{16,24},{20,28},{1,9},{5,13},{9,17},{1... | collective-permute-start | bytes 1572872 | tf_op jit(solution)/shard_map/ppermute | solution.py:15
  7.8 3.4 %collective-permute-start = (bf16[512,512]{0,1:T(8,128)(2,1)S(1)}, bf16[512,512]{0,1:T(8,128)(2,1)S(1)}, u32[]{:S(2)}, u32[]{:S(2)}) collective-permute-start(bf16[512,512]{0,1:T(8,128)(2,1)S(1)} %pad_maximum_fusion), channel_id=1, source_target_pairs={{0,4},{4,8},{8,12},{12,16},{16,20},{20,24},{24,28},{1,5},{5,9},{9,... | collective-permute-start | bytes 1572872 | tf_op jit(solution)/shard_map/ppermute | solution.py:15
  15.7 1.5 %select_convert_fusion.2 = (bf16[4,256,256]{2,1,0:T(8,128)(2,1)S(1)}, f32[4,256,256]{2,1,0:T(8,128)}) fusion(pred[256,256]{1,0:T(8,128)(4,1)S(1)} %copy.130, f32[4,256,256]{2,1,0:T(8,128)S(1)} %convolution_multiply_fusion.5, bf16[4,256,128]{2,1,0:T(8,128)(2,1)S(1)} %fusion.16, s32[256]{0:T(256)S(1)} %bitcast.250), kind=kOutput, calls=%fused_computation.46 | convolution fusion | flops 68976640 | bytes 2950144 | tf_op jit(solution)/shard_map/vqx,px->vqp/dot_general | solution.py:161
  18.0 1.1 convolution_bitcast_fusion.2
  21.0 1.1 fusion.71
  22.0 1.5 %select_convert_fusion = (bf16[4,256,256]{2,1,0:T(8,128)(2,1)S(1)}, f32[4,256,256]{2,1,0:T(8,128)}) fusion(pred[256,256]{1,0:T(8,128)(4,1)S(1)} %copy.143, f32[4,256,256]{2,1,0:T(8,128)S(1)} %fusion.55, bf16[256,4,128]{0,2,1:T(8,128)(2,1)S(1)} %bitcast.211, bf16[256,4,128]{0,2,1:T(8,128)(2,1)S(1)} %bitcast.241), kind=kOutput, calls=%fused_computation.42 | convolution fusion | flops 69206016 | bytes 3211264 | tf_op jit(solution)/shard_map/ihd,jhd->hij/dot_general | solution.py:176
  25.2 1.5 %select_convert_fusion.1 = (bf16[4,256,256]{2,1,0:T(8,128)(2,1)S(1)}, f32[4,256,256]{2,1,0:T(8,128)}) fusion(pred[256,256]{1,0:T(8,128)(4,1)S(1)} %copy.138, f32[4,256,256]{2,1,0:T(8,128)S(1)} %fusion.51, bf16[256,4,128]{0,2,1:T(8,128)(2,1)S(1)} %bitcast.212, bf16[256,4,128]{0,2,1:T(8,128)(2,1)S(1)} %bitcast.242), kind=kOutput, calls=%fused_computation.44 | convolution fusion | flops 69206016 | bytes 3211264 | tf_op jit(solution)/shard_map/ihd,jhd->hij/dot_general | solution.py:176
  28.6 0.9 fusion.22
  30.2 0.9 convolution_convert_fusion
  31.3 0.9 convolution_convert_fusion.1
  32.6 1.0 copy.162
  38.8 1.1 fusion.68
  41.5 1.6 %collective-permute-start.3 = (f32[1,65536]{1,0:T(1,128)S(1)}, f32[1,65536]{1,0:T(1,128)}, u32[]{:S(2)}, u32[]{:S(2)}) collective-permute-start(f32[1,65536]{1,0:T(1,128)S(1)} %constant_dynamic-slice_fusion), channel_id=1, source_target_pairs={{0,2},{1,3},{2,0},{3,1},{4,6},{5,7},{6,4},{7,5},{8,10},{9,11},{10,... | collective-permute-start | bytes 786440 | tf_op jit(solution)/shard_map/ppermute | solution.py:21
  45.1 1.6 %collective-permute-start.4 = (bf16[512,512]{1,0:T(8,128)(2,1)}, bf16[512,512]{1,0:T(8,128)(2,1)}, u32[]{:S(2)}, u32[]{:S(2)}) collective-permute-start(bf16[512,512]{1,0:T(8,128)(2,1)} %pad_maximum_fusion.1), channel_id=1, source_target_pairs={{8,0},{12,4},{16,8},{20,12},{24,16},{28,20},{9,1},{13,5},{17,9},{2... | collective-permute-start | bytes 1572872 | tf_op jit(solution)/shard_map/ppermute | solution.py:15
  46.7 3.4 %collective-permute-done.3 = f32[1,65536]{1,0:T(1,128)} collective-permute-done((f32[1,65536]{1,0:T(1,128)S(1)}, f32[1,65536]{1,0:T(1,128)}, u32[]{:S(2)}, u32[]{:S(2)}) %collective-permute-start.3) | collective-permute-done | bytes 262176 | tf_op jit(solution)/shard_map/ppermute | solution.py:21
  50.1 2.0 %dynamic-slice_add_fusion = f32[1,65536]{1,0:T(1,128)} fusion(f32[1,65536]{1,0:T(1,128)} %collective-permute-done.3, f32[2,65536]{1,0:T(2,128)S(1)} %bitcast_add_fusion, s32[]{:T(128)S(6)} %select_n.144), kind=kLoop, calls=%fused_computation.77 | loop fusion | flops 65536 | bytes 786436 | tf_op jit(solution)/shard_map/add | solution.py:71
  53.5 0.9 fusion.15
  54.8 11.8 %all-to-all-start = ((f32[8,1,8192]{2,1,0:T(1,128)}), f32[8,1,8192]{2,1,0:T(1,128)}, u32[]{:S(2)}, u32[]{:S(2)}) async-start(f32[8,1,8192]{2,1,0:T(1,128)} %bitcast.58), calls=%async_computation | async-start | bytes 524288 | tf_op jit(solution)/shard_map/all_to_all | solution.py:82
  66.9 1.1 copy.165
  68.9 1.3 %collective-permute-start.5 = (bf16[512,512]{1,0:T(8,128)(2,1)}, bf16[512,512]{1,0:T(8,128)(2,1)}, u32[]{:S(2)}, u32[]{:S(2)}) collective-permute-start(bf16[512,512]{1,0:T(8,128)(2,1)} %pad_maximum_fusion.2), channel_id=1, source_target_pairs={{4,0},{8,4},{12,8},{16,12},{20,16},{24,20},{28,24},{5,1},{9,5},{13... | collective-permute-start | bytes 1572872 | tf_op jit(solution)/shard_map/ppermute | solution.py:15
  75.5 7.3 %all-to-all-start.2 = ((f32[32,1,2048]{2,1,0:T(1,128)}), f32[32,1,2048]{2,1,0:T(1,128)S(1)}, u32[]{:S(2)}, u32[]{:S(2)}) async-start(f32[32,1,2048]{2,1,0:T(1,128)} %bitcast.59), calls=%async_computation.2 | async-start | bytes 524288 | tf_op jit(solution)/shard_map/all_to_all | solution.py:82
  85.1 1.2 reduce_sum.92
  86.9 1.4 %reduce.6 = bf16[8,8192]{1,0:T(8,128)(2,1)S(1)} reduce(bf16[8,1,8192]{2,1,0:T(2,128)(2,1)S(1)} %broadcast_in_dim.73, bf16[]{:T(256)} %broadcast.593), dimensions={1}, to_apply=%broadcast_in_dim.73.reduce_sub_computation | reduce | bytes 262146 | tf_op jit(solution)/shard_map/broadcast_in_dim | solution.py:84
  89.1 4.2 %all-to-all-done.2 = f32[32,1,2048]{2,1,0:T(1,128)S(1)} async-done(((f32[32,1,2048]{2,1,0:T(1,128)}), f32[32,1,2048]{2,1,0:T(1,128)S(1)}, u32[]{:S(2)}, u32[]{:S(2)}) %all-to-all-start.2) | async-done | bytes 262176 | tf_op jit(solution)/shard_map/all_to_all | solution.py:82
  93.3 3.4 %all-to-all-start.1 = ((bf16[8,2,4096]{2,1,0:T(2,128)(2,1)}), bf16[8,2,4096]{2,1,0:T(2,128)(2,1)S(1)}, u32[]{:S(2)}, u32[]{:S(2)}) async-start(bf16[8,2,4096]{2,1,0:T(2,128)(2,1)} %reshape.795), calls=%async_computation.1 | async-start | bytes 262144 | tf_op jit(solution)/shard_map/all_to_all | solution.py:85
  96.7 1.4 %fusion.18 = bf16[512,512]{1,0:T(8,128)(2,1)S(1)} fusion(f32[256,512]{1,0:T(8,128)S(1)} %copy-done.2, f32[256,512]{1,0:T(8,128)S(1)} %copy.161, bf16[512,512]{1,0:T(8,128)(2,1)} %collective-permute-done.4, bf16[512,512]{1,0:T(8,128)(2,1)} %collective-permute-done.5), kind=kLoop, calls=%fused_computation.41 | loop fusion | flops 1572864 | bytes 2621440 | tf_op jit(solution)/shard_map/convert.5
  98.5 1.4 %reduce.7 = bf16[32,2048]{1,0:T(8,128)(2,1)S(1)} reduce(bf16[32,1,2048]{2,1,0:T(2,128)(2,1)S(1)} %broadcast_in_dim.75, bf16[]{:T(256)} %broadcast.593), dimensions={1}, to_apply=%broadcast_in_dim.75.reduce_sub_computation | reduce | bytes 262146 | tf_op jit(solution)/shard_map/broadcast_in_dim | solution.py:84
  100.6 3.4 %all-to-all-done.1 = bf16[8,2,4096]{2,1,0:T(2,128)(2,1)S(1)} async-done(((bf16[8,2,4096]{2,1,0:T(2,128)(2,1)}), bf16[8,2,4096]{2,1,0:T(2,128)(2,1)S(1)}, u32[]{:S(2)}, u32[]{:S(2)}) %all-to-all-start.1) | async-done | bytes 131104 | tf_op jit(solution)/shard_map/all_to_all | solution.py:85
  104.0 2.6 %all-to-all-start.3 = ((bf16[32,2,1024]{2,1,0:T(2,128)(2,1)}), bf16[32,2,1024]{2,1,0:T(2,128)(2,1)S(1)}, u32[]{:S(2)}, u32[]{:S(2)}) async-start(bf16[32,2,1024]{2,1,0:T(2,128)(2,1)} %reshape.797), calls=%async_computation.3 | async-start | bytes 262144 | tf_op jit(solution)/shard_map/all_to_all | solution.py:85
  109.0 5.8 %all-to-all-done.3 = bf16[32,2,1024]{2,1,0:T(2,128)(2,1)S(1)} async-done(((bf16[32,2,1024]{2,1,0:T(2,128)(2,1)}), bf16[32,2,1024]{2,1,0:T(2,128)(2,1)S(1)}, u32[]{:S(2)}, u32[]{:S(2)}) %all-to-all-start.3) | async-done | bytes 131104 | tf_op jit(solution)/shard_map/all_to_all | solution.py:85
  114.9 1.0 convert_element_type.171
  (167 shorter events, 35.7 us)
Async XLA Ops:
  0.6 26.7 %copy-start = (bf16[512,512]{1,0:T(8,128)(2,1)S(1)}, bf16[512,512]{1,0:T(8,128)(2,1)}, u32[]{:S(2)}) copy-start(bf16[512,512]{1,0:T(8,128)(2,1)} %param.19) | copy-start | bytes 1572868
  0.6 1.2 %copy-start.14 = (bf16[1,256,512]{2,1,0:T(8,128)(2,1)S(1)}, bf16[1,256,512]{2,1,0:T(8,128)(2,1)}, u32[]{:S(2)}) copy-start(bf16[1,256,512]{2,1,0:T(8,128)(2,1)} %param.11) | copy-start | bytes 786436
  2.0 12.1 %copy-start.3 = (bf16[512,512]{0,1:T(8,128)(2,1)}, bf16[512,512]{0,1:T(8,128)(2,1)S(1)}, u32[]{:S(2)}) copy-start(bf16[512,512]{0,1:T(8,128)(2,1)S(1)} %pad_maximum_fusion) | copy-start | bytes 1572868
  2.0 18.9 %collective-permute-start.1 = (bf16[512,512]{0,1:T(8,128)(2,1)S(1)}, bf16[512,512]{0,1:T(8,128)(2,1)}, u32[]{:S(2)}, u32[]{:S(2)}) collective-permute-start(bf16[512,512]{0,1:T(8,128)(2,1)S(1)} %pad_maximum_fusion), channel_id=1, source_target_pairs={{0,8},{4,12},{8,16},{12,20},{16,24},{20,28},{1,9},{5,13},{9,17},{1... | collective-permute-start | bytes 1572872 | tf_op jit(solution)/shard_map/ppermute | solution.py:15
  7.8 16.6 %collective-permute-start = (bf16[512,512]{0,1:T(8,128)(2,1)S(1)}, bf16[512,512]{0,1:T(8,128)(2,1)S(1)}, u32[]{:S(2)}, u32[]{:S(2)}) collective-permute-start(bf16[512,512]{0,1:T(8,128)(2,1)S(1)} %pad_maximum_fusion), channel_id=1, source_target_pairs={{0,4},{4,8},{8,12},{12,16},{16,20},{20,24},{24,28},{1,5},{5,9},{9,... | collective-permute-start | bytes 1572872 | tf_op jit(solution)/shard_map/ppermute | solution.py:15
  11.4 1.6 %copy-start.32 = (s32[1,6]{1,0:T(1,128)S(1)}, s32[1,6]{1,0:T(1,128)}, u32[]{:S(2)}) copy-start(s32[1,6]{1,0:T(1,128)} %param.16) | copy-start | bytes 76
  11.4 2.7 %copy-start.23 = (bf16[1,256,512]{2,1,0:T(8,128)(2,1)S(1)}, bf16[1,256,512]{2,1,0:T(8,128)(2,1)}, u32[]{:S(2)}) copy-start(bf16[1,256,512]{2,1,0:T(8,128)(2,1)} %param.10) | copy-start | bytes 786436
  19.5 5.6 %copy-start.25 = (pred[256,256]{1,0:T(8,128)(4,1)}, pred[256,256]{1,0:T(8,128)(4,1)S(1)}, u32[]{:S(2)}) copy-start(pred[256,256]{1,0:T(8,128)(4,1)S(1)} %copy.138) | copy-start | bytes 196612
  20.0 2.0 %copy-start.27 = (pred[256,256]{1,0:T(8,128)(4,1)}, pred[256,256]{1,0:T(8,128)(4,1)S(1)}, u32[]{:S(2)}) copy-start(pred[256,256]{1,0:T(8,128)(4,1)S(1)} %copy.143) | copy-start | bytes 196612
  25.2 1.5 %copy-start.11 = (f32[256,4,128]{0,2,1:T(8,128)S(1)}, f32[256,4,128]{0,2,1:T(8,128)}, u32[]{:S(2)}) copy-start(f32[256,4,128]{0,2,1:T(8,128)} %convolution_bitcast_fusion.2) | copy-start | bytes 1572868
  27.1 1.0 copy-start.21
  30.2 1.0 copy-start.10
  31.3 1.0 copy-start.8
  32.6 1.0 copy-start.19
  38.3 1.6 %copy-start.35 = (f32[4,256,256]{2,1,0:T(8,128)S(1)}, f32[4,256,256]{2,1,0:T(8,128)}, u32[]{:S(2)}) copy-start(f32[4,256,256]{2,1,0:T(8,128)} %get-tuple-element.78) | copy-start | bytes 3145732
  38.7 1.2 %copy-start.13 = (bf16[256,512]{1,0:T(8,128)(2,1)S(1)}, bf16[256,512]{1,0:T(8,128)(2,1)}, u32[]{:S(2)}) copy-start(bf16[256,512]{1,0:T(8,128)(2,1)} %copy-done.12) | copy-start | bytes 786436
  38.7 1.2 %copy-start.28 = (pred[256,256]{1,0:T(8,128)(4,1)S(1)}, pred[256,256]{1,0:T(8,128)(4,1)}, u32[]{:S(2)}) copy-start(pred[256,256]{1,0:T(8,128)(4,1)} %copy-done.27) | copy-start | bytes 196612
  38.7 2.0 %collective-permute-start.2 = (f32[2,65536]{1,0:T(2,128)S(1)}, f32[2,65536]{1,0:T(2,128)S(1)}, u32[]{:S(2)}, u32[]{:S(2)}) collective-permute-start(f32[2,65536]{1,0:T(2,128)S(1)} %bitcast.236), channel_id=1, source_target_pairs={{0,1},{1,0},{2,3},{3,2},{4,5},{5,4},{6,7},{7,6},{8,9},{9,8},{10,11... | collective-permute-start | bytes 1572872 | tf_op jit(solution)/shard_map/ppermute | solution.py:21
  41.5 8.6 %collective-permute-start.3 = (f32[1,65536]{1,0:T(1,128)S(1)}, f32[1,65536]{1,0:T(1,128)}, u32[]{:S(2)}, u32[]{:S(2)}) collective-permute-start(f32[1,65536]{1,0:T(1,128)S(1)} %constant_dynamic-slice_fusion), channel_id=1, source_target_pairs={{0,2},{1,3},{2,0},{3,1},{4,6},{5,7},{6,4},{7,5},{8,10},{9,11},{10,... | collective-permute-start | bytes 786440 | tf_op jit(solution)/shard_map/ppermute | solution.py:21
  45.1 7.0 %copy-start.6 = (bf16[512,512]{0,1:T(8,128)(2,1)S(1)}, bf16[512,512]{0,1:T(8,128)(2,1)}, u32[]{:S(2)}) copy-start(bf16[512,512]{0,1:T(8,128)(2,1)} %copy-done.5) | copy-start | bytes 1572868
  45.1 7.8 %copy-start.34 = (f32[4,256,256]{2,1,0:T(8,128)S(1)}, f32[4,256,256]{2,1,0:T(8,128)}, u32[]{:S(2)}) copy-start(f32[4,256,256]{2,1,0:T(8,128)} %get-tuple-element.82) | copy-start | bytes 3145732
  45.1 25.8 %collective-permute-start.4 = (bf16[512,512]{1,0:T(8,128)(2,1)}, bf16[512,512]{1,0:T(8,128)(2,1)}, u32[]{:S(2)}, u32[]{:S(2)}) collective-permute-start(bf16[512,512]{1,0:T(8,128)(2,1)} %pad_maximum_fusion.1), channel_id=1, source_target_pairs={{8,0},{12,4},{16,8},{20,12},{24,16},{28,20},{9,1},{13,5},{17,9},{2... | collective-permute-start | bytes 1572872 | tf_op jit(solution)/shard_map/ppermute | solution.py:15
  54.8 20.7 %all-to-all-start = ((f32[8,1,8192]{2,1,0:T(1,128)}), f32[8,1,8192]{2,1,0:T(1,128)}, u32[]{:S(2)}, u32[]{:S(2)}) async-start(f32[8,1,8192]{2,1,0:T(1,128)} %bitcast.58), calls=%async_computation | async-start | bytes 524288 | tf_op jit(solution)/shard_map/all_to_all | solution.py:82
  66.9 1.2 copy-start.16
  68.1 2.1 %copy-start.15 = (bf16[256,512]{0,1:T(8,128)(2,1)S(1)}, bf16[256,512]{0,1:T(8,128)(2,1)}, u32[]{:S(2)}) copy-start(bf16[256,512]{0,1:T(8,128)(2,1)} %get-tuple-element.62) | copy-start | bytes 786436
  68.9 27.8 %collective-permute-start.5 = (bf16[512,512]{1,0:T(8,128)(2,1)}, bf16[512,512]{1,0:T(8,128)(2,1)}, u32[]{:S(2)}, u32[]{:S(2)}) collective-permute-start(bf16[512,512]{1,0:T(8,128)(2,1)} %pad_maximum_fusion.2), channel_id=1, source_target_pairs={{4,0},{8,4},{12,8},{16,12},{20,16},{24,20},{28,24},{5,1},{9,5},{13... | collective-permute-start | bytes 1572872 | tf_op jit(solution)/shard_map/ppermute | solution.py:15
  70.5 1.0 copy-start.4
  70.6 1.8 %copy-start.33 = (f32[4,256,256]{2,1,0:T(8,128)S(1)}, f32[4,256,256]{2,1,0:T(8,128)}, u32[]{:S(2)}) copy-start(f32[4,256,256]{2,1,0:T(8,128)} %get-tuple-element.80) | copy-start | bytes 3145732
  75.5 17.9 %all-to-all-start.2 = ((f32[32,1,2048]{2,1,0:T(1,128)}), f32[32,1,2048]{2,1,0:T(1,128)S(1)}, u32[]{:S(2)}, u32[]{:S(2)}) async-start(f32[32,1,2048]{2,1,0:T(1,128)} %bitcast.59), calls=%async_computation.2 | async-start | bytes 524288 | tf_op jit(solution)/shard_map/all_to_all | solution.py:82
  86.4 10.3 %copy-start.2 = (f32[256,512]{1,0:T(8,128)S(1)}, f32[256,512]{1,0:T(8,128)}, u32[]{:S(2)}) copy-start(f32[256,512]{1,0:T(8,128)} %copy.162) | copy-start | bytes 1572868
  93.3 10.7 %all-to-all-start.1 = ((bf16[8,2,4096]{2,1,0:T(2,128)(2,1)}), bf16[8,2,4096]{2,1,0:T(2,128)(2,1)S(1)}, u32[]{:S(2)}, u32[]{:S(2)}) async-start(bf16[8,2,4096]{2,1,0:T(2,128)(2,1)} %reshape.795), calls=%async_computation.1 | async-start | bytes 262144 | tf_op jit(solution)/shard_map/all_to_all | solution.py:85
  104.0 10.8 %all-to-all-start.3 = ((bf16[32,2,1024]{2,1,0:T(2,128)(2,1)}), bf16[32,2,1024]{2,1,0:T(2,128)(2,1)S(1)}, u32[]{:S(2)}, u32[]{:S(2)}) async-start(bf16[32,2,1024]{2,1,0:T(2,128)(2,1)} %reshape.797), calls=%async_computation.3 | async-start | bytes 262144 | tf_op jit(solution)/shard_map/all_to_all | solution.py:85
  (14 other events, 11.7 us)

commit v23 on v21

--- a/solution.py
+++ b/solution.py
@@ -235,8 +235,6 @@
     for distance in (2, 1, 0):
         visible, scores, weights, key_bucket_indicator = tiles[distance]
         pair = slot(window[distance])
-        if distance == 0:
-            sent[2], pair = lax.optimization_barrier((sent[2], pair))
         key_heads = pair[:local_rows].reshape(local_rows, head_count, head_dim)
         value_heads = pair[local_rows:].reshape(local_rows, head_count, head_dim)
         weight_grad = jnp.einsum(

time: 116 us -> 124 us (1.069)
  waiting for transfers between devices: 19.1 us -> 22.6 us
  local copies, waits for them, and re-layouts: 24.6 us -> 27.5 us
  matrix products: 16.7 us -> 18.6 us
  starting transfers between devices: 38.7 us -> 36.9 us
    all_to_all x2, waiting for transfers between devices: 6.25 us -> 10.3 us  [summed_by_exchange(): pieces = lax.all_to_all(flat.reshape(size, -1), axes, 0, 0, tiled=True)]
    mul x3, local copies, waits for them, and re-layouts: 1.47 us -> 2.97 us  [shards(): jnp.einsum('hij,ihd->jhd', score_gradient, query_heads, preferred_element...]
    unnamed x85 -> x93, local copies, waits for them, and re-layouts: 9.6 us -> 11 us
  transfers between devices with their start and end apart: 10 -> 10, of which waited for: 6 -> 6; matrix products, arithmetic and copies ran while one was open for 30% -> 27% of each run, Pallas kernels for 0% -> 0%
where the time goes in v23:
time: 124 us; the launch traced here: 122 us
  starting transfers between devices  36.9 us (30%)
  local copies, waits for them, and re-layouts  27.5 us (22%)
  waiting for transfers between devices  22.6 us (18%)
  matrix products  18.6 us (15%)
  other arithmetic  15.3 us (12%)
  between operations  1.53 us (1%)
    all_to_all x2, starting transfers between devices, summed_by_exchange(): pieces = lax.all_to_all(flat.reshape(size, -1), axes, 0, 0, tiled=True)  18 us
    ppermute x4, starting transfers between devices, passed_along(): return lax.ppermute(value, axis, pairs)  11.3 us
    unnamed x93, local copies, waits for them, and re-layouts  11 us
    all_to_all x2, waiting for transfers between devices, summed_by_exchange(): pieces = lax.all_to_all(flat.reshape(size, -1), axes, 0, 0, tiled=True)  10.3 us
    all_to_all x2, waiting for transfers between devices, summed_by_exchange(): gathered = lax.all_to_all(spread, axes, 0, 0, tiled=True)  9.32 us
    all_to_all x2, starting transfers between devices, summed_by_exchange(): gathered = lax.all_to_all(spread, axes, 0, 0, tiled=True)  6.03 us
    dot_general x3, matrix products, shards(): jnp.einsum('ihd,jhd->hij', query_heads, forward_key_heads, preferred_elem...  3.38 us
    mul x3, local copies, waits for them, and re-layouts, shards(): jnp.einsum('hij,ihd->jhd', score_gradient, query_heads, preferred_element...  2.97 us
  transfers between devices with their start and end apart: 10, of which 6 were waited for; matrix products, arithmetic and copies ran while one was open for 27% of the time, Pallas kernels for 0%

profile of v23, /device:TPU:0, one launch (start us, length us, event | category | flops | bytes accessed | tf_op | source)
XLA Modules:
  0.0 122.4 jit_solution(12471961664130917289)
XLA Ops:
  0.7 1.2 copy.183
  2.8 5.0 %collective-permute-start.1 = (bf16[512,512]{0,1:T(8,128)(2,1)}, bf16[512,512]{0,1:T(8,128)(2,1)S(1)}, u32[]{:S(2)}, u32[]{:S(2)}) collective-permute-start(bf16[512,512]{0,1:T(8,128)(2,1)} %pad_maximum_fusion), channel_id=1, source_target_pairs={{0,8},{4,12},{8,16},{12,20},{16,24},{20,28},{1,9},{5,13},{9,17},{1... | collective-permute-start | bytes 1572872 | tf_op jit(solution)/shard_map/ppermute | solution.py:15
  7.8 3.4 %collective-permute-start = (bf16[512,512]{0,1:T(8,128)(2,1)}, bf16[512,512]{0,1:T(8,128)(2,1)S(1)}, u32[]{:S(2)}, u32[]{:S(2)}) collective-permute-start(bf16[512,512]{0,1:T(8,128)(2,1)} %pad_maximum_fusion), channel_id=1, source_target_pairs={{0,4},{4,8},{8,12},{12,16},{16,20},{20,24},{24,28},{1,5},{5,9},{9,... | collective-permute-start | bytes 1572872 | tf_op jit(solution)/shard_map/ppermute | solution.py:15
  15.8 1.5 %select_convert_fusion.2 = (bf16[4,256,256]{2,1,0:T(8,128)(2,1)S(1)}, f32[4,256,256]{2,1,0:T(8,128)}) fusion(pred[256,256]{1,0:T(8,128)(4,1)S(1)} %copy.133, f32[4,256,256]{2,1,0:T(8,128)S(1)} %convolution_multiply_fusion.5, bf16[4,256,128]{2,1,0:T(8,128)(2,1)S(1)} %fusion.18, s32[256]{0:T(256)S(1)} %bitcast.245), kind=kOutput, calls=%fused_computation.46 | convolution fusion | flops 68976640 | bytes 2950144 | tf_op jit(solution)/shard_map/vqx,px->vqp/dot_general | solution.py:161
  17.2 1.1 convolution_bitcast_fusion.3
  21.9 1.5 %select_convert_fusion = (bf16[4,256,256]{2,1,0:T(8,128)(2,1)S(1)}, f32[4,256,256]{2,1,0:T(8,128)}) fusion(pred[256,256]{1,0:T(8,128)(4,1)S(1)} %copy-done.32, f32[4,256,256]{2,1,0:T(8,128)S(1)} %fusion.47, bf16[256,4,128]{0,2,1:T(8,128)(2,1)S(1)} %bitcast.203, bf16[256,4,128]{0,2,1:T(8,128)(2,1)S(1)} %bitcast.236), kind=kOutput, calls=%fused_computation.42 | convolution fusion | flops 69206016 | bytes 3211264 | tf_op jit(solution)/shard_map/ihd,jhd->hij/dot_general | solution.py:176
  24.6 1.5 %select_convert_fusion.1 = (bf16[4,256,256]{2,1,0:T(8,128)(2,1)S(1)}, f32[4,256,256]{2,1,0:T(8,128)}) fusion(pred[256,256]{1,0:T(8,128)(4,1)S(1)} %copy-done.30, f32[4,256,256]{2,1,0:T(8,128)S(1)} %fusion.43, bf16[256,4,128]{0,2,1:T(8,128)(2,1)S(1)} %bitcast.204, bf16[256,4,128]{0,2,1:T(8,128)(2,1)S(1)} %bitcast.237), kind=kOutput, calls=%fused_computation.44 | convolution fusion | flops 69206016 | bytes 3211264 | tf_op jit(solution)/shard_map/ihd,jhd->hij/dot_general | solution.py:176
  27.2 1.4 %fusion.33 = (f32[256]{0:T(256)S(1)}, f32[256]{0:T(256)S(1)}, f32[256,512]{1,0:T(8,128)S(1)}) fusion(bf16[1,256,512]{2,1,0:T(8,128)(2,1)S(1)} %copy-done.5, f32[256]{0:T(256)S(1)} %add_rsqrt_fusion, f32[256,512]{1,0:T(8,128)S(1)} %copy.151, f32[256]{0:T(256)S(1)} %broadcast_multiply_fusion.2, bf16[512,512]{1,0:T(8,128)(2,1)S(1)} %copy-done, ...), kind=kOutput, calls=%fused_computation.79 | convolution fusion | flops 135134720 | bytes 2101248 | tf_op jit(solution)/shard_map/dot_general | solution.py:194
  28.7 1.0 fusion.21
  29.7 1.1 copy.184
  31.9 0.9 convolution_convert_fusion.1
  36.9 1.0 copy.162
  38.2 1.0 copy.161
  45.9 1.5 %collective-permute-start.3 = (f32[1,65536]{1,0:T(1,128)}, f32[1,65536]{1,0:T(1,128)}, u32[]{:S(2)}, u32[]{:S(2)}) collective-permute-start(f32[1,65536]{1,0:T(1,128)} %constant_dynamic-slice_fusion), channel_id=1, source_target_pairs={{0,2},{1,3},{2,0},{3,1},{4,6},{5,7},{6,4},{7,5},{8,10},{9,11},{10,... | collective-permute-start | bytes 786440 | tf_op jit(solution)/shard_map/ppermute | solution.py:21
  48.3 1.1 copy.169
  50.3 1.6 %collective-permute-start.5 = (bf16[512,512]{1,0:T(8,128)(2,1)}, bf16[512,512]{1,0:T(8,128)(2,1)}, u32[]{:S(2)}, u32[]{:S(2)}) collective-permute-start(bf16[512,512]{1,0:T(8,128)(2,1)} %pad_maximum_fusion.2), channel_id=1, source_target_pairs={{8,0},{12,4},{16,8},{20,12},{24,16},{28,20},{9,1},{13,5},{17,9},{2... | collective-permute-start | bytes 1572872 | tf_op jit(solution)/shard_map/ppermute | solution.py:15
  51.9 2.6 %collective-permute-done.3 = f32[1,65536]{1,0:T(1,128)} collective-permute-done((f32[1,65536]{1,0:T(1,128)}, f32[1,65536]{1,0:T(1,128)}, u32[]{:S(2)}, u32[]{:S(2)}) %collective-permute-start.3) | collective-permute-done | bytes 262176 | tf_op jit(solution)/shard_map/ppermute | solution.py:21
  54.5 2.0 %dynamic-slice_add_fusion = f32[1,65536]{1,0:T(1,128)} fusion(f32[1,65536]{1,0:T(1,128)} %collective-permute-done.3, f32[2,65536]{1,0:T(2,128)S(1)} %bitcast_add_fusion, s32[]{:T(128)S(6)} %select_n.144), kind=kLoop, calls=%fused_computation.70 | loop fusion | flops 65536 | bytes 786436 | tf_op jit(solution)/shard_map/add | solution.py:71
  60.7 13.3 %all-to-all-start = ((f32[8,1,8192]{2,1,0:T(1,128)}), f32[8,1,8192]{2,1,0:T(1,128)S(1)}, u32[]{:S(2)}, u32[]{:S(2)}) async-start(f32[8,1,8192]{2,1,0:T(1,128)} %bitcast.225), calls=%async_computation | async-start | bytes 524288 | tf_op jit(solution)/shard_map/all_to_all | solution.py:82
  76.5 1.3 %collective-permute-start.4 = (bf16[512,512]{1,0:T(8,128)(2,1)}, bf16[512,512]{1,0:T(8,128)(2,1)}, u32[]{:S(2)}, u32[]{:S(2)}) collective-permute-start(bf16[512,512]{1,0:T(8,128)(2,1)} %pad_maximum_fusion.1), channel_id=1, source_target_pairs={{4,0},{8,4},{12,8},{16,12},{20,16},{24,20},{28,24},{5,1},{9,5},{13... | collective-permute-start | bytes 1572872 | tf_op jit(solution)/shard_map/ppermute | solution.py:15
  77.8 1.3 %fusion.26 = f32[4,128,128]{2,1,0:T(8,128)} fusion(f32[4,256,128]{2,1,0:T(8,128)S(1)} %convolution_add_fusion.1, f32[256,128]{0,1:T(8,128)S(1)} %copy.171), kind=kOutput, calls=%fused_computation.68 | convolution fusion | flops 201326592 | bytes 917504 | tf_op jit(solution)/shard_map/cqp,cqk->cpk/dot_general | solution.py:270
  79.4 3.3 %all-to-all-done = f32[8,1,8192]{2,1,0:T(1,128)S(1)} async-done(((f32[8,1,8192]{2,1,0:T(1,128)}), f32[8,1,8192]{2,1,0:T(1,128)S(1)}, u32[]{:S(2)}, u32[]{:S(2)}) %all-to-all-start) | async-done | bytes 262176 | tf_op jit(solution)/shard_map/all_to_all | solution.py:82
  82.7 4.7 %all-to-all-start.2 = ((f32[32,1,2048]{2,1,0:T(1,128)}), f32[32,1,2048]{2,1,0:T(1,128)S(1)}, u32[]{:S(2)}, u32[]{:S(2)}) async-start(f32[32,1,2048]{2,1,0:T(1,128)} %bitcast.57), calls=%async_computation.2 | async-start | bytes 524288 | tf_op jit(solution)/shard_map/all_to_all | solution.py:82
  90.4 1.4 %reduce.6 = bf16[8,8192]{1,0:T(8,128)(2,1)S(1)} reduce(bf16[8,1,8192]{2,1,0:T(2,128)(2,1)S(1)} %broadcast_in_dim.73, bf16[]{:T(256)} %broadcast.591), dimensions={1}, to_apply=%broadcast_in_dim.73.reduce_sub_computation | reduce | bytes 262146 | tf_op jit(solution)/shard_map/broadcast_in_dim | solution.py:84
  92.6 7.0 %all-to-all-done.2 = f32[32,1,2048]{2,1,0:T(1,128)S(1)} async-done(((f32[32,1,2048]{2,1,0:T(1,128)}), f32[32,1,2048]{2,1,0:T(1,128)S(1)}, u32[]{:S(2)}, u32[]{:S(2)}) %all-to-all-start.2) | async-done | bytes 262176 | tf_op jit(solution)/shard_map/all_to_all | solution.py:82
  99.6 3.5 %all-to-all-start.1 = ((bf16[8,2,4096]{2,1,0:T(2,128)(2,1)}), bf16[8,2,4096]{2,1,0:T(2,128)(2,1)S(1)}, u32[]{:S(2)}, u32[]{:S(2)}) async-start(bf16[8,2,4096]{2,1,0:T(2,128)(2,1)} %reshape.788), calls=%async_computation.1 | async-start | bytes 262144 | tf_op jit(solution)/shard_map/all_to_all | solution.py:85
  103.4 1.4 %reduce.7 = bf16[32,2048]{1,0:T(8,128)(2,1)S(1)} reduce(bf16[32,1,2048]{2,1,0:T(2,128)(2,1)S(1)} %broadcast_in_dim.75, bf16[]{:T(256)} %broadcast.591), dimensions={1}, to_apply=%broadcast_in_dim.75.reduce_sub_computation | reduce | bytes 262146 | tf_op jit(solution)/shard_map/broadcast_in_dim | solution.py:84
  105.5 1.4 %fusion.20 = bf16[512,512]{1,0:T(8,128)(2,1)S(1)} fusion(f32[256,512]{1,0:T(8,128)S(1)} %copy-done.6, f32[256,512]{1,0:T(8,128)S(1)} %copy-done.7, bf16[512,512]{1,0:T(8,128)(2,1)} %collective-permute-done.5, bf16[512,512]{1,0:T(8,128)(2,1)} %collective-permute-done.4), kind=kLoop, calls=%fused_computation.41 | loop fusion | flops 1572864 | bytes 2621440 | tf_op jit(solution)/shard_map/convert.5
  106.9 3.6 %all-to-all-done.1 = bf16[8,2,4096]{2,1,0:T(2,128)(2,1)S(1)} async-done(((bf16[8,2,4096]{2,1,0:T(2,128)(2,1)}), bf16[8,2,4096]{2,1,0:T(2,128)(2,1)S(1)}, u32[]{:S(2)}, u32[]{:S(2)}) %all-to-all-start.1) | async-done | bytes 131104 | tf_op jit(solution)/shard_map/all_to_all | solution.py:85
  110.5 2.6 %all-to-all-start.3 = ((bf16[32,2,1024]{2,1,0:T(2,128)(2,1)}), bf16[32,2,1024]{2,1,0:T(2,128)(2,1)S(1)}, u32[]{:S(2)}, u32[]{:S(2)}) async-start(bf16[32,2,1024]{2,1,0:T(2,128)(2,1)} %reshape.790), calls=%async_computation.3 | async-start | bytes 262144 | tf_op jit(solution)/shard_map/all_to_all | solution.py:85
  115.5 5.8 %all-to-all-done.3 = bf16[32,2,1024]{2,1,0:T(2,128)(2,1)S(1)} async-done(((bf16[32,2,1024]{2,1,0:T(2,128)(2,1)}), bf16[32,2,1024]{2,1,0:T(2,128)(2,1)S(1)}, u32[]{:S(2)}, u32[]{:S(2)}) %all-to-all-start.3) | async-done | bytes 131104 | tf_op jit(solution)/shard_map/all_to_all | solution.py:85
  121.4 1.0 convert_element_type.162
  (174 shorter events, 38.9 us)
Async XLA Ops:
  0.6 26.6 %copy-start = (bf16[512,512]{1,0:T(8,128)(2,1)S(1)}, bf16[512,512]{1,0:T(8,128)(2,1)}, u32[]{:S(2)}) copy-start(bf16[512,512]{1,0:T(8,128)(2,1)} %param.19) | copy-start | bytes 1572868
  0.6 1.2 copy-start.17
  1.8 13.6 %copy-start.3 = (bf16[1,256,512]{1,2,0:T(8,128)(2,1)}, bf16[1,256,512]{1,2,0:T(8,128)(2,1)S(1)}, u32[]{:S(2)}) copy-start(bf16[1,256,512]{1,2,0:T(8,128)(2,1)S(1)} %copy.183) | copy-start | bytes 786436
  2.8 18.3 %collective-permute-start.1 = (bf16[512,512]{0,1:T(8,128)(2,1)}, bf16[512,512]{0,1:T(8,128)(2,1)S(1)}, u32[]{:S(2)}, u32[]{:S(2)}) collective-permute-start(bf16[512,512]{0,1:T(8,128)(2,1)} %pad_maximum_fusion), channel_id=1, source_target_pairs={{0,8},{4,12},{8,16},{12,20},{16,24},{20,28},{1,9},{5,13},{9,17},{1... | collective-permute-start | bytes 1572872 | tf_op jit(solution)/shard_map/ppermute | solution.py:15
  7.8 16.0 %collective-permute-start = (bf16[512,512]{0,1:T(8,128)(2,1)}, bf16[512,512]{0,1:T(8,128)(2,1)S(1)}, u32[]{:S(2)}, u32[]{:S(2)}) collective-permute-start(bf16[512,512]{0,1:T(8,128)(2,1)} %pad_maximum_fusion), channel_id=1, source_target_pairs={{0,4},{4,8},{8,12},{12,16},{16,20},{20,24},{24,28},{1,5},{5,9},{9,... | collective-permute-start | bytes 1572872 | tf_op jit(solution)/shard_map/ppermute | solution.py:15
  11.4 1.6 %copy-start.37 = (s32[1,6]{1,0:T(1,128)S(1)}, s32[1,6]{1,0:T(1,128)}, u32[]{:S(2)}) copy-start(s32[1,6]{1,0:T(1,128)} %param.16) | copy-start | bytes 76
  11.5 2.7 %copy-start.26 = (bf16[1,256,512]{2,1,0:T(8,128)(2,1)S(1)}, bf16[1,256,512]{2,1,0:T(8,128)(2,1)}, u32[]{:S(2)}) copy-start(bf16[1,256,512]{2,1,0:T(8,128)(2,1)} %param.10) | copy-start | bytes 786436
  14.2 1.6 %copy-start.28 = (pred[256,256]{1,0:T(8,128)(4,1)}, pred[256,256]{1,0:T(8,128)(4,1)S(1)}, u32[]{:S(2)}) copy-start(pred[256,256]{1,0:T(8,128)(4,1)S(1)} %copy.133) | copy-start | bytes 196612
  17.2 1.1 copy-start.12
  18.5 1.6 %copy-start.5 = (bf16[1,256,512]{2,1,0:T(8,128)(2,1)S(1)}, bf16[1,256,512]{2,1,0:T(8,128)(2,1)}, u32[]{:S(2)}) copy-start(bf16[1,256,512]{2,1,0:T(8,128)(2,1)} %param.13) | copy-start | bytes 786436
  24.6 1.5 %copy-start.14 = (f32[256,4,128]{0,2,1:T(8,128)S(1)}, f32[256,4,128]{0,2,1:T(8,128)}, u32[]{:S(2)}) copy-start(f32[256,4,128]{0,2,1:T(8,128)} %convolution_bitcast_fusion.3) | copy-start | bytes 1572868
  30.8 3.2 %copy-start.1 = (bf16[256,512]{0,1:T(8,128)(2,1)}, bf16[256,512]{0,1:T(8,128)(2,1)S(1)}, u32[]{:S(2)}) copy-start(bf16[256,512]{0,1:T(8,128)(2,1)S(1)} %copy.184) | copy-start | bytes 786436
  30.8 1.1 copy-start.16
  31.9 1.0 copy-start.13
  33.0 1.2 %copy-start.38 = (f32[4,256,256]{2,1,0:T(8,128)S(1)}, f32[4,256,256]{2,1,0:T(8,128)}, u32[]{:S(2)}) copy-start(f32[4,256,256]{2,1,0:T(8,128)} %get-tuple-element.74) | copy-start | bytes 3145732
  41.9 1.0 copy-start.11
  41.9 1.4 %copy-start.40 = (f32[4,256,256]{2,1,0:T(8,128)S(1)}, f32[4,256,256]{2,1,0:T(8,128)}, u32[]{:S(2)}) copy-start(f32[4,256,256]{2,1,0:T(8,128)} %get-tuple-element.72) | copy-start | bytes 3145732
  42.4 1.1 copy-start.2
  42.4 1.1 copy-start.33
  42.4 2.0 %collective-permute-start.2 = (f32[2,65536]{1,0:T(2,128)S(1)}, f32[2,65536]{1,0:T(2,128)S(1)}, u32[]{:S(2)}, u32[]{:S(2)}) collective-permute-start(f32[2,65536]{1,0:T(2,128)S(1)} %bitcast.232), channel_id=1, source_target_pairs={{0,1},{1,0},{2,3},{3,2},{4,5},{5,4},{6,7},{7,6},{8,9},{9,8},{10,11... | collective-permute-start | bytes 1572872 | tf_op jit(solution)/shard_map/ppermute | solution.py:21
  45.9 8.7 %collective-permute-start.3 = (f32[1,65536]{1,0:T(1,128)}, f32[1,65536]{1,0:T(1,128)}, u32[]{:S(2)}, u32[]{:S(2)}) collective-permute-start(f32[1,65536]{1,0:T(1,128)} %constant_dynamic-slice_fusion), channel_id=1, source_target_pairs={{0,2},{1,3},{2,0},{3,1},{4,6},{5,7},{6,4},{7,5},{8,10},{9,11},{10,... | collective-permute-start | bytes 786440 | tf_op jit(solution)/shard_map/ppermute | solution.py:21
  48.3 1.1 copy-start.20
  50.3 6.2 %copy-start.9 = (bf16[512,512]{0,1:T(8,128)(2,1)S(1)}, bf16[512,512]{0,1:T(8,128)(2,1)}, u32[]{:S(2)}) copy-start(bf16[512,512]{0,1:T(8,128)(2,1)} %copy-done.8) | copy-start | bytes 1572868
  50.3 6.3 %copy-start.39 = (f32[4,256,256]{2,1,0:T(8,128)S(1)}, f32[4,256,256]{2,1,0:T(8,128)}, u32[]{:S(2)}) copy-start(f32[4,256,256]{2,1,0:T(8,128)} %get-tuple-element.76) | copy-start | bytes 3145732
  50.3 55.2 %collective-permute-start.5 = (bf16[512,512]{1,0:T(8,128)(2,1)}, bf16[512,512]{1,0:T(8,128)(2,1)}, u32[]{:S(2)}, u32[]{:S(2)}) collective-permute-start(bf16[512,512]{1,0:T(8,128)(2,1)} %pad_maximum_fusion.2), channel_id=1, source_target_pairs={{8,0},{12,4},{16,8},{20,12},{24,16},{28,20},{9,1},{13,5},{17,9},{2... | collective-permute-start | bytes 1572872 | tf_op jit(solution)/shard_map/ppermute | solution.py:15
  60.7 22.0 %all-to-all-start = ((f32[8,1,8192]{2,1,0:T(1,128)}), f32[8,1,8192]{2,1,0:T(1,128)S(1)}, u32[]{:S(2)}, u32[]{:S(2)}) async-start(f32[8,1,8192]{2,1,0:T(1,128)} %bitcast.225), calls=%async_computation | async-start | bytes 524288 | tf_op jit(solution)/shard_map/all_to_all | solution.py:82
  76.5 29.0 %collective-permute-start.4 = (bf16[512,512]{1,0:T(8,128)(2,1)}, bf16[512,512]{1,0:T(8,128)(2,1)}, u32[]{:S(2)}, u32[]{:S(2)}) collective-permute-start(bf16[512,512]{1,0:T(8,128)(2,1)} %pad_maximum_fusion.1), channel_id=1, source_target_pairs={{4,0},{8,4},{12,8},{16,12},{20,16},{24,20},{28,24},{5,1},{9,5},{13... | collective-permute-start | bytes 1572872 | tf_op jit(solution)/shard_map/ppermute | solution.py:15
  82.7 16.8 %all-to-all-start.2 = ((f32[32,1,2048]{2,1,0:T(1,128)}), f32[32,1,2048]{2,1,0:T(1,128)S(1)}, u32[]{:S(2)}, u32[]{:S(2)}) async-start(f32[32,1,2048]{2,1,0:T(1,128)} %bitcast.57), calls=%async_computation.2 | async-start | bytes 524288 | tf_op jit(solution)/shard_map/all_to_all | solution.py:82
  99.6 10.9 %all-to-all-start.1 = ((bf16[8,2,4096]{2,1,0:T(2,128)(2,1)}), bf16[8,2,4096]{2,1,0:T(2,128)(2,1)S(1)}, u32[]{:S(2)}, u32[]{:S(2)}) async-start(bf16[8,2,4096]{2,1,0:T(2,128)(2,1)} %reshape.788), calls=%async_computation.1 | async-start | bytes 262144 | tf_op jit(solution)/shard_map/all_to_all | solution.py:85
  103.0 2.5 %copy-start.7 = (f32[256,512]{1,0:T(8,128)S(1)}, f32[256,512]{1,0:T(8,128)}, u32[]{:S(2)}) copy-start(f32[256,512]{1,0:T(8,128)} %copy.161) | copy-start | bytes 1572868
  103.2 2.3 %copy-start.6 = (f32[256,512]{1,0:T(8,128)S(1)}, f32[256,512]{1,0:T(8,128)}, u32[]{:S(2)}) copy-start(f32[256,512]{1,0:T(8,128)} %copy.162) | copy-start | bytes 1572868
  110.5 10.8 %all-to-all-start.3 = ((bf16[32,2,1024]{2,1,0:T(2,128)(2,1)}), bf16[32,2,1024]{2,1,0:T(2,128)(2,1)S(1)}, u32[]{:S(2)}, u32[]{:S(2)}) async-start(bf16[32,2,1024]{2,1,0:T(2,128)(2,1)} %reshape.790), calls=%async_computation.3 | async-start | bytes 262144 | tf_op jit(solution)/shard_map/all_to_all | solution.py:85
  (19 other events, 16.8 us)

commit v24 on v21

--- a/solution.py
+++ b/solution.py
@@ -277,7 +277,7 @@
     key_grad = gathered[:local_rows].astype(jnp.bfloat16)
     value_grad = gathered[local_rows:].astype(jnp.bfloat16)
     projection_grad = weight_state[0].reshape(width // dp_size, width)
-    table_grad = summed_by_exchange(table_local.reshape(-1), ("ctx", "dp")).reshape(
+    table_grad = summed_by_exchange(table_local.reshape(-1), ("dp", "ctx")).reshape(
         table_local.shape
     )
     return (

time: 116 us -> 116 us (level)
  no operation moved by 1% of the time
where the time goes in v24:
time: 116 us; the launch traced here: 115 us
  starting transfers between devices  38.7 us (33%)
  local copies, waits for them, and re-layouts  24.6 us (21%)
  waiting for transfers between devices  18.6 us (16%)
  matrix products  16.7 us (14%)
  other arithmetic  14.6 us (13%)
  between operations  1.58 us (1%)
    all_to_all x2, starting transfers between devices, summed_by_exchange(): pieces = lax.all_to_all(flat.reshape(size, -1), axes, 0, 0, tiled=True)  19 us
    ppermute x4, starting transfers between devices, passed_along(): return lax.ppermute(value, axis, pairs)  12.1 us
    unnamed x85, local copies, waits for them, and re-layouts  9.6 us
    all_to_all x2, waiting for transfers between devices, summed_by_exchange(): gathered = lax.all_to_all(spread, axes, 0, 0, tiled=True)  8.81 us
    all_to_all x2, waiting for transfers between devices, summed_by_exchange(): pieces = lax.all_to_all(flat.reshape(size, -1), axes, 0, 0, tiled=True)  6.12 us
    all_to_all x2, starting transfers between devices, summed_by_exchange(): gathered = lax.all_to_all(spread, axes, 0, 0, tiled=True)  5.95 us
    ppermute x2, waiting for transfers between devices, exchanged(): return lax.ppermute(value, axis, pairs)  3.65 us
    dot_general x3, matrix products, shards(): jnp.einsum('ihd,jhd->hij', query_heads, forward_key_heads, preferred_elem...  3.38 us
  transfers between devices with their start and end apart: 10, of which 6 were waited for; matrix products, arithmetic and copies ran while one was open for 30% of the time, Pallas kernels for 0%

profile of v24, /device:TPU:0, one launch (start us, length us, event | category | flops | bytes accessed | tf_op | source)
XLA Modules:
  0.0 114.8 jit_solution(17486656881085450730)
XLA Ops:
  0.7 1.2 %copy.177 = bf16[1,256,512]{1,2,0:T(8,128)(2,1)S(1)} copy(bf16[1,256,512]{2,1,0:T(8,128)(2,1)} %param.12) | data formatting | bytes 524288 | tf_op jit(solution)/shard_map/reshape;squeeze | solution.py:174
  2.0 5.8 %collective-permute-start.1 = (bf16[512,512]{0,1:T(8,128)(2,1)S(1)}, bf16[512,512]{0,1:T(8,128)(2,1)}, u32[]{:S(2)}, u32[]{:S(2)}) collective-permute-start(bf16[512,512]{0,1:T(8,128)(2,1)S(1)} %pad_maximum_fusion), channel_id=1, source_target_pairs={{0,8},{4,12},{8,16},{12,20},{16,24},{20,28},{1,9},{5,13},{9,17},{1... | collective-permute-start | bytes 1572872 | tf_op jit(solution)/shard_map/ppermute | solution.py:15
  7.8 3.4 %collective-permute-start = (bf16[512,512]{0,1:T(8,128)(2,1)S(1)}, bf16[512,512]{0,1:T(8,128)(2,1)S(1)}, u32[]{:S(2)}, u32[]{:S(2)}) collective-permute-start(bf16[512,512]{0,1:T(8,128)(2,1)S(1)} %pad_maximum_fusion), channel_id=1, source_target_pairs={{0,4},{4,8},{8,12},{12,16},{16,20},{20,24},{24,28},{1,5},{5,9},{9,... | collective-permute-start | bytes 1572872 | tf_op jit(solution)/shard_map/ppermute | solution.py:15
  15.8 1.5 %select_convert_fusion.2 = (bf16[4,256,256]{2,1,0:T(8,128)(2,1)S(1)}, f32[4,256,256]{2,1,0:T(8,128)}) fusion(pred[256,256]{1,0:T(8,128)(4,1)S(1)} %copy.130, f32[4,256,256]{2,1,0:T(8,128)S(1)} %convolution_multiply_fusion.5, bf16[4,256,128]{2,1,0:T(8,128)(2,1)S(1)} %fusion.16, s32[256]{0:T(256)S(1)} %bitcast.251), kind=kOutput, calls=%fused_computation.44 | convolution fusion | flops 68976640 | bytes 2950144 | tf_op jit(solution)/shard_map/vqx,px->vqp/dot_general | solution.py:161
  17.3 1.1 convolution_bitcast_fusion.2
  20.4 1.1 fusion.67
  21.5 1.5 %select_convert_fusion = (bf16[4,256,256]{2,1,0:T(8,128)(2,1)S(1)}, f32[4,256,256]{2,1,0:T(8,128)}) fusion(pred[256,256]{1,0:T(8,128)(4,1)S(1)} %copy.143, f32[4,256,256]{2,1,0:T(8,128)S(1)} %fusion.50, bf16[256,4,128]{0,2,1:T(8,128)(2,1)S(1)} %bitcast.212, bf16[256,4,128]{0,2,1:T(8,128)(2,1)S(1)} %bitcast.242), kind=kOutput, calls=%fused_computation.40 | convolution fusion | flops 69206016 | bytes 3211264 | tf_op jit(solution)/shard_map/ihd,jhd->hij/dot_general | solution.py:176
  24.6 1.5 %select_convert_fusion.1 = (bf16[4,256,256]{2,1,0:T(8,128)(2,1)S(1)}, f32[4,256,256]{2,1,0:T(8,128)}) fusion(pred[256,256]{1,0:T(8,128)(4,1)S(1)} %copy.138, f32[4,256,256]{2,1,0:T(8,128)S(1)} %fusion.46, bf16[256,4,128]{0,2,1:T(8,128)(2,1)S(1)} %bitcast.213, bf16[256,4,128]{0,2,1:T(8,128)(2,1)S(1)} %bitcast.243), kind=kOutput, calls=%fused_computation.42 | convolution fusion | flops 69206016 | bytes 3211264 | tf_op jit(solution)/shard_map/ihd,jhd->hij/dot_general | solution.py:176
  30.7 0.9 convolution_convert_fusion.1
  32.1 1.0 copy.162
  38.3 1.1 fusion.64
  41.0 1.6 %collective-permute-start.3 = (f32[1,65536]{1,0:T(1,128)S(1)}, f32[1,65536]{1,0:T(1,128)}, u32[]{:S(2)}, u32[]{:S(2)}) collective-permute-start(f32[1,65536]{1,0:T(1,128)S(1)} %constant_dynamic-slice_fusion), channel_id=1, source_target_pairs={{0,2},{1,3},{2,0},{3,1},{4,6},{5,7},{6,4},{7,5},{8,10},{9,11},{10,... | collective-permute-start | bytes 786440 | tf_op jit(solution)/shard_map/ppermute | solution.py:21
  44.6 1.6 %collective-permute-start.4 = (bf16[512,512]{1,0:T(8,128)(2,1)}, bf16[512,512]{1,0:T(8,128)(2,1)}, u32[]{:S(2)}, u32[]{:S(2)}) collective-permute-start(bf16[512,512]{1,0:T(8,128)(2,1)} %pad_maximum_fusion.1), channel_id=1, source_target_pairs={{8,0},{12,4},{16,8},{20,12},{24,16},{28,20},{9,1},{13,5},{17,9},{2... | collective-permute-start | bytes 1572872 | tf_op jit(solution)/shard_map/ppermute | solution.py:15
  46.2 3.4 %collective-permute-done.3 = f32[1,65536]{1,0:T(1,128)} collective-permute-done((f32[1,65536]{1,0:T(1,128)S(1)}, f32[1,65536]{1,0:T(1,128)}, u32[]{:S(2)}, u32[]{:S(2)}) %collective-permute-start.3) | collective-permute-done | bytes 262176 | tf_op jit(solution)/shard_map/ppermute | solution.py:21
  49.6 2.0 %dynamic-slice_add_fusion = f32[1,65536]{1,0:T(1,128)} fusion(f32[1,65536]{1,0:T(1,128)} %collective-permute-done.3, f32[2,65536]{1,0:T(2,128)S(1)} %bitcast_add_fusion, s32[]{:T(128)S(6)} %select_n.144), kind=kLoop, calls=%fused_computation.72 | loop fusion | flops 65536 | bytes 786436 | tf_op jit(solution)/shard_map/add | solution.py:71
  53.0 0.9 fusion.15
  54.3 12.3 %all-to-all-start = ((f32[8,1,8192]{2,1,0:T(1,128)}), f32[8,1,8192]{2,1,0:T(1,128)}, u32[]{:S(2)}, u32[]{:S(2)}) async-start(f32[8,1,8192]{2,1,0:T(1,128)} %bitcast.58), calls=%async_computation | async-start | bytes 524288 | tf_op jit(solution)/shard_map/all_to_all | solution.py:82
  66.9 1.1 copy.165
  68.9 1.3 %collective-permute-start.5 = (bf16[512,512]{1,0:T(8,128)(2,1)}, bf16[512,512]{1,0:T(8,128)(2,1)}, u32[]{:S(2)}, u32[]{:S(2)}) collective-permute-start(bf16[512,512]{1,0:T(8,128)(2,1)} %pad_maximum_fusion.2), channel_id=1, source_target_pairs={{4,0},{8,4},{12,8},{16,12},{20,16},{24,20},{28,24},{5,1},{9,5},{13... | collective-permute-start | bytes 1572872 | tf_op jit(solution)/shard_map/ppermute | solution.py:15
  72.9 1.3 %fusion.28 = f32[4,128,128]{2,1,0:T(8,128)} fusion(f32[4,256,128]{2,1,0:T(8,128)S(1)} %convolution_add_fusion.1, f32[256,128]{0,1:T(8,128)S(1)} %copy.167), kind=kOutput, calls=%fused_computation.70 | convolution fusion | flops 201326592 | bytes 917504 | tf_op jit(solution)/shard_map/cqp,cqk->cpk/dot_general | solution.py:272
  74.2 1.3 %all-to-all-done = f32[8,1,8192]{2,1,0:T(1,128)} async-done(((f32[8,1,8192]{2,1,0:T(1,128)}), f32[8,1,8192]{2,1,0:T(1,128)}, u32[]{:S(2)}, u32[]{:S(2)}) %all-to-all-start) | async-done | bytes 262176 | tf_op jit(solution)/shard_map/all_to_all | solution.py:82
  75.5 6.7 %all-to-all-start.2 = ((f32[32,1,2048]{2,1,0:T(1,128)}), f32[32,1,2048]{2,1,0:T(1,128)S(1)}, u32[]{:S(2)}, u32[]{:S(2)}) async-start(f32[32,1,2048]{2,1,0:T(1,128)} %bitcast.59), calls=%async_computation.2 | async-start | bytes 524288 | tf_op jit(solution)/shard_map/all_to_all | solution.py:82
  83.8 1.2 %reduce_sum.92 = bf16[8192]{0:T(1024)(128)(2,1)S(1)} reduce(f32[8,1,8192]{2,1,0:T(1,128)} %all-to-all-done, f32[]{:T(128)} %constant.214.clone.1), dimensions={0,1}, to_apply=%region_8.9 | reduce | flops 57344 | bytes 278532 | tf_op jit(solution)/shard_map/reduce_sum | solution.py:83
  85.7 1.4 %reduce.6 = bf16[8,8192]{1,0:T(8,128)(2,1)S(1)} reduce(bf16[8,1,8192]{2,1,0:T(2,128)(2,1)S(1)} %broadcast_in_dim.73, bf16[]{:T(256)} %broadcast.593), dimensions={1}, to_apply=%broadcast_in_dim.73.reduce_sub_computation | reduce | bytes 262146 | tf_op jit(solution)/shard_map/broadcast_in_dim | solution.py:84
  87.8 4.9 %all-to-all-done.2 = f32[32,1,2048]{2,1,0:T(1,128)S(1)} async-done(((f32[32,1,2048]{2,1,0:T(1,128)}), f32[32,1,2048]{2,1,0:T(1,128)S(1)}, u32[]{:S(2)}, u32[]{:S(2)}) %all-to-all-start.2) | async-done | bytes 262176 | tf_op jit(solution)/shard_map/all_to_all | solution.py:82
  92.7 3.4 %all-to-all-start.1 = ((bf16[8,2,4096]{2,1,0:T(2,128)(2,1)}), bf16[8,2,4096]{2,1,0:T(2,128)(2,1)S(1)}, u32[]{:S(2)}, u32[]{:S(2)}) async-start(bf16[8,2,4096]{2,1,0:T(2,128)(2,1)} %reshape.796), calls=%async_computation.1 | async-start | bytes 262144 | tf_op jit(solution)/shard_map/all_to_all | solution.py:85
  96.1 1.4 %fusion.18 = bf16[512,512]{1,0:T(8,128)(2,1)S(1)} fusion(f32[256,512]{1,0:T(8,128)S(1)} %copy-done.2, f32[256,512]{1,0:T(8,128)S(1)} %copy.161, bf16[512,512]{1,0:T(8,128)(2,1)} %collective-permute-done.4, bf16[512,512]{1,0:T(8,128)(2,1)} %collective-permute-done.5), kind=kLoop, calls=%fused_computation.39 | loop fusion | flops 1572864 | bytes 2621440 | tf_op jit(solution)/shard_map/convert.5
  97.8 1.4 %reduce.7 = bf16[32,2048]{1,0:T(8,128)(2,1)S(1)} reduce(bf16[32,1,2048]{2,1,0:T(2,128)(2,1)S(1)} %broadcast_in_dim.75, bf16[]{:T(256)} %broadcast.593), dimensions={1}, to_apply=%broadcast_in_dim.75.reduce_sub_computation | reduce | bytes 262146 | tf_op jit(solution)/shard_map/broadcast_in_dim | solution.py:84
  99.9 3.4 %all-to-all-done.1 = bf16[8,2,4096]{2,1,0:T(2,128)(2,1)S(1)} async-done(((bf16[8,2,4096]{2,1,0:T(2,128)(2,1)}), bf16[8,2,4096]{2,1,0:T(2,128)(2,1)S(1)}, u32[]{:S(2)}, u32[]{:S(2)}) %all-to-all-start.1) | async-done | bytes 131104 | tf_op jit(solution)/shard_map/all_to_all | solution.py:85
  103.4 2.6 %all-to-all-start.3 = ((bf16[32,2,1024]{2,1,0:T(2,128)(2,1)}), bf16[32,2,1024]{2,1,0:T(2,128)(2,1)S(1)}, u32[]{:S(2)}, u32[]{:S(2)}) async-start(bf16[32,2,1024]{2,1,0:T(2,128)(2,1)} %reshape.798), calls=%async_computation.3 | async-start | bytes 262144 | tf_op jit(solution)/shard_map/all_to_all | solution.py:85
  108.4 5.4 %all-to-all-done.3 = bf16[32,2,1024]{2,1,0:T(2,128)(2,1)S(1)} async-done(((bf16[32,2,1024]{2,1,0:T(2,128)(2,1)}), bf16[32,2,1024]{2,1,0:T(2,128)(2,1)S(1)}, u32[]{:S(2)}, u32[]{:S(2)}) %all-to-all-start.3) | async-done | bytes 131104 | tf_op jit(solution)/shard_map/all_to_all | solution.py:85
  113.9 1.0 convert_element_type.159
  (167 shorter events, 33.8 us)
Async XLA Ops:
  0.6 26.2 %copy-start = (bf16[512,512]{1,0:T(8,128)(2,1)S(1)}, bf16[512,512]{1,0:T(8,128)(2,1)}, u32[]{:S(2)}) copy-start(bf16[512,512]{1,0:T(8,128)(2,1)} %param.19) | copy-start | bytes 1572868
  0.6 1.2 %copy-start.14 = (bf16[1,256,512]{2,1,0:T(8,128)(2,1)S(1)}, bf16[1,256,512]{2,1,0:T(8,128)(2,1)}, u32[]{:S(2)}) copy-start(bf16[1,256,512]{2,1,0:T(8,128)(2,1)} %param.11) | copy-start | bytes 786436
  2.0 12.1 %copy-start.3 = (bf16[512,512]{0,1:T(8,128)(2,1)}, bf16[512,512]{0,1:T(8,128)(2,1)S(1)}, u32[]{:S(2)}) copy-start(bf16[512,512]{0,1:T(8,128)(2,1)S(1)} %pad_maximum_fusion) | copy-start | bytes 1572868
  2.0 18.4 %collective-permute-start.1 = (bf16[512,512]{0,1:T(8,128)(2,1)S(1)}, bf16[512,512]{0,1:T(8,128)(2,1)}, u32[]{:S(2)}, u32[]{:S(2)}) collective-permute-start(bf16[512,512]{0,1:T(8,128)(2,1)S(1)} %pad_maximum_fusion), channel_id=1, source_target_pairs={{0,8},{4,12},{8,16},{12,20},{16,24},{20,28},{1,9},{5,13},{9,17},{1... | collective-permute-start | bytes 1572872 | tf_op jit(solution)/shard_map/ppermute | solution.py:15
  7.8 16.0 %collective-permute-start = (bf16[512,512]{0,1:T(8,128)(2,1)S(1)}, bf16[512,512]{0,1:T(8,128)(2,1)S(1)}, u32[]{:S(2)}, u32[]{:S(2)}) collective-permute-start(bf16[512,512]{0,1:T(8,128)(2,1)S(1)} %pad_maximum_fusion), channel_id=1, source_target_pairs={{0,4},{4,8},{8,12},{12,16},{16,20},{20,24},{24,28},{1,5},{5,9},{9,... | collective-permute-start | bytes 1572872 | tf_op jit(solution)/shard_map/ppermute | solution.py:15
  11.4 1.6 %copy-start.33 = (s32[1,6]{1,0:T(1,128)S(1)}, s32[1,6]{1,0:T(1,128)}, u32[]{:S(2)}) copy-start(s32[1,6]{1,0:T(1,128)} %param.16) | copy-start | bytes 76
  11.5 2.7 %copy-start.22 = (bf16[1,256,512]{2,1,0:T(8,128)(2,1)S(1)}, bf16[1,256,512]{2,1,0:T(8,128)(2,1)}, u32[]{:S(2)}) copy-start(bf16[1,256,512]{2,1,0:T(8,128)(2,1)} %param.10) | copy-start | bytes 786436
  14.2 1.6 %copy-start.24 = (pred[256,256]{1,0:T(8,128)(4,1)}, pred[256,256]{1,0:T(8,128)(4,1)S(1)}, u32[]{:S(2)}) copy-start(pred[256,256]{1,0:T(8,128)(4,1)S(1)} %copy.130) | copy-start | bytes 196612
  17.3 1.1 copy-start.7
  18.8 5.8 %copy-start.26 = (pred[256,256]{1,0:T(8,128)(4,1)}, pred[256,256]{1,0:T(8,128)(4,1)S(1)}, u32[]{:S(2)}) copy-start(pred[256,256]{1,0:T(8,128)(4,1)S(1)} %copy.138) | copy-start | bytes 196612
  19.5 2.0 %copy-start.28 = (pred[256,256]{1,0:T(8,128)(4,1)}, pred[256,256]{1,0:T(8,128)(4,1)S(1)}, u32[]{:S(2)}) copy-start(pred[256,256]{1,0:T(8,128)(4,1)S(1)} %copy.143) | copy-start | bytes 196612
  24.6 1.5 %copy-start.11 = (f32[256,4,128]{0,2,1:T(8,128)S(1)}, f32[256,4,128]{0,2,1:T(8,128)}, u32[]{:S(2)}) copy-start(f32[256,4,128]{0,2,1:T(8,128)} %convolution_bitcast_fusion.2) | copy-start | bytes 1572868
  29.7 1.0 copy-start.10
  37.7 1.6 %copy-start.36 = (f32[4,256,256]{2,1,0:T(8,128)S(1)}, f32[4,256,256]{2,1,0:T(8,128)}, u32[]{:S(2)}) copy-start(f32[4,256,256]{2,1,0:T(8,128)} %get-tuple-element.78) | copy-start | bytes 3145732
  38.2 1.2 %copy-start.13 = (bf16[256,512]{1,0:T(8,128)(2,1)S(1)}, bf16[256,512]{1,0:T(8,128)(2,1)}, u32[]{:S(2)}) copy-start(bf16[256,512]{1,0:T(8,128)(2,1)} %copy-done.12) | copy-start | bytes 786436
  38.2 1.2 %copy-start.29 = (pred[256,256]{1,0:T(8,128)(4,1)S(1)}, pred[256,256]{1,0:T(8,128)(4,1)}, u32[]{:S(2)}) copy-start(pred[256,256]{1,0:T(8,128)(4,1)} %copy-done.28) | copy-start | bytes 196612
  38.2 2.0 %collective-permute-start.2 = (f32[2,65536]{1,0:T(2,128)S(1)}, f32[2,65536]{1,0:T(2,128)S(1)}, u32[]{:S(2)}, u32[]{:S(2)}) collective-permute-start(f32[2,65536]{1,0:T(2,128)S(1)} %bitcast.237), channel_id=1, source_target_pairs={{0,1},{1,0},{2,3},{3,2},{4,5},{5,4},{6,7},{7,6},{8,9},{9,8},{10,11... | collective-permute-start | bytes 1572872 | tf_op jit(solution)/shard_map/ppermute | solution.py:21
  41.0 8.6 %collective-permute-start.3 = (f32[1,65536]{1,0:T(1,128)S(1)}, f32[1,65536]{1,0:T(1,128)}, u32[]{:S(2)}, u32[]{:S(2)}) collective-permute-start(f32[1,65536]{1,0:T(1,128)S(1)} %constant_dynamic-slice_fusion), channel_id=1, source_target_pairs={{0,2},{1,3},{2,0},{3,1},{4,6},{5,7},{6,4},{7,5},{8,10},{9,11},{10,... | collective-permute-start | bytes 786440 | tf_op jit(solution)/shard_map/ppermute | solution.py:21
  44.6 7.0 %copy-start.6 = (bf16[512,512]{0,1:T(8,128)(2,1)S(1)}, bf16[512,512]{0,1:T(8,128)(2,1)}, u32[]{:S(2)}) copy-start(bf16[512,512]{0,1:T(8,128)(2,1)} %copy-done.5) | copy-start | bytes 1572868
  44.6 7.7 %copy-start.35 = (f32[4,256,256]{2,1,0:T(8,128)S(1)}, f32[4,256,256]{2,1,0:T(8,128)}, u32[]{:S(2)}) copy-start(f32[4,256,256]{2,1,0:T(8,128)} %get-tuple-element.82) | copy-start | bytes 3145732
  44.6 26.3 %collective-permute-start.4 = (bf16[512,512]{1,0:T(8,128)(2,1)}, bf16[512,512]{1,0:T(8,128)(2,1)}, u32[]{:S(2)}, u32[]{:S(2)}) collective-permute-start(bf16[512,512]{1,0:T(8,128)(2,1)} %pad_maximum_fusion.1), channel_id=1, source_target_pairs={{8,0},{12,4},{16,8},{20,12},{24,16},{28,20},{9,1},{13,5},{17,9},{2... | collective-permute-start | bytes 1572872 | tf_op jit(solution)/shard_map/ppermute | solution.py:15
  54.3 21.2 %all-to-all-start = ((f32[8,1,8192]{2,1,0:T(1,128)}), f32[8,1,8192]{2,1,0:T(1,128)}, u32[]{:S(2)}, u32[]{:S(2)}) async-start(f32[8,1,8192]{2,1,0:T(1,128)} %bitcast.58), calls=%async_computation | async-start | bytes 524288 | tf_op jit(solution)/shard_map/all_to_all | solution.py:82
  66.9 1.2 %copy-start.16 = (bf16[256,512]{1,0:T(8,128)(2,1)S(1)}, bf16[256,512]{1,0:T(8,128)(2,1)}, u32[]{:S(2)}) copy-start(bf16[256,512]{1,0:T(8,128)(2,1)} %copy.166) | copy-start | bytes 786436
  68.1 2.1 %copy-start.15 = (bf16[256,512]{0,1:T(8,128)(2,1)S(1)}, bf16[256,512]{0,1:T(8,128)(2,1)}, u32[]{:S(2)}) copy-start(bf16[256,512]{0,1:T(8,128)(2,1)} %get-tuple-element.62) | copy-start | bytes 786436
  68.9 27.1 %collective-permute-start.5 = (bf16[512,512]{1,0:T(8,128)(2,1)}, bf16[512,512]{1,0:T(8,128)(2,1)}, u32[]{:S(2)}, u32[]{:S(2)}) collective-permute-start(bf16[512,512]{1,0:T(8,128)(2,1)} %pad_maximum_fusion.2), channel_id=1, source_target_pairs={{4,0},{8,4},{12,8},{16,12},{20,16},{24,20},{28,24},{5,1},{9,5},{13... | collective-permute-start | bytes 1572872 | tf_op jit(solution)/shard_map/ppermute | solution.py:15
  70.5 1.0 copy-start.4
  70.6 1.4 %copy-start.34 = (f32[4,256,256]{2,1,0:T(8,128)S(1)}, f32[4,256,256]{2,1,0:T(8,128)}, u32[]{:S(2)}) copy-start(f32[4,256,256]{2,1,0:T(8,128)} %get-tuple-element.80) | copy-start | bytes 3145732
  70.9 1.1 copy-start.25
  75.5 17.2 %all-to-all-start.2 = ((f32[32,1,2048]{2,1,0:T(1,128)}), f32[32,1,2048]{2,1,0:T(1,128)S(1)}, u32[]{:S(2)}, u32[]{:S(2)}) async-start(f32[32,1,2048]{2,1,0:T(1,128)} %bitcast.59), calls=%async_computation.2 | async-start | bytes 524288 | tf_op jit(solution)/shard_map/all_to_all | solution.py:82
  85.1 10.9 %copy-start.2 = (f32[256,512]{1,0:T(8,128)S(1)}, f32[256,512]{1,0:T(8,128)}, u32[]{:S(2)}) copy-start(f32[256,512]{1,0:T(8,128)} %copy.162) | copy-start | bytes 1572868
  92.7 10.7 %all-to-all-start.1 = ((bf16[8,2,4096]{2,1,0:T(2,128)(2,1)}), bf16[8,2,4096]{2,1,0:T(2,128)(2,1)S(1)}, u32[]{:S(2)}, u32[]{:S(2)}) async-start(bf16[8,2,4096]{2,1,0:T(2,128)(2,1)} %reshape.796), calls=%async_computation.1 | async-start | bytes 262144 | tf_op jit(solution)/shard_map/all_to_all | solution.py:85
  103.4 10.4 %all-to-all-start.3 = ((bf16[32,2,1024]{2,1,0:T(2,128)(2,1)}), bf16[32,2,1024]{2,1,0:T(2,128)(2,1)S(1)}, u32[]{:S(2)}, u32[]{:S(2)}) async-start(bf16[32,2,1024]{2,1,0:T(2,128)(2,1)} %reshape.798), calls=%async_computation.3 | async-start | bytes 262144 | tf_op jit(solution)/shard_map/all_to_all | solution.py:85
  (15 other events, 13.0 us)
